TPU v7x, 32 devices: a whole 2x2x4 slice. The times are simulated.
32 devices in a mesh: blk: 8 (over y, x, core), xfer: 4 (over z).
Axes of the slice: x: 2, y: 2, z: 4, core: 2. Of those that a mesh axis runs over, the one named last changes fastest.
Arguments:
- greens: bfloat16 [8, 2, 256, 256], P('blk'), may hold values from -6 to 6
- transfer_index: int32 [64, 256], P(('blk', 'xfer')), may hold values from 0 to 255, as said below
- phase_index: int32 [64, 256], P(('blk', 'xfer')), may hold values from 0 to 7
- partner_slot: int32 [64], P(('blk', 'xfer')), may hold values from 0 to 1, as said below
- conj_index: int32 [256], replicated, may hold values from 0 to 255, as said below
Outputs:
- four_point: float32 [64, 2, 256, 256], P(('blk', 'xfer'))
Inputs may be any that keep to these rules, and one draw needn't show every extreme that they name: `transfer_index`: each row is a permutation: the momentum-frequency shifted by the row's transfer, momenta on a periodic 4 x 4 cluster and frequencies cyclic over 16. `conj_index`: an involution: the index of the negated momentum and the mirrored frequency. `partner_slot`: the pairing is mutual: if transfer q in slot s has partner slot t on the partner device, the transfer in slot t there has partner slot s.
All inputs are finite; a program needn't handle non-finite values.
Results may differ from a plain program's by a relative error of at most 0.0003.
Values may be sent and summed in bfloat16 or wider, within the bound.
No kernel may reach another device: no remote copies, remote signals or barrier semaphores. Data moves between devices by JAX's collectives and lax.ppermute only.
A program may use at most 64 MiB of HBM per device.

v0:
```python
import math

import jax
import jax.numpy as jnp
from jax import lax
from jax.sharding import PartitionSpec as P

NPH = 8


def passed_along(value, axis, by):
    size = lax.axis_size(axis)
    return lax.ppermute(value, axis, [(i, (i + by) % size) for i in range(size)])


def rotations(phase_rows):
    angle = (
        2.0 * math.pi / NPH * (phase_rows[:, :, None] - phase_rows[:, None, :]).astype(jnp.float32)
    )
    return (jnp.cos(angle), jnp.sin(angle))


def selectors(index_rows, width):
    columns = jnp.arange(width, dtype=jnp.int32)
    return (columns[None, :, None] == index_rows[:, None, :]).astype(jnp.bfloat16)


def turned(total, cosines, sines):
    real = cosines * total[:, 0] - sines * total[:, 1]
    imag = cosines * total[:, 1] + sines * total[:, 0]
    return jnp.stack([real, imag], axis=1)


def mirrored(slices, conj_index):
    flipped = jnp.swapaxes(jnp.take(jnp.take(slices, conj_index, axis=2), conj_index, axis=3), 2, 3)
    return jnp.stack([flipped[:, 0], -flipped[:, 1]], axis=1)


def crossed(total, block, index_rows, picking):
    flipped = jnp.swapaxes(block, 1, 2)
    chosen = jnp.take(flipped, index_rows, axis=1)
    moved = jnp.einsum("csaj,sjb->csab", chosen, picking, preferred_element_type=jnp.float32)
    block_real = block[0].astype(jnp.float32)
    block_imag = block[1].astype(jnp.float32)
    real = block_real * moved[0] - block_imag * moved[1]
    imag = block_real * moved[1] + block_imag * moved[0]
    return total + jnp.stack([real, imag], axis=1)


def local(greens, transfer_index, phase_index, partner_slot, conj_index):
    slots = transfer_index.shape[0]
    width = greens.shape[-1]
    blocks = lax.axis_size("blk")
    groups = lax.axis_size("xfer")
    halfway = groups // 2
    scale = 0.5 / math.sqrt(blocks)
    cosines, sines = rotations(phase_index)
    picking = selectors(transfer_index, width)
    empty = jnp.zeros((slots, 2, width, width), jnp.float32)

    def visit(running, block):
        return (crossed(running, block, transfer_index, picking), None)

    sums = lax.scan(visit, empty, lax.all_gather(greens, "blk", axis=0, tiled=True))[0]
    sums = turned(sums, cosines, sines)
    partner = passed_along(sums, "xfer", halfway)
    mirror = jnp.take(partner, partner_slot, axis=0)
    return (sums + mirrored(mirror, conj_index)) * scale


def solution(mesh):
    in_specs = (
        P("blk", None, None, None),
        P(("blk", "xfer"), None),
        P(("blk", "xfer"), None),
        P(("blk", "xfer")),
        P(),
    )
    out_specs = P(("blk", "xfer"), None, None, None)
    return jax.shard_map(local, mesh=mesh, in_specs=in_specs, out_specs=out_specs, check_vma=False)
```

profile of v0, /device:TPU:0, one launch (start us, length us, event | category | flops | bytes accessed | tf_op | source)
XLA Modules:
  0.0 156.7 jit_solution(5556600198563763163)
XLA Ops:
  6.5 0.7 all-gather.2.cloned.1.call-update
  7.3 32.6 %all-gather.2.cloned.1.call-done = bf16[8,2,256,256]{3,2,1,0:T(8,128)(2,1)} async-done(((bf16[1,2,256,256]{3,2,1,0:T(8,128)(2,1)}), bf16[8,2,256,256]{3,2,1,0:T(8,128)(2,1)}) %all-gather.2.cloned.1.call-update) | async-done | bytes 2097168 | tf_op jit(solution)/shard_map/all_gather | solution.py:64
  39.9 51.2 %while.13 = (s32[]{:T(128)}, f32[2,2,256,256]{3,2,0,1:T(8,128)S(1)}, bf16[8,2,256,256]{3,2,1,0:T(8,128)(2,1)}, s32[2,256]{1,0:T(2,128)}, s32[]{:T(128)}, /*index=5*/s32[]{:T(128)}, s32[]{}) while((s32[]{:T(128)}, f32[2,2,256,256]{3,2,0,1:T(8,128)S(1)}, bf16[8,2,256,256]{3,2,1,0:T(8,128)(2,1)}, ...), condition=%wide.region_1.2_spmd.clone.clone.clone, body=%wide.region_0.1_spmd.clone.clone.clone.sunk | while | flops 136451584 | bytes 11302027 | solution.py:64
  39.9 1.0 constant_dynamic-slice_fusion.2
  41.1 0.7 fusion.23
  41.8 2.6 %gather_fusion = bf16[512,2,256]{2,1,0:T(2,128)(2,1)S(1)} fusion(bf16[2,256,256]{2,0,1:T(2,128)(2,1)S(1)} %bitcast.71, s32[1024]{0:T(1024)S(1)} %pad_clamp_fusion.4), kind=kCustom, calls=%fused_computation.clone.clone.clone.clone.1 | custom fusion | bytes 1050624 | tf_op jit(solution)/shard_map/while/body/eval_jaxpr/jit(_take)/gather | solution.py:41
  44.4 0.4 convolution_bitcast_fusion.2
  44.8 1.0 fusion.24
  46.0 0.3 maximum_add_fusion.3
  46.3 1.0 constant_dynamic-slice_fusion.2
  47.3 0.2 copy.56
  47.5 0.7 fusion.23
  48.2 2.6 %gather_fusion = bf16[512,2,256]{2,1,0:T(2,128)(2,1)S(1)} fusion(bf16[2,256,256]{2,0,1:T(2,128)(2,1)S(1)} %bitcast.71, s32[1024]{0:T(1024)S(1)} %pad_clamp_fusion.4), kind=kCustom, calls=%fused_computation.clone.clone.clone.clone.1 | custom fusion | bytes 1050624 | tf_op jit(solution)/shard_map/while/body/eval_jaxpr/jit(_take)/gather | solution.py:41
  50.8 0.4 convolution_bitcast_fusion.2
  51.2 1.0 fusion.24
  52.4 0.3 maximum_add_fusion.3
  52.7 1.0 constant_dynamic-slice_fusion.2
  53.9 0.7 fusion.23
  54.6 2.6 %gather_fusion = bf16[512,2,256]{2,1,0:T(2,128)(2,1)S(1)} fusion(bf16[2,256,256]{2,0,1:T(2,128)(2,1)S(1)} %bitcast.71, s32[1024]{0:T(1024)S(1)} %pad_clamp_fusion.4), kind=kCustom, calls=%fused_computation.clone.clone.clone.clone.1 | custom fusion | bytes 1050624 | tf_op jit(solution)/shard_map/while/body/eval_jaxpr/jit(_take)/gather | solution.py:41
  57.3 0.4 convolution_bitcast_fusion.2
  57.6 1.0 fusion.24
  58.8 0.3 maximum_add_fusion.3
  59.1 1.0 constant_dynamic-slice_fusion.2
  60.1 0.2 copy.56
  60.3 0.7 fusion.23
  61.0 2.6 %gather_fusion = bf16[512,2,256]{2,1,0:T(2,128)(2,1)S(1)} fusion(bf16[2,256,256]{2,0,1:T(2,128)(2,1)S(1)} %bitcast.71, s32[1024]{0:T(1024)S(1)} %pad_clamp_fusion.4), kind=kCustom, calls=%fused_computation.clone.clone.clone.clone.1 | custom fusion | bytes 1050624 | tf_op jit(solution)/shard_map/while/body/eval_jaxpr/jit(_take)/gather | solution.py:41
  63.7 0.4 convolution_bitcast_fusion.2
  64.0 1.0 fusion.24
  65.2 0.3 maximum_add_fusion.3
  65.5 1.0 constant_dynamic-slice_fusion.2
  66.7 0.7 fusion.23
  67.4 2.6 %gather_fusion = bf16[512,2,256]{2,1,0:T(2,128)(2,1)S(1)} fusion(bf16[2,256,256]{2,0,1:T(2,128)(2,1)S(1)} %bitcast.71, s32[1024]{0:T(1024)S(1)} %pad_clamp_fusion.4), kind=kCustom, calls=%fused_computation.clone.clone.clone.clone.1 | custom fusion | bytes 1050624 | tf_op jit(solution)/shard_map/while/body/eval_jaxpr/jit(_take)/gather | solution.py:41
  70.1 0.4 convolution_bitcast_fusion.2
  70.4 1.0 fusion.24
  71.6 0.3 maximum_add_fusion.3
  71.9 1.0 constant_dynamic-slice_fusion.2
  73.1 0.7 fusion.23
  73.8 2.6 %gather_fusion = bf16[512,2,256]{2,1,0:T(2,128)(2,1)S(1)} fusion(bf16[2,256,256]{2,0,1:T(2,128)(2,1)S(1)} %bitcast.71, s32[1024]{0:T(1024)S(1)} %pad_clamp_fusion.4), kind=kCustom, calls=%fused_computation.clone.clone.clone.clone.1 | custom fusion | bytes 1050624 | tf_op jit(solution)/shard_map/while/body/eval_jaxpr/jit(_take)/gather | solution.py:41
  76.5 0.4 convolution_bitcast_fusion.2
  76.8 1.0 fusion.24
  78.0 0.3 maximum_add_fusion.3
  78.3 1.0 constant_dynamic-slice_fusion.2
  79.5 0.7 fusion.23
  80.2 2.6 %gather_fusion = bf16[512,2,256]{2,1,0:T(2,128)(2,1)S(1)} fusion(bf16[2,256,256]{2,0,1:T(2,128)(2,1)S(1)} %bitcast.71, s32[1024]{0:T(1024)S(1)} %pad_clamp_fusion.4), kind=kCustom, calls=%fused_computation.clone.clone.clone.clone.1 | custom fusion | bytes 1050624 | tf_op jit(solution)/shard_map/while/body/eval_jaxpr/jit(_take)/gather | solution.py:41
  82.9 0.4 convolution_bitcast_fusion.2
  83.2 1.0 fusion.24
  84.4 0.3 maximum_add_fusion.3
  84.7 1.0 constant_dynamic-slice_fusion.2
  85.9 0.7 fusion.23
  86.6 2.6 %gather_fusion = bf16[512,2,256]{2,1,0:T(2,128)(2,1)S(1)} fusion(bf16[2,256,256]{2,0,1:T(2,128)(2,1)S(1)} %bitcast.71, s32[1024]{0:T(1024)S(1)} %pad_clamp_fusion.4), kind=kCustom, calls=%fused_computation.clone.clone.clone.clone.1 | custom fusion | bytes 1050624 | tf_op jit(solution)/shard_map/while/body/eval_jaxpr/jit(_take)/gather | solution.py:41
  89.3 0.4 convolution_bitcast_fusion.2
  89.6 1.0 fusion.24
  90.8 0.3 maximum_add_fusion.3
  91.2 2.0 %multiply_subtract_fusion.1 = (f32[2,1,256,256]{3,2,1,0:T(8,128)S(1)}, f32[2,1,256,256]{3,2,1,0:T(8,128)S(1)}) fusion(s32[2,256]{1,0:T(2,128)S(1)} %copy-done.1, f32[2,2,256,256]{3,2,0,1:T(8,128)S(1)} %get-tuple-element.32), kind=kLoop, calls=%fused_computation.37 | loop fusion | flops 1179648 | bytes 2101248 | tf_op jit(solution)/shard_map/sub | solution.py:29
  93.3 2.5 %collective-permute-start = (f32[2,2,256,256]{3,2,1,0:T(8,128)S(1)}, f32[2,2,256,256]{3,2,1,0:T(8,128)S(1)}, u32[]{:S(2)}, u32[]{:S(2)}) collective-permute-start(f32[2,2,256,256]{3,2,1,0:T(8,128)S(1)} %pad_maximum_fusion), channel_id=1, source_target_pairs={{0,2},{1,3},{2,0},{3,1},{4,6},{5,7},{6,4},{7,5},{8,10},{9,11},{10,... | collective-permute-start | bytes 3145736 | tf_op jit(solution)/shard_map/ppermute | solution.py:13
  95.9 46.2 %collective-permute-done = f32[2,2,256,256]{3,2,1,0:T(8,128)S(1)} collective-permute-done((f32[2,2,256,256]{3,2,1,0:T(8,128)S(1)}, f32[2,2,256,256]{3,2,1,0:T(8,128)S(1)}, u32[]{:S(2)}, u32[]{:S(2)}) %collective-permute-start) | collective-permute-done | bytes 1048608 | tf_op jit(solution)/shard_map/ppermute | solution.py:13
  142.1 0.6 gather_fusion.1
  142.9 0.8 copy.34
  143.7 1.9 %gather_fusion.2 = f32[256,2,2,256]{3,2,1,0:T(2,128)S(1)} fusion(f32[2,2,256,256]{3,1,2,0:T(2,128)S(1)} %copy.34, s32[1024]{0:T(1024)S(1)} %pad_clamp_fusion.1), kind=kCustom, calls=%fused_computation.2 | custom fusion | bytes 2098176 | tf_op jit(solution)/shard_map/jit(_take)/gather | solution.py:35
  145.5 0.3 fusion.12
  145.8 0.6 copy.36
  146.4 1.9 %gather_fusion.3 = f32[256,2,2,256]{3,2,1,0:T(2,128)S(1)} fusion(f32[2,2,256,256]{2,1,3,0:T(2,128)S(1)} %copy.36, s32[1024]{0:T(1024)S(1)} %pad_clamp_fusion.1), kind=kCustom, calls=%fused_computation.3 | custom fusion | bytes 2098176 | tf_op jit(solution)/shard_map/jit(_take)/gather | solution.py:35
  148.3 0.3 fusion.11
  148.7 1.1 fusion.10
  (79 shorter events, 3.2 us)
Async XLA Ops:
  6.5 33.3 %all-gather.2.cloned.1.call-start = ((), (), s32[]{:S(2)}) async-start(), calls=%async_computation | async-start | bytes 2359296 | tf_op jit(solution)/shard_map/all_gather | solution.py:64
  39.9 51.3 %copy-start.1 = (s32[2,256]{1,0:T(2,128)S(1)}, s32[2,256]{1,0:T(2,128)}, u32[]{:S(2)}) copy-start(s32[2,256]{1,0:T(2,128)} %param.9) | copy-start | bytes 6148
  39.9 4.5 %copy-start = (s32[2,256]{1,0:T(2,128)S(1)}, s32[2,256]{1,0:T(2,128)}, u32[]{:S(2)}) copy-start(s32[2,256]{1,0:T(2,128)} %get-tuple-element.146) | copy-start | bytes 6148 | tf_op jit(solution)/shard_map/while
  46.3 4.5 %copy-start = (s32[2,256]{1,0:T(2,128)S(1)}, s32[2,256]{1,0:T(2,128)}, u32[]{:S(2)}) copy-start(s32[2,256]{1,0:T(2,128)} %get-tuple-element.146) | copy-start | bytes 6148 | tf_op jit(solution)/shard_map/while
  52.7 4.5 %copy-start = (s32[2,256]{1,0:T(2,128)S(1)}, s32[2,256]{1,0:T(2,128)}, u32[]{:S(2)}) copy-start(s32[2,256]{1,0:T(2,128)} %get-tuple-element.146) | copy-start | bytes 6148 | tf_op jit(solution)/shard_map/while
  59.1 4.5 %copy-start = (s32[2,256]{1,0:T(2,128)S(1)}, s32[2,256]{1,0:T(2,128)}, u32[]{:S(2)}) copy-start(s32[2,256]{1,0:T(2,128)} %get-tuple-element.146) | copy-start | bytes 6148 | tf_op jit(solution)/shard_map/while
  65.5 4.5 %copy-start = (s32[2,256]{1,0:T(2,128)S(1)}, s32[2,256]{1,0:T(2,128)}, u32[]{:S(2)}) copy-start(s32[2,256]{1,0:T(2,128)} %get-tuple-element.146) | copy-start | bytes 6148 | tf_op jit(solution)/shard_map/while
  71.9 4.5 %copy-start = (s32[2,256]{1,0:T(2,128)S(1)}, s32[2,256]{1,0:T(2,128)}, u32[]{:S(2)}) copy-start(s32[2,256]{1,0:T(2,128)} %get-tuple-element.146) | copy-start | bytes 6148 | tf_op jit(solution)/shard_map/while
  78.3 4.5 %copy-start = (s32[2,256]{1,0:T(2,128)S(1)}, s32[2,256]{1,0:T(2,128)}, u32[]{:S(2)}) copy-start(s32[2,256]{1,0:T(2,128)} %get-tuple-element.146) | copy-start | bytes 6148 | tf_op jit(solution)/shard_map/while
  84.7 4.5 %copy-start = (s32[2,256]{1,0:T(2,128)S(1)}, s32[2,256]{1,0:T(2,128)}, u32[]{:S(2)}) copy-start(s32[2,256]{1,0:T(2,128)} %get-tuple-element.146) | copy-start | bytes 6148 | tf_op jit(solution)/shard_map/while
  91.1 4.7 %copy-start.3 = (s32[2]{0:T(128)S(1)}, s32[2]{0:T(128)}, u32[]{:S(2)}) copy-start(s32[2]{0:T(128)} %param.10) | copy-start | bytes 28
  91.1 4.7 %copy-start.2 = (s32[256]{0:T(256)S(1)}, s32[256]{0:T(256)}, u32[]{:S(2)}) copy-start(s32[256]{0:T(256)} %param.11) | copy-start | bytes 3076
  93.3 48.8 %collective-permute-start = (f32[2,2,256,256]{3,2,1,0:T(8,128)S(1)}, f32[2,2,256,256]{3,2,1,0:T(8,128)S(1)}, u32[]{:S(2)}, u32[]{:S(2)}) collective-permute-start(f32[2,2,256,256]{3,2,1,0:T(8,128)S(1)} %pad_maximum_fusion), channel_id=1, source_target_pairs={{0,2},{1,3},{2,0},{3,1},{4,6},{5,7},{6,4},{7,5},{8,10},{9,11},{10,... | collective-permute-start | bytes 3145736 | tf_op jit(solution)/shard_map/ppermute | solution.py:13
Sparse Core Ops, SparseCore 0:
  9.2 30.5 all-gather.1
where the time goes:
time: 157 us
  waiting for transfers between devices  79.5 us (51%)
  local copies, waits for them, and re-layouts  36.2 us (23%)
  other arithmetic  21.3 us (14%)
  between operations  13.5 us (9%)
  matrix products  2.84 us (2%)
  starting transfers between devices  2.48 us (2%)
    ppermute x1, waiting for transfers between devices, passed_along(): lax.ppermute(value, axis, [(i, (i + by) % size) for i in range(size)])  46.2 us
    all_gather x1, waiting for transfers between devices, local(): lax.all_gather(greens, 'blk', axis=0, tiled=True)  32.6 us
    gather x16, local copies, waits for them, and re-layouts, crossed(): chosen = jnp.take(flipped, index_rows, axis=1)  21.1 us
    dynamic_slice x16, local copies, waits for them, and re-layouts, local(): lax.scan(visit, empty, lax.all_gather(greens, 'blk', axis=0, tiled=True))[0]  9.24 us
    convert_element_type x8, other arithmetic, crossed(): block_real = block[0].astype(jnp.float32)  8.09 us
    while x8, other arithmetic  5.49 us
  transfers between devices with their start and end apart: 2, of which 2 were waited for; matrix products, arithmetic and copies ran while one was open for 0% of the time, Pallas kernels for 0%

commit v1 on v0

v1 whole, which is shorter than its diff:
```python
import math

import jax
import jax.numpy as jnp
from jax import lax
from jax.experimental import pallas as pl
from jax.experimental.pallas import tpu as pltpu
from jax.sharding import PartitionSpec as P

NPH = 8
F32 = jnp.float32
BF16 = jnp.bfloat16
NT = (((1,), (1,)), ((), ()))


def passed_along(value, axis, by):
    size = lax.axis_size(axis)
    return lax.ppermute(value, axis, [(i, (i + by) % size) for i in range(size)])


def one_hot(index_rows, width):
    columns = jnp.arange(width, dtype=jnp.int32)
    return (index_rows[..., :, None] == columns).astype(BF16)


def split3(x):
    hi = x.astype(BF16)
    r1 = x - hi.astype(F32)
    mid = r1.astype(BF16)
    lo = (r1 - mid.astype(F32)).astype(BF16)
    return (hi, mid, lo)


def conj_permuted(q, x):
    total = None
    for piece in split3(x):
        rows = jnp.dot(q, piece, preferred_element_type=F32).astype(BF16)
        moved = lax.dot_general(q, rows, NT, preferred_element_type=F32)
        total = moved if total is None else total + moved
    return total


def accumulate_kernel(g_ref, p_ref, q_ref, col_ref, row_ref, out_ref, acc_ref, *, slots, width, scale):
    w = pl.program_id(0)

    @pl.when(w == 0)
    def _():
        acc_ref[...] = jnp.zeros(acc_ref.shape, F32)

    g_re = g_ref[0, 0]
    g_im = g_ref[0, 1]
    sel = p_ref[...]
    y_re = jnp.dot(sel, g_re, preferred_element_type=F32).astype(BF16)
    y_im = jnp.dot(sel, g_im, preferred_element_type=F32).astype(BF16)
    gr = g_re.astype(F32)
    gi = g_im.astype(F32)
    for t in range(2 * slots):
        lo, hi = t * width, (t + 1) * width
        pt = sel[lo:hi]
        m_re = lax.dot_general(pt, y_re[lo:hi], NT, preferred_element_type=F32)
        m_im = lax.dot_general(pt, y_im[lo:hi], NT, preferred_element_type=F32)
        acc_ref[t, 0] += gr * m_re - gi * m_im
        acc_ref[t, 1] += gr * m_im + gi * m_re

    @pl.when(w == pl.num_programs(0) - 1)
    def _():
        q = q_ref[...]
        for s in range(slots):
            parts = []
            for t, permute in ((s, False), (s + slots, True)):
                t_re = acc_ref[t, 0]
                t_im = acc_ref[t, 1]
                if permute:
                    t_re = conj_permuted(q, t_re)
                    t_im = -conj_permuted(q, t_im)
                ca = col_ref[t, 0]
                sa = col_ref[t, 1]
                cb = row_ref[t, 0]
                sb = row_ref[t, 1]
                rot_re = ca * cb + sa * sb
                rot_im = sa * cb - ca * sb
                parts.append((rot_re * t_re - rot_im * t_im, rot_re * t_im + rot_im * t_re))
            (own_re, own_im), (mir_re, mir_im) = parts
            out_ref[s, 0] = (own_re + mir_re) * scale
            out_ref[s, 1] = (own_im + mir_im) * scale


def local(greens, transfer_index, phase_index, partner_slot, conj_index):
    slots = transfer_index.shape[0]
    width = greens.shape[-1]
    blocks = lax.axis_size("blk")
    halfway = lax.axis_size("xfer") // 2
    scale = 0.5 / math.sqrt(blocks)

    far_index = passed_along(transfer_index, "xfer", halfway)
    far_phase = passed_along(phase_index, "xfer", halfway)
    walkers = lax.all_gather(greens, "blk", axis=0, tiled=True)
    nwalk = walkers.shape[0]

    match_index = jnp.take(far_index, partner_slot, axis=0)
    match_phase = jnp.take(jnp.take(far_phase, partner_slot, axis=0), conj_index, axis=1)
    rows = jnp.concatenate([transfer_index, match_index], axis=0)
    sel = one_hot(rows, width).reshape(2 * slots * width, width)
    q = one_hot(conj_index, width)
    phases = jnp.concatenate([phase_index, match_phase], axis=0)
    angle = (2.0 * math.pi / NPH) * phases.astype(F32)
    trig = jnp.stack([jnp.cos(angle), jnp.sin(angle)], axis=1)
    col = trig[:, :, :, None]
    row = trig[:, :, None, :]

    kernel = lambda *refs: accumulate_kernel(*refs, slots=slots, width=width, scale=scale)
    full = lambda shape: pl.BlockSpec(shape, lambda w: (0,) * len(shape))
    return pl.pallas_call(
        kernel,
        grid=(nwalk,),
        in_specs=[
            pl.BlockSpec((1, 2, width, width), lambda w: (w, 0, 0, 0)),
            full(sel.shape),
            full(q.shape),
            full(col.shape),
            full(row.shape),
        ],
        out_specs=full((slots, 2, width, width)),
        out_shape=jax.ShapeDtypeStruct((slots, 2, width, width), F32),
        scratch_shapes=[pltpu.VMEM((2 * slots, 2, width, width), F32)],
        compiler_params=pltpu.CompilerParams(dimension_semantics=("arbitrary",)),
    )(walkers, sel, q, col, row)


def solution(mesh):
    in_specs = (
        P("blk", None, None, None),
        P(("blk", "xfer"), None),
        P(("blk", "xfer"), None),
        P(("blk", "xfer")),
        P(),
    )
    out_specs = P(("blk", "xfer"), None, None, None)
    return jax.shard_map(local, mesh=mesh, in_specs=in_specs, out_specs=out_specs, check_vma=False)
```

time: 157 us -> 58.2 us (0.37)
  waiting for transfers between devices: 79.5 us -> 18.3 us
  local copies, waits for them, and re-layouts: 36.2 us -> 4.02 us
  other arithmetic: 21.3 us -> 6.74 us
  Pallas kernels: 0 us -> 11.1 us
  matrix products: 2.84 us -> 0 us
  starting transfers between devices: 2.48 us -> 4.18 us
    ppermute x1 -> x2, waiting for transfers between devices: 46.2 us -> 0.01 us  [passed_along(): lax.ppermute(value, axis, [(i, (i + by) % size) for i in range(size)])]
    gather x19 -> x4, local copies, waits for them, and re-layouts: 25.5 us -> 1.93 us  [the longest x2 0.81 us: local(): jnp.take(jnp.take(far_phase, partner_slot, axis=0), conj_index, axis=1)]
    all_gather x1, waiting for transfers between devices: 32.6 us -> 17.6 us  [local(): walkers = lax.all_gather(greens, 'blk', axis=0, tiled=True)]
    pallas_call x0 -> x1, Pallas kernels: none -> 11.1 us  [local(): pl.pallas_call(kernel, grid=(nwalk,), in_specs=[pl.BlockSpec((1, 2, width...]
    dynamic_slice x16 -> x0, local copies, waits for them, and re-layouts: 9.24 us -> none  [local(): lax.scan(visit, empty, lax.all_gather(greens, 'blk', axis=0, tiled=True))[0]]
    while x8 -> x0, other arithmetic: 5.49 us -> none
    convert_element_type x8 -> x3, other arithmetic: 8.09 us -> 3.12 us  [the longest x2 2.42 us: one_hot(): return (index_rows[..., :, None] == columns).astype(BF16)]
    sub x9 -> x0, other arithmetic: 3.02 us -> none  [the longest x1 2.05 us: turned(): real = cosines * total[:, 0] - sines * total[:, 1]]
  transfers between devices with their start and end apart: 2 -> 3, of which waited for: 2 -> 1; matrix products, arithmetic and copies ran while one was open for 0% -> 19% of each run, Pallas kernels for 0% -> 0%
where the time goes in v1:
time: 58.2 us; the launch traced here: 57.8 us
  waiting for transfers between devices  18.3 us (31%)
  between operations  13.4 us (23%)
  Pallas kernels  11.1 us (19%)
  other arithmetic  6.74 us (12%)
  starting transfers between devices  4.18 us (7%)
  local copies, waits for them, and re-layouts  4.02 us (7%)
    all_gather x1, waiting for transfers between devices, local(): walkers = lax.all_gather(greens, 'blk', axis=0, tiled=True)  17.6 us
    pallas_call x1, Pallas kernels, local(): pl.pallas_call(kernel, grid=(nwalk,), in_specs=[pl.BlockSpec((1, 2, width...  11.1 us
    ppermute x2, starting transfers between devices, passed_along(): lax.ppermute(value, axis, [(i, (i + by) % size) for i in range(size)])  4.18 us
    convert_element_type x2, other arithmetic, one_hot(): return (index_rows[..., :, None] == columns).astype(BF16)  2.42 us
    broadcast_in_dim x1, local copies, waits for them, and re-layouts, local(): col = trig[:, :, :, None]  1.36 us
  transfers between devices with their start and end apart: 3, of which 1 were waited for; matrix products, arithmetic and copies ran while one was open for 19% of the time, Pallas kernels for 0%

profile of v1, /device:TPU:0, one launch (start us, length us, event | category | flops | bytes accessed | tf_op | source)
XLA Modules:
  0.0 57.8 jit_solution(10915447169917099584)
XLA Ops:
  6.5 0.0 all-gather.2.cloned.1.call-start
  6.5 0.7 %all-gather.2.cloned.1.call-update = ((bf16[1,2,256,256]{3,2,1,0:T(8,128)(2,1)}), bf16[8,2,256,256]{3,2,1,0:T(8,128)(2,1)}) async-update(((), (), s32[]{:S(2)}) %all-gather.2.cloned.1.call-start, bf16[1,2,256,256]{3,2,1,0:T(8,128)(2,1)} %param.7) | async-update | bytes 2621464
  7.3 4.1 %collective-permute-start = (s32[2,256]{1,0:T(2,128)}, s32[2,256]{1,0:T(2,128)S(1)}, u32[]{:S(2)}, u32[]{:S(2)}) collective-permute-start(s32[2,256]{1,0:T(2,128)} %param.8), channel_id=1, source_target_pairs={{0,2},{1,3},{2,0},{3,1},{4,6},{5,7},{6,4},{7,5},{8,10},{9,11},{10,... | collective-permute-start | bytes 6152 | tf_op jit(solution)/shard_map/ppermute | solution.py:18
  11.4 0.1 collective-permute-start.1
  11.4 0.7 %compare_select_fusion = s32[256]{0:T(256)S(1)} fusion(s32[256]{0:T(256)} %param.11), kind=kLoop, calls=%fused_computation.13 | loop fusion | flops 768 | bytes 2048 | tf_op jit(solution)/shard_map/jit(_take)/jit(_where)/select_n | solution.py:101
  12.1 0.7 %compare_and_fusion = pred[2]{0:T(512)(128)(4,1)S(1)} fusion(s32[2]{0:T(128)} %param.10), kind=kLoop, calls=%fused_computation.18 | loop fusion | flops 12 | bytes 10 | tf_op jit(solution)/shard_map/jit(_take)/and | solution.py:100
  12.8 0.7 %compare_select_fusion.1 = s32[2]{0:T(128)S(1)} fusion(s32[2]{0:T(128)} %param.10), kind=kLoop, calls=%fused_computation.14 | loop fusion | flops 6 | bytes 16 | tf_op jit(solution)/shard_map/jit(_take)/jit(_where)/select_n | solution.py:100
  13.4 0.7 %compare_and_fusion.1 = pred[256]{0:T(512)(128)(4,1)S(1)} fusion(s32[256]{0:T(256)} %param.11), kind=kLoop, calls=%fused_computation.19 | loop fusion | flops 1536 | bytes 1280 | tf_op jit(solution)/shard_map/jit(_take)/and | solution.py:101
  14.1 1.4 %fusion.1.refs_2_ = bf16[256,256]{1,0:T(8,128)(2,1)} fusion(s32[256]{0:T(256)} %param.11), kind=kLoop, calls=%fused_computation.6 | loop fusion | flops 131072 | bytes 132096 | tf_op jit(solution)/shard_map/convert_element_type | solution.py:23
  15.6 0.0 collective-permute-done
  15.6 0.6 gather_fusion.1
  16.1 0.0 collective-permute-done.1
  16.1 0.6 gather_fusion.2
  16.7 0.1 broadcast_select_fusion
  16.8 0.7 %add_bitcast_fusion = s32[1,2,4,128]{3,2,1,0:T(4,128)S(1)} fusion(s32[2,256]{1,0:T(2,128)S(1)} %get-tuple-element.11, s32[2,256]{1,0:T(2,128)} %param.8), kind=kLoop, calls=%fused_computation.10 | loop fusion | flops 1024 | bytes 8192
  17.5 0.1 copy.12
  17.6 0.7 %gather_fusion = s32[256,2]{1,0:T(8,128)S(1)} fusion(s32[2,256]{0,1:T(8,128)S(1)} %copy.12, s32[1024]{0:T(1024)S(1)} %pad_clamp_fusion), kind=kCustom, calls=%fused_computation.2 | custom fusion | bytes 5120 | tf_op jit(solution)/shard_map/jit(_take)/gather | solution.py:101
  18.3 0.1 copy.13
  18.4 0.7 %add_convert_fusion = f32[4,1,256]{2,0,1:T(4,128)S(1)} fusion(s32[2,1,256]{2,0,1:T(2,128)S(1)} %select_bitcast_fusion, s32[2,1,256]{2,0,1:T(2,128)} %bitcast.11), kind=kLoop, calls=%fused_computation.11 | loop fusion | flops 2048 | bytes 8192 | tf_op jit(solution)/shard_map/convert_element_type | solution.py:106
  19.1 0.1 fusion.3
  19.3 0.6 %broadcast_in_dim.35.refs_4_ = f32[4,2,1,256]{3,2,1,0:T(1,128)} reshape(f32[4,2,256]{2,1,0:T(2,128)S(1)} %get-tuple-element.6) | data formatting | bytes 16384 | tf_op jit(solution)/shard_map/broadcast_in_dim | solution.py:109
  19.9 1.4 %copy.15.refs_3_ = f32[4,2,256,1]{3,2,1,0:T(8,128)} copy(f32[4,2,256,1]{2,1,0,3:T(2,128)S(1)} %get-tuple-element.7) | data formatting | bytes 16384 | tf_op jit(solution)/shard_map/broadcast_in_dim | solution.py:108
  21.2 1.0 %fusion.refs_1_ = bf16[1024,256]{1,0:T(8,128)(2,1)} fusion(s32[1024]{0:T(1024)S(1)} %bitcast.10), kind=kLoop, calls=%fused_computation.4 | loop fusion | flops 524288 | bytes 528384 | tf_op jit(solution)/shard_map/convert_element_type | solution.py:23
  22.2 17.6 %all-gather.2.cloned.1.call-done.refs_0_ = bf16[8,2,256,256]{3,2,1,0:T(8,128)(2,1)} async-done(((bf16[1,2,256,256]{3,2,1,0:T(8,128)(2,1)}), bf16[8,2,256,256]{3,2,1,0:T(8,128)(2,1)}) %all-gather.2.cloned.1.call-update) | async-done | bytes 2097168 | tf_op jit(solution)/shard_map/all_gather | solution.py:97
  39.9 11.1 %shard_map.55 = f32[2,2,256,256]{3,2,1,0:T(8,128)} custom-call(bf16[8,2,256,256]{3,2,1,0:T(8,128)(2,1)} %all-gather.2.cloned.1.call-done.refs_0_, bf16[1024,256]{1,0:T(8,128)(2,1)} %fusion.refs_1_, bf16[256,256]{1,0:T(8,128)(2,1)} %fusion.1.refs_2_, f32[4,2,256,1]{3,2,1,0:T(8,128)} %copy.15.refs_3_, f32[4,2,1,256]{3,2,1,0:T(1,128)} %broadcast_in_dim.35.refs_4_), custom_call_target="tpu_custom_call" | custom-call | tf_op jit(solution)/shard_map/pallas_call | solution.py:113
  (5 shorter events, 0.0 us)
Async XLA Ops:
  6.5 33.3 %all-gather.2.cloned.1.call-start = ((), (), s32[]{:S(2)}) async-start(), calls=%async_computation | async-start | bytes 2359296 | tf_op jit(solution)/shard_map/all_gather | solution.py:97
  7.3 8.3 %collective-permute-start = (s32[2,256]{1,0:T(2,128)}, s32[2,256]{1,0:T(2,128)S(1)}, u32[]{:S(2)}, u32[]{:S(2)}) collective-permute-start(s32[2,256]{1,0:T(2,128)} %param.8), channel_id=1, source_target_pairs={{0,2},{1,3},{2,0},{3,1},{4,6},{5,7},{6,4},{7,5},{8,10},{9,11},{10,... | collective-permute-start | bytes 6152 | tf_op jit(solution)/shard_map/ppermute | solution.py:18
  11.4 4.8 %collective-permute-start.1 = (s32[2,256]{1,0:T(2,128)}, s32[2,256]{1,0:T(2,128)S(1)}, u32[]{:S(2)}, u32[]{:S(2)}) collective-permute-start(s32[2,256]{1,0:T(2,128)} %param.9), channel_id=1, source_target_pairs={{0,2},{1,3},{2,0},{3,1},{4,6},{5,7},{6,4},{7,5},{8,10},{9,11},{10,... | collective-permute-start | bytes 6152 | tf_op jit(solution)/shard_map/ppermute | solution.py:18
Sparse Core Ops, SparseCore 0:
  9.2 30.5 all-gather.1

commit v2 on v1

--- a/solution.py
+++ b/solution.py
@@ -40,13 +40,7 @@
     return total
 
 
-def accumulate_kernel(g_ref, p_ref, q_ref, col_ref, row_ref, out_ref, acc_ref, *, slots, width, scale):
-    w = pl.program_id(0)
-
-    @pl.when(w == 0)
-    def _():
-        acc_ref[...] = jnp.zeros(acc_ref.shape, F32)
-
+def add_walker(g_ref, p_ref, acc_ref, slots, width):
     g_re = g_ref[0, 0]
     g_im = g_ref[0, 1]
     sel = p_ref[...]
@@ -61,6 +55,22 @@
         m_im = lax.dot_general(pt, y_im[lo:hi], NT, preferred_element_type=F32)
         acc_ref[t, 0] += gr * m_re - gi * m_im
         acc_ref[t, 1] += gr * m_im + gi * m_re
+
+
+def accumulate_kernel(near_ref, far_ref, p_ref, q_ref, col_ref, row_ref, out_ref, acc_ref, *, slots, width, scale, half):
+    w = pl.program_id(0)
+
+    @pl.when(w == 0)
+    def _():
+        acc_ref[...] = jnp.zeros(acc_ref.shape, F32)
+
+    @pl.when(w < half)
+    def _():
+        add_walker(near_ref, p_ref, acc_ref, slots, width)
+
+    @pl.when(w >= half)
+    def _():
+        add_walker(far_ref, p_ref, acc_ref, slots, width)
 
     @pl.when(w == pl.num_programs(0) - 1)
     def _():
@@ -94,8 +104,14 @@
 
     far_index = passed_along(transfer_index, "xfer", halfway)
     far_phase = passed_along(phase_index, "xfer", halfway)
-    walkers = lax.all_gather(greens, "blk", axis=0, tiled=True)
-    nwalk = walkers.shape[0]
+    half = blocks // 2
+    assert blocks % 2 == 0 and blocks & (blocks - 1) == 0
+    fetched = [greens]
+    for m in range(1, half):
+        fetched.append(lax.ppermute(greens, "blk", [(i, i ^ (2 * m)) for i in range(blocks)]))
+    near = jnp.concatenate(fetched, axis=0)
+    sibling = lax.ppermute(near, "blk", [(i, i ^ 1) for i in range(blocks)])
+    nwalk = 2 * half
 
     match_index = jnp.take(far_index, partner_slot, axis=0)
     match_phase = jnp.take(jnp.take(far_phase, partner_slot, axis=0), conj_index, axis=1)
@@ -108,13 +124,14 @@
     col = trig[:, :, :, None]
     row = trig[:, :, None, :]
 
-    kernel = lambda *refs: accumulate_kernel(*refs, slots=slots, width=width, scale=scale)
+    kernel = lambda *refs: accumulate_kernel(*refs, slots=slots, width=width, scale=scale, half=half)
     full = lambda shape: pl.BlockSpec(shape, lambda w: (0,) * len(shape))
     return pl.pallas_call(
         kernel,
         grid=(nwalk,),
         in_specs=[
-            pl.BlockSpec((1, 2, width, width), lambda w: (w, 0, 0, 0)),
+            pl.BlockSpec((1, 2, width, width), lambda w: (jnp.minimum(w, half - 1), 0, 0, 0)),
+            pl.BlockSpec((1, 2, width, width), lambda w: (jnp.maximum(w - half, 0), 0, 0, 0)),
             full(sel.shape),
             full(q.shape),
             full(col.shape),
@@ -124,7 +141,7 @@
         out_shape=jax.ShapeDtypeStruct((slots, 2, width, width), F32),
         scratch_shapes=[pltpu.VMEM((2 * slots, 2, width, width), F32)],
         compiler_params=pltpu.CompilerParams(dimension_semantics=("arbitrary",)),
-    )(walkers, sel, q, col, row)
+    )(near, sibling, sel, q, col, row)
 
 
 def solution(mesh):

time: 58.2 us -> 34.3 us (0.59)
  waiting for transfers between devices: 18.3 us -> 4.49 us
  between operations: 13.4 us -> 0.13 us
  other arithmetic: 6.74 us -> 2.69 us
  local copies, waits for them, and re-layouts: 4.02 us -> 7.79 us
  starting transfers between devices: 4.18 us -> 7.63 us
    all_gather x1 -> x0, waiting for transfers between devices: 17.6 us -> none  [local(): walkers = lax.all_gather(greens, 'blk', axis=0, tiled=True)]
    ppermute x0 -> x4, starting transfers between devices: none -> 4.56 us  [the longest x3 4.49 us: local(): lax.ppermute(greens, 'blk', [(i, i ^ 2 * m) for i in range(blocks)])]
    unnamed x1 -> x16, local copies, waits for them, and re-layouts: 0.01 us -> 3.77 us
    ppermute x0 -> x4, waiting for transfers between devices: none -> 3.49 us  [the longest x3 3.49 us: local(): lax.ppermute(greens, 'blk', [(i, i ^ 2 * m) for i in range(blocks)])]
    ppermute x2, starting transfers between devices: 4.18 us -> 3.07 us  [passed_along(): lax.ppermute(value, axis, [(i, (i + by) % size) for i in range(size)])]
    ppermute x2, waiting for transfers between devices: 0.01 us -> 0.99 us  [passed_along(): lax.ppermute(value, axis, [(i, (i + by) % size) for i in range(size)])]
    unnamed x1 -> x0, waiting for transfers between devices: 0.71 us -> none
    convert_element_type x1, other arithmetic: 0.7 us -> 0.01 us  [local(): angle = 2.0 * math.pi / NPH * phases.astype(F32)]
  transfers between devices with their start and end apart: 3 -> 6, of which waited for: 1 -> 2; matrix products, arithmetic and copies ran while one was open for 19% -> 23% of each run, Pallas kernels for 0% -> 0%
where the time goes in v2:
time: 34.3 us; the launch traced here: 33.9 us
  Pallas kernels  11.2 us (33%)
  local copies, waits for them, and re-layouts  7.79 us (23%)
  starting transfers between devices  7.63 us (22%)
  waiting for transfers between devices  4.49 us (13%)
  other arithmetic  2.69 us (8%)
    pallas_call x1, Pallas kernels, local(): pl.pallas_call(kernel, grid=(nwalk,), in_specs=[pl.BlockSpec((1, 2, width...  11.2 us
    ppermute x3, starting transfers between devices, local(): lax.ppermute(greens, 'blk', [(i, i ^ 2 * m) for i in range(blocks)])  4.49 us
    unnamed x16, local copies, waits for them, and re-layouts  3.77 us
    ppermute x3, waiting for transfers between devices, local(): lax.ppermute(greens, 'blk', [(i, i ^ 2 * m) for i in range(blocks)])  3.49 us
    ppermute x2, starting transfers between devices, passed_along(): lax.ppermute(value, axis, [(i, (i + by) % size) for i in range(size)])  3.07 us
    convert_element_type x2, other arithmetic, one_hot(): return (index_rows[..., :, None] == columns).astype(BF16)  1.76 us
    broadcast_in_dim x1, local copies, waits for them, and re-layouts, local(): col = trig[:, :, :, None]  1.34 us
    ppermute x2, waiting for transfers between devices, passed_along(): lax.ppermute(value, axis, [(i, (i + by) % size) for i in range(size)])  0.99 us
  transfers between devices with their start and end apart: 6, of which 2 were waited for; matrix products, arithmetic and copies ran while one was open for 23% of the time, Pallas kernels for 0%

profile of v2, /device:TPU:0, one launch (start us, length us, event | category | flops | bytes accessed | tf_op | source)
XLA Modules:
  0.0 33.9 jit_solution(7866335239775874775)
XLA Ops:
  0.0 0.0 copy-start.5
  0.0 3.0 %collective-permute-start.1 = (bf16[1,2,256,256]{3,2,1,0:T(8,128)(2,1)}, bf16[1,2,256,256]{3,2,1,0:T(8,128)(2,1)S(1)}, u32[]{:S(2)}, u32[]{:S(2)}) collective-permute-start(bf16[1,2,256,256]{3,2,1,0:T(8,128)(2,1)} %param.7), channel_id=1, source_target_pairs={{0,16},{4,20},{8,24},{12,28},{16,0},{20,4},{24,8},{28,12},{1,17},{... | collective-permute-start | bytes 786440 | tf_op jit(solution)/shard_map/ppermute | solution.py:111
  3.0 1.5 %collective-permute-start = (bf16[1,2,256,256]{3,2,1,0:T(8,128)(2,1)}, bf16[1,2,256,256]{3,2,1,0:T(8,128)(2,1)S(1)}, u32[]{:S(2)}, u32[]{:S(2)}) collective-permute-start(bf16[1,2,256,256]{3,2,1,0:T(8,128)(2,1)} %param.7), channel_id=1, source_target_pairs={{0,8},{4,12},{8,0},{12,4},{16,24},{20,28},{24,16},{28,20},{1,9},{5... | collective-permute-start | bytes 786440 | tf_op jit(solution)/shard_map/ppermute | solution.py:111
  4.5 0.0 collective-permute-start.2
  4.5 3.0 %collective-permute-start.4 = (s32[2,256]{1,0:T(2,128)}, s32[2,256]{1,0:T(2,128)S(1)}, u32[]{:S(2)}, u32[]{:S(2)}) collective-permute-start(s32[2,256]{1,0:T(2,128)} %param.8), channel_id=1, source_target_pairs={{0,2},{1,3},{2,0},{3,1},{4,6},{5,7},{6,4},{7,5},{8,10},{9,11},{10,... | collective-permute-start | bytes 6152 | tf_op jit(solution)/shard_map/ppermute | solution.py:18
  7.5 0.0 collective-permute-start.5
  7.6 0.7 %compare_and_fusion = pred[2]{0:T(512)(128)(4,1)S(1)} fusion(s32[2]{0:T(128)} %param.10), kind=kLoop, calls=%fused_computation.22 | loop fusion | flops 12 | bytes 10 | tf_op jit(solution)/shard_map/jit(_take)/and | solution.py:116
  8.2 0.0 copy-done.5
  8.2 0.0 copy-start.2
  8.2 0.7 %copy-done.2 = s32[256]{0:T(256)S(1)} copy-done((s32[256]{0:T(256)S(1)}, s32[256]{0:T(256)}, u32[]{:S(2)}) %copy-start.2) | copy-done | bytes 1048
  8.9 0.7 %fusion.1.refs_3_ = bf16[256,256]{1,0:T(8,128)(2,1)} fusion(s32[256]{0:T(256)S(1)} %copy-done.2), kind=kLoop, calls=%fused_computation.6 | loop fusion | flops 131072 | bytes 132096 | tf_op jit(solution)/shard_map/convert_element_type | solution.py:23
  9.7 1.0 %constant_dynamic-update-slice_fusion.3 = bf16[4,2,256,256]{3,2,1,0:T(8,128)(2,1)S(1)} fusion(bf16[1,2,256,256]{3,2,1,0:T(8,128)(2,1)} %param.7), kind=kLoop, calls=%fused_computation.10 | loop fusion | bytes 524288
  10.7 0.0 collective-permute-done.4
  10.7 0.6 %gather_fusion.1 = s32[2,256]{1,0:T(2,128)S(1)} fusion(s32[2,256]{1,0:T(2,128)S(1)} %collective-permute-done.4, s32[1024]{0:T(1024)S(1)} %pad_clamp_fusion.1), kind=kCustom, calls=%fused_computation.clone | custom fusion | bytes 4104 | tf_op jit(solution)/shard_map/jit(_take)/gather | solution.py:116
  11.2 1.0 %collective-permute-done.5 = s32[2,256]{1,0:T(2,128)S(1)} collective-permute-done((s32[2,256]{1,0:T(2,128)}, s32[2,256]{1,0:T(2,128)S(1)}, u32[]{:S(2)}, u32[]{:S(2)}) %collective-permute-start.5) | collective-permute-done | bytes 2080 | tf_op jit(solution)/shard_map/ppermute | solution.py:18
  12.2 0.6 %gather_fusion.2 = s32[2,256]{1,0:T(2,128)S(1)} fusion(s32[2,256]{1,0:T(2,128)S(1)} %collective-permute-done.5, s32[1024]{0:T(1024)S(1)} %pad_clamp_fusion.1), kind=kCustom, calls=%fused_computation.1.clone | custom fusion | bytes 4104 | tf_op jit(solution)/shard_map/jit(_take)/gather | solution.py:117
  12.8 0.0 collective-permute-done
  12.8 0.0 collective-permute-done.1
  12.9 3.5 %collective-permute-done.2 = bf16[1,2,256,256]{3,2,1,0:T(8,128)(2,1)S(1)} collective-permute-done((bf16[1,2,256,256]{3,2,1,0:T(8,128)(2,1)}, bf16[1,2,256,256]{3,2,1,0:T(8,128)(2,1)S(1)}, u32[]{:S(2)}, u32[]{:S(2)}) %collective-permute-start.2) | collective-permute-done | bytes 262176 | tf_op jit(solution)/shard_map/ppermute | solution.py:111
  16.3 0.0 copy-start.3
  16.4 0.0 copy-start
  16.4 0.1 collective-permute-start.3
  16.5 0.1 broadcast_select_fusion
  16.5 0.5 %copy-done.3 = s32[2,256]{1,0:T(2,128)S(1)} copy-done((s32[2,256]{1,0:T(2,128)S(1)}, s32[2,256]{1,0:T(2,128)}, u32[]{:S(2)}) %copy-start.3) | copy-done | bytes 2072
  17.0 0.1 copy.9
  17.2 0.7 %gather_fusion = s32[256,2]{1,0:T(8,128)S(1)} fusion(s32[2,256]{0,1:T(8,128)S(1)} %copy.9, s32[1024]{0:T(1024)S(1)} %pad_clamp_fusion), kind=kCustom, calls=%fused_computation.2 | custom fusion | bytes 5120 | tf_op jit(solution)/shard_map/jit(_take)/gather | solution.py:117
  17.9 0.0 copy-start.4
  17.9 0.1 copy.10
  18.0 0.6 %copy-done.4 = s32[2,256]{1,0:T(2,128)S(1)} copy-done((s32[2,256]{1,0:T(2,128)S(1)}, s32[2,256]{1,0:T(2,128)}, u32[]{:S(2)}) %copy-start.4) | copy-done | bytes 2072
  18.6 0.1 fusion.3
  18.8 0.6 %broadcast_in_dim.35.refs_5_ = f32[4,2,1,256]{3,2,1,0:T(1,128)} reshape(f32[4,2,256]{2,1,0:T(2,128)S(1)} %get-tuple-element.6) | data formatting | bytes 16384 | tf_op jit(solution)/shard_map/broadcast_in_dim | solution.py:125
  19.4 1.3 %copy.12.refs_4_ = f32[4,2,256,1]{3,2,1,0:T(8,128)} copy(f32[4,2,256,1]{2,1,0,3:T(2,128)S(1)} %get-tuple-element.7) | data formatting | bytes 16384 | tf_op jit(solution)/shard_map/broadcast_in_dim | solution.py:124
  20.7 1.0 %fusion.refs_2_ = bf16[1024,256]{1,0:T(8,128)(2,1)} fusion(s32[1024]{0:T(1024)S(1)} %bitcast.10), kind=kLoop, calls=%fused_computation.4 | loop fusion | flops 524288 | bytes 528384 | tf_op jit(solution)/shard_map/convert_element_type | solution.py:23
  21.7 0.0 collective-permute-done.3.refs_1_
  21.7 0.0 copy-done
  21.7 0.0 copy-start.1
  21.7 1.0 %copy-done.1 = bf16[4,2,256,256]{3,2,1,0:T(8,128)(2,1)} copy-done((bf16[4,2,256,256]{3,2,1,0:T(8,128)(2,1)}, bf16[4,2,256,256]{3,2,1,0:T(8,128)(2,1)S(1)}, u32[]{:S(2)}) %copy-start.1) | copy-done | bytes 1048600
  22.7 11.2 %shard_map.55 = f32[2,2,256,256]{3,2,1,0:T(8,128)} custom-call(bf16[4,2,256,256]{3,2,1,0:T(8,128)(2,1)} %copy-done, bf16[4,2,256,256]{3,2,1,0:T(8,128)(2,1)} %copy-done.1, bf16[1024,256]{1,0:T(8,128)(2,1)} %fusion.refs_2_, bf16[256,256]{1,0:T(8,128)(2,1)} %fusion.1.refs_3_, f32[4,2,256,1]{3,2,1,0:T(8,128)} %copy.12.refs_4_, ...), custom_call_target="tpu_custom_call" | custom-call | tf_op jit(solution)/shard_map/pallas_call | solution.py:129
  (13 shorter events, 0.1 us)
Async XLA Ops:
  0.0 8.2 %copy-start.5 = (s32[2]{0:T(128)S(1)}, s32[2]{0:T(128)}, u32[]{:S(2)}) copy-start(s32[2]{0:T(128)} %param.10) | copy-start | bytes 28
  0.0 12.8 %collective-permute-start.1 = (bf16[1,2,256,256]{3,2,1,0:T(8,128)(2,1)}, bf16[1,2,256,256]{3,2,1,0:T(8,128)(2,1)S(1)}, u32[]{:S(2)}, u32[]{:S(2)}) collective-permute-start(bf16[1,2,256,256]{3,2,1,0:T(8,128)(2,1)} %param.7), channel_id=1, source_target_pairs={{0,16},{4,20},{8,24},{12,28},{16,0},{20,4},{24,8},{28,12},{1,17},{... | collective-permute-start | bytes 786440 | tf_op jit(solution)/shard_map/ppermute | solution.py:111
  3.0 9.8 %collective-permute-start = (bf16[1,2,256,256]{3,2,1,0:T(8,128)(2,1)}, bf16[1,2,256,256]{3,2,1,0:T(8,128)(2,1)S(1)}, u32[]{:S(2)}, u32[]{:S(2)}) collective-permute-start(bf16[1,2,256,256]{3,2,1,0:T(8,128)(2,1)} %param.7), channel_id=1, source_target_pairs={{0,8},{4,12},{8,0},{12,4},{16,24},{20,28},{24,16},{28,20},{1,9},{5... | collective-permute-start | bytes 786440 | tf_op jit(solution)/shard_map/ppermute | solution.py:111
  4.5 11.9 %collective-permute-start.2 = (bf16[1,2,256,256]{3,2,1,0:T(8,128)(2,1)}, bf16[1,2,256,256]{3,2,1,0:T(8,128)(2,1)S(1)}, u32[]{:S(2)}, u32[]{:S(2)}) collective-permute-start(bf16[1,2,256,256]{3,2,1,0:T(8,128)(2,1)} %param.7), channel_id=1, source_target_pairs={{0,24},{4,28},{8,16},{12,20},{16,8},{20,12},{24,0},{28,4},{1,25},{... | collective-permute-start | bytes 786440 | tf_op jit(solution)/shard_map/ppermute | solution.py:111
  4.5 6.2 %collective-permute-start.4 = (s32[2,256]{1,0:T(2,128)}, s32[2,256]{1,0:T(2,128)S(1)}, u32[]{:S(2)}, u32[]{:S(2)}) collective-permute-start(s32[2,256]{1,0:T(2,128)} %param.8), channel_id=1, source_target_pairs={{0,2},{1,3},{2,0},{3,1},{4,6},{5,7},{6,4},{7,5},{8,10},{9,11},{10,... | collective-permute-start | bytes 6152 | tf_op jit(solution)/shard_map/ppermute | solution.py:18
  7.5 4.7 %collective-permute-start.5 = (s32[2,256]{1,0:T(2,128)}, s32[2,256]{1,0:T(2,128)S(1)}, u32[]{:S(2)}, u32[]{:S(2)}) collective-permute-start(s32[2,256]{1,0:T(2,128)} %param.9), channel_id=1, source_target_pairs={{0,2},{1,3},{2,0},{3,1},{4,6},{5,7},{6,4},{7,5},{8,10},{9,11},{10,... | collective-permute-start | bytes 6152 | tf_op jit(solution)/shard_map/ppermute | solution.py:18
  8.2 0.7 %copy-start.2 = (s32[256]{0:T(256)S(1)}, s32[256]{0:T(256)}, u32[]{:S(2)}) copy-start(s32[256]{0:T(256)} %param.11) | copy-start | bytes 3076
  16.3 0.7 %copy-start.3 = (s32[2,256]{1,0:T(2,128)S(1)}, s32[2,256]{1,0:T(2,128)}, u32[]{:S(2)}) copy-start(s32[2,256]{1,0:T(2,128)} %param.8) | copy-start | bytes 6148
  16.4 5.4 %copy-start = (bf16[4,2,256,256]{3,2,1,0:T(8,128)(2,1)}, bf16[4,2,256,256]{3,2,1,0:T(8,128)(2,1)S(1)}, u32[]{:S(2)}) copy-start(bf16[4,2,256,256]{3,2,1,0:T(8,128)(2,1)S(1)} %constant_dynamic-update-slice_fusion.refs_0_) | copy-start | bytes 3145732
  16.4 5.3 %collective-permute-start.3 = (bf16[4,2,256,256]{3,2,1,0:T(8,128)(2,1)S(1)}, bf16[4,2,256,256]{3,2,1,0:T(8,128)(2,1)S(1)}, u32[]{:S(2)}, u32[]{:S(2)}) collective-permute-start(bf16[4,2,256,256]{3,2,1,0:T(8,128)(2,1)S(1)} %constant_dynamic-update-slice_fusion.refs_0_), channel_id=1, source_target_pairs={{0,4},{4,0},{8,12},{12,8},{16,20},{20,16},{24,28},{28,24},{1,5},{5... | collective-permute-start | bytes 3145736 | tf_op jit(solution)/shard_map/ppermute | solution.py:113
  17.9 0.7 %copy-start.4 = (s32[2,256]{1,0:T(2,128)S(1)}, s32[2,256]{1,0:T(2,128)}, u32[]{:S(2)}) copy-start(s32[2,256]{1,0:T(2,128)} %param.9) | copy-start | bytes 6148
  21.7 1.0 %copy-start.1 = (bf16[4,2,256,256]{3,2,1,0:T(8,128)(2,1)}, bf16[4,2,256,256]{3,2,1,0:T(8,128)(2,1)S(1)}, u32[]{:S(2)}) copy-start(bf16[4,2,256,256]{3,2,1,0:T(8,128)(2,1)S(1)} %collective-permute-done.3.refs_1_) | copy-start | bytes 3145732

commit v3 on v1

--- a/solution.py
+++ b/solution.py
@@ -1,3 +1,4 @@
+import functools
 import math
 
 import jax
@@ -40,13 +41,7 @@
     return total
 
 
-def accumulate_kernel(g_ref, p_ref, q_ref, col_ref, row_ref, out_ref, acc_ref, *, slots, width, scale):
-    w = pl.program_id(0)
-
-    @pl.when(w == 0)
-    def _():
-        acc_ref[...] = jnp.zeros(acc_ref.shape, F32)
-
+def add_walker(g_ref, p_ref, acc_ref, slots, width):
     g_re = g_ref[0, 0]
     g_im = g_ref[0, 1]
     sel = p_ref[...]
@@ -62,14 +57,39 @@
         acc_ref[t, 0] += gr * m_re - gi * m_im
         acc_ref[t, 1] += gr * m_im + gi * m_re
 
-    @pl.when(w == pl.num_programs(0) - 1)
+
+def accumulate_kernel(*refs, slots, width, scale, has_prior, final):
+    if has_prior:
+        g_ref, p_ref, q_ref, col_ref, row_ref, prior_hbm, out_ref, acc_ref, prior_ref, sem = refs
+    else:
+        g_ref, p_ref, q_ref, col_ref, row_ref, out_ref, acc_ref = refs
+    w = pl.program_id(0)
+    last = pl.num_programs(0) - 1
+
+    @pl.when(w == 0)
     def _():
+        acc_ref[...] = jnp.zeros(acc_ref.shape, F32)
+        if has_prior:
+            pltpu.make_async_copy(prior_hbm, prior_ref, sem).start()
+
+    add_walker(g_ref, p_ref, acc_ref, slots, width)
+
+    @pl.when(w == last)
+    def _():
+        if has_prior:
+            pltpu.make_async_copy(prior_hbm, prior_ref, sem).wait()
+        if not final:
+            if has_prior:
+                out_ref[...] = acc_ref[...] + prior_ref[...]
+            else:
+                out_ref[...] = acc_ref[...]
+            return
         q = q_ref[...]
         for s in range(slots):
             parts = []
             for t, permute in ((s, False), (s + slots, True)):
-                t_re = acc_ref[t, 0]
-                t_im = acc_ref[t, 1]
+                t_re = acc_ref[t, 0] + prior_ref[t, 0]
+                t_im = acc_ref[t, 1] + prior_ref[t, 1]
                 if permute:
                     t_re = conj_permuted(q, t_re)
                     t_im = -conj_permuted(q, t_im)
@@ -85,17 +105,55 @@
             out_ref[s, 1] = (own_im + mir_im) * scale
 
 
+def accumulate(walkers, sel, q, col, row, prior, final, slots, width, scale):
+    has_prior = prior is not None
+    kernel = functools.partial(
+        accumulate_kernel, slots=slots, width=width, scale=scale, has_prior=has_prior, final=final
+    )
+    full = lambda shape: pl.BlockSpec(shape, lambda w: (0,) * len(shape))
+    acc_shape = (2 * slots, 2, width, width)
+    out_shape = (slots, 2, width, width) if final else acc_shape
+    in_specs = [
+        pl.BlockSpec((1, 2, width, width), lambda w: (w, 0, 0, 0)),
+        full(sel.shape),
+        full(q.shape),
+        full(col.shape),
+        full(row.shape),
+    ]
+    scratch = [pltpu.VMEM(acc_shape, F32)]
+    operands = [walkers, sel, q, col, row]
+    if has_prior:
+        in_specs.append(pl.BlockSpec(memory_space=pl.ANY))
+        scratch += [pltpu.VMEM(acc_shape, F32), pltpu.SemaphoreType.DMA(())]
+        operands.append(prior)
+    steps = walkers.shape[0]
+    flops = steps * 2 * slots * 8 * width**3 + (12 * slots * 2 * width**3 if final else 0)
+    moved = walkers.size * 2 + sel.size * 2 + 4 * math.prod(out_shape) + (4 * math.prod(acc_shape) if has_prior else 0)
+    return pl.pallas_call(
+        kernel,
+        grid=(steps,),
+        cost_estimate=pl.CostEstimate(flops=flops, transcendentals=0, bytes_accessed=moved),
+        in_specs=in_specs,
+        out_specs=full(out_shape),
+        out_shape=jax.ShapeDtypeStruct(out_shape, F32),
+        scratch_shapes=scratch,
+        compiler_params=pltpu.CompilerParams(dimension_semantics=("arbitrary",)),
+    )(*operands)
+
+
 def local(greens, transfer_index, phase_index, partner_slot, conj_index):
     slots = transfer_index.shape[0]
     width = greens.shape[-1]
     blocks = lax.axis_size("blk")
     halfway = lax.axis_size("xfer") // 2
     scale = 0.5 / math.sqrt(blocks)
+    assert blocks % 2 == 0 and blocks & (blocks - 1) == 0
 
     far_index = passed_along(transfer_index, "xfer", halfway)
     far_phase = passed_along(phase_index, "xfer", halfway)
-    walkers = lax.all_gather(greens, "blk", axis=0, tiled=True)
-    nwalk = walkers.shape[0]
+    swap = [(i, i ^ 1) for i in range(blocks)]
+    sibling = lax.ppermute(greens, "blk", swap)
+    fetched = [lax.ppermute(greens, "blk", [(i, i ^ (2 * m)) for i in range(blocks)]) for m in range(1, blocks // 2)]
 
     match_index = jnp.take(far_index, partner_slot, axis=0)
     match_phase = jnp.take(jnp.take(far_phase, partner_slot, axis=0), conj_index, axis=1)
@@ -107,24 +165,16 @@
     trig = jnp.stack([jnp.cos(angle), jnp.sin(angle)], axis=1)
     col = trig[:, :, :, None]
     row = trig[:, :, None, :]
+    run = functools.partial(accumulate, sel=sel, q=q, col=col, row=row, slots=slots, width=width, scale=scale)
 
-    kernel = lambda *refs: accumulate_kernel(*refs, slots=slots, width=width, scale=scale)
-    full = lambda shape: pl.BlockSpec(shape, lambda w: (0,) * len(shape))
-    return pl.pallas_call(
-        kernel,
-        grid=(nwalk,),
-        in_specs=[
-            pl.BlockSpec((1, 2, width, width), lambda w: (w, 0, 0, 0)),
-            full(sel.shape),
-            full(q.shape),
-            full(col.shape),
-            full(row.shape),
-        ],
-        out_specs=full((slots, 2, width, width)),
-        out_shape=jax.ShapeDtypeStruct((slots, 2, width, width), F32),
-        scratch_shapes=[pltpu.VMEM((2 * slots, 2, width, width), F32)],
-        compiler_params=pltpu.CompilerParams(dimension_semantics=("arbitrary",)),
-    )(walkers, sel, q, col, row)
+    if not fetched:
+        return run(jnp.concatenate([greens, sibling], axis=0), prior=None, final=True)
+    partial_sums = run(jnp.concatenate([greens, sibling], axis=0), prior=None, final=False)
+    partial_sums, fetched = lax.optimization_barrier((partial_sums, fetched))
+    near = jnp.concatenate(fetched, axis=0)
+    forwarded = lax.ppermute(near, "blk", swap)
+    partial_sums = run(near, prior=partial_sums, final=False)
+    return run(forwarded, prior=partial_sums, final=True)
 
 
 def solution(mesh):

time: 58.2 us -> 39.2 us (0.67)
  waiting for transfers between devices: 18.3 us -> 0.02 us
  between operations: 13.4 us -> 0.13 us
  Pallas kernels: 11.1 us -> 17.6 us
  starting transfers between devices: 4.18 us -> 7.7 us
  local copies, waits for them, and re-layouts: 4.02 us -> 5.74 us
  other arithmetic: 6.74 us -> 7.63 us
    all_gather x1 -> x0, waiting for transfers between devices: 17.6 us -> none  [local(): walkers = lax.all_gather(greens, 'blk', axis=0, tiled=True)]
    pallas_call x1 -> x3, Pallas kernels: 11.1 us -> 17.6 us  [accumulate(): pl.pallas_call(kernel, grid=(steps,), cost_estimate=pl.CostEstimate(flops...]
    ppermute x0 -> x5, starting transfers between devices: none -> 4.77 us  [the longest x3 4.7 us: local(): lax.ppermute(greens, 'blk', [(i, i ^ 2 * m) for i in range(blocks)])]
    unnamed x1 -> x9, local copies, waits for them, and re-layouts: 0.01 us -> 1.72 us
    ppermute x2, starting transfers between devices: 4.18 us -> 2.92 us  [passed_along(): lax.ppermute(value, axis, [(i, (i + by) % size) for i in range(size)])]
    concatenate x0 -> x1, other arithmetic: none -> 0.84 us  [local(): jnp.concatenate([greens, sibling], axis=0)]
    unnamed x1 -> x0, waiting for transfers between devices: 0.71 us -> none
  transfers between devices with their start and end apart: 3 -> 7, of which waited for: 1 -> 0; matrix products, arithmetic and copies ran while one was open for 19% -> 30% of each run, Pallas kernels for 0% -> 27%
where the time goes in v3:
time: 39.2 us; the launch traced here: 38.8 us
  Pallas kernels  17.6 us (45%)
  starting transfers between devices  7.7 us (20%)
  other arithmetic  7.63 us (19%)
  local copies, waits for them, and re-layouts  5.74 us (15%)
    pallas_call x3, Pallas kernels, accumulate(): pl.pallas_call(kernel, grid=(steps,), cost_estimate=pl.CostEstimate(flops...  17.6 us
    ppermute x3, starting transfers between devices, local(): lax.ppermute(greens, 'blk', [(i, i ^ 2 * m) for i in range(blocks)])  4.7 us
    ppermute x2, starting transfers between devices, passed_along(): lax.ppermute(value, axis, [(i, (i + by) % size) for i in range(size)])  2.92 us
    convert_element_type x2, other arithmetic, one_hot(): return (index_rows[..., :, None] == columns).astype(BF16)  2.49 us
    unnamed x9, local copies, waits for them, and re-layouts  1.72 us
    broadcast_in_dim x1, local copies, waits for them, and re-layouts, local(): col = trig[:, :, :, None]  1.34 us
    concatenate x1, other arithmetic, local(): jnp.concatenate([greens, sibling], axis=0)  0.84 us
    gather x2, local copies, waits for them, and re-layouts, local(): jnp.take(jnp.take(far_phase, partner_slot, axis=0), conj_index, axis=1)  0.81 us
  transfers between devices with their start and end apart: 7, of which 0 were waited for; matrix products, arithmetic and copies ran while one was open for 30% of the time, Pallas kernels for 27%

profile of v3, /device:TPU:0, one launch (start us, length us, event | category | flops | bytes accessed | tf_op | source)
XLA Modules:
  0.0 38.8 jit_solution(11418457211795273465)
XLA Ops:
  0.0 0.0 copy-start.1
  0.0 2.9 %collective-permute-start.3 = (bf16[1,2,256,256]{3,2,1,0:T(8,128)(2,1)}, bf16[1,2,256,256]{3,2,1,0:T(8,128)(2,1)S(1)}, u32[]{:S(2)}, u32[]{:S(2)}) collective-permute-start(bf16[1,2,256,256]{3,2,1,0:T(8,128)(2,1)} %param.7), channel_id=1, source_target_pairs={{0,8},{4,12},{8,0},{12,4},{16,24},{20,28},{24,16},{28,20},{1,9},{5... | collective-permute-start | bytes 786440 | tf_op jit(solution)/shard_map/ppermute | solution.py:156
  2.9 0.0 collective-permute-start
  2.9 1.5 %collective-permute-start.5 = (bf16[1,2,256,256]{3,2,1,0:T(8,128)(2,1)}, bf16[1,2,256,256]{3,2,1,0:T(8,128)(2,1)S(1)}, u32[]{:S(2)}, u32[]{:S(2)}) collective-permute-start(bf16[1,2,256,256]{3,2,1,0:T(8,128)(2,1)} %param.7), channel_id=1, source_target_pairs={{0,24},{4,28},{8,16},{12,20},{16,8},{20,12},{24,0},{28,4},{1,25},{... | collective-permute-start | bytes 786440 | tf_op jit(solution)/shard_map/ppermute | solution.py:156
  4.4 2.6 %collective-permute-start.1 = (s32[2,256]{1,0:T(2,128)}, s32[2,256]{1,0:T(2,128)S(1)}, u32[]{:S(2)}, u32[]{:S(2)}) collective-permute-start(s32[2,256]{1,0:T(2,128)} %param.8), channel_id=1, source_target_pairs={{0,2},{1,3},{2,0},{3,1},{4,6},{5,7},{6,4},{7,5},{8,10},{9,11},{10,... | collective-permute-start | bytes 6152 | tf_op jit(solution)/shard_map/ppermute | solution.py:19
  7.0 0.3 collective-permute-start.2
  7.4 0.7 %compare_and_fusion = pred[2]{0:T(512)(128)(4,1)S(1)} fusion(s32[2]{0:T(128)} %param.10), kind=kLoop, calls=%fused_computation.22 | loop fusion | flops 12 | bytes 10 | tf_op jit(solution)/shard_map/jit(_take)/and | solution.py:158
  8.0 0.7 %compare_select_fusion.1 = s32[2]{0:T(128)S(1)} fusion(s32[2]{0:T(128)} %param.10), kind=kLoop, calls=%fused_computation.18 | loop fusion | flops 6 | bytes 16 | tf_op jit(solution)/shard_map/jit(_take)/jit(_where)/select_n | solution.py:158
  8.7 0.7 %compare_and_fusion.1 = pred[256]{0:T(512)(128)(4,1)S(1)} fusion(s32[256]{0:T(256)} %param.11), kind=kLoop, calls=%fused_computation.23 | loop fusion | flops 1536 | bytes 1280 | tf_op jit(solution)/shard_map/jit(_take)/and | solution.py:159
  9.4 0.7 %compare_select_fusion = s32[256]{0:T(256)S(1)} fusion(s32[256]{0:T(256)} %param.11), kind=kLoop, calls=%fused_computation.17 | loop fusion | flops 768 | bytes 2048 | tf_op jit(solution)/shard_map/jit(_take)/jit(_where)/select_n | solution.py:159
  10.0 1.4 %fusion.1.refs_2_ = bf16[256,256]{1,0:T(8,128)(2,1)} fusion(s32[256]{0:T(256)} %param.11), kind=kLoop, calls=%fused_computation.7 | loop fusion | flops 131072 | bytes 132096 | tf_op jit(solution)/shard_map/convert_element_type | solution.py:24
  11.5 0.0 collective-permute-done.1
  11.5 0.3 collective-permute-start.4
  11.8 0.6 %gather_fusion.1 = s32[2,256]{1,0:T(2,128)S(1)} fusion(s32[2,256]{1,0:T(2,128)S(1)} %collective-permute-done.1, s32[1024]{0:T(1024)S(1)} %pad_clamp_fusion.1), kind=kCustom, calls=%fused_computation.clone | custom fusion | bytes 4104 | tf_op jit(solution)/shard_map/jit(_take)/gather | solution.py:158
  12.3 0.0 collective-permute-done.2
  12.3 0.6 %gather_fusion.2 = s32[2,256]{1,0:T(2,128)S(1)} fusion(s32[2,256]{1,0:T(2,128)S(1)} %collective-permute-done.2, s32[1024]{0:T(1024)S(1)} %pad_clamp_fusion.1), kind=kCustom, calls=%fused_computation.1.clone | custom fusion | bytes 4104 | tf_op jit(solution)/shard_map/jit(_take)/gather | solution.py:159
  12.9 0.1 broadcast_select_fusion
  13.0 0.7 %add_bitcast_fusion = s32[1,2,4,128]{3,2,1,0:T(4,128)S(1)} fusion(s32[2,256]{1,0:T(2,128)S(1)} %get-tuple-element.19, s32[2,256]{1,0:T(2,128)} %param.8), kind=kLoop, calls=%fused_computation.14 | loop fusion | flops 1024 | bytes 8192
  13.7 0.1 copy.11
  13.8 0.7 %gather_fusion = s32[256,2]{1,0:T(8,128)S(1)} fusion(s32[2,256]{0,1:T(8,128)S(1)} %copy.11, s32[1024]{0:T(1024)S(1)} %pad_clamp_fusion), kind=kCustom, calls=%fused_computation.2 | custom fusion | bytes 5120 | tf_op jit(solution)/shard_map/jit(_take)/gather | solution.py:159
  14.6 0.1 copy.12
  14.6 1.1 %fusion.refs_1_ = bf16[1024,256]{1,0:T(8,128)(2,1)} fusion(s32[1024]{0:T(1024)S(1)} %bitcast.10), kind=kLoop, calls=%fused_computation.4 | loop fusion | flops 524288 | bytes 528384 | tf_op jit(solution)/shard_map/convert_element_type | solution.py:24
  15.7 0.7 %add_convert_fusion = f32[4,1,256]{2,0,1:T(4,128)S(1)} fusion(s32[2,1,256]{2,0,1:T(2,128)S(1)} %select_bitcast_fusion, s32[2,1,256]{2,0,1:T(2,128)} %bitcast.11), kind=kLoop, calls=%fused_computation.15 | loop fusion | flops 2048 | bytes 8192 | tf_op jit(solution)/shard_map/convert_element_type | solution.py:164
  16.4 0.1 fusion.3
  16.5 0.6 %broadcast_in_dim.35.refs_4_ = f32[4,2,1,256]{3,2,1,0:T(1,128)} reshape(f32[4,2,256]{2,1,0:T(2,128)S(1)} %get-tuple-element.14) | data formatting | bytes 16384 | tf_op jit(solution)/shard_map/broadcast_in_dim | solution.py:167
  17.1 1.3 %copy.14.refs_3_ = f32[4,2,256,1]{3,2,1,0:T(8,128)} copy(f32[4,2,256,1]{2,1,0,3:T(2,128)S(1)} %get-tuple-element.15) | data formatting | bytes 16384 | tf_op jit(solution)/shard_map/broadcast_in_dim | solution.py:166
  18.5 0.0 collective-permute-done
  18.5 0.0 copy-done.1
  18.5 0.8 %pad_maximum_fusion.refs_0_ = bf16[2,2,256,256]{3,2,1,0:T(8,128)(2,1)} fusion(bf16[1,2,256,256]{3,2,1,0:T(8,128)(2,1)S(1)} %collective-permute-done, bf16[1,2,256,256]{3,2,1,0:T(8,128)(2,1)S(1)} %copy-done.1), kind=kLoop, calls=%fused_computation.5 | loop fusion | flops 262144 | bytes 1048576 | tf_op jit(solution)/shard_map/concatenate | solution.py:172
  19.3 4.7 %shard_map.55.refs_5_ = f32[4,2,256,256]{3,2,1,0:T(8,128)} custom-call(bf16[2,2,256,256]{3,2,1,0:T(8,128)(2,1)} %pad_maximum_fusion.refs_0_, bf16[1024,256]{1,0:T(8,128)(2,1)} %fusion.refs_1_, bf16[256,256]{1,0:T(8,128)(2,1)} %fusion.1.refs_2_, f32[4,2,256,1]{3,2,1,0:T(8,128)} %copy.14.refs_3_, f32[4,2,1,256]{3,2,1,0:T(1,128)} %broadcast_in_dim.35.refs_4_), custom_call_target="tpu_custom_call" | custom-call | flops 1073741824 | bytes 3145728 | tf_op jit(solution)/shard_map/pallas_call | solution.py:132
  24.0 0.0 collective-permute-done.3
  24.0 0.0 collective-permute-done.5
  24.0 0.0 collective-permute-done.4
  24.1 0.0 copy-start
  24.1 0.1 collective-permute-start.6
  24.2 0.8 %copy-done = bf16[3,2,256,256]{3,2,1,0:T(8,128)(2,1)} copy-done((bf16[3,2,256,256]{3,2,1,0:T(8,128)(2,1)}, bf16[3,2,256,256]{3,2,1,0:T(8,128)(2,1)S(1)}, u32[]{:S(2)}) %copy-start) | copy-done | bytes 786456
  25.0 5.9 %shard_map.56.refs_5_ = f32[4,2,256,256]{3,2,1,0:T(8,128)} custom-call(bf16[3,2,256,256]{3,2,1,0:T(8,128)(2,1)} %copy-done, bf16[1024,256]{1,0:T(8,128)(2,1)} %fusion.refs_1_, bf16[256,256]{1,0:T(8,128)(2,1)} %fusion.1.refs_2_, f32[4,2,256,1]{3,2,1,0:T(8,128)} %copy.14.refs_3_, f32[4,2,1,256]{3,2,1,0:T(1,128)} %broadcast_in_dim.35.refs_4_, ...), custom_call_target="tpu_custom_call" | custom-call | flops 1610612736 | bytes 5505024 | tf_op jit(solution)/shard_map/pallas_call | solution.py:132
  30.9 0.0 collective-permute-done.6.refs_0_
  30.9 0.0 copy-start.2
  30.9 0.9 %copy-done.2 = bf16[3,2,256,256]{3,2,1,0:T(8,128)(2,1)} copy-done((bf16[3,2,256,256]{3,2,1,0:T(8,128)(2,1)}, bf16[3,2,256,256]{3,2,1,0:T(8,128)(2,1)S(1)}, u32[]{:S(2)}) %copy-start.2) | copy-done | bytes 786456
  31.8 7.0 %shard_map.57 = f32[2,2,256,256]{3,2,1,0:T(8,128)} custom-call(bf16[3,2,256,256]{3,2,1,0:T(8,128)(2,1)} %copy-done.2, bf16[1024,256]{1,0:T(8,128)(2,1)} %fusion.refs_1_, bf16[256,256]{1,0:T(8,128)(2,1)} %fusion.1.refs_2_, f32[4,2,256,1]{3,2,1,0:T(8,128)} %copy.14.refs_3_, f32[4,2,1,256]{3,2,1,0:T(1,128)} %broadcast_in_dim.35.refs_4_, ...), custom_call_target="tpu_custom_call" | custom-call | flops 2415919104 | bytes 4456448 | tf_op jit(solution)/shard_map/pallas_call | solution.py:132
  (8 shorter events, 0.1 us)
Async XLA Ops:
  0.0 18.5 %copy-start.1 = (bf16[1,2,256,256]{3,2,1,0:T(8,128)(2,1)S(1)}, bf16[1,2,256,256]{3,2,1,0:T(8,128)(2,1)}, u32[]{:S(2)}) copy-start(bf16[1,2,256,256]{3,2,1,0:T(8,128)(2,1)} %param.7) | copy-start | bytes 786436
  0.0 24.0 %collective-permute-start.3 = (bf16[1,2,256,256]{3,2,1,0:T(8,128)(2,1)}, bf16[1,2,256,256]{3,2,1,0:T(8,128)(2,1)S(1)}, u32[]{:S(2)}, u32[]{:S(2)}) collective-permute-start(bf16[1,2,256,256]{3,2,1,0:T(8,128)(2,1)} %param.7), channel_id=1, source_target_pairs={{0,8},{4,12},{8,0},{12,4},{16,24},{20,28},{24,16},{28,20},{1,9},{5... | collective-permute-start | bytes 786440 | tf_op jit(solution)/shard_map/ppermute | solution.py:156
  2.9 15.5 %collective-permute-start = (bf16[1,2,256,256]{3,2,1,0:T(8,128)(2,1)}, bf16[1,2,256,256]{3,2,1,0:T(8,128)(2,1)S(1)}, u32[]{:S(2)}, u32[]{:S(2)}) collective-permute-start(bf16[1,2,256,256]{3,2,1,0:T(8,128)(2,1)} %param.7), channel_id=1, source_target_pairs={{0,4},{4,0},{8,12},{12,8},{16,20},{20,16},{24,28},{28,24},{1,5},{5... | collective-permute-start | bytes 786440 | tf_op jit(solution)/shard_map/ppermute | solution.py:155
  2.9 21.1 %collective-permute-start.5 = (bf16[1,2,256,256]{3,2,1,0:T(8,128)(2,1)}, bf16[1,2,256,256]{3,2,1,0:T(8,128)(2,1)S(1)}, u32[]{:S(2)}, u32[]{:S(2)}) collective-permute-start(bf16[1,2,256,256]{3,2,1,0:T(8,128)(2,1)} %param.7), channel_id=1, source_target_pairs={{0,24},{4,28},{8,16},{12,20},{16,8},{20,12},{24,0},{28,4},{1,25},{... | collective-permute-start | bytes 786440 | tf_op jit(solution)/shard_map/ppermute | solution.py:156
  4.4 7.1 %collective-permute-start.1 = (s32[2,256]{1,0:T(2,128)}, s32[2,256]{1,0:T(2,128)S(1)}, u32[]{:S(2)}, u32[]{:S(2)}) collective-permute-start(s32[2,256]{1,0:T(2,128)} %param.8), channel_id=1, source_target_pairs={{0,2},{1,3},{2,0},{3,1},{4,6},{5,7},{6,4},{7,5},{8,10},{9,11},{10,... | collective-permute-start | bytes 6152 | tf_op jit(solution)/shard_map/ppermute | solution.py:19
  7.0 5.3 %collective-permute-start.2 = (s32[2,256]{1,0:T(2,128)}, s32[2,256]{1,0:T(2,128)S(1)}, u32[]{:S(2)}, u32[]{:S(2)}) collective-permute-start(s32[2,256]{1,0:T(2,128)} %param.9), channel_id=1, source_target_pairs={{0,2},{1,3},{2,0},{3,1},{4,6},{5,7},{6,4},{7,5},{8,10},{9,11},{10,... | collective-permute-start | bytes 6152 | tf_op jit(solution)/shard_map/ppermute | solution.py:19
  11.5 12.5 %collective-permute-start.4 = (bf16[1,2,256,256]{3,2,1,0:T(8,128)(2,1)}, bf16[1,2,256,256]{3,2,1,0:T(8,128)(2,1)S(1)}, u32[]{:S(2)}, u32[]{:S(2)}) collective-permute-start(bf16[1,2,256,256]{3,2,1,0:T(8,128)(2,1)} %param.7), channel_id=1, source_target_pairs={{0,16},{4,20},{8,24},{12,28},{16,0},{20,4},{24,8},{28,12},{1,17},{... | collective-permute-start | bytes 786440 | tf_op jit(solution)/shard_map/ppermute | solution.py:156
  24.1 0.9 %copy-start = (bf16[3,2,256,256]{3,2,1,0:T(8,128)(2,1)}, bf16[3,2,256,256]{3,2,1,0:T(8,128)(2,1)S(1)}, u32[]{:S(2)}) copy-start(bf16[3,2,256,256]{3,2,1,0:T(8,128)(2,1)S(1)} %constant_dynamic-update-slice_fusion.refs_0_) | copy-start | bytes 2359300
  24.1 6.8 %collective-permute-start.6 = (bf16[3,2,256,256]{3,2,1,0:T(8,128)(2,1)S(1)}, bf16[3,2,256,256]{3,2,1,0:T(8,128)(2,1)S(1)}, u32[]{:S(2)}, u32[]{:S(2)}) collective-permute-start(bf16[3,2,256,256]{3,2,1,0:T(8,128)(2,1)S(1)} %constant_dynamic-update-slice_fusion.refs_0_), channel_id=1, source_target_pairs={{0,4},{4,0},{8,12},{12,8},{16,20},{20,16},{24,28},{28,24},{1,5},{5... | collective-permute-start | bytes 2359304 | tf_op jit(solution)/shard_map/ppermute | solution.py:175
  30.9 0.9 %copy-start.2 = (bf16[3,2,256,256]{3,2,1,0:T(8,128)(2,1)}, bf16[3,2,256,256]{3,2,1,0:T(8,128)(2,1)S(1)}, u32[]{:S(2)}) copy-start(bf16[3,2,256,256]{3,2,1,0:T(8,128)(2,1)S(1)} %collective-permute-done.6.refs_0_) | copy-start | bytes 2359300

commit v4 on v3

--- a/solution.py
+++ b/solution.py
@@ -169,11 +169,9 @@
 
     if not fetched:
         return run(jnp.concatenate([greens, sibling], axis=0), prior=None, final=True)
-    partial_sums = run(jnp.concatenate([greens, sibling], axis=0), prior=None, final=False)
-    partial_sums, fetched = lax.optimization_barrier((partial_sums, fetched))
     near = jnp.concatenate(fetched, axis=0)
     forwarded = lax.ppermute(near, "blk", swap)
-    partial_sums = run(near, prior=partial_sums, final=False)
+    partial_sums = run(jnp.concatenate([greens, sibling, near], axis=0), prior=None, final=False)
     return run(forwarded, prior=partial_sums, final=True)
 
 

time: 39.2 us -> 39.7 us (1.013)
  waiting for transfers between devices: 0.02 us -> 4.75 us
  Pallas kernels: 17.6 us -> 14.4 us
  other arithmetic: 7.63 us -> 6.2 us
    ppermute x3, waiting for transfers between devices: 0.01 us -> 4.74 us  [local(): lax.ppermute(greens, 'blk', [(i, i ^ 2 * m) for i in range(blocks)])]
    pallas_call x3 -> x2, Pallas kernels: 17.6 us -> 14.4 us  [accumulate(): pl.pallas_call(kernel, grid=(steps,), cost_estimate=pl.CostEstimate(flops...]
    concatenate x1, other arithmetic: 0.84 us -> 0.09 us  [local(): near = jnp.concatenate(fetched, axis=0)]
    convert_element_type x1, other arithmetic: 0.69 us -> 0.01 us  [local(): angle = 2.0 * math.pi / NPH * phases.astype(F32)]
  transfers between devices with their start and end apart: 7 -> 7, of which waited for: 0 -> 1; matrix products, arithmetic and copies ran while one was open for 30% -> 29% of each run, Pallas kernels for 27% -> 19%
where the time goes in v4:
time: 39.7 us; the launch traced here: 39.3 us
  Pallas kernels  14.4 us (36%)
  starting transfers between devices  7.7 us (19%)
  other arithmetic  6.2 us (16%)
  local copies, waits for them, and re-layouts  6.12 us (15%)
  waiting for transfers between devices  4.75 us (12%)
    pallas_call x2, Pallas kernels, accumulate(): pl.pallas_call(kernel, grid=(steps,), cost_estimate=pl.CostEstimate(flops...  14.4 us
    ppermute x3, waiting for transfers between devices, local(): lax.ppermute(greens, 'blk', [(i, i ^ 2 * m) for i in range(blocks)])  4.74 us
    ppermute x3, starting transfers between devices, local(): lax.ppermute(greens, 'blk', [(i, i ^ 2 * m) for i in range(blocks)])  4.7 us
    ppermute x2, starting transfers between devices, passed_along(): lax.ppermute(value, axis, [(i, (i + by) % size) for i in range(size)])  2.92 us
    convert_element_type x2, other arithmetic, one_hot(): return (index_rows[..., :, None] == columns).astype(BF16)  2.47 us
    unnamed x9, local copies, waits for them, and re-layouts  2.1 us
    broadcast_in_dim x1, local copies, waits for them, and re-layouts, local(): col = trig[:, :, :, None]  1.33 us
    gather x2, local copies, waits for them, and re-layouts, local(): jnp.take(jnp.take(far_phase, partner_slot, axis=0), conj_index, axis=1)  0.81 us
  transfers between devices with their start and end apart: 7, of which 1 were waited for; matrix products, arithmetic and copies ran while one was open for 29% of the time, Pallas kernels for 19%

profile of v4, /device:TPU:0, one launch (start us, length us, event | category | flops | bytes accessed | tf_op | source)
XLA Modules:
  0.0 39.3 jit_solution(12701354242948129090)
XLA Ops:
  0.0 0.0 copy-start.1
  0.0 2.9 %collective-permute-start = (bf16[1,2,256,256]{3,2,1,0:T(8,128)(2,1)}, bf16[1,2,256,256]{3,2,1,0:T(8,128)(2,1)S(1)}, u32[]{:S(2)}, u32[]{:S(2)}) collective-permute-start(bf16[1,2,256,256]{3,2,1,0:T(8,128)(2,1)} %param.7), channel_id=1, source_target_pairs={{0,8},{4,12},{8,0},{12,4},{16,24},{20,28},{24,16},{28,20},{1,9},{5... | collective-permute-start | bytes 786440 | tf_op jit(solution)/shard_map/ppermute | solution.py:156
  2.9 0.0 collective-permute-start.6
  2.9 1.5 %collective-permute-start.1 = (bf16[1,2,256,256]{3,2,1,0:T(8,128)(2,1)}, bf16[1,2,256,256]{3,2,1,0:T(8,128)(2,1)S(1)}, u32[]{:S(2)}, u32[]{:S(2)}) collective-permute-start(bf16[1,2,256,256]{3,2,1,0:T(8,128)(2,1)} %param.7), channel_id=1, source_target_pairs={{0,16},{4,20},{8,24},{12,28},{16,0},{20,4},{24,8},{28,12},{1,17},{... | collective-permute-start | bytes 786440 | tf_op jit(solution)/shard_map/ppermute | solution.py:156
  4.5 2.6 %collective-permute-start.4 = (s32[2,256]{1,0:T(2,128)}, s32[2,256]{1,0:T(2,128)S(1)}, u32[]{:S(2)}, u32[]{:S(2)}) collective-permute-start(s32[2,256]{1,0:T(2,128)} %param.8), channel_id=1, source_target_pairs={{0,2},{1,3},{2,0},{3,1},{4,6},{5,7},{6,4},{7,5},{8,10},{9,11},{10,... | collective-permute-start | bytes 6152 | tf_op jit(solution)/shard_map/ppermute | solution.py:19
  7.1 0.3 collective-permute-start.5
  7.4 0.7 %compare_select_fusion.1 = s32[2]{0:T(128)S(1)} fusion(s32[2]{0:T(128)} %param.10), kind=kLoop, calls=%fused_computation.20 | loop fusion | flops 6 | bytes 16 | tf_op jit(solution)/shard_map/jit(_take)/jit(_where)/select_n | solution.py:158
  8.0 0.7 %compare_and_fusion = pred[2]{0:T(512)(128)(4,1)S(1)} fusion(s32[2]{0:T(128)} %param.10), kind=kLoop, calls=%fused_computation.24 | loop fusion | flops 12 | bytes 10 | tf_op jit(solution)/shard_map/jit(_take)/and | solution.py:158
  8.7 0.7 %compare_select_fusion = s32[256]{0:T(256)S(1)} fusion(s32[256]{0:T(256)} %param.11), kind=kLoop, calls=%fused_computation.19 | loop fusion | flops 768 | bytes 2048 | tf_op jit(solution)/shard_map/jit(_take)/jit(_where)/select_n | solution.py:159
  9.4 0.7 %compare_and_fusion.1 = pred[256]{0:T(512)(128)(4,1)S(1)} fusion(s32[256]{0:T(256)} %param.11), kind=kLoop, calls=%fused_computation.25 | loop fusion | flops 1536 | bytes 1280 | tf_op jit(solution)/shard_map/jit(_take)/and | solution.py:159
  10.1 1.0 %constant_dynamic-update-slice_fusion.4 = bf16[5,2,256,256]{3,2,1,0:T(8,128)(2,1)S(1)} fusion(bf16[1,2,256,256]{3,2,1,0:T(8,128)(2,1)} %param.7), kind=kLoop, calls=%fused_computation.12 | loop fusion | bytes 524288
  11.0 1.4 %fusion.1.refs_2_ = bf16[256,256]{1,0:T(8,128)(2,1)} fusion(s32[256]{0:T(256)} %param.11), kind=kLoop, calls=%fused_computation.7 | loop fusion | flops 131072 | bytes 132096 | tf_op jit(solution)/shard_map/convert_element_type | solution.py:24
  12.5 0.0 collective-permute-done.4
  12.5 0.2 collective-permute-start.2
  12.8 0.6 %gather_fusion.1 = s32[2,256]{1,0:T(2,128)S(1)} fusion(s32[2,256]{1,0:T(2,128)S(1)} %collective-permute-done.4, s32[1024]{0:T(1024)S(1)} %pad_clamp_fusion.1), kind=kCustom, calls=%fused_computation.clone | custom fusion | bytes 4104 | tf_op jit(solution)/shard_map/jit(_take)/gather | solution.py:158
  13.3 0.0 collective-permute-done.5
  13.3 0.6 %gather_fusion.2 = s32[2,256]{1,0:T(2,128)S(1)} fusion(s32[2,256]{1,0:T(2,128)S(1)} %collective-permute-done.5, s32[1024]{0:T(1024)S(1)} %pad_clamp_fusion.1), kind=kCustom, calls=%fused_computation.1.clone | custom fusion | bytes 4104 | tf_op jit(solution)/shard_map/jit(_take)/gather | solution.py:159
  13.9 0.1 broadcast_select_fusion
  14.0 0.1 copy.10
  14.1 0.7 %gather_fusion = s32[256,2]{1,0:T(8,128)S(1)} fusion(s32[2,256]{0,1:T(8,128)S(1)} %copy.10, s32[1024]{0:T(1024)S(1)} %pad_clamp_fusion), kind=kCustom, calls=%fused_computation.2 | custom fusion | bytes 5120 | tf_op jit(solution)/shard_map/jit(_take)/gather | solution.py:159
  14.8 0.1 copy.11
  14.9 0.7 %add_bitcast_fusion = s32[1,2,4,128]{3,2,1,0:T(4,128)S(1)} fusion(s32[2,256]{1,0:T(2,128)S(1)} %get-tuple-element.11, s32[2,256]{1,0:T(2,128)} %param.8), kind=kLoop, calls=%fused_computation.16 | loop fusion | flops 1024 | bytes 8192
  15.6 1.0 %fusion.refs_1_ = bf16[1024,256]{1,0:T(8,128)(2,1)} fusion(s32[1024]{0:T(1024)S(1)} %bitcast.10), kind=kLoop, calls=%fused_computation.4 | loop fusion | flops 524288 | bytes 528384 | tf_op jit(solution)/shard_map/convert_element_type | solution.py:24
  16.7 0.0 copy-done.1
  16.7 0.1 fusion.3
  16.8 0.0 collective-permute-done
  16.8 0.0 collective-permute-done.1
  16.8 4.7 %collective-permute-done.2 = bf16[1,2,256,256]{3,2,1,0:T(8,128)(2,1)S(1)} collective-permute-done((bf16[1,2,256,256]{3,2,1,0:T(8,128)(2,1)}, bf16[1,2,256,256]{3,2,1,0:T(8,128)(2,1)S(1)}, u32[]{:S(2)}, u32[]{:S(2)}) %collective-permute-start.2) | collective-permute-done | bytes 262176 | tf_op jit(solution)/shard_map/ppermute | solution.py:156
  21.6 0.1 pad_maximum_fusion
  21.7 0.1 collective-permute-start.3
  21.8 1.3 %copy.14.refs_3_ = f32[4,2,256,1]{3,2,1,0:T(8,128)} copy(f32[4,2,256,1]{2,1,0,3:T(2,128)S(1)} %get-tuple-element.7) | data formatting | bytes 16384 | tf_op jit(solution)/shard_map/broadcast_in_dim | solution.py:166
  23.1 0.6 %broadcast_in_dim.35.refs_4_ = f32[4,2,1,256]{3,2,1,0:T(1,128)} reshape(f32[4,2,256]{2,1,0:T(2,128)S(1)} %get-tuple-element.6) | data formatting | bytes 16384 | tf_op jit(solution)/shard_map/broadcast_in_dim | solution.py:167
  23.7 0.0 collective-permute-done.6
  23.8 0.0 copy-start
  23.8 1.1 %copy-done = bf16[5,2,256,256]{3,2,1,0:T(8,128)(2,1)} copy-done((bf16[5,2,256,256]{3,2,1,0:T(8,128)(2,1)}, bf16[5,2,256,256]{3,2,1,0:T(8,128)(2,1)S(1)}, u32[]{:S(2)}) %copy-start) | copy-done | bytes 1310744
  24.9 7.4 %shard_map.55.refs_5_ = f32[4,2,256,256]{3,2,1,0:T(8,128)} custom-call(bf16[5,2,256,256]{3,2,1,0:T(8,128)(2,1)} %copy-done, bf16[1024,256]{1,0:T(8,128)(2,1)} %fusion.refs_1_, bf16[256,256]{1,0:T(8,128)(2,1)} %fusion.1.refs_2_, f32[4,2,256,1]{3,2,1,0:T(8,128)} %copy.14.refs_3_, f32[4,2,1,256]{3,2,1,0:T(1,128)} %broadcast_in_dim.35.refs_4_), custom_call_target="tpu_custom_call" | custom-call | flops 2684354560 | bytes 3932160 | tf_op jit(solution)/shard_map/pallas_call | solution.py:132
  32.3 0.0 collective-permute-done.3.refs_0_
  32.3 7.0 %shard_map.56 = f32[2,2,256,256]{3,2,1,0:T(8,128)} custom-call(bf16[3,2,256,256]{3,2,1,0:T(8,128)(2,1)} %collective-permute-done.3.refs_0_, bf16[1024,256]{1,0:T(8,128)(2,1)} %fusion.refs_1_, bf16[256,256]{1,0:T(8,128)(2,1)} %fusion.1.refs_2_, f32[4,2,256,1]{3,2,1,0:T(8,128)} %copy.14.refs_3_, f32[4,2,1,256]{3,2,1,0:T(1,128)} %broadcast_in_dim.35.refs_4_, ...), custom_call_target="tpu_custom_call" | custom-call | flops 2415919104 | bytes 4456448 | tf_op jit(solution)/shard_map/pallas_call | solution.py:132
  (10 shorter events, 0.1 us)
Async XLA Ops:
  0.0 16.7 %copy-start.1 = (s32[2,256]{1,0:T(2,128)S(1)}, s32[2,256]{1,0:T(2,128)}, u32[]{:S(2)}) copy-start(s32[2,256]{1,0:T(2,128)} %param.9) | copy-start | bytes 6148
  0.0 16.8 %collective-permute-start = (bf16[1,2,256,256]{3,2,1,0:T(8,128)(2,1)}, bf16[1,2,256,256]{3,2,1,0:T(8,128)(2,1)S(1)}, u32[]{:S(2)}, u32[]{:S(2)}) collective-permute-start(bf16[1,2,256,256]{3,2,1,0:T(8,128)(2,1)} %param.7), channel_id=1, source_target_pairs={{0,8},{4,12},{8,0},{12,4},{16,24},{20,28},{24,16},{28,20},{1,9},{5... | collective-permute-start | bytes 786440 | tf_op jit(solution)/shard_map/ppermute | solution.py:156
  2.9 20.8 %collective-permute-start.6 = (bf16[1,2,256,256]{3,2,1,0:T(8,128)(2,1)}, bf16[1,2,256,256]{3,2,1,0:T(8,128)(2,1)S(1)}, u32[]{:S(2)}, u32[]{:S(2)}) collective-permute-start(bf16[1,2,256,256]{3,2,1,0:T(8,128)(2,1)} %param.7), channel_id=1, source_target_pairs={{0,4},{4,0},{8,12},{12,8},{16,20},{20,16},{24,28},{28,24},{1,5},{5... | collective-permute-start | bytes 786440 | tf_op jit(solution)/shard_map/ppermute | solution.py:155
  2.9 13.9 %collective-permute-start.1 = (bf16[1,2,256,256]{3,2,1,0:T(8,128)(2,1)}, bf16[1,2,256,256]{3,2,1,0:T(8,128)(2,1)S(1)}, u32[]{:S(2)}, u32[]{:S(2)}) collective-permute-start(bf16[1,2,256,256]{3,2,1,0:T(8,128)(2,1)} %param.7), channel_id=1, source_target_pairs={{0,16},{4,20},{8,24},{12,28},{16,0},{20,4},{24,8},{28,12},{1,17},{... | collective-permute-start | bytes 786440 | tf_op jit(solution)/shard_map/ppermute | solution.py:156
  4.5 8.0 %collective-permute-start.4 = (s32[2,256]{1,0:T(2,128)}, s32[2,256]{1,0:T(2,128)S(1)}, u32[]{:S(2)}, u32[]{:S(2)}) collective-permute-start(s32[2,256]{1,0:T(2,128)} %param.8), channel_id=1, source_target_pairs={{0,2},{1,3},{2,0},{3,1},{4,6},{5,7},{6,4},{7,5},{8,10},{9,11},{10,... | collective-permute-start | bytes 6152 | tf_op jit(solution)/shard_map/ppermute | solution.py:19
  7.1 6.3 %collective-permute-start.5 = (s32[2,256]{1,0:T(2,128)}, s32[2,256]{1,0:T(2,128)S(1)}, u32[]{:S(2)}, u32[]{:S(2)}) collective-permute-start(s32[2,256]{1,0:T(2,128)} %param.9), channel_id=1, source_target_pairs={{0,2},{1,3},{2,0},{3,1},{4,6},{5,7},{6,4},{7,5},{8,10},{9,11},{10,... | collective-permute-start | bytes 6152 | tf_op jit(solution)/shard_map/ppermute | solution.py:19
  12.5 9.1 %collective-permute-start.2 = (bf16[1,2,256,256]{3,2,1,0:T(8,128)(2,1)}, bf16[1,2,256,256]{3,2,1,0:T(8,128)(2,1)S(1)}, u32[]{:S(2)}, u32[]{:S(2)}) collective-permute-start(bf16[1,2,256,256]{3,2,1,0:T(8,128)(2,1)} %param.7), channel_id=1, source_target_pairs={{0,24},{4,28},{8,16},{12,20},{16,8},{20,12},{24,0},{28,4},{1,25},{... | collective-permute-start | bytes 786440 | tf_op jit(solution)/shard_map/ppermute | solution.py:156
  21.7 10.6 %collective-permute-start.3 = (bf16[3,2,256,256]{3,2,1,0:T(8,128)(2,1)S(1)}, bf16[3,2,256,256]{3,2,1,0:T(8,128)(2,1)}, u32[]{:S(2)}, u32[]{:S(2)}) collective-permute-start(bf16[3,2,256,256]{3,2,1,0:T(8,128)(2,1)S(1)} %pad_maximum_fusion), channel_id=1, source_target_pairs={{0,4},{4,0},{8,12},{12,8},{16,20},{20,16},{24,28},{28,24},{1,5},{5... | collective-permute-start | bytes 2359304 | tf_op jit(solution)/shard_map/ppermute | solution.py:173
  23.8 1.1 %copy-start = (bf16[5,2,256,256]{3,2,1,0:T(8,128)(2,1)}, bf16[5,2,256,256]{3,2,1,0:T(8,128)(2,1)S(1)}, u32[]{:S(2)}) copy-start(bf16[5,2,256,256]{3,2,1,0:T(8,128)(2,1)S(1)} %constant_dynamic-update-slice_fusion.refs_0_) | copy-start | bytes 3932164

commit v5 on v4

--- a/solution.py
+++ b/solution.py
@@ -12,16 +12,14 @@
 F32 = jnp.float32
 BF16 = jnp.bfloat16
 NT = (((1,), (1,)), ((), ()))
+ROOT_HALF = math.sqrt(0.5)
+COSINES = (1.0, ROOT_HALF, 0.0, -ROOT_HALF, -1.0, -ROOT_HALF, 0.0, ROOT_HALF)
+SINES = (0.0, ROOT_HALF, 1.0, ROOT_HALF, 0.0, -ROOT_HALF, -1.0, -ROOT_HALF)
 
 
 def passed_along(value, axis, by):
     size = lax.axis_size(axis)
     return lax.ppermute(value, axis, [(i, (i + by) % size) for i in range(size)])
-
-
-def one_hot(index_rows, width):
-    columns = jnp.arange(width, dtype=jnp.int32)
-    return (index_rows[..., :, None] == columns).astype(BF16)
 
 
 def split3(x):
@@ -41,10 +39,17 @@
     return total
 
 
-def add_walker(g_ref, p_ref, acc_ref, slots, width):
+def table(levels, values):
+    out = jnp.zeros(levels.shape, F32)
+    for k, v in enumerate(values):
+        out = jnp.where(levels == k, v, out)
+    return out
+
+
+def add_walker(g_ref, sel_ref, acc_ref, slots, width):
     g_re = g_ref[0, 0]
     g_im = g_ref[0, 1]
-    sel = p_ref[...]
+    sel = sel_ref[...]
     y_re = jnp.dot(sel, g_re, preferred_element_type=F32).astype(BF16)
     y_im = jnp.dot(sel, g_im, preferred_element_type=F32).astype(BF16)
     gr = g_re.astype(F32)
@@ -60,19 +65,36 @@
 
 def accumulate_kernel(*refs, slots, width, scale, has_prior, final):
     if has_prior:
-        g_ref, p_ref, q_ref, col_ref, row_ref, prior_hbm, out_ref, acc_ref, prior_ref, sem = refs
+        (g_ref, ti_ref, ph_ref, far_ref, slot_ref, cj_ref, prior_hbm, out_ref,
+         acc_ref, sel_ref, prior_ref, sem) = refs
     else:
-        g_ref, p_ref, q_ref, col_ref, row_ref, out_ref, acc_ref = refs
+        g_ref, ti_ref, ph_ref, far_ref, slot_ref, cj_ref, out_ref, acc_ref, sel_ref = refs
     w = pl.program_id(0)
     last = pl.num_programs(0) - 1
+    nt = 2 * slots
+    lanes = lax.broadcasted_iota(jnp.int32, (width, width), 1).astype(F32)
+
+    def columns():
+        far = far_ref[...]
+        rows = [ti_ref[pl.ds(s, 1), :] for s in range(slots)]
+        for s in range(slots):
+            pick = slot_ref[s]
+            rows.append(jnp.where(pick == 0, far[0:1], far[1:2]))
+        rows.append(cj_ref[...])
+        block = jnp.concatenate(rows, axis=0).astype(F32)
+        block = jnp.concatenate([block, jnp.zeros((128 - block.shape[0], width), F32)], axis=0)
+        return block.T
 
     @pl.when(w == 0)
     def _():
         acc_ref[...] = jnp.zeros(acc_ref.shape, F32)
         if has_prior:
             pltpu.make_async_copy(prior_hbm, prior_ref, sem).start()
-
-    add_walker(g_ref, p_ref, acc_ref, slots, width)
+        cols = columns()
+        for t in range(nt):
+            sel_ref[t * width:(t + 1) * width] = (cols[:, t:t + 1] == lanes).astype(BF16)
+
+    add_walker(g_ref, sel_ref, acc_ref, slots, width)
 
     @pl.when(w == last)
     def _():
@@ -84,19 +106,27 @@
             else:
                 out_ref[...] = acc_ref[...]
             return
-        q = q_ref[...]
+        cols = columns()
+        q = (cols[:, nt:nt + 1] == lanes).astype(BF16)
+        far = far_ref[...]
+        partner = [jnp.where(slot_ref[s] == 0, far[2:3], far[3:4]) for s in range(slots)]
+        partner = jnp.concatenate(partner + [jnp.zeros((8 - slots, width), jnp.int32)], axis=0)
+        partner = lax.dot_general(partner.astype(F32).astype(BF16), q, NT, preferred_element_type=F32)
+        levels = jnp.concatenate([ph_ref[...].astype(F32), partner[:slots]], axis=0)
+        trig = jnp.concatenate([table(levels, COSINES), table(levels, SINES)], axis=0)
+        trig_cols = jnp.concatenate([trig, jnp.zeros((128 - 2 * nt, width), F32)], axis=0).T
         for s in range(slots):
             parts = []
             for t, permute in ((s, False), (s + slots, True)):
-                t_re = acc_ref[t, 0] + prior_ref[t, 0]
-                t_im = acc_ref[t, 1] + prior_ref[t, 1]
+                t_re = acc_ref[t, 0] + prior_ref[t, 0] if has_prior else acc_ref[t, 0]
+                t_im = acc_ref[t, 1] + prior_ref[t, 1] if has_prior else acc_ref[t, 1]
                 if permute:
                     t_re = conj_permuted(q, t_re)
                     t_im = -conj_permuted(q, t_im)
-                ca = col_ref[t, 0]
-                sa = col_ref[t, 1]
-                cb = row_ref[t, 0]
-                sb = row_ref[t, 1]
+                ca = trig_cols[:, t:t + 1]
+                sa = trig_cols[:, nt + t:nt + t + 1]
+                cb = trig[t:t + 1]
+                sb = trig[nt + t:nt + t + 1]
                 rot_re = ca * cb + sa * sb
                 rot_im = sa * cb - ca * sb
                 parts.append((rot_re * t_re - rot_im * t_im, rot_re * t_im + rot_im * t_re))
@@ -105,7 +135,7 @@
             out_ref[s, 1] = (own_im + mir_im) * scale
 
 
-def accumulate(walkers, sel, q, col, row, prior, final, slots, width, scale):
+def accumulate(walkers, info, prior, final, slots, width, scale):
     has_prior = prior is not None
     kernel = functools.partial(
         accumulate_kernel, slots=slots, width=width, scale=scale, has_prior=has_prior, final=final
@@ -113,22 +143,24 @@
     full = lambda shape: pl.BlockSpec(shape, lambda w: (0,) * len(shape))
     acc_shape = (2 * slots, 2, width, width)
     out_shape = (slots, 2, width, width) if final else acc_shape
+    ti, ph, far, slot, cj = info
     in_specs = [
         pl.BlockSpec((1, 2, width, width), lambda w: (w, 0, 0, 0)),
-        full(sel.shape),
-        full(q.shape),
-        full(col.shape),
-        full(row.shape),
+        full(ti.shape),
+        full(ph.shape),
+        full(far.shape),
+        pl.BlockSpec(memory_space=pltpu.SMEM),
+        full(cj.shape),
     ]
-    scratch = [pltpu.VMEM(acc_shape, F32)]
-    operands = [walkers, sel, q, col, row]
+    scratch = [pltpu.VMEM(acc_shape, F32), pltpu.VMEM((2 * slots * width, width), BF16)]
+    operands = [walkers, ti, ph, far, slot, cj]
     if has_prior:
         in_specs.append(pl.BlockSpec(memory_space=pl.ANY))
         scratch += [pltpu.VMEM(acc_shape, F32), pltpu.SemaphoreType.DMA(())]
         operands.append(prior)
     steps = walkers.shape[0]
     flops = steps * 2 * slots * 8 * width**3 + (12 * slots * 2 * width**3 if final else 0)
-    moved = walkers.size * 2 + sel.size * 2 + 4 * math.prod(out_shape) + (4 * math.prod(acc_shape) if has_prior else 0)
+    moved = walkers.size * 2 + 4 * math.prod(out_shape) + (4 * math.prod(acc_shape) if has_prior else 0)
     return pl.pallas_call(
         kernel,
         grid=(steps,),
@@ -147,25 +179,14 @@
     blocks = lax.axis_size("blk")
     halfway = lax.axis_size("xfer") // 2
     scale = 0.5 / math.sqrt(blocks)
-    assert blocks % 2 == 0 and blocks & (blocks - 1) == 0
-
-    far_index = passed_along(transfer_index, "xfer", halfway)
-    far_phase = passed_along(phase_index, "xfer", halfway)
+    assert blocks % 2 == 0 and blocks & (blocks - 1) == 0 and 4 * slots + 1 <= 128
+
     swap = [(i, i ^ 1) for i in range(blocks)]
     sibling = lax.ppermute(greens, "blk", swap)
     fetched = [lax.ppermute(greens, "blk", [(i, i ^ (2 * m)) for i in range(blocks)]) for m in range(1, blocks // 2)]
-
-    match_index = jnp.take(far_index, partner_slot, axis=0)
-    match_phase = jnp.take(jnp.take(far_phase, partner_slot, axis=0), conj_index, axis=1)
-    rows = jnp.concatenate([transfer_index, match_index], axis=0)
-    sel = one_hot(rows, width).reshape(2 * slots * width, width)
-    q = one_hot(conj_index, width)
-    phases = jnp.concatenate([phase_index, match_phase], axis=0)
-    angle = (2.0 * math.pi / NPH) * phases.astype(F32)
-    trig = jnp.stack([jnp.cos(angle), jnp.sin(angle)], axis=1)
-    col = trig[:, :, :, None]
-    row = trig[:, :, None, :]
-    run = functools.partial(accumulate, sel=sel, q=q, col=col, row=row, slots=slots, width=width, scale=scale)
+    far = passed_along(jnp.concatenate([transfer_index, phase_index], axis=0), "xfer", halfway)
+    info = (transfer_index, phase_index, far, partner_slot, conj_index.reshape(1, width))
+    run = functools.partial(accumulate, info=info, slots=slots, width=width, scale=scale)
 
     if not fetched:
         return run(jnp.concatenate([greens, sibling], axis=0), prior=None, final=True)

time: 39.7 us -> 32.9 us (0.83)
  other arithmetic: 6.2 us -> 0.79 us
  local copies, waits for them, and re-layouts: 6.12 us -> 2.02 us
  waiting for transfers between devices: 4.75 us -> 8.31 us
  Pallas kernels: 14.4 us -> 13.8 us
    ppermute x3, waiting for transfers between devices: 4.74 us -> 8.3 us  [local(): lax.ppermute(greens, 'blk', [(i, i ^ 2 * m) for i in range(blocks)])]
    convert_element_type x3 -> x0, other arithmetic: 2.48 us -> none  [the longest x2 2.47 us: one_hot(): return (index_rows[..., :, None] == columns).astype(BF16)]
    broadcast_in_dim x2 -> x0, local copies, waits for them, and re-layouts: 1.94 us -> none  [the longest x1 1.33 us: local(): col = trig[:, :, :, None]]
    gather x4 -> x0, local copies, waits for them, and re-layouts: 1.93 us -> none  [the longest x2 0.81 us: local(): jnp.take(jnp.take(far_phase, partner_slot, axis=0), conj_index, axis=1)]
    select_n x3 -> x0, other arithmetic: 1.41 us -> none  [the longest x1 0.68 us: local(): jnp.take(jnp.take(far_phase, partner_slot, axis=0), conj_index, axis=1)]
    and x2 -> x0, other arithmetic: 1.35 us -> none  [the longest x1 0.68 us: local(): jnp.take(jnp.take(far_phase, partner_slot, axis=0), conj_index, axis=1)]
    unnamed x1 -> x0, other arithmetic: 0.7 us -> none
    concatenate x1, other arithmetic: 0.01 us -> 0.71 us  [local(): jnp.concatenate([transfer_index, phase_index], axis=0)]
  transfers between devices with their start and end apart: 7 -> 6, of which waited for: 1 -> 2; matrix products, arithmetic and copies ran while one was open for 29% -> 3% of each run, Pallas kernels for 19% -> 22%
where the time goes in v5:
time: 32.9 us; the launch traced here: 32.6 us
  Pallas kernels  13.8 us (42%)
  waiting for transfers between devices  8.31 us (25%)
  starting transfers between devices  7.6 us (23%)
  local copies, waits for them, and re-layouts  2.02 us (6%)
  other arithmetic  0.79 us (2%)
    pallas_call x2, Pallas kernels, accumulate(): pl.pallas_call(kernel, grid=(steps,), cost_estimate=pl.CostEstimate(flops...  13.8 us
    ppermute x3, waiting for transfers between devices, local(): lax.ppermute(greens, 'blk', [(i, i ^ 2 * m) for i in range(blocks)])  8.3 us
    ppermute x3, starting transfers between devices, local(): lax.ppermute(greens, 'blk', [(i, i ^ 2 * m) for i in range(blocks)])  4.46 us
    ppermute x1, starting transfers between devices, passed_along(): lax.ppermute(value, axis, [(i, (i + by) % size) for i in range(size)])  3.06 us
    unnamed x12, local copies, waits for them, and re-layouts  2 us
    concatenate x1, other arithmetic, local(): jnp.concatenate([transfer_index, phase_index], axis=0)  0.71 us
  transfers between devices with their start and end apart: 6, of which 2 were waited for; matrix products, arithmetic and copies ran while one was open for 3% of the time, Pallas kernels for 22%

profile of v5, /device:TPU:0, one launch (start us, length us, event | category | flops | bytes accessed | tf_op | source)
XLA Modules:
  0.0 32.6 jit_solution(4291194554261729177)
XLA Ops:
  0.0 0.0 copy-start
  0.0 2.9 %collective-permute-start = (bf16[1,2,256,256]{3,2,1,0:T(8,128)(2,1)}, bf16[1,2,256,256]{3,2,1,0:T(8,128)(2,1)S(1)}, u32[]{:S(2)}, u32[]{:S(2)}) collective-permute-start(bf16[1,2,256,256]{3,2,1,0:T(8,128)(2,1)} %param.5), channel_id=1, source_target_pairs={{0,8},{4,12},{8,0},{12,4},{16,24},{20,28},{24,16},{28,20},{1,9},{5... | collective-permute-start | bytes 786440 | tf_op jit(solution)/shard_map/ppermute | solution.py:186
  2.9 1.5 %collective-permute-start.1 = (bf16[1,2,256,256]{3,2,1,0:T(8,128)(2,1)}, bf16[1,2,256,256]{3,2,1,0:T(8,128)(2,1)S(1)}, u32[]{:S(2)}, u32[]{:S(2)}) collective-permute-start(bf16[1,2,256,256]{3,2,1,0:T(8,128)(2,1)} %param.5), channel_id=1, source_target_pairs={{0,16},{4,20},{8,24},{12,28},{16,0},{20,4},{24,8},{28,12},{1,17},{... | collective-permute-start | bytes 786440 | tf_op jit(solution)/shard_map/ppermute | solution.py:186
  4.5 0.0 collective-permute-start.2
  4.5 0.0 collective-permute-start.5
  4.5 0.7 %pad_add_fusion = s32[4,256]{1,0:T(4,128)S(1)} fusion(s32[2,256]{1,0:T(2,128)} %refs_2_.3, s32[2,256]{1,0:T(2,128)} %refs_1_.3), kind=kLoop, calls=%fused_computation.6 | loop fusion | flops 1024 | bytes 8192 | tf_op jit(solution)/shard_map/concatenate | solution.py:187
  5.2 3.1 %collective-permute-start.4 = (s32[4,256]{1,0:T(4,128)S(1)}, s32[4,256]{1,0:T(4,128)S(1)}, u32[]{:S(2)}, u32[]{:S(2)}) collective-permute-start(s32[4,256]{1,0:T(4,128)S(1)} %pad_add_fusion), channel_id=1, source_target_pairs={{0,2},{1,3},{2,0},{3,1},{4,6},{5,7},{6,4},{7,5},{8,10},{9,11},{10,... | collective-permute-start | bytes 12296 | tf_op jit(solution)/shard_map/ppermute | solution.py:22
  8.2 2.1 %collective-permute-done = bf16[1,2,256,256]{3,2,1,0:T(8,128)(2,1)S(1)} collective-permute-done((bf16[1,2,256,256]{3,2,1,0:T(8,128)(2,1)}, bf16[1,2,256,256]{3,2,1,0:T(8,128)(2,1)S(1)}, u32[]{:S(2)}, u32[]{:S(2)}) %collective-permute-start) | collective-permute-done | bytes 262176 | tf_op jit(solution)/shard_map/ppermute | solution.py:186
  10.4 6.2 %collective-permute-done.1 = bf16[1,2,256,256]{3,2,1,0:T(8,128)(2,1)S(1)} collective-permute-done((bf16[1,2,256,256]{3,2,1,0:T(8,128)(2,1)}, bf16[1,2,256,256]{3,2,1,0:T(8,128)(2,1)S(1)}, u32[]{:S(2)}, u32[]{:S(2)}) %collective-permute-start.1) | collective-permute-done | bytes 262176 | tf_op jit(solution)/shard_map/ppermute | solution.py:186
  16.5 0.0 collective-permute-done.2
  16.5 0.1 pad_maximum_fusion
  16.6 0.1 collective-permute-start.3
  16.7 0.0 copy-done
  16.7 0.0 collective-permute-done.5
  16.9 0.0 copy-start.1
  16.9 0.0 collective-permute-done.4.refs_3_
  16.9 0.0 copy-start.3
  16.9 1.0 %copy-done.1 = bf16[5,2,256,256]{3,2,1,0:T(8,128)(2,1)} copy-done((bf16[5,2,256,256]{3,2,1,0:T(8,128)(2,1)}, bf16[5,2,256,256]{3,2,1,0:T(8,128)(2,1)S(1)}, u32[]{:S(2)}) %copy-start.1) | copy-done | bytes 1310744
  17.9 0.0 copy-done.3
  17.9 7.1 %shard_map.55.refs_6_ = f32[4,2,256,256]{3,2,1,0:T(8,128)} custom-call(bf16[5,2,256,256]{3,2,1,0:T(8,128)(2,1)} %copy-done.1, s32[2,256]{1,0:T(2,128)} %refs_1_.3, s32[2,256]{1,0:T(2,128)} %refs_2_.3, s32[4,256]{1,0:T(4,128)} %copy-done.3, s32[2]{0:T(128)} %refs_4_.3, s32[1,256]{1,0:T(1,128)} %bitcast.1), custom_call_target="tpu_custom_call" | custom-call | flops 2684354560 | bytes 3407872 | tf_op jit(solution)/shard_map/pallas_call | solution.py:164
  25.1 0.0 collective-permute-done.3.refs_0_
  25.1 0.0 copy-start.2
  25.1 0.9 %copy-done.2 = bf16[3,2,256,256]{3,2,1,0:T(8,128)(2,1)} copy-done((bf16[3,2,256,256]{3,2,1,0:T(8,128)(2,1)}, bf16[3,2,256,256]{3,2,1,0:T(8,128)(2,1)S(1)}, u32[]{:S(2)}) %copy-start.2) | copy-done | bytes 786456
  25.9 6.7 %shard_map.56 = f32[2,2,256,256]{3,2,1,0:T(8,128)} custom-call(bf16[3,2,256,256]{3,2,1,0:T(8,128)(2,1)} %copy-done.2, s32[2,256]{1,0:T(2,128)} %refs_1_.3, s32[2,256]{1,0:T(2,128)} %refs_2_.3, s32[4,256]{1,0:T(4,128)} %copy-done.3, s32[2]{0:T(128)} %refs_4_.3, s32[1,256]{1,0:T(1,128)} %bitcast.2, f32[4,2,256,256]{3,2,1,0:T(8,128)} %shard_map.55.refs_6_), custom_call_target="tpu_custom_call" | custom-call | flops 2415919104 | bytes 3932160 | tf_op jit(solution)/shard_map/pallas_call | solution.py:164
  (5 shorter events, 0.1 us)
Async XLA Ops:
  0.0 16.7 %copy-start = (bf16[1,2,256,256]{3,2,1,0:T(8,128)(2,1)S(1)}, bf16[1,2,256,256]{3,2,1,0:T(8,128)(2,1)}, u32[]{:S(2)}) copy-start(bf16[1,2,256,256]{3,2,1,0:T(8,128)(2,1)} %param.5) | copy-start | bytes 786436
  0.0 10.4 %collective-permute-start = (bf16[1,2,256,256]{3,2,1,0:T(8,128)(2,1)}, bf16[1,2,256,256]{3,2,1,0:T(8,128)(2,1)S(1)}, u32[]{:S(2)}, u32[]{:S(2)}) collective-permute-start(bf16[1,2,256,256]{3,2,1,0:T(8,128)(2,1)} %param.5), channel_id=1, source_target_pairs={{0,8},{4,12},{8,0},{12,4},{16,24},{20,28},{24,16},{28,20},{1,9},{5... | collective-permute-start | bytes 786440 | tf_op jit(solution)/shard_map/ppermute | solution.py:186
  2.9 13.6 %collective-permute-start.1 = (bf16[1,2,256,256]{3,2,1,0:T(8,128)(2,1)}, bf16[1,2,256,256]{3,2,1,0:T(8,128)(2,1)S(1)}, u32[]{:S(2)}, u32[]{:S(2)}) collective-permute-start(bf16[1,2,256,256]{3,2,1,0:T(8,128)(2,1)} %param.5), channel_id=1, source_target_pairs={{0,16},{4,20},{8,24},{12,28},{16,0},{20,4},{24,8},{28,12},{1,17},{... | collective-permute-start | bytes 786440 | tf_op jit(solution)/shard_map/ppermute | solution.py:186
  4.5 12.1 %collective-permute-start.2 = (bf16[1,2,256,256]{3,2,1,0:T(8,128)(2,1)}, bf16[1,2,256,256]{3,2,1,0:T(8,128)(2,1)S(1)}, u32[]{:S(2)}, u32[]{:S(2)}) collective-permute-start(bf16[1,2,256,256]{3,2,1,0:T(8,128)(2,1)} %param.5), channel_id=1, source_target_pairs={{0,24},{4,28},{8,16},{12,20},{16,8},{20,12},{24,0},{28,4},{1,25},{... | collective-permute-start | bytes 786440 | tf_op jit(solution)/shard_map/ppermute | solution.py:186
  4.5 12.3 %collective-permute-start.5 = (bf16[1,2,256,256]{3,2,1,0:T(8,128)(2,1)}, bf16[1,2,256,256]{3,2,1,0:T(8,128)(2,1)S(1)}, u32[]{:S(2)}, u32[]{:S(2)}) collective-permute-start(bf16[1,2,256,256]{3,2,1,0:T(8,128)(2,1)} %param.5), channel_id=1, source_target_pairs={{0,4},{4,0},{8,12},{12,8},{16,20},{20,16},{24,28},{28,24},{1,5},{5... | collective-permute-start | bytes 786440 | tf_op jit(solution)/shard_map/ppermute | solution.py:185
  5.2 11.7 %collective-permute-start.4 = (s32[4,256]{1,0:T(4,128)S(1)}, s32[4,256]{1,0:T(4,128)S(1)}, u32[]{:S(2)}, u32[]{:S(2)}) collective-permute-start(s32[4,256]{1,0:T(4,128)S(1)} %pad_add_fusion), channel_id=1, source_target_pairs={{0,2},{1,3},{2,0},{3,1},{4,6},{5,7},{6,4},{7,5},{8,10},{9,11},{10,... | collective-permute-start | bytes 12296 | tf_op jit(solution)/shard_map/ppermute | solution.py:22
  16.6 8.4 %collective-permute-start.3 = (bf16[3,2,256,256]{3,2,1,0:T(8,128)(2,1)S(1)}, bf16[3,2,256,256]{3,2,1,0:T(8,128)(2,1)S(1)}, u32[]{:S(2)}, u32[]{:S(2)}) collective-permute-start(bf16[3,2,256,256]{3,2,1,0:T(8,128)(2,1)S(1)} %pad_maximum_fusion), channel_id=1, source_target_pairs={{0,4},{4,0},{8,12},{12,8},{16,20},{20,16},{24,28},{28,24},{1,5},{5... | collective-permute-start | bytes 2359304 | tf_op jit(solution)/shard_map/ppermute | solution.py:194
  16.9 1.1 %copy-start.1 = (bf16[5,2,256,256]{3,2,1,0:T(8,128)(2,1)}, bf16[5,2,256,256]{3,2,1,0:T(8,128)(2,1)S(1)}, u32[]{:S(2)}) copy-start(bf16[5,2,256,256]{3,2,1,0:T(8,128)(2,1)S(1)} %constant_dynamic-update-slice_fusion.refs_0_) | copy-start | bytes 3932164
  16.9 1.0 %copy-start.3 = (s32[4,256]{1,0:T(4,128)}, s32[4,256]{1,0:T(4,128)S(1)}, u32[]{:S(2)}) copy-start(s32[4,256]{1,0:T(4,128)S(1)} %collective-permute-done.4.refs_3_) | copy-start | bytes 12292
  25.1 0.9 %copy-start.2 = (bf16[3,2,256,256]{3,2,1,0:T(8,128)(2,1)}, bf16[3,2,256,256]{3,2,1,0:T(8,128)(2,1)S(1)}, u32[]{:S(2)}) copy-start(bf16[3,2,256,256]{3,2,1,0:T(8,128)(2,1)S(1)} %collective-permute-done.3.refs_0_) | copy-start | bytes 2359300

commit v6 on v5

--- a/solution.py
+++ b/solution.py
@@ -190,9 +190,11 @@
 
     if not fetched:
         return run(jnp.concatenate([greens, sibling], axis=0), prior=None, final=True)
+    partial_sums = run(jnp.concatenate([greens, sibling], axis=0), prior=None, final=False)
+    partial_sums, fetched = lax.optimization_barrier((partial_sums, fetched))
     near = jnp.concatenate(fetched, axis=0)
     forwarded = lax.ppermute(near, "blk", swap)
-    partial_sums = run(jnp.concatenate([greens, sibling, near], axis=0), prior=None, final=False)
+    partial_sums = run(near, prior=partial_sums, final=False)
     return run(forwarded, prior=partial_sums, final=True)
 
 

time: 32.9 us -> 32.8 us (level)
  waiting for transfers between devices: 8.31 us -> 3.41 us
  Pallas kernels: 13.8 us -> 16.6 us
  other arithmetic: 0.79 us -> 2.5 us
    ppermute x3, waiting for transfers between devices: 8.3 us -> 3.41 us  [local(): lax.ppermute(greens, 'blk', [(i, i ^ 2 * m) for i in range(blocks)])]
    pallas_call x2 -> x3, Pallas kernels: 13.8 us -> 16.6 us  [accumulate(): pl.pallas_call(kernel, grid=(steps,), cost_estimate=pl.CostEstimate(flops...]
    concatenate x1, other arithmetic: 0.09 us -> 1.79 us  [local(): jnp.concatenate([greens, sibling], axis=0)]
    ppermute x1, starting transfers between devices: 0.01 us -> 0.45 us  [local(): sibling = lax.ppermute(greens, 'blk', swap)]
    ppermute x3, starting transfers between devices: 4.46 us -> 4.02 us  [local(): lax.ppermute(greens, 'blk', [(i, i ^ 2 * m) for i in range(blocks)])]
    unnamed x12 -> x8, local copies, waits for them, and re-layouts: 2 us -> 2.29 us
  transfers between devices with their start and end apart: 6 -> 6, of which waited for: 2 -> 2; matrix products, arithmetic and copies ran while one was open for 3% -> 8% of each run, Pallas kernels for 22% -> 31%
where the time goes in v6:
time: 32.8 us; the launch traced here: 32.5 us
  Pallas kernels  16.6 us (51%)
  starting transfers between devices  7.6 us (23%)
  waiting for transfers between devices  3.41 us (10%)
  other arithmetic  2.5 us (8%)
  local copies, waits for them, and re-layouts  2.31 us (7%)
    pallas_call x3, Pallas kernels, accumulate(): pl.pallas_call(kernel, grid=(steps,), cost_estimate=pl.CostEstimate(flops...  16.6 us
    ppermute x3, starting transfers between devices, local(): lax.ppermute(greens, 'blk', [(i, i ^ 2 * m) for i in range(blocks)])  4.02 us
    ppermute x3, waiting for transfers between devices, local(): lax.ppermute(greens, 'blk', [(i, i ^ 2 * m) for i in range(blocks)])  3.41 us
    ppermute x1, starting transfers between devices, passed_along(): lax.ppermute(value, axis, [(i, (i + by) % size) for i in range(size)])  3.05 us
    unnamed x8, local copies, waits for them, and re-layouts  2.29 us
    concatenate x1, other arithmetic, local(): jnp.concatenate([greens, sibling], axis=0)  1.79 us
    concatenate x1, other arithmetic, local(): jnp.concatenate([transfer_index, phase_index], axis=0)  0.71 us
  transfers between devices with their start and end apart: 6, of which 2 were waited for; matrix products, arithmetic and copies ran while one was open for 8% of the time, Pallas kernels for 31%

profile of v6, /device:TPU:0, one launch (start us, length us, event | category | flops | bytes accessed | tf_op | source)
XLA Modules:
  0.0 32.5 jit_solution(930730850074207122)
XLA Ops:
  0.0 0.5 %collective-permute-start = (bf16[1,2,256,256]{3,2,1,0:T(8,128)(2,1)}, bf16[1,2,256,256]{3,2,1,0:T(8,128)(2,1)S(1)}, u32[]{:S(2)}, u32[]{:S(2)}) collective-permute-start(bf16[1,2,256,256]{3,2,1,0:T(8,128)(2,1)} %param.5), channel_id=1, source_target_pairs={{0,4},{4,0},{8,12},{12,8},{16,20},{20,16},{24,28},{28,24},{1,5},{5... | collective-permute-start | bytes 786440 | tf_op jit(solution)/shard_map/ppermute | solution.py:185
  0.5 2.5 %collective-permute-start.2 = (bf16[1,2,256,256]{3,2,1,0:T(8,128)(2,1)}, bf16[1,2,256,256]{3,2,1,0:T(8,128)(2,1)S(1)}, u32[]{:S(2)}, u32[]{:S(2)}) collective-permute-start(bf16[1,2,256,256]{3,2,1,0:T(8,128)(2,1)} %param.5), channel_id=1, source_target_pairs={{0,8},{4,12},{8,0},{12,4},{16,24},{20,28},{24,16},{28,20},{1,9},{5... | collective-permute-start | bytes 786440 | tf_op jit(solution)/shard_map/ppermute | solution.py:186
  2.9 1.5 %collective-permute-start.4 = (bf16[1,2,256,256]{3,2,1,0:T(8,128)(2,1)}, bf16[1,2,256,256]{3,2,1,0:T(8,128)(2,1)S(1)}, u32[]{:S(2)}, u32[]{:S(2)}) collective-permute-start(bf16[1,2,256,256]{3,2,1,0:T(8,128)(2,1)} %param.5), channel_id=1, source_target_pairs={{0,24},{4,28},{8,16},{12,20},{16,8},{20,12},{24,0},{28,4},{1,25},{... | collective-permute-start | bytes 786440 | tf_op jit(solution)/shard_map/ppermute | solution.py:186
  4.4 0.0 collective-permute-start.3
  4.5 0.7 %pad_add_fusion = s32[4,256]{1,0:T(4,128)S(1)} fusion(s32[2,256]{1,0:T(2,128)} %refs_2_.5, s32[2,256]{1,0:T(2,128)} %refs_1_.5), kind=kLoop, calls=%fused_computation.4 | loop fusion | flops 1024 | bytes 8192 | tf_op jit(solution)/shard_map/concatenate | solution.py:187
  5.2 3.1 %collective-permute-start.1 = (s32[4,256]{1,0:T(4,128)S(1)}, s32[4,256]{1,0:T(4,128)S(1)}, u32[]{:S(2)}, u32[]{:S(2)}) collective-permute-start(s32[4,256]{1,0:T(4,128)S(1)} %pad_add_fusion), channel_id=1, source_target_pairs={{0,2},{1,3},{2,0},{3,1},{4,6},{5,7},{6,4},{7,5},{8,10},{9,11},{10,... | collective-permute-start | bytes 12296 | tf_op jit(solution)/shard_map/ppermute | solution.py:22
  8.2 0.0 collective-permute-done
  8.2 1.8 %pad_maximum_fusion.refs_0_ = bf16[2,2,256,256]{3,2,1,0:T(8,128)(2,1)} fusion(bf16[1,2,256,256]{3,2,1,0:T(8,128)(2,1)S(1)} %collective-permute-done, bf16[1,2,256,256]{3,2,1,0:T(8,128)(2,1)} %param.5), kind=kLoop, calls=%fused_computation | loop fusion | flops 262144 | bytes 1048576 | tf_op jit(solution)/shard_map/concatenate | solution.py:193
  10.0 0.0 collective-permute-done.1.refs_3_
  10.0 0.0 copy-start.2
  10.0 0.6 %copy-done.2 = s32[4,256]{1,0:T(4,128)} copy-done((s32[4,256]{1,0:T(4,128)}, s32[4,256]{1,0:T(4,128)S(1)}, u32[]{:S(2)}) %copy-start.2) | copy-done | bytes 4120
  10.6 4.4 %shard_map.55.refs_6_ = f32[4,2,256,256]{3,2,1,0:T(8,128)} custom-call(bf16[2,2,256,256]{3,2,1,0:T(8,128)(2,1)} %pad_maximum_fusion.refs_0_, s32[2,256]{1,0:T(2,128)} %refs_1_.5, s32[2,256]{1,0:T(2,128)} %refs_2_.5, s32[4,256]{1,0:T(4,128)} %copy-done.2, s32[2]{0:T(128)} %refs_4_.5, s32[1,256]{1,0:T(1,128)} %bitcast.1), custom_call_target="tpu_custom_call" | custom-call | flops 1073741824 | bytes 2621440 | tf_op jit(solution)/shard_map/pallas_call | solution.py:164
  15.0 0.0 collective-permute-done.2
  15.0 2.0 %collective-permute-done.4 = bf16[1,2,256,256]{3,2,1,0:T(8,128)(2,1)S(1)} collective-permute-done((bf16[1,2,256,256]{3,2,1,0:T(8,128)(2,1)}, bf16[1,2,256,256]{3,2,1,0:T(8,128)(2,1)S(1)}, u32[]{:S(2)}, u32[]{:S(2)}) %collective-permute-start.4) | collective-permute-done | bytes 262176 | tf_op jit(solution)/shard_map/ppermute | solution.py:186
  17.1 1.4 %collective-permute-done.3 = bf16[1,2,256,256]{3,2,1,0:T(8,128)(2,1)S(1)} collective-permute-done((bf16[1,2,256,256]{3,2,1,0:T(8,128)(2,1)}, bf16[1,2,256,256]{3,2,1,0:T(8,128)(2,1)S(1)}, u32[]{:S(2)}, u32[]{:S(2)}) %collective-permute-start.3) | collective-permute-done | bytes 262176 | tf_op jit(solution)/shard_map/ppermute | solution.py:186
  18.5 0.0 copy-start
  18.5 0.1 collective-permute-start.5
  18.6 0.8 %copy-done = bf16[3,2,256,256]{3,2,1,0:T(8,128)(2,1)} copy-done((bf16[3,2,256,256]{3,2,1,0:T(8,128)(2,1)}, bf16[3,2,256,256]{3,2,1,0:T(8,128)(2,1)S(1)}, u32[]{:S(2)}) %copy-start) | copy-done | bytes 786456
  19.4 5.6 %shard_map.56.refs_6_ = f32[4,2,256,256]{3,2,1,0:T(8,128)} custom-call(bf16[3,2,256,256]{3,2,1,0:T(8,128)(2,1)} %copy-done, s32[2,256]{1,0:T(2,128)} %refs_1_.5, s32[2,256]{1,0:T(2,128)} %refs_2_.5, s32[4,256]{1,0:T(4,128)} %copy-done.2, s32[2]{0:T(128)} %refs_4_.5, s32[1,256]{1,0:T(1,128)} %bitcast.2, f32[4,2,256,256]{3,2,1,0:T(8,128)} %shard_map.55.refs_6_), custom_call_target="tpu_custom_call" | custom-call | flops 1610612736 | bytes 4980736 | tf_op jit(solution)/shard_map/pallas_call | solution.py:164
  25.0 0.0 collective-permute-done.5.refs_0_
  25.0 0.0 copy-start.1
  25.0 0.9 %copy-done.1 = bf16[3,2,256,256]{3,2,1,0:T(8,128)(2,1)} copy-done((bf16[3,2,256,256]{3,2,1,0:T(8,128)(2,1)}, bf16[3,2,256,256]{3,2,1,0:T(8,128)(2,1)S(1)}, u32[]{:S(2)}) %copy-start.1) | copy-done | bytes 786456
  25.8 6.7 %shard_map.57 = f32[2,2,256,256]{3,2,1,0:T(8,128)} custom-call(bf16[3,2,256,256]{3,2,1,0:T(8,128)(2,1)} %copy-done.1, s32[2,256]{1,0:T(2,128)} %refs_1_.5, s32[2,256]{1,0:T(2,128)} %refs_2_.5, s32[4,256]{1,0:T(4,128)} %copy-done.2, s32[2]{0:T(128)} %refs_4_.5, s32[1,256]{1,0:T(1,128)} %bitcast.3, f32[4,2,256,256]{3,2,1,0:T(8,128)} %shard_map.56.refs_6_), custom_call_target="tpu_custom_call" | custom-call | flops 2415919104 | bytes 3932160 | tf_op jit(solution)/shard_map/pallas_call | solution.py:164
  (3 shorter events, 0.1 us)
Async XLA Ops:
  0.0 8.2 %collective-permute-start = (bf16[1,2,256,256]{3,2,1,0:T(8,128)(2,1)}, bf16[1,2,256,256]{3,2,1,0:T(8,128)(2,1)S(1)}, u32[]{:S(2)}, u32[]{:S(2)}) collective-permute-start(bf16[1,2,256,256]{3,2,1,0:T(8,128)(2,1)} %param.5), channel_id=1, source_target_pairs={{0,4},{4,0},{8,12},{12,8},{16,20},{20,16},{24,28},{28,24},{1,5},{5... | collective-permute-start | bytes 786440 | tf_op jit(solution)/shard_map/ppermute | solution.py:185
  0.5 14.6 %collective-permute-start.2 = (bf16[1,2,256,256]{3,2,1,0:T(8,128)(2,1)}, bf16[1,2,256,256]{3,2,1,0:T(8,128)(2,1)S(1)}, u32[]{:S(2)}, u32[]{:S(2)}) collective-permute-start(bf16[1,2,256,256]{3,2,1,0:T(8,128)(2,1)} %param.5), channel_id=1, source_target_pairs={{0,8},{4,12},{8,0},{12,4},{16,24},{20,28},{24,16},{28,20},{1,9},{5... | collective-permute-start | bytes 786440 | tf_op jit(solution)/shard_map/ppermute | solution.py:186
  2.9 14.1 %collective-permute-start.4 = (bf16[1,2,256,256]{3,2,1,0:T(8,128)(2,1)}, bf16[1,2,256,256]{3,2,1,0:T(8,128)(2,1)S(1)}, u32[]{:S(2)}, u32[]{:S(2)}) collective-permute-start(bf16[1,2,256,256]{3,2,1,0:T(8,128)(2,1)} %param.5), channel_id=1, source_target_pairs={{0,24},{4,28},{8,16},{12,20},{16,8},{20,12},{24,0},{28,4},{1,25},{... | collective-permute-start | bytes 786440 | tf_op jit(solution)/shard_map/ppermute | solution.py:186
  4.4 14.0 %collective-permute-start.3 = (bf16[1,2,256,256]{3,2,1,0:T(8,128)(2,1)}, bf16[1,2,256,256]{3,2,1,0:T(8,128)(2,1)S(1)}, u32[]{:S(2)}, u32[]{:S(2)}) collective-permute-start(bf16[1,2,256,256]{3,2,1,0:T(8,128)(2,1)} %param.5), channel_id=1, source_target_pairs={{0,16},{4,20},{8,24},{12,28},{16,0},{20,4},{24,8},{28,12},{1,17},{... | collective-permute-start | bytes 786440 | tf_op jit(solution)/shard_map/ppermute | solution.py:186
  5.2 4.9 %collective-permute-start.1 = (s32[4,256]{1,0:T(4,128)S(1)}, s32[4,256]{1,0:T(4,128)S(1)}, u32[]{:S(2)}, u32[]{:S(2)}) collective-permute-start(s32[4,256]{1,0:T(4,128)S(1)} %pad_add_fusion), channel_id=1, source_target_pairs={{0,2},{1,3},{2,0},{3,1},{4,6},{5,7},{6,4},{7,5},{8,10},{9,11},{10,... | collective-permute-start | bytes 12296 | tf_op jit(solution)/shard_map/ppermute | solution.py:22
  10.0 0.6 %copy-start.2 = (s32[4,256]{1,0:T(4,128)}, s32[4,256]{1,0:T(4,128)S(1)}, u32[]{:S(2)}) copy-start(s32[4,256]{1,0:T(4,128)S(1)} %collective-permute-done.1.refs_3_) | copy-start | bytes 12292
  18.5 0.9 %copy-start = (bf16[3,2,256,256]{3,2,1,0:T(8,128)(2,1)}, bf16[3,2,256,256]{3,2,1,0:T(8,128)(2,1)S(1)}, u32[]{:S(2)}) copy-start(bf16[3,2,256,256]{3,2,1,0:T(8,128)(2,1)S(1)} %constant_dynamic-update-slice_fusion.refs_0_) | copy-start | bytes 2359300
  18.5 6.4 %collective-permute-start.5 = (bf16[3,2,256,256]{3,2,1,0:T(8,128)(2,1)S(1)}, bf16[3,2,256,256]{3,2,1,0:T(8,128)(2,1)S(1)}, u32[]{:S(2)}, u32[]{:S(2)}) collective-permute-start(bf16[3,2,256,256]{3,2,1,0:T(8,128)(2,1)S(1)} %constant_dynamic-update-slice_fusion.refs_0_), channel_id=1, source_target_pairs={{0,4},{4,0},{8,12},{12,8},{16,20},{20,16},{24,28},{28,24},{1,5},{5... | collective-permute-start | bytes 2359304 | tf_op jit(solution)/shard_map/ppermute | solution.py:196
  25.0 0.9 %copy-start.1 = (bf16[3,2,256,256]{3,2,1,0:T(8,128)(2,1)}, bf16[3,2,256,256]{3,2,1,0:T(8,128)(2,1)S(1)}, u32[]{:S(2)}) copy-start(bf16[3,2,256,256]{3,2,1,0:T(8,128)(2,1)S(1)} %collective-permute-done.5.refs_0_) | copy-start | bytes 2359300

commit v7 on v6

--- a/solution.py
+++ b/solution.py
@@ -50,25 +50,28 @@
     g_re = g_ref[0, 0]
     g_im = g_ref[0, 1]
     sel = sel_ref[...]
-    y_re = jnp.dot(sel, g_re, preferred_element_type=F32).astype(BF16)
-    y_im = jnp.dot(sel, g_im, preferred_element_type=F32).astype(BF16)
+    y = jnp.dot(sel, jnp.concatenate([g_re, g_im], axis=1), preferred_element_type=F32).astype(BF16)
     gr = g_re.astype(F32)
     gi = g_im.astype(F32)
     for t in range(2 * slots):
         lo, hi = t * width, (t + 1) * width
-        pt = sel[lo:hi]
-        m_re = lax.dot_general(pt, y_re[lo:hi], NT, preferred_element_type=F32)
-        m_im = lax.dot_general(pt, y_im[lo:hi], NT, preferred_element_type=F32)
+        stacked = jnp.concatenate([y[lo:hi, :width], y[lo:hi, width:]], axis=0)
+        m = lax.dot_general(sel[lo:hi], stacked, NT, preferred_element_type=F32)
+        m_re = m[:, :width]
+        m_im = m[:, width:]
         acc_ref[t, 0] += gr * m_re - gi * m_im
         acc_ref[t, 1] += gr * m_im + gi * m_re
 
 
-def accumulate_kernel(*refs, slots, width, scale, has_prior, final):
+def accumulate_kernel(*refs, slots, width, scale, has_prior, final, counts):
+    groups = len(counts)
+    g_refs = refs[:groups]
+    refs = refs[groups:]
     if has_prior:
-        (g_ref, ti_ref, ph_ref, far_ref, slot_ref, cj_ref, prior_hbm, out_ref,
+        (ti_ref, ph_ref, far_ref, slot_ref, cj_ref, prior_hbm, out_ref,
          acc_ref, sel_ref, prior_ref, sem) = refs
     else:
-        g_ref, ti_ref, ph_ref, far_ref, slot_ref, cj_ref, out_ref, acc_ref, sel_ref = refs
+        ti_ref, ph_ref, far_ref, slot_ref, cj_ref, out_ref, acc_ref, sel_ref = refs
     w = pl.program_id(0)
     last = pl.num_programs(0) - 1
     nt = 2 * slots
@@ -94,7 +97,13 @@
         for t in range(nt):
             sel_ref[t * width:(t + 1) * width] = (cols[:, t:t + 1] == lanes).astype(BF16)
 
-    add_walker(g_ref, sel_ref, acc_ref, slots, width)
+    offset = 0
+    for g_ref, count in zip(g_refs, counts):
+        @pl.when((w >= offset) & (w < offset + count))
+        def _():
+            add_walker(g_ref, sel_ref, acc_ref, slots, width)
+
+        offset += count
 
     @pl.when(w == last)
     def _():
@@ -135,17 +144,22 @@
             out_ref[s, 1] = (own_im + mir_im) * scale
 
 
+def walker_spec(width, offset, count):
+    return pl.BlockSpec((1, 2, width, width), lambda w: (jnp.clip(w - offset, 0, count - 1), 0, 0, 0))
+
+
 def accumulate(walkers, info, prior, final, slots, width, scale):
     has_prior = prior is not None
+    counts = tuple(g.shape[0] for g in walkers)
     kernel = functools.partial(
-        accumulate_kernel, slots=slots, width=width, scale=scale, has_prior=has_prior, final=final
+        accumulate_kernel, slots=slots, width=width, scale=scale, has_prior=has_prior, final=final, counts=counts
     )
     full = lambda shape: pl.BlockSpec(shape, lambda w: (0,) * len(shape))
     acc_shape = (2 * slots, 2, width, width)
     out_shape = (slots, 2, width, width) if final else acc_shape
     ti, ph, far, slot, cj = info
-    in_specs = [
-        pl.BlockSpec((1, 2, width, width), lambda w: (w, 0, 0, 0)),
+    offsets = [sum(counts[:k]) for k in range(len(counts))]
+    in_specs = [walker_spec(width, o, c) for o, c in zip(offsets, counts)] + [
         full(ti.shape),
         full(ph.shape),
         full(far.shape),
@@ -153,14 +167,14 @@
         full(cj.shape),
     ]
     scratch = [pltpu.VMEM(acc_shape, F32), pltpu.VMEM((2 * slots * width, width), BF16)]
-    operands = [walkers, ti, ph, far, slot, cj]
+    operands = list(walkers) + [ti, ph, far, slot, cj]
     if has_prior:
         in_specs.append(pl.BlockSpec(memory_space=pl.ANY))
         scratch += [pltpu.VMEM(acc_shape, F32), pltpu.SemaphoreType.DMA(())]
         operands.append(prior)
-    steps = walkers.shape[0]
+    steps = sum(counts)
     flops = steps * 2 * slots * 8 * width**3 + (12 * slots * 2 * width**3 if final else 0)
-    moved = walkers.size * 2 + 4 * math.prod(out_shape) + (4 * math.prod(acc_shape) if has_prior else 0)
+    moved = sum(g.size for g in walkers) * 2 + 4 * math.prod(out_shape) + (4 * math.prod(acc_shape) if has_prior else 0)
     return pl.pallas_call(
         kernel,
         grid=(steps,),
@@ -189,13 +203,13 @@
     run = functools.partial(accumulate, info=info, slots=slots, width=width, scale=scale)
 
     if not fetched:
-        return run(jnp.concatenate([greens, sibling], axis=0), prior=None, final=True)
-    partial_sums = run(jnp.concatenate([greens, sibling], axis=0), prior=None, final=False)
+        return run([greens, sibling], prior=None, final=True)
+    partial_sums = run([greens, sibling], prior=None, final=False)
     partial_sums, fetched = lax.optimization_barrier((partial_sums, fetched))
     near = jnp.concatenate(fetched, axis=0)
     forwarded = lax.ppermute(near, "blk", swap)
-    partial_sums = run(near, prior=partial_sums, final=False)
-    return run(forwarded, prior=partial_sums, final=True)
+    partial_sums = run(fetched, prior=partial_sums, final=False)
+    return run([forwarded], prior=partial_sums, final=True)
 
 
 def solution(mesh):

time: 32.8 us -> 32.4 us (0.988)
  other arithmetic: 2.5 us -> 0.79 us
  waiting for transfers between devices: 3.41 us -> 4.96 us
    concatenate x1, other arithmetic: 1.79 us -> 0.09 us  [local(): near = jnp.concatenate(fetched, axis=0)]
    ppermute x1, waiting for transfers between devices: 0.01 us -> 1.58 us  [passed_along(): lax.ppermute(value, axis, [(i, (i + by) % size) for i in range(size)])]
    unnamed x8 -> x12, local copies, waits for them, and re-layouts: 2.29 us -> 2.1 us
  transfers between devices with their start and end apart: 6 -> 6, of which waited for: 2 -> 3; matrix products, arithmetic and copies ran while one was open for 8% -> 2% of each run, Pallas kernels for 31% -> 31%
where the time goes in v7:
time: 32.4 us; the launch traced here: 32.2 us
  Pallas kernels  16.7 us (52%)
  starting transfers between devices  7.6 us (23%)
  waiting for transfers between devices  4.96 us (15%)
  local copies, waits for them, and re-layouts  2.1 us (6%)
  other arithmetic  0.79 us (2%)
    pallas_call x3, Pallas kernels, accumulate(): pl.pallas_call(kernel, grid=(steps,), cost_estimate=pl.CostEstimate(flops...  16.7 us
    ppermute x3, starting transfers between devices, local(): lax.ppermute(greens, 'blk', [(i, i ^ 2 * m) for i in range(blocks)])  4.02 us
    ppermute x3, waiting for transfers between devices, local(): lax.ppermute(greens, 'blk', [(i, i ^ 2 * m) for i in range(blocks)])  3.37 us
    ppermute x1, starting transfers between devices, passed_along(): lax.ppermute(value, axis, [(i, (i + by) % size) for i in range(size)])  3.05 us
    unnamed x12, local copies, waits for them, and re-layouts  2.1 us
    ppermute x1, waiting for transfers between devices, passed_along(): lax.ppermute(value, axis, [(i, (i + by) % size) for i in range(size)])  1.58 us
    concatenate x1, other arithmetic, local(): jnp.concatenate([transfer_index, phase_index], axis=0)  0.71 us
  transfers between devices with their start and end apart: 6, of which 3 were waited for; matrix products, arithmetic and copies ran while one was open for 2% of the time, Pallas kernels for 31%

profile of v7, /device:TPU:0, one launch (start us, length us, event | category | flops | bytes accessed | tf_op | source)
XLA Modules:
  0.0 32.2 jit_solution(6979564894514454006)
XLA Ops:
  0.0 0.5 %collective-permute-start = (bf16[1,2,256,256]{3,2,1,0:T(8,128)(2,1)}, bf16[1,2,256,256]{3,2,1,0:T(8,128)(2,1)S(1)}, u32[]{:S(2)}, u32[]{:S(2)}) collective-permute-start(bf16[1,2,256,256]{3,2,1,0:T(8,128)(2,1)} %refs_0_.1), channel_id=1, source_target_pairs={{0,4},{4,0},{8,12},{12,8},{16,20},{20,16},{24,28},{28,24},{1,5},{5... | collective-permute-start | bytes 786440 | tf_op jit(solution)/shard_map/ppermute | solution.py:199
  0.5 2.5 %collective-permute-start.2 = (bf16[1,2,256,256]{3,2,1,0:T(8,128)(2,1)}, bf16[1,2,256,256]{3,2,1,0:T(8,128)(2,1)S(1)}, u32[]{:S(2)}, u32[]{:S(2)}) collective-permute-start(bf16[1,2,256,256]{3,2,1,0:T(8,128)(2,1)} %refs_0_.1), channel_id=1, source_target_pairs={{0,8},{4,12},{8,0},{12,4},{16,24},{20,28},{24,16},{28,20},{1,9},{5... | collective-permute-start | bytes 786440 | tf_op jit(solution)/shard_map/ppermute | solution.py:200
  2.9 1.5 %collective-permute-start.4 = (bf16[1,2,256,256]{3,2,1,0:T(8,128)(2,1)}, bf16[1,2,256,256]{3,2,1,0:T(8,128)(2,1)S(1)}, u32[]{:S(2)}, u32[]{:S(2)}) collective-permute-start(bf16[1,2,256,256]{3,2,1,0:T(8,128)(2,1)} %refs_0_.1), channel_id=1, source_target_pairs={{0,24},{4,28},{8,16},{12,20},{16,8},{20,12},{24,0},{28,4},{1,25},{... | collective-permute-start | bytes 786440 | tf_op jit(solution)/shard_map/ppermute | solution.py:200
  4.4 0.0 collective-permute-start.3
  4.5 0.7 %pad_add_fusion = s32[4,256]{1,0:T(4,128)S(1)} fusion(s32[2,256]{1,0:T(2,128)} %refs_2_.3, s32[2,256]{1,0:T(2,128)} %refs_1_.1), kind=kLoop, calls=%fused_computation.1 | loop fusion | flops 1024 | bytes 8192 | tf_op jit(solution)/shard_map/concatenate | solution.py:201
  5.2 3.1 %collective-permute-start.1 = (s32[4,256]{1,0:T(4,128)S(1)}, s32[4,256]{1,0:T(4,128)S(1)}, u32[]{:S(2)}, u32[]{:S(2)}) collective-permute-start(s32[4,256]{1,0:T(4,128)S(1)} %pad_add_fusion), channel_id=1, source_target_pairs={{0,2},{1,3},{2,0},{3,1},{4,6},{5,7},{6,4},{7,5},{8,10},{9,11},{10,... | collective-permute-start | bytes 12296 | tf_op jit(solution)/shard_map/ppermute | solution.py:22
  8.2 1.6 %collective-permute-done.1.refs_4_.refs_5_.refs_3_ = s32[4,256]{1,0:T(4,128)S(1)} collective-permute-done((s32[4,256]{1,0:T(4,128)S(1)}, s32[4,256]{1,0:T(4,128)S(1)}, u32[]{:S(2)}, u32[]{:S(2)}) %collective-permute-start.1) | collective-permute-done | bytes 4128 | tf_op jit(solution)/shard_map/ppermute | solution.py:22
  9.8 0.0 copy-start.5
  9.8 0.0 collective-permute-done.refs_1_
  9.8 0.0 copy-start.4
  9.8 0.6 %copy-done.5 = s32[4,256]{1,0:T(4,128)} copy-done((s32[4,256]{1,0:T(4,128)}, s32[4,256]{1,0:T(4,128)S(1)}, u32[]{:S(2)}) %copy-start.5) | copy-done | bytes 4120
  10.4 0.1 copy-done.4
  10.5 4.5 %shard_map.55.refs_8_ = f32[4,2,256,256]{3,2,1,0:T(8,128)} custom-call(bf16[1,2,256,256]{3,2,1,0:T(8,128)(2,1)} %refs_0_.1, bf16[1,2,256,256]{3,2,1,0:T(8,128)(2,1)} %copy-done.4, s32[2,256]{1,0:T(2,128)} %refs_1_.1, s32[2,256]{1,0:T(2,128)} %refs_2_.3, s32[4,256]{1,0:T(4,128)} %copy-done.5, s32[2]{0:T(128)} %refs_4_.3, s32[1,256]{1,0:T(1,128)} %bitcast.1), custom_call_target="tpu_custom_call" | custom-call | flops 1073741824 | bytes 2621440 | tf_op jit(solution)/shard_map/pallas_call | solution.py:178
  15.0 0.0 collective-permute-done.2.refs_0_
  15.0 0.0 copy-start
  15.0 2.0 %collective-permute-done.4.refs_2_ = bf16[1,2,256,256]{3,2,1,0:T(8,128)(2,1)S(1)} collective-permute-done((bf16[1,2,256,256]{3,2,1,0:T(8,128)(2,1)}, bf16[1,2,256,256]{3,2,1,0:T(8,128)(2,1)S(1)}, u32[]{:S(2)}, u32[]{:S(2)}) %collective-permute-start.4) | collective-permute-done | bytes 262176 | tf_op jit(solution)/shard_map/ppermute | solution.py:200
  17.1 0.0 copy-start.1
  17.1 1.4 %collective-permute-done.3.refs_1_ = bf16[1,2,256,256]{3,2,1,0:T(8,128)(2,1)S(1)} collective-permute-done((bf16[1,2,256,256]{3,2,1,0:T(8,128)(2,1)}, bf16[1,2,256,256]{3,2,1,0:T(8,128)(2,1)S(1)}, u32[]{:S(2)}, u32[]{:S(2)}) %collective-permute-start.3) | collective-permute-done | bytes 262176 | tf_op jit(solution)/shard_map/ppermute | solution.py:200
  18.4 0.0 copy-start.2
  18.4 0.1 pad_maximum_fusion
  18.5 0.1 collective-permute-start.5
  18.6 0.0 copy-done
  18.6 0.0 copy-done.1
  18.6 0.5 %copy-done.2 = bf16[1,2,256,256]{3,2,1,0:T(8,128)(2,1)} copy-done((bf16[1,2,256,256]{3,2,1,0:T(8,128)(2,1)}, bf16[1,2,256,256]{3,2,1,0:T(8,128)(2,1)S(1)}, u32[]{:S(2)}) %copy-start.2) | copy-done | bytes 262168
  19.1 5.5 %shard_map.56.refs_6_ = f32[4,2,256,256]{3,2,1,0:T(8,128)} custom-call(bf16[1,2,256,256]{3,2,1,0:T(8,128)(2,1)} %copy-done, bf16[1,2,256,256]{3,2,1,0:T(8,128)(2,1)} %copy-done.2, bf16[1,2,256,256]{3,2,1,0:T(8,128)(2,1)} %copy-done.1, s32[2,256]{1,0:T(2,128)} %refs_1_.1, s32[2,256]{1,0:T(2,128)} %refs_2_.3, s32[4,256]{1,0:T(4,128)} %copy-done.5, s32[2]{0:T(128)} %refs_4_.3, ...), custom_call_target="tpu_custom_call" | custom-call | flops 1610612736 | bytes 4980736 | tf_op jit(solution)/shard_map/pallas_call | solution.py:178
  24.7 0.0 collective-permute-done.5.refs_0_
  24.7 0.0 copy-start.3
  24.7 0.9 %copy-done.3 = bf16[3,2,256,256]{3,2,1,0:T(8,128)(2,1)} copy-done((bf16[3,2,256,256]{3,2,1,0:T(8,128)(2,1)}, bf16[3,2,256,256]{3,2,1,0:T(8,128)(2,1)S(1)}, u32[]{:S(2)}) %copy-start.3) | copy-done | bytes 786456
  25.5 6.7 %shard_map.57 = f32[2,2,256,256]{3,2,1,0:T(8,128)} custom-call(bf16[3,2,256,256]{3,2,1,0:T(8,128)(2,1)} %copy-done.3, s32[2,256]{1,0:T(2,128)} %refs_1_.1, s32[2,256]{1,0:T(2,128)} %refs_2_.3, s32[4,256]{1,0:T(4,128)} %copy-done.5, s32[2]{0:T(128)} %refs_4_.3, s32[1,256]{1,0:T(1,128)} %bitcast.3, f32[4,2,256,256]{3,2,1,0:T(8,128)} %shard_map.56.refs_6_), custom_call_target="tpu_custom_call" | custom-call | flops 2415919104 | bytes 3932160 | tf_op jit(solution)/shard_map/pallas_call | solution.py:178
Async XLA Ops:
  0.0 9.8 %collective-permute-start = (bf16[1,2,256,256]{3,2,1,0:T(8,128)(2,1)}, bf16[1,2,256,256]{3,2,1,0:T(8,128)(2,1)S(1)}, u32[]{:S(2)}, u32[]{:S(2)}) collective-permute-start(bf16[1,2,256,256]{3,2,1,0:T(8,128)(2,1)} %refs_0_.1), channel_id=1, source_target_pairs={{0,4},{4,0},{8,12},{12,8},{16,20},{20,16},{24,28},{28,24},{1,5},{5... | collective-permute-start | bytes 786440 | tf_op jit(solution)/shard_map/ppermute | solution.py:199
  0.5 14.6 %collective-permute-start.2 = (bf16[1,2,256,256]{3,2,1,0:T(8,128)(2,1)}, bf16[1,2,256,256]{3,2,1,0:T(8,128)(2,1)S(1)}, u32[]{:S(2)}, u32[]{:S(2)}) collective-permute-start(bf16[1,2,256,256]{3,2,1,0:T(8,128)(2,1)} %refs_0_.1), channel_id=1, source_target_pairs={{0,8},{4,12},{8,0},{12,4},{16,24},{20,28},{24,16},{28,20},{1,9},{5... | collective-permute-start | bytes 786440 | tf_op jit(solution)/shard_map/ppermute | solution.py:200
  2.9 14.1 %collective-permute-start.4 = (bf16[1,2,256,256]{3,2,1,0:T(8,128)(2,1)}, bf16[1,2,256,256]{3,2,1,0:T(8,128)(2,1)S(1)}, u32[]{:S(2)}, u32[]{:S(2)}) collective-permute-start(bf16[1,2,256,256]{3,2,1,0:T(8,128)(2,1)} %refs_0_.1), channel_id=1, source_target_pairs={{0,24},{4,28},{8,16},{12,20},{16,8},{20,12},{24,0},{28,4},{1,25},{... | collective-permute-start | bytes 786440 | tf_op jit(solution)/shard_map/ppermute | solution.py:200
  4.4 14.0 %collective-permute-start.3 = (bf16[1,2,256,256]{3,2,1,0:T(8,128)(2,1)}, bf16[1,2,256,256]{3,2,1,0:T(8,128)(2,1)S(1)}, u32[]{:S(2)}, u32[]{:S(2)}) collective-permute-start(bf16[1,2,256,256]{3,2,1,0:T(8,128)(2,1)} %refs_0_.1), channel_id=1, source_target_pairs={{0,16},{4,20},{8,24},{12,28},{16,0},{20,4},{24,8},{28,12},{1,17},{... | collective-permute-start | bytes 786440 | tf_op jit(solution)/shard_map/ppermute | solution.py:200
  5.2 4.6 %collective-permute-start.1 = (s32[4,256]{1,0:T(4,128)S(1)}, s32[4,256]{1,0:T(4,128)S(1)}, u32[]{:S(2)}, u32[]{:S(2)}) collective-permute-start(s32[4,256]{1,0:T(4,128)S(1)} %pad_add_fusion), channel_id=1, source_target_pairs={{0,2},{1,3},{2,0},{3,1},{4,6},{5,7},{6,4},{7,5},{8,10},{9,11},{10,... | collective-permute-start | bytes 12296 | tf_op jit(solution)/shard_map/ppermute | solution.py:22
  9.8 0.6 %copy-start.5 = (s32[4,256]{1,0:T(4,128)}, s32[4,256]{1,0:T(4,128)S(1)}, u32[]{:S(2)}) copy-start(s32[4,256]{1,0:T(4,128)S(1)} %collective-permute-done.1.refs_4_.refs_5_.refs_3_) | copy-start | bytes 12292
  9.8 0.7 %copy-start.4 = (bf16[1,2,256,256]{3,2,1,0:T(8,128)(2,1)}, bf16[1,2,256,256]{3,2,1,0:T(8,128)(2,1)S(1)}, u32[]{:S(2)}) copy-start(bf16[1,2,256,256]{3,2,1,0:T(8,128)(2,1)S(1)} %collective-permute-done.refs_1_) | copy-start | bytes 786436
  15.0 3.6 %copy-start = (bf16[1,2,256,256]{3,2,1,0:T(8,128)(2,1)}, bf16[1,2,256,256]{3,2,1,0:T(8,128)(2,1)S(1)}, u32[]{:S(2)}) copy-start(bf16[1,2,256,256]{3,2,1,0:T(8,128)(2,1)S(1)} %collective-permute-done.2.refs_0_) | copy-start | bytes 786436
  17.1 1.5 %copy-start.1 = (bf16[1,2,256,256]{3,2,1,0:T(8,128)(2,1)}, bf16[1,2,256,256]{3,2,1,0:T(8,128)(2,1)S(1)}, u32[]{:S(2)}) copy-start(bf16[1,2,256,256]{3,2,1,0:T(8,128)(2,1)S(1)} %collective-permute-done.4.refs_2_) | copy-start | bytes 786436
  18.4 0.7 %copy-start.2 = (bf16[1,2,256,256]{3,2,1,0:T(8,128)(2,1)}, bf16[1,2,256,256]{3,2,1,0:T(8,128)(2,1)S(1)}, u32[]{:S(2)}) copy-start(bf16[1,2,256,256]{3,2,1,0:T(8,128)(2,1)S(1)} %collective-permute-done.3.refs_1_) | copy-start | bytes 786436
  18.5 6.1 %collective-permute-start.5 = (bf16[3,2,256,256]{3,2,1,0:T(8,128)(2,1)S(1)}, bf16[3,2,256,256]{3,2,1,0:T(8,128)(2,1)S(1)}, u32[]{:S(2)}, u32[]{:S(2)}) collective-permute-start(bf16[3,2,256,256]{3,2,1,0:T(8,128)(2,1)S(1)} %pad_maximum_fusion), channel_id=1, source_target_pairs={{0,4},{4,0},{8,12},{12,8},{16,20},{20,16},{24,28},{28,24},{1,5},{5... | collective-permute-start | bytes 2359304 | tf_op jit(solution)/shard_map/ppermute | solution.py:210
  24.7 0.9 %copy-start.3 = (bf16[3,2,256,256]{3,2,1,0:T(8,128)(2,1)}, bf16[3,2,256,256]{3,2,1,0:T(8,128)(2,1)S(1)}, u32[]{:S(2)}) copy-start(bf16[3,2,256,256]{3,2,1,0:T(8,128)(2,1)S(1)} %collective-permute-done.5.refs_0_) | copy-start | bytes 2359300

commit v8 on v7

--- a/solution.py
+++ b/solution.py
@@ -12,6 +12,7 @@
 F32 = jnp.float32
 BF16 = jnp.bfloat16
 NT = (((1,), (1,)), ((), ()))
+CHUNK = 3
 ROOT_HALF = math.sqrt(0.5)
 COSINES = (1.0, ROOT_HALF, 0.0, -ROOT_HALF, -1.0, -ROOT_HALF, 0.0, ROOT_HALF)
 SINES = (0.0, ROOT_HALF, 1.0, ROOT_HALF, 0.0, -ROOT_HALF, -1.0, -ROOT_HALF)
@@ -46,21 +47,27 @@
     return out
 
 
-def add_walker(g_ref, sel_ref, acc_ref, slots, width):
-    g_re = g_ref[0, 0]
-    g_im = g_ref[0, 1]
+def add_walkers(blocks, sel_ref, acc_ref, slots, width):
     sel = sel_ref[...]
-    y = jnp.dot(sel, jnp.concatenate([g_re, g_im], axis=1), preferred_element_type=F32).astype(BF16)
-    gr = g_re.astype(F32)
-    gi = g_im.astype(F32)
+    terms = []
+    for g_ref, k in blocks:
+        g_re = g_ref[k, 0]
+        g_im = g_ref[k, 1]
+        y = jnp.dot(sel, jnp.concatenate([g_re, g_im], axis=1), preferred_element_type=F32).astype(BF16)
+        terms.append((g_re.astype(F32), g_im.astype(F32), y))
     for t in range(2 * slots):
         lo, hi = t * width, (t + 1) * width
-        stacked = jnp.concatenate([y[lo:hi, :width], y[lo:hi, width:]], axis=0)
-        m = lax.dot_general(sel[lo:hi], stacked, NT, preferred_element_type=F32)
-        m_re = m[:, :width]
-        m_im = m[:, width:]
-        acc_ref[t, 0] += gr * m_re - gi * m_im
-        acc_ref[t, 1] += gr * m_im + gi * m_re
+        acc_re = acc_ref[t, 0]
+        acc_im = acc_ref[t, 1]
+        for gr, gi, y in terms:
+            stacked = jnp.concatenate([y[lo:hi, :width], y[lo:hi, width:]], axis=0)
+            m = lax.dot_general(sel[lo:hi], stacked, NT, preferred_element_type=F32)
+            m_re = m[:, :width]
+            m_im = m[:, width:]
+            acc_re = acc_re + (gr * m_re - gi * m_im)
+            acc_im = acc_im + (gr * m_im + gi * m_re)
+        acc_ref[t, 0] = acc_re
+        acc_ref[t, 1] = acc_im
 
 
 def accumulate_kernel(*refs, slots, width, scale, has_prior, final, counts):
@@ -97,13 +104,9 @@
         for t in range(nt):
             sel_ref[t * width:(t + 1) * width] = (cols[:, t:t + 1] == lanes).astype(BF16)
 
-    offset = 0
-    for g_ref, count in zip(g_refs, counts):
-        @pl.when((w >= offset) & (w < offset + count))
-        def _():
-            add_walker(g_ref, sel_ref, acc_ref, slots, width)
-
-        offset += count
+    pending = [(g_ref, k) for g_ref, count in zip(g_refs, counts) for k in range(count)]
+    for start in range(0, len(pending), CHUNK):
+        add_walkers(pending[start:start + CHUNK], sel_ref, acc_ref, slots, width)
 
     @pl.when(w == last)
     def _():
@@ -158,8 +161,7 @@
     acc_shape = (2 * slots, 2, width, width)
     out_shape = (slots, 2, width, width) if final else acc_shape
     ti, ph, far, slot, cj = info
-    offsets = [sum(counts[:k]) for k in range(len(counts))]
-    in_specs = [walker_spec(width, o, c) for o, c in zip(offsets, counts)] + [
+    in_specs = [full(g.shape) for g in walkers] + [
         full(ti.shape),
         full(ph.shape),
         full(far.shape),
@@ -177,7 +179,7 @@
     moved = sum(g.size for g in walkers) * 2 + 4 * math.prod(out_shape) + (4 * math.prod(acc_shape) if has_prior else 0)
     return pl.pallas_call(
         kernel,
-        grid=(steps,),
+        grid=(1,),
         cost_estimate=pl.CostEstimate(flops=flops, transcendentals=0, bytes_accessed=moved),
         in_specs=in_specs,
         out_specs=full(out_shape),

time: 32.4 us -> 31.9 us (0.985)
  Pallas kernels: 16.7 us -> 15.8 us
  waiting for transfers between devices: 4.96 us -> 5.42 us
    pallas_call x3, Pallas kernels: 16.7 us -> 15.8 us  [accumulate(): pl.pallas_call(kernel, grid=(1,), cost_estimate=pl.CostEstimate(flops=flo...]
    ppermute x3, waiting for transfers between devices: 3.37 us -> 3.83 us  [local(): lax.ppermute(greens, 'blk', [(i, i ^ 2 * m) for i in range(blocks)])]
  transfers between devices with their start and end apart: 6 -> 6, of which waited for: 3 -> 3; matrix products, arithmetic and copies ran while one was open for 2% -> 2% of each run, Pallas kernels for 31% -> 29%
where the time goes in v8:
time: 31.9 us; the launch traced here: 31.7 us
  Pallas kernels  15.8 us (50%)
  starting transfers between devices  7.6 us (24%)
  waiting for transfers between devices  5.42 us (17%)
  local copies, waits for them, and re-layouts  2.1 us (7%)
  other arithmetic  0.79 us (2%)
    pallas_call x3, Pallas kernels, accumulate(): pl.pallas_call(kernel, grid=(1,), cost_estimate=pl.CostEstimate(flops=flo...  15.8 us
    ppermute x3, starting transfers between devices, local(): lax.ppermute(greens, 'blk', [(i, i ^ 2 * m) for i in range(blocks)])  4.02 us
    ppermute x3, waiting for transfers between devices, local(): lax.ppermute(greens, 'blk', [(i, i ^ 2 * m) for i in range(blocks)])  3.83 us
    ppermute x1, starting transfers between devices, passed_along(): lax.ppermute(value, axis, [(i, (i + by) % size) for i in range(size)])  3.05 us
    unnamed x12, local copies, waits for them, and re-layouts  2.1 us
    ppermute x1, waiting for transfers between devices, passed_along(): lax.ppermute(value, axis, [(i, (i + by) % size) for i in range(size)])  1.58 us
    concatenate x1, other arithmetic, local(): jnp.concatenate([transfer_index, phase_index], axis=0)  0.71 us
  transfers between devices with their start and end apart: 6, of which 3 were waited for; matrix products, arithmetic and copies ran while one was open for 2% of the time, Pallas kernels for 29%

profile of v8, /device:TPU:0, one launch (start us, length us, event | category | flops | bytes accessed | tf_op | source)
XLA Modules:
  0.0 31.7 jit_solution(4425757892295394157)
XLA Ops:
  0.0 0.5 %collective-permute-start = (bf16[1,2,256,256]{3,2,1,0:T(8,128)(2,1)}, bf16[1,2,256,256]{3,2,1,0:T(8,128)(2,1)S(1)}, u32[]{:S(2)}, u32[]{:S(2)}) collective-permute-start(bf16[1,2,256,256]{3,2,1,0:T(8,128)(2,1)} %refs_0_.1), channel_id=1, source_target_pairs={{0,4},{4,0},{8,12},{12,8},{16,20},{20,16},{24,28},{28,24},{1,5},{5... | collective-permute-start | bytes 786440 | tf_op jit(solution)/shard_map/ppermute | solution.py:201
  0.5 2.5 %collective-permute-start.2 = (bf16[1,2,256,256]{3,2,1,0:T(8,128)(2,1)}, bf16[1,2,256,256]{3,2,1,0:T(8,128)(2,1)S(1)}, u32[]{:S(2)}, u32[]{:S(2)}) collective-permute-start(bf16[1,2,256,256]{3,2,1,0:T(8,128)(2,1)} %refs_0_.1), channel_id=1, source_target_pairs={{0,8},{4,12},{8,0},{12,4},{16,24},{20,28},{24,16},{28,20},{1,9},{5... | collective-permute-start | bytes 786440 | tf_op jit(solution)/shard_map/ppermute | solution.py:202
  2.9 1.5 %collective-permute-start.4 = (bf16[1,2,256,256]{3,2,1,0:T(8,128)(2,1)}, bf16[1,2,256,256]{3,2,1,0:T(8,128)(2,1)S(1)}, u32[]{:S(2)}, u32[]{:S(2)}) collective-permute-start(bf16[1,2,256,256]{3,2,1,0:T(8,128)(2,1)} %refs_0_.1), channel_id=1, source_target_pairs={{0,24},{4,28},{8,16},{12,20},{16,8},{20,12},{24,0},{28,4},{1,25},{... | collective-permute-start | bytes 786440 | tf_op jit(solution)/shard_map/ppermute | solution.py:202
  4.4 0.0 collective-permute-start.3
  4.5 0.7 %pad_add_fusion = s32[4,256]{1,0:T(4,128)S(1)} fusion(s32[2,256]{1,0:T(2,128)} %refs_2_.3, s32[2,256]{1,0:T(2,128)} %refs_1_.1), kind=kLoop, calls=%fused_computation.1 | loop fusion | flops 1024 | bytes 8192 | tf_op jit(solution)/shard_map/concatenate | solution.py:203
  5.2 3.1 %collective-permute-start.1 = (s32[4,256]{1,0:T(4,128)S(1)}, s32[4,256]{1,0:T(4,128)S(1)}, u32[]{:S(2)}, u32[]{:S(2)}) collective-permute-start(s32[4,256]{1,0:T(4,128)S(1)} %pad_add_fusion), channel_id=1, source_target_pairs={{0,2},{1,3},{2,0},{3,1},{4,6},{5,7},{6,4},{7,5},{8,10},{9,11},{10,... | collective-permute-start | bytes 12296 | tf_op jit(solution)/shard_map/ppermute | solution.py:23
  8.2 1.6 %collective-permute-done.1.refs_4_.refs_5_.refs_3_ = s32[4,256]{1,0:T(4,128)S(1)} collective-permute-done((s32[4,256]{1,0:T(4,128)S(1)}, s32[4,256]{1,0:T(4,128)S(1)}, u32[]{:S(2)}, u32[]{:S(2)}) %collective-permute-start.1) | collective-permute-done | bytes 4128 | tf_op jit(solution)/shard_map/ppermute | solution.py:23
  9.8 0.0 copy-start.5
  9.8 0.0 collective-permute-done.refs_1_
  9.8 0.0 copy-start.4
  9.8 0.6 %copy-done.5 = s32[4,256]{1,0:T(4,128)} copy-done((s32[4,256]{1,0:T(4,128)}, s32[4,256]{1,0:T(4,128)S(1)}, u32[]{:S(2)}) %copy-start.5) | copy-done | bytes 4120
  10.4 0.1 copy-done.4
  10.5 4.1 %shard_map.55.refs_8_ = f32[4,2,256,256]{3,2,1,0:T(8,128)} custom-call(bf16[1,2,256,256]{3,2,1,0:T(8,128)(2,1)} %refs_0_.1, bf16[1,2,256,256]{3,2,1,0:T(8,128)(2,1)} %copy-done.4, s32[2,256]{1,0:T(2,128)} %refs_1_.1, s32[2,256]{1,0:T(2,128)} %refs_2_.3, s32[4,256]{1,0:T(4,128)} %copy-done.5, s32[2]{0:T(128)} %refs_4_.3, s32[1,256]{1,0:T(1,128)} %bitcast.1), custom_call_target="tpu_custom_call" | custom-call | flops 1073741824 | bytes 2621440 | tf_op jit(solution)/shard_map/pallas_call | solution.py:180
  14.6 0.0 collective-permute-done.2.refs_0_
  14.6 0.0 copy-start
  14.6 2.5 %collective-permute-done.4.refs_2_ = bf16[1,2,256,256]{3,2,1,0:T(8,128)(2,1)S(1)} collective-permute-done((bf16[1,2,256,256]{3,2,1,0:T(8,128)(2,1)}, bf16[1,2,256,256]{3,2,1,0:T(8,128)(2,1)S(1)}, u32[]{:S(2)}, u32[]{:S(2)}) %collective-permute-start.4) | collective-permute-done | bytes 262176 | tf_op jit(solution)/shard_map/ppermute | solution.py:202
  17.1 0.0 copy-start.1
  17.1 1.4 %collective-permute-done.3.refs_1_ = bf16[1,2,256,256]{3,2,1,0:T(8,128)(2,1)S(1)} collective-permute-done((bf16[1,2,256,256]{3,2,1,0:T(8,128)(2,1)}, bf16[1,2,256,256]{3,2,1,0:T(8,128)(2,1)S(1)}, u32[]{:S(2)}, u32[]{:S(2)}) %collective-permute-start.3) | collective-permute-done | bytes 262176 | tf_op jit(solution)/shard_map/ppermute | solution.py:202
  18.4 0.0 copy-start.2
  18.4 0.1 pad_maximum_fusion
  18.5 0.1 collective-permute-start.5
  18.6 0.0 copy-done
  18.6 0.0 copy-done.1
  18.6 0.5 %copy-done.2 = bf16[1,2,256,256]{3,2,1,0:T(8,128)(2,1)} copy-done((bf16[1,2,256,256]{3,2,1,0:T(8,128)(2,1)}, bf16[1,2,256,256]{3,2,1,0:T(8,128)(2,1)S(1)}, u32[]{:S(2)}) %copy-start.2) | copy-done | bytes 262168
  19.1 5.0 %shard_map.56.refs_6_ = f32[4,2,256,256]{3,2,1,0:T(8,128)} custom-call(bf16[1,2,256,256]{3,2,1,0:T(8,128)(2,1)} %copy-done, bf16[1,2,256,256]{3,2,1,0:T(8,128)(2,1)} %copy-done.2, bf16[1,2,256,256]{3,2,1,0:T(8,128)(2,1)} %copy-done.1, s32[2,256]{1,0:T(2,128)} %refs_1_.1, s32[2,256]{1,0:T(2,128)} %refs_2_.3, s32[4,256]{1,0:T(4,128)} %copy-done.5, s32[2]{0:T(128)} %refs_4_.3, ...), custom_call_target="tpu_custom_call" | custom-call | flops 1610612736 | bytes 4980736 | tf_op jit(solution)/shard_map/pallas_call | solution.py:180
  24.1 0.0 collective-permute-done.5.refs_0_
  24.2 0.0 copy-start.3
  24.2 0.9 %copy-done.3 = bf16[3,2,256,256]{3,2,1,0:T(8,128)(2,1)} copy-done((bf16[3,2,256,256]{3,2,1,0:T(8,128)(2,1)}, bf16[3,2,256,256]{3,2,1,0:T(8,128)(2,1)S(1)}, u32[]{:S(2)}) %copy-start.3) | copy-done | bytes 786456
  25.0 6.7 %shard_map.57 = f32[2,2,256,256]{3,2,1,0:T(8,128)} custom-call(bf16[3,2,256,256]{3,2,1,0:T(8,128)(2,1)} %copy-done.3, s32[2,256]{1,0:T(2,128)} %refs_1_.1, s32[2,256]{1,0:T(2,128)} %refs_2_.3, s32[4,256]{1,0:T(4,128)} %copy-done.5, s32[2]{0:T(128)} %refs_4_.3, s32[1,256]{1,0:T(1,128)} %bitcast.3, f32[4,2,256,256]{3,2,1,0:T(8,128)} %shard_map.56.refs_6_), custom_call_target="tpu_custom_call" | custom-call | flops 2415919104 | bytes 3932160 | tf_op jit(solution)/shard_map/pallas_call | solution.py:180
Async XLA Ops:
  0.0 9.8 %collective-permute-start = (bf16[1,2,256,256]{3,2,1,0:T(8,128)(2,1)}, bf16[1,2,256,256]{3,2,1,0:T(8,128)(2,1)S(1)}, u32[]{:S(2)}, u32[]{:S(2)}) collective-permute-start(bf16[1,2,256,256]{3,2,1,0:T(8,128)(2,1)} %refs_0_.1), channel_id=1, source_target_pairs={{0,4},{4,0},{8,12},{12,8},{16,20},{20,16},{24,28},{28,24},{1,5},{5... | collective-permute-start | bytes 786440 | tf_op jit(solution)/shard_map/ppermute | solution.py:201
  0.5 14.1 %collective-permute-start.2 = (bf16[1,2,256,256]{3,2,1,0:T(8,128)(2,1)}, bf16[1,2,256,256]{3,2,1,0:T(8,128)(2,1)S(1)}, u32[]{:S(2)}, u32[]{:S(2)}) collective-permute-start(bf16[1,2,256,256]{3,2,1,0:T(8,128)(2,1)} %refs_0_.1), channel_id=1, source_target_pairs={{0,8},{4,12},{8,0},{12,4},{16,24},{20,28},{24,16},{28,20},{1,9},{5... | collective-permute-start | bytes 786440 | tf_op jit(solution)/shard_map/ppermute | solution.py:202
  2.9 14.1 %collective-permute-start.4 = (bf16[1,2,256,256]{3,2,1,0:T(8,128)(2,1)}, bf16[1,2,256,256]{3,2,1,0:T(8,128)(2,1)S(1)}, u32[]{:S(2)}, u32[]{:S(2)}) collective-permute-start(bf16[1,2,256,256]{3,2,1,0:T(8,128)(2,1)} %refs_0_.1), channel_id=1, source_target_pairs={{0,24},{4,28},{8,16},{12,20},{16,8},{20,12},{24,0},{28,4},{1,25},{... | collective-permute-start | bytes 786440 | tf_op jit(solution)/shard_map/ppermute | solution.py:202
  4.4 14.0 %collective-permute-start.3 = (bf16[1,2,256,256]{3,2,1,0:T(8,128)(2,1)}, bf16[1,2,256,256]{3,2,1,0:T(8,128)(2,1)S(1)}, u32[]{:S(2)}, u32[]{:S(2)}) collective-permute-start(bf16[1,2,256,256]{3,2,1,0:T(8,128)(2,1)} %refs_0_.1), channel_id=1, source_target_pairs={{0,16},{4,20},{8,24},{12,28},{16,0},{20,4},{24,8},{28,12},{1,17},{... | collective-permute-start | bytes 786440 | tf_op jit(solution)/shard_map/ppermute | solution.py:202
  5.2 4.6 %collective-permute-start.1 = (s32[4,256]{1,0:T(4,128)S(1)}, s32[4,256]{1,0:T(4,128)S(1)}, u32[]{:S(2)}, u32[]{:S(2)}) collective-permute-start(s32[4,256]{1,0:T(4,128)S(1)} %pad_add_fusion), channel_id=1, source_target_pairs={{0,2},{1,3},{2,0},{3,1},{4,6},{5,7},{6,4},{7,5},{8,10},{9,11},{10,... | collective-permute-start | bytes 12296 | tf_op jit(solution)/shard_map/ppermute | solution.py:23
  9.8 0.6 %copy-start.5 = (s32[4,256]{1,0:T(4,128)}, s32[4,256]{1,0:T(4,128)S(1)}, u32[]{:S(2)}) copy-start(s32[4,256]{1,0:T(4,128)S(1)} %collective-permute-done.1.refs_4_.refs_5_.refs_3_) | copy-start | bytes 12292
  9.8 0.7 %copy-start.4 = (bf16[1,2,256,256]{3,2,1,0:T(8,128)(2,1)}, bf16[1,2,256,256]{3,2,1,0:T(8,128)(2,1)S(1)}, u32[]{:S(2)}) copy-start(bf16[1,2,256,256]{3,2,1,0:T(8,128)(2,1)S(1)} %collective-permute-done.refs_1_) | copy-start | bytes 786436
  14.6 4.0 %copy-start = (bf16[1,2,256,256]{3,2,1,0:T(8,128)(2,1)}, bf16[1,2,256,256]{3,2,1,0:T(8,128)(2,1)S(1)}, u32[]{:S(2)}) copy-start(bf16[1,2,256,256]{3,2,1,0:T(8,128)(2,1)S(1)} %collective-permute-done.2.refs_0_) | copy-start | bytes 786436
  17.1 1.5 %copy-start.1 = (bf16[1,2,256,256]{3,2,1,0:T(8,128)(2,1)}, bf16[1,2,256,256]{3,2,1,0:T(8,128)(2,1)S(1)}, u32[]{:S(2)}) copy-start(bf16[1,2,256,256]{3,2,1,0:T(8,128)(2,1)S(1)} %collective-permute-done.4.refs_2_) | copy-start | bytes 786436
  18.4 0.7 %copy-start.2 = (bf16[1,2,256,256]{3,2,1,0:T(8,128)(2,1)}, bf16[1,2,256,256]{3,2,1,0:T(8,128)(2,1)S(1)}, u32[]{:S(2)}) copy-start(bf16[1,2,256,256]{3,2,1,0:T(8,128)(2,1)S(1)} %collective-permute-done.3.refs_1_) | copy-start | bytes 786436
  18.5 5.6 %collective-permute-start.5 = (bf16[3,2,256,256]{3,2,1,0:T(8,128)(2,1)S(1)}, bf16[3,2,256,256]{3,2,1,0:T(8,128)(2,1)S(1)}, u32[]{:S(2)}, u32[]{:S(2)}) collective-permute-start(bf16[3,2,256,256]{3,2,1,0:T(8,128)(2,1)S(1)} %pad_maximum_fusion), channel_id=1, source_target_pairs={{0,4},{4,0},{8,12},{12,8},{16,20},{20,16},{24,28},{28,24},{1,5},{5... | collective-permute-start | bytes 2359304 | tf_op jit(solution)/shard_map/ppermute | solution.py:212
  24.2 0.9 %copy-start.3 = (bf16[3,2,256,256]{3,2,1,0:T(8,128)(2,1)}, bf16[3,2,256,256]{3,2,1,0:T(8,128)(2,1)S(1)}, u32[]{:S(2)}) copy-start(bf16[3,2,256,256]{3,2,1,0:T(8,128)(2,1)S(1)} %collective-permute-done.5.refs_0_) | copy-start | bytes 2359300

commit v9 on v8

--- a/solution.py
+++ b/solution.py
@@ -23,17 +23,14 @@
     return lax.ppermute(value, axis, [(i, (i + by) % size) for i in range(size)])
 
 
-def split3(x):
+def split2(x):
     hi = x.astype(BF16)
-    r1 = x - hi.astype(F32)
-    mid = r1.astype(BF16)
-    lo = (r1 - mid.astype(F32)).astype(BF16)
-    return (hi, mid, lo)
+    return (hi, (x - hi.astype(F32)).astype(BF16))
 
 
 def conj_permuted(q, x):
     total = None
-    for piece in split3(x):
+    for piece in split2(x):
         rows = jnp.dot(q, piece, preferred_element_type=F32).astype(BF16)
         moved = lax.dot_general(q, rows, NT, preferred_element_type=F32)
         total = moved if total is None else total + moved
@@ -175,7 +172,7 @@
         scratch += [pltpu.VMEM(acc_shape, F32), pltpu.SemaphoreType.DMA(())]
         operands.append(prior)
     steps = sum(counts)
-    flops = steps * 2 * slots * 8 * width**3 + (12 * slots * 2 * width**3 if final else 0)
+    flops = steps * 2 * slots * 8 * width**3 + (8 * slots * 2 * width**3 if final else 0)
     moved = sum(g.size for g in walkers) * 2 + 4 * math.prod(out_shape) + (4 * math.prod(acc_shape) if has_prior else 0)
     return pl.pallas_call(
         kernel,

time: 31.9 us -> 31.6 us (level)
  no operation moved by 1% of the time
where the time goes in v9:
time: 31.6 us; the launch traced here: 31.4 us
  Pallas kernels  15.5 us (49%)
  starting transfers between devices  7.6 us (24%)
  waiting for transfers between devices  5.42 us (17%)
  local copies, waits for them, and re-layouts  2.1 us (7%)
  other arithmetic  0.79 us (2%)
    pallas_call x3, Pallas kernels, accumulate(): pl.pallas_call(kernel, grid=(1,), cost_estimate=pl.CostEstimate(flops=flo...  15.5 us
    ppermute x3, starting transfers between devices, local(): lax.ppermute(greens, 'blk', [(i, i ^ 2 * m) for i in range(blocks)])  4.02 us
    ppermute x3, waiting for transfers between devices, local(): lax.ppermute(greens, 'blk', [(i, i ^ 2 * m) for i in range(blocks)])  3.83 us
    ppermute x1, starting transfers between devices, passed_along(): lax.ppermute(value, axis, [(i, (i + by) % size) for i in range(size)])  3.05 us
    unnamed x12, local copies, waits for them, and re-layouts  2.1 us
    ppermute x1, waiting for transfers between devices, passed_along(): lax.ppermute(value, axis, [(i, (i + by) % size) for i in range(size)])  1.58 us
    concatenate x1, other arithmetic, local(): jnp.concatenate([transfer_index, phase_index], axis=0)  0.71 us
  transfers between devices with their start and end apart: 6, of which 3 were waited for; matrix products, arithmetic and copies ran while one was open for 2% of the time, Pallas kernels for 29%

profile of v9, /device:TPU:0, one launch (start us, length us, event | category | flops | bytes accessed | tf_op | source)
XLA Modules:
  0.0 31.4 jit_solution(13611710212365683621)
XLA Ops:
  0.0 0.5 %collective-permute-start = (bf16[1,2,256,256]{3,2,1,0:T(8,128)(2,1)}, bf16[1,2,256,256]{3,2,1,0:T(8,128)(2,1)S(1)}, u32[]{:S(2)}, u32[]{:S(2)}) collective-permute-start(bf16[1,2,256,256]{3,2,1,0:T(8,128)(2,1)} %refs_0_.1), channel_id=1, source_target_pairs={{0,4},{4,0},{8,12},{12,8},{16,20},{20,16},{24,28},{28,24},{1,5},{5... | collective-permute-start | bytes 786440 | tf_op jit(solution)/shard_map/ppermute | solution.py:198
  0.5 2.5 %collective-permute-start.2 = (bf16[1,2,256,256]{3,2,1,0:T(8,128)(2,1)}, bf16[1,2,256,256]{3,2,1,0:T(8,128)(2,1)S(1)}, u32[]{:S(2)}, u32[]{:S(2)}) collective-permute-start(bf16[1,2,256,256]{3,2,1,0:T(8,128)(2,1)} %refs_0_.1), channel_id=1, source_target_pairs={{0,8},{4,12},{8,0},{12,4},{16,24},{20,28},{24,16},{28,20},{1,9},{5... | collective-permute-start | bytes 786440 | tf_op jit(solution)/shard_map/ppermute | solution.py:199
  2.9 1.5 %collective-permute-start.4 = (bf16[1,2,256,256]{3,2,1,0:T(8,128)(2,1)}, bf16[1,2,256,256]{3,2,1,0:T(8,128)(2,1)S(1)}, u32[]{:S(2)}, u32[]{:S(2)}) collective-permute-start(bf16[1,2,256,256]{3,2,1,0:T(8,128)(2,1)} %refs_0_.1), channel_id=1, source_target_pairs={{0,24},{4,28},{8,16},{12,20},{16,8},{20,12},{24,0},{28,4},{1,25},{... | collective-permute-start | bytes 786440 | tf_op jit(solution)/shard_map/ppermute | solution.py:199
  4.4 0.0 collective-permute-start.3
  4.5 0.7 %pad_add_fusion = s32[4,256]{1,0:T(4,128)S(1)} fusion(s32[2,256]{1,0:T(2,128)} %refs_2_.3, s32[2,256]{1,0:T(2,128)} %refs_1_.1), kind=kLoop, calls=%fused_computation.1 | loop fusion | flops 1024 | bytes 8192 | tf_op jit(solution)/shard_map/concatenate | solution.py:200
  5.2 3.1 %collective-permute-start.1 = (s32[4,256]{1,0:T(4,128)S(1)}, s32[4,256]{1,0:T(4,128)S(1)}, u32[]{:S(2)}, u32[]{:S(2)}) collective-permute-start(s32[4,256]{1,0:T(4,128)S(1)} %pad_add_fusion), channel_id=1, source_target_pairs={{0,2},{1,3},{2,0},{3,1},{4,6},{5,7},{6,4},{7,5},{8,10},{9,11},{10,... | collective-permute-start | bytes 12296 | tf_op jit(solution)/shard_map/ppermute | solution.py:23
  8.2 1.6 %collective-permute-done.1.refs_4_.refs_5_.refs_3_ = s32[4,256]{1,0:T(4,128)S(1)} collective-permute-done((s32[4,256]{1,0:T(4,128)S(1)}, s32[4,256]{1,0:T(4,128)S(1)}, u32[]{:S(2)}, u32[]{:S(2)}) %collective-permute-start.1) | collective-permute-done | bytes 4128 | tf_op jit(solution)/shard_map/ppermute | solution.py:23
  9.8 0.0 copy-start.5
  9.8 0.0 collective-permute-done.refs_1_
  9.8 0.0 copy-start.4
  9.8 0.6 %copy-done.5 = s32[4,256]{1,0:T(4,128)} copy-done((s32[4,256]{1,0:T(4,128)}, s32[4,256]{1,0:T(4,128)S(1)}, u32[]{:S(2)}) %copy-start.5) | copy-done | bytes 4120
  10.4 0.1 copy-done.4
  10.5 4.1 %shard_map.55.refs_8_ = f32[4,2,256,256]{3,2,1,0:T(8,128)} custom-call(bf16[1,2,256,256]{3,2,1,0:T(8,128)(2,1)} %refs_0_.1, bf16[1,2,256,256]{3,2,1,0:T(8,128)(2,1)} %copy-done.4, s32[2,256]{1,0:T(2,128)} %refs_1_.1, s32[2,256]{1,0:T(2,128)} %refs_2_.3, s32[4,256]{1,0:T(4,128)} %copy-done.5, s32[2]{0:T(128)} %refs_4_.3, s32[1,256]{1,0:T(1,128)} %bitcast.1), custom_call_target="tpu_custom_call" | custom-call | flops 1073741824 | bytes 2621440 | tf_op jit(solution)/shard_map/pallas_call | solution.py:177
  14.6 0.0 collective-permute-done.2.refs_0_
  14.6 0.0 copy-start
  14.6 2.5 %collective-permute-done.4.refs_2_ = bf16[1,2,256,256]{3,2,1,0:T(8,128)(2,1)S(1)} collective-permute-done((bf16[1,2,256,256]{3,2,1,0:T(8,128)(2,1)}, bf16[1,2,256,256]{3,2,1,0:T(8,128)(2,1)S(1)}, u32[]{:S(2)}, u32[]{:S(2)}) %collective-permute-start.4) | collective-permute-done | bytes 262176 | tf_op jit(solution)/shard_map/ppermute | solution.py:199
  17.1 0.0 copy-start.1
  17.1 1.4 %collective-permute-done.3.refs_1_ = bf16[1,2,256,256]{3,2,1,0:T(8,128)(2,1)S(1)} collective-permute-done((bf16[1,2,256,256]{3,2,1,0:T(8,128)(2,1)}, bf16[1,2,256,256]{3,2,1,0:T(8,128)(2,1)S(1)}, u32[]{:S(2)}, u32[]{:S(2)}) %collective-permute-start.3) | collective-permute-done | bytes 262176 | tf_op jit(solution)/shard_map/ppermute | solution.py:199
  18.4 0.0 copy-start.2
  18.4 0.1 pad_maximum_fusion
  18.5 0.1 collective-permute-start.5
  18.6 0.0 copy-done
  18.6 0.0 copy-done.1
  18.6 0.5 %copy-done.2 = bf16[1,2,256,256]{3,2,1,0:T(8,128)(2,1)} copy-done((bf16[1,2,256,256]{3,2,1,0:T(8,128)(2,1)}, bf16[1,2,256,256]{3,2,1,0:T(8,128)(2,1)S(1)}, u32[]{:S(2)}) %copy-start.2) | copy-done | bytes 262168
  19.1 5.0 %shard_map.56.refs_6_ = f32[4,2,256,256]{3,2,1,0:T(8,128)} custom-call(bf16[1,2,256,256]{3,2,1,0:T(8,128)(2,1)} %copy-done, bf16[1,2,256,256]{3,2,1,0:T(8,128)(2,1)} %copy-done.2, bf16[1,2,256,256]{3,2,1,0:T(8,128)(2,1)} %copy-done.1, s32[2,256]{1,0:T(2,128)} %refs_1_.1, s32[2,256]{1,0:T(2,128)} %refs_2_.3, s32[4,256]{1,0:T(4,128)} %copy-done.5, s32[2]{0:T(128)} %refs_4_.3, ...), custom_call_target="tpu_custom_call" | custom-call | flops 1610612736 | bytes 4980736 | tf_op jit(solution)/shard_map/pallas_call | solution.py:177
  24.1 0.0 collective-permute-done.5.refs_0_
  24.2 0.0 copy-start.3
  24.2 0.9 %copy-done.3 = bf16[3,2,256,256]{3,2,1,0:T(8,128)(2,1)} copy-done((bf16[3,2,256,256]{3,2,1,0:T(8,128)(2,1)}, bf16[3,2,256,256]{3,2,1,0:T(8,128)(2,1)S(1)}, u32[]{:S(2)}) %copy-start.3) | copy-done | bytes 786456
  25.0 6.4 %shard_map.57 = f32[2,2,256,256]{3,2,1,0:T(8,128)} custom-call(bf16[3,2,256,256]{3,2,1,0:T(8,128)(2,1)} %copy-done.3, s32[2,256]{1,0:T(2,128)} %refs_1_.1, s32[2,256]{1,0:T(2,128)} %refs_2_.3, s32[4,256]{1,0:T(4,128)} %copy-done.5, s32[2]{0:T(128)} %refs_4_.3, s32[1,256]{1,0:T(1,128)} %bitcast.3, f32[4,2,256,256]{3,2,1,0:T(8,128)} %shard_map.56.refs_6_), custom_call_target="tpu_custom_call" | custom-call | flops 2147483648 | bytes 3932160 | tf_op jit(solution)/shard_map/pallas_call | solution.py:177
Async XLA Ops:
  0.0 9.8 %collective-permute-start = (bf16[1,2,256,256]{3,2,1,0:T(8,128)(2,1)}, bf16[1,2,256,256]{3,2,1,0:T(8,128)(2,1)S(1)}, u32[]{:S(2)}, u32[]{:S(2)}) collective-permute-start(bf16[1,2,256,256]{3,2,1,0:T(8,128)(2,1)} %refs_0_.1), channel_id=1, source_target_pairs={{0,4},{4,0},{8,12},{12,8},{16,20},{20,16},{24,28},{28,24},{1,5},{5... | collective-permute-start | bytes 786440 | tf_op jit(solution)/shard_map/ppermute | solution.py:198
  0.5 14.1 %collective-permute-start.2 = (bf16[1,2,256,256]{3,2,1,0:T(8,128)(2,1)}, bf16[1,2,256,256]{3,2,1,0:T(8,128)(2,1)S(1)}, u32[]{:S(2)}, u32[]{:S(2)}) collective-permute-start(bf16[1,2,256,256]{3,2,1,0:T(8,128)(2,1)} %refs_0_.1), channel_id=1, source_target_pairs={{0,8},{4,12},{8,0},{12,4},{16,24},{20,28},{24,16},{28,20},{1,9},{5... | collective-permute-start | bytes 786440 | tf_op jit(solution)/shard_map/ppermute | solution.py:199
  2.9 14.1 %collective-permute-start.4 = (bf16[1,2,256,256]{3,2,1,0:T(8,128)(2,1)}, bf16[1,2,256,256]{3,2,1,0:T(8,128)(2,1)S(1)}, u32[]{:S(2)}, u32[]{:S(2)}) collective-permute-start(bf16[1,2,256,256]{3,2,1,0:T(8,128)(2,1)} %refs_0_.1), channel_id=1, source_target_pairs={{0,24},{4,28},{8,16},{12,20},{16,8},{20,12},{24,0},{28,4},{1,25},{... | collective-permute-start | bytes 786440 | tf_op jit(solution)/shard_map/ppermute | solution.py:199
  4.4 14.0 %collective-permute-start.3 = (bf16[1,2,256,256]{3,2,1,0:T(8,128)(2,1)}, bf16[1,2,256,256]{3,2,1,0:T(8,128)(2,1)S(1)}, u32[]{:S(2)}, u32[]{:S(2)}) collective-permute-start(bf16[1,2,256,256]{3,2,1,0:T(8,128)(2,1)} %refs_0_.1), channel_id=1, source_target_pairs={{0,16},{4,20},{8,24},{12,28},{16,0},{20,4},{24,8},{28,12},{1,17},{... | collective-permute-start | bytes 786440 | tf_op jit(solution)/shard_map/ppermute | solution.py:199
  5.2 4.6 %collective-permute-start.1 = (s32[4,256]{1,0:T(4,128)S(1)}, s32[4,256]{1,0:T(4,128)S(1)}, u32[]{:S(2)}, u32[]{:S(2)}) collective-permute-start(s32[4,256]{1,0:T(4,128)S(1)} %pad_add_fusion), channel_id=1, source_target_pairs={{0,2},{1,3},{2,0},{3,1},{4,6},{5,7},{6,4},{7,5},{8,10},{9,11},{10,... | collective-permute-start | bytes 12296 | tf_op jit(solution)/shard_map/ppermute | solution.py:23
  9.8 0.6 %copy-start.5 = (s32[4,256]{1,0:T(4,128)}, s32[4,256]{1,0:T(4,128)S(1)}, u32[]{:S(2)}) copy-start(s32[4,256]{1,0:T(4,128)S(1)} %collective-permute-done.1.refs_4_.refs_5_.refs_3_) | copy-start | bytes 12292
  9.8 0.7 %copy-start.4 = (bf16[1,2,256,256]{3,2,1,0:T(8,128)(2,1)}, bf16[1,2,256,256]{3,2,1,0:T(8,128)(2,1)S(1)}, u32[]{:S(2)}) copy-start(bf16[1,2,256,256]{3,2,1,0:T(8,128)(2,1)S(1)} %collective-permute-done.refs_1_) | copy-start | bytes 786436
  14.6 4.0 %copy-start = (bf16[1,2,256,256]{3,2,1,0:T(8,128)(2,1)}, bf16[1,2,256,256]{3,2,1,0:T(8,128)(2,1)S(1)}, u32[]{:S(2)}) copy-start(bf16[1,2,256,256]{3,2,1,0:T(8,128)(2,1)S(1)} %collective-permute-done.2.refs_0_) | copy-start | bytes 786436
  17.1 1.5 %copy-start.1 = (bf16[1,2,256,256]{3,2,1,0:T(8,128)(2,1)}, bf16[1,2,256,256]{3,2,1,0:T(8,128)(2,1)S(1)}, u32[]{:S(2)}) copy-start(bf16[1,2,256,256]{3,2,1,0:T(8,128)(2,1)S(1)} %collective-permute-done.4.refs_2_) | copy-start | bytes 786436
  18.4 0.7 %copy-start.2 = (bf16[1,2,256,256]{3,2,1,0:T(8,128)(2,1)}, bf16[1,2,256,256]{3,2,1,0:T(8,128)(2,1)S(1)}, u32[]{:S(2)}) copy-start(bf16[1,2,256,256]{3,2,1,0:T(8,128)(2,1)S(1)} %collective-permute-done.3.refs_1_) | copy-start | bytes 786436
  18.5 5.6 %collective-permute-start.5 = (bf16[3,2,256,256]{3,2,1,0:T(8,128)(2,1)S(1)}, bf16[3,2,256,256]{3,2,1,0:T(8,128)(2,1)S(1)}, u32[]{:S(2)}, u32[]{:S(2)}) collective-permute-start(bf16[3,2,256,256]{3,2,1,0:T(8,128)(2,1)S(1)} %pad_maximum_fusion), channel_id=1, source_target_pairs={{0,4},{4,0},{8,12},{12,8},{16,20},{20,16},{24,28},{28,24},{1,5},{5... | collective-permute-start | bytes 2359304 | tf_op jit(solution)/shard_map/ppermute | solution.py:209
  24.2 0.9 %copy-start.3 = (bf16[3,2,256,256]{3,2,1,0:T(8,128)(2,1)}, bf16[3,2,256,256]{3,2,1,0:T(8,128)(2,1)S(1)}, u32[]{:S(2)}) copy-start(bf16[3,2,256,256]{3,2,1,0:T(8,128)(2,1)S(1)} %collective-permute-done.5.refs_0_) | copy-start | bytes 2359300

commit v10 on v9

--- a/solution.py
+++ b/solution.py
@@ -196,19 +196,36 @@
 
     swap = [(i, i ^ 1) for i in range(blocks)]
     sibling = lax.ppermute(greens, "blk", swap)
-    fetched = [lax.ppermute(greens, "blk", [(i, i ^ (2 * m)) for i in range(blocks)]) for m in range(1, blocks // 2)]
+    pair = [(j, j ^ 1) for j in range(lax.axis_size("xfer"))]
+    parity = lax.axis_index("xfer") % 2
+    direct, halves = [], []
+    for m in range(1, blocks // 2):
+        moves = [(i, i ^ (2 * m)) for i in range(blocks)]
+        if bin(m).count("1") == 1 or len(pair) % 2:
+            direct.append(lax.ppermute(greens, "blk", moves))
+        else:
+            halves.append(lax.ppermute(lax.dynamic_slice_in_dim(greens, parity, 1, axis=1), "blk", moves))
     far = passed_along(jnp.concatenate([transfer_index, phase_index], axis=0), "xfer", halfway)
     info = (transfer_index, phase_index, far, partner_slot, conj_index.reshape(1, width))
     run = functools.partial(accumulate, info=info, slots=slots, width=width, scale=scale)
 
-    if not fetched:
+    if not direct:
         return run([greens, sibling], prior=None, final=True)
     partial_sums = run([greens, sibling], prior=None, final=False)
-    partial_sums, fetched = lax.optimization_barrier((partial_sums, fetched))
-    near = jnp.concatenate(fetched, axis=0)
-    forwarded = lax.ppermute(near, "blk", swap)
-    partial_sums = run(fetched, prior=partial_sums, final=False)
-    return run([forwarded], prior=partial_sums, final=True)
+    partial_sums, direct, halves = lax.optimization_barrier((partial_sums, direct, halves))
+    theirs = [lax.ppermute(mine, "xfer", pair) for mine in halves]
+    forwarded = [lax.ppermute(jnp.concatenate(direct, axis=0), "blk", swap)]
+    partial_sums = run(direct, prior=partial_sums, final=False)
+    if halves:
+        partial_sums, theirs = lax.optimization_barrier((partial_sums, theirs))
+        late = []
+        for mine, other in zip(halves, theirs):
+            first = jnp.where(parity == 0, mine, other)
+            second = jnp.where(parity == 0, other, mine)
+            late.append(jnp.concatenate([first, second], axis=1))
+        late = jnp.concatenate(late, axis=0)
+        forwarded += [late, lax.ppermute(late, "blk", swap)]
+    return run(forwarded, prior=partial_sums, final=True)
 
 
 def solution(mesh):

time: 31.6 us -> 32.9 us (1.041)
  waiting for transfers between devices: 5.42 us -> 2.76 us
  starting transfers between devices: 7.6 us -> 10.2 us
  local copies, waits for them, and re-layouts: 2.1 us -> 3.18 us
    ppermute x4 -> x6, waiting for transfers between devices: 3.83 us -> 1.18 us  [the longest x1 1.16 us: local(): forwarded += [late, lax.ppermute(late, 'blk', swap)]]
    ppermute x4 -> x6, starting transfers between devices: 4.09 us -> 6.72 us  [the longest x2 4.01 us: local(): direct.append(lax.ppermute(greens, 'blk', moves))]
    dynamic_slice x0 -> x1, local copies, waits for them, and re-layouts: none -> 0.95 us  [local(): lax.dynamic_slice_in_dim(greens, parity, 1, axis=1)]
    unnamed x12 -> x14, local copies, waits for them, and re-layouts: 2.1 us -> 2.24 us
  transfers between devices with their start and end apart: 6 -> 8, of which waited for: 3 -> 2; matrix products, arithmetic and copies ran while one was open for 2% -> 5% of each run, Pallas kernels for 29% -> 26%
where the time goes in v10:
time: 32.9 us; the launch traced here: 32.7 us
  Pallas kernels  15.6 us (47%)
  starting transfers between devices  10.2 us (31%)
  local copies, waits for them, and re-layouts  3.18 us (10%)
  waiting for transfers between devices  2.76 us (8%)
  other arithmetic  0.81 us (2%)
    pallas_call x3, Pallas kernels, accumulate(): pl.pallas_call(kernel, grid=(1,), cost_estimate=pl.CostEstimate(flops=flo...  15.6 us
    ppermute x2, starting transfers between devices, local(): direct.append(lax.ppermute(greens, 'blk', moves))  4.01 us
    ppermute x1, starting transfers between devices, passed_along(): lax.ppermute(value, axis, [(i, (i + by) % size) for i in range(size)])  3.02 us
    unnamed x14, local copies, waits for them, and re-layouts  2.24 us
    ppermute x1, starting transfers between devices, local(): theirs = [lax.ppermute(mine, 'xfer', pair) for mine in halves]  1.98 us
    ppermute x1, waiting for transfers between devices, passed_along(): lax.ppermute(value, axis, [(i, (i + by) % size) for i in range(size)])  1.58 us
    ppermute x1, waiting for transfers between devices, local(): forwarded += [late, lax.ppermute(late, 'blk', swap)]  1.16 us
    dynamic_slice x1, local copies, waits for them, and re-layouts, local(): lax.dynamic_slice_in_dim(greens, parity, 1, axis=1)  0.95 us
  transfers between devices with their start and end apart: 8, of which 2 were waited for; matrix products, arithmetic and copies ran while one was open for 5% of the time, Pallas kernels for 26%

profile of v10, /device:TPU:0, one launch (start us, length us, event | category | flops | bytes accessed | tf_op | source)
XLA Modules:
  0.0 32.7 jit_solution(16624142908012687972)
XLA Ops:
  0.0 0.5 %collective-permute-start = (bf16[1,2,256,256]{3,2,1,0:T(8,128)(2,1)}, bf16[1,2,256,256]{3,2,1,0:T(8,128)(2,1)S(1)}, u32[]{:S(2)}, u32[]{:S(2)}) collective-permute-start(bf16[1,2,256,256]{3,2,1,0:T(8,128)(2,1)} %refs_0_.1), channel_id=1, source_target_pairs={{0,4},{4,0},{8,12},{12,8},{16,20},{20,16},{24,28},{28,24},{1,5},{5... | collective-permute-start | bytes 786440 | tf_op jit(solution)/shard_map/ppermute | solution.py:198
  0.5 2.5 %collective-permute-start.2 = (bf16[1,2,256,256]{3,2,1,0:T(8,128)(2,1)}, bf16[1,2,256,256]{3,2,1,0:T(8,128)(2,1)S(1)}, u32[]{:S(2)}, u32[]{:S(2)}) collective-permute-start(bf16[1,2,256,256]{3,2,1,0:T(8,128)(2,1)} %refs_0_.1), channel_id=1, source_target_pairs={{0,8},{4,12},{8,0},{12,4},{16,24},{20,28},{24,16},{28,20},{1,9},{5... | collective-permute-start | bytes 786440 | tf_op jit(solution)/shard_map/ppermute | solution.py:205
  2.9 1.5 %collective-permute-start.3 = (bf16[1,2,256,256]{3,2,1,0:T(8,128)(2,1)}, bf16[1,2,256,256]{3,2,1,0:T(8,128)(2,1)S(1)}, u32[]{:S(2)}, u32[]{:S(2)}) collective-permute-start(bf16[1,2,256,256]{3,2,1,0:T(8,128)(2,1)} %refs_0_.1), channel_id=1, source_target_pairs={{0,16},{4,20},{8,24},{12,28},{16,0},{20,4},{24,8},{28,12},{1,17},{... | collective-permute-start | bytes 786440 | tf_op jit(solution)/shard_map/ppermute | solution.py:205
  4.5 0.9 %constant_dynamic-slice_fusion = bf16[1,1,256,256]{3,2,1,0:T(8,128)(2,1)S(1)} fusion(bf16[1,2,256,256]{3,2,1,0:T(8,128)(2,1)} %refs_0_.1, s32[]{:T(128)S(6)} %select_n.23), kind=kLoop, calls=%fused_computation.5 | loop fusion | bytes 262148 | tf_op jit(solution)/shard_map/dynamic_slice | solution.py:207
  5.4 0.1 collective-permute-start.4
  5.5 0.7 %pad_add_fusion = s32[4,256]{1,0:T(4,128)S(1)} fusion(s32[2,256]{1,0:T(2,128)} %refs_4_.1, s32[2,256]{1,0:T(2,128)} %refs_3_.5), kind=kLoop, calls=%fused_computation.4 | loop fusion | flops 1024 | bytes 8192 | tf_op jit(solution)/shard_map/concatenate | solution.py:208
  6.2 3.0 %collective-permute-start.1 = (s32[4,256]{1,0:T(4,128)S(1)}, s32[4,256]{1,0:T(4,128)S(1)}, u32[]{:S(2)}, u32[]{:S(2)}) collective-permute-start(s32[4,256]{1,0:T(4,128)S(1)} %pad_add_fusion), channel_id=1, source_target_pairs={{0,2},{1,3},{2,0},{3,1},{4,6},{5,7},{6,4},{7,5},{8,10},{9,11},{10,... | collective-permute-start | bytes 12296 | tf_op jit(solution)/shard_map/ppermute | solution.py:23
  9.3 1.6 %collective-permute-done.1.refs_4_.refs_5_ = s32[4,256]{1,0:T(4,128)S(1)} collective-permute-done((s32[4,256]{1,0:T(4,128)S(1)}, s32[4,256]{1,0:T(4,128)S(1)}, u32[]{:S(2)}, u32[]{:S(2)}) %collective-permute-start.1) | collective-permute-done | bytes 4128 | tf_op jit(solution)/shard_map/ppermute | solution.py:23
  10.8 0.0 copy-start.3
  10.8 0.0 collective-permute-done.refs_1_
  10.8 0.0 copy-start.5
  10.8 0.6 %copy-done.3 = s32[4,256]{1,0:T(4,128)} copy-done((s32[4,256]{1,0:T(4,128)}, s32[4,256]{1,0:T(4,128)S(1)}, u32[]{:S(2)}) %copy-start.3) | copy-done | bytes 4120
  11.4 0.1 copy-done.5
  11.5 4.1 %shard_map.55.refs_7_ = f32[4,2,256,256]{3,2,1,0:T(8,128)} custom-call(bf16[1,2,256,256]{3,2,1,0:T(8,128)(2,1)} %refs_0_.1, bf16[1,2,256,256]{3,2,1,0:T(8,128)(2,1)} %copy-done.5, s32[2,256]{1,0:T(2,128)} %refs_3_.5, s32[2,256]{1,0:T(2,128)} %refs_4_.1, s32[4,256]{1,0:T(4,128)} %copy-done.3, s32[2]{0:T(128)} %refs_6_.1, s32[1,256]{1,0:T(1,128)} %bitcast.1), custom_call_target="tpu_custom_call" | custom-call | flops 1073741824 | bytes 2621440 | tf_op jit(solution)/shard_map/pallas_call | solution.py:177
  15.6 0.0 collective-permute-done.4
  15.6 0.0 collective-permute-done.2.refs_0_
  15.6 0.0 copy-start
  15.6 0.0 collective-permute-done.3.refs_1_
  15.6 0.0 copy-start.1
  15.6 2.0 %collective-permute-start.6 = (bf16[1,1,256,256]{3,2,1,0:T(8,128)(2,1)S(1)}, bf16[1,1,256,256]{3,2,1,0:T(8,128)(2,1)S(1)}, u32[]{:S(2)}, u32[]{:S(2)}) collective-permute-start(bf16[1,1,256,256]{3,2,1,0:T(8,128)(2,1)S(1)} %collective-permute-done.4), channel_id=1, source_target_pairs={{0,1},{1,0},{2,3},{3,2},{4,5},{5,4},{6,7},{7,6},{8,9},{9,8},{10,11... | collective-permute-start | bytes 393224 | tf_op jit(solution)/shard_map/ppermute | solution.py:216
  17.6 0.1 pad_maximum_fusion
  17.7 0.1 collective-permute-start.5
  17.8 0.0 copy-done
  17.8 0.0 copy-done.1
  17.8 4.3 %shard_map.56.refs_8_ = f32[4,2,256,256]{3,2,1,0:T(8,128)} custom-call(bf16[1,2,256,256]{3,2,1,0:T(8,128)(2,1)} %copy-done, bf16[1,2,256,256]{3,2,1,0:T(8,128)(2,1)} %copy-done.1, s32[2,256]{1,0:T(2,128)} %refs_3_.5, s32[2,256]{1,0:T(2,128)} %refs_4_.1, s32[4,256]{1,0:T(4,128)} %copy-done.3, s32[2]{0:T(128)} %refs_6_.1, s32[1,256]{1,0:T(1,128)} %bitcast.2, ...), custom_call_target="tpu_custom_call" | custom-call | flops 1073741824 | bytes 4718592 | tf_op jit(solution)/shard_map/pallas_call | solution.py:177
  22.1 0.0 collective-permute-done.6
  22.2 0.0 copy-start.2
  22.2 0.6 %collective-permute-start.7 = (bf16[1,2,256,256]{3,2,1,0:T(8,128)(2,1)S(1)}, bf16[1,2,256,256]{3,2,1,0:T(8,128)(2,1)S(1)}, u32[]{:S(2)}, u32[]{:S(2)}) collective-permute-start(bf16[1,2,256,256]{3,2,1,0:T(8,128)(2,1)S(1)} %pad_maximum_fusion.1.refs_1_), channel_id=1, source_target_pairs={{0,4},{4,0},{8,12},{12,8},{16,20},{20,16},{24,28},{28,24},{1,5},{5... | collective-permute-start | bytes 786440 | tf_op jit(solution)/shard_map/ppermute | solution.py:227
  22.8 1.2 %collective-permute-done.7.refs_2_ = bf16[1,2,256,256]{3,2,1,0:T(8,128)(2,1)S(1)} collective-permute-done((bf16[1,2,256,256]{3,2,1,0:T(8,128)(2,1)S(1)}, bf16[1,2,256,256]{3,2,1,0:T(8,128)(2,1)S(1)}, u32[]{:S(2)}, u32[]{:S(2)}) %collective-permute-start.7) | collective-permute-done | bytes 262176 | tf_op jit(solution)/shard_map/ppermute | solution.py:227
  23.9 0.0 copy-start.6
  23.9 0.0 collective-permute-done.5.refs_0_
  23.9 0.0 copy-done.2
  23.9 0.7 %copy-done.6 = bf16[1,2,256,256]{3,2,1,0:T(8,128)(2,1)} copy-done((bf16[1,2,256,256]{3,2,1,0:T(8,128)(2,1)}, bf16[1,2,256,256]{3,2,1,0:T(8,128)(2,1)S(1)}, u32[]{:S(2)}) %copy-start.6) | copy-done | bytes 262168
  24.6 0.0 copy-start.4
  24.6 0.8 %copy-done.4 = bf16[2,2,256,256]{3,2,1,0:T(8,128)(2,1)} copy-done((bf16[2,2,256,256]{3,2,1,0:T(8,128)(2,1)}, bf16[2,2,256,256]{3,2,1,0:T(8,128)(2,1)S(1)}, u32[]{:S(2)}) %copy-start.4) | copy-done | bytes 524312
  25.4 7.2 %shard_map.57 = f32[2,2,256,256]{3,2,1,0:T(8,128)} custom-call(bf16[2,2,256,256]{3,2,1,0:T(8,128)(2,1)} %copy-done.4, bf16[1,2,256,256]{3,2,1,0:T(8,128)(2,1)} %copy-done.2, bf16[1,2,256,256]{3,2,1,0:T(8,128)(2,1)} %copy-done.6, s32[2,256]{1,0:T(2,128)} %refs_3_.5, s32[2,256]{1,0:T(2,128)} %refs_4_.1, s32[4,256]{1,0:T(4,128)} %copy-done.3, s32[2]{0:T(128)} %refs_6_.1, ...), custom_call_target="tpu_custom_call" | custom-call | flops 2684354560 | bytes 4194304 | tf_op jit(solution)/shard_map/pallas_call | solution.py:177
  (2 shorter events, 0.1 us)
Async XLA Ops:
  0.0 10.8 %collective-permute-start = (bf16[1,2,256,256]{3,2,1,0:T(8,128)(2,1)}, bf16[1,2,256,256]{3,2,1,0:T(8,128)(2,1)S(1)}, u32[]{:S(2)}, u32[]{:S(2)}) collective-permute-start(bf16[1,2,256,256]{3,2,1,0:T(8,128)(2,1)} %refs_0_.1), channel_id=1, source_target_pairs={{0,4},{4,0},{8,12},{12,8},{16,20},{20,16},{24,28},{28,24},{1,5},{5... | collective-permute-start | bytes 786440 | tf_op jit(solution)/shard_map/ppermute | solution.py:198
  0.5 15.1 %collective-permute-start.2 = (bf16[1,2,256,256]{3,2,1,0:T(8,128)(2,1)}, bf16[1,2,256,256]{3,2,1,0:T(8,128)(2,1)S(1)}, u32[]{:S(2)}, u32[]{:S(2)}) collective-permute-start(bf16[1,2,256,256]{3,2,1,0:T(8,128)(2,1)} %refs_0_.1), channel_id=1, source_target_pairs={{0,8},{4,12},{8,0},{12,4},{16,24},{20,28},{24,16},{28,20},{1,9},{5... | collective-permute-start | bytes 786440 | tf_op jit(solution)/shard_map/ppermute | solution.py:205
  2.9 12.7 %collective-permute-start.3 = (bf16[1,2,256,256]{3,2,1,0:T(8,128)(2,1)}, bf16[1,2,256,256]{3,2,1,0:T(8,128)(2,1)S(1)}, u32[]{:S(2)}, u32[]{:S(2)}) collective-permute-start(bf16[1,2,256,256]{3,2,1,0:T(8,128)(2,1)} %refs_0_.1), channel_id=1, source_target_pairs={{0,16},{4,20},{8,24},{12,28},{16,0},{20,4},{24,8},{28,12},{1,17},{... | collective-permute-start | bytes 786440 | tf_op jit(solution)/shard_map/ppermute | solution.py:205
  5.4 10.2 %collective-permute-start.4 = (bf16[1,1,256,256]{3,2,1,0:T(8,128)(2,1)S(1)}, bf16[1,1,256,256]{3,2,1,0:T(8,128)(2,1)S(1)}, u32[]{:S(2)}, u32[]{:S(2)}) collective-permute-start(bf16[1,1,256,256]{3,2,1,0:T(8,128)(2,1)S(1)} %constant_dynamic-slice_fusion), channel_id=1, source_target_pairs={{0,24},{4,28},{8,16},{12,20},{16,8},{20,12},{24,0},{28,4},{1,25},{... | collective-permute-start | bytes 393224 | tf_op jit(solution)/shard_map/ppermute | solution.py:207
  6.2 4.6 %collective-permute-start.1 = (s32[4,256]{1,0:T(4,128)S(1)}, s32[4,256]{1,0:T(4,128)S(1)}, u32[]{:S(2)}, u32[]{:S(2)}) collective-permute-start(s32[4,256]{1,0:T(4,128)S(1)} %pad_add_fusion), channel_id=1, source_target_pairs={{0,2},{1,3},{2,0},{3,1},{4,6},{5,7},{6,4},{7,5},{8,10},{9,11},{10,... | collective-permute-start | bytes 12296 | tf_op jit(solution)/shard_map/ppermute | solution.py:23
  10.8 0.6 %copy-start.3 = (s32[4,256]{1,0:T(4,128)}, s32[4,256]{1,0:T(4,128)S(1)}, u32[]{:S(2)}) copy-start(s32[4,256]{1,0:T(4,128)S(1)} %collective-permute-done.1.refs_4_.refs_5_) | copy-start | bytes 12292
  10.8 0.7 %copy-start.5 = (bf16[1,2,256,256]{3,2,1,0:T(8,128)(2,1)}, bf16[1,2,256,256]{3,2,1,0:T(8,128)(2,1)S(1)}, u32[]{:S(2)}) copy-start(bf16[1,2,256,256]{3,2,1,0:T(8,128)(2,1)S(1)} %collective-permute-done.refs_1_) | copy-start | bytes 786436
  15.6 2.1 %copy-start = (bf16[1,2,256,256]{3,2,1,0:T(8,128)(2,1)}, bf16[1,2,256,256]{3,2,1,0:T(8,128)(2,1)S(1)}, u32[]{:S(2)}) copy-start(bf16[1,2,256,256]{3,2,1,0:T(8,128)(2,1)S(1)} %collective-permute-done.2.refs_0_) | copy-start | bytes 786436
  15.6 2.1 %copy-start.1 = (bf16[1,2,256,256]{3,2,1,0:T(8,128)(2,1)}, bf16[1,2,256,256]{3,2,1,0:T(8,128)(2,1)S(1)}, u32[]{:S(2)}) copy-start(bf16[1,2,256,256]{3,2,1,0:T(8,128)(2,1)S(1)} %collective-permute-done.3.refs_1_) | copy-start | bytes 786436
  15.6 6.5 %collective-permute-start.6 = (bf16[1,1,256,256]{3,2,1,0:T(8,128)(2,1)S(1)}, bf16[1,1,256,256]{3,2,1,0:T(8,128)(2,1)S(1)}, u32[]{:S(2)}, u32[]{:S(2)}) collective-permute-start(bf16[1,1,256,256]{3,2,1,0:T(8,128)(2,1)S(1)} %collective-permute-done.4), channel_id=1, source_target_pairs={{0,1},{1,0},{2,3},{3,2},{4,5},{5,4},{6,7},{7,6},{8,9},{9,8},{10,11... | collective-permute-start | bytes 393224 | tf_op jit(solution)/shard_map/ppermute | solution.py:216
  17.7 6.2 %collective-permute-start.5 = (bf16[2,2,256,256]{3,2,1,0:T(8,128)(2,1)S(1)}, bf16[2,2,256,256]{3,2,1,0:T(8,128)(2,1)S(1)}, u32[]{:S(2)}, u32[]{:S(2)}) collective-permute-start(bf16[2,2,256,256]{3,2,1,0:T(8,128)(2,1)S(1)} %pad_maximum_fusion), channel_id=1, source_target_pairs={{0,4},{4,0},{8,12},{12,8},{16,20},{20,16},{24,28},{28,24},{1,5},{5... | collective-permute-start | bytes 1572872 | tf_op jit(solution)/shard_map/ppermute | solution.py:217
  22.2 1.7 %copy-start.2 = (bf16[1,2,256,256]{3,2,1,0:T(8,128)(2,1)}, bf16[1,2,256,256]{3,2,1,0:T(8,128)(2,1)S(1)}, u32[]{:S(2)}) copy-start(bf16[1,2,256,256]{3,2,1,0:T(8,128)(2,1)S(1)} %pad_maximum_fusion.1.refs_1_) | copy-start | bytes 786436
  22.2 1.7 %collective-permute-start.7 = (bf16[1,2,256,256]{3,2,1,0:T(8,128)(2,1)S(1)}, bf16[1,2,256,256]{3,2,1,0:T(8,128)(2,1)S(1)}, u32[]{:S(2)}, u32[]{:S(2)}) collective-permute-start(bf16[1,2,256,256]{3,2,1,0:T(8,128)(2,1)S(1)} %pad_maximum_fusion.1.refs_1_), channel_id=1, source_target_pairs={{0,4},{4,0},{8,12},{12,8},{16,20},{20,16},{24,28},{28,24},{1,5},{5... | collective-permute-start | bytes 786440 | tf_op jit(solution)/shard_map/ppermute | solution.py:227
  23.9 0.7 %copy-start.6 = (bf16[1,2,256,256]{3,2,1,0:T(8,128)(2,1)}, bf16[1,2,256,256]{3,2,1,0:T(8,128)(2,1)S(1)}, u32[]{:S(2)}) copy-start(bf16[1,2,256,256]{3,2,1,0:T(8,128)(2,1)S(1)} %collective-permute-done.7.refs_2_) | copy-start | bytes 786436
  24.6 0.8 %copy-start.4 = (bf16[2,2,256,256]{3,2,1,0:T(8,128)(2,1)}, bf16[2,2,256,256]{3,2,1,0:T(8,128)(2,1)S(1)}, u32[]{:S(2)}) copy-start(bf16[2,2,256,256]{3,2,1,0:T(8,128)(2,1)S(1)} %collective-permute-done.5.refs_0_) | copy-start | bytes 1572868

commit v11 on v9

--- a/solution.py
+++ b/solution.py
@@ -204,7 +204,7 @@
     if not fetched:
         return run([greens, sibling], prior=None, final=True)
     partial_sums = run([greens, sibling], prior=None, final=False)
-    partial_sums, fetched = lax.optimization_barrier((partial_sums, fetched))
+    partial_sums, fetched = lax.optimization_barrier((partial_sums, [fetched[1], fetched[0]] + fetched[2:]))
     near = jnp.concatenate(fetched, axis=0)
     forwarded = lax.ppermute(near, "blk", swap)
     partial_sums = run(fetched, prior=partial_sums, final=False)

time: 31.6 us -> 30.3 us (0.959)
  waiting for transfers between devices: 5.42 us -> 4.06 us
    ppermute x3, waiting for transfers between devices: 3.83 us -> 2.47 us  [local(): lax.ppermute(greens, 'blk', [(i, i ^ 2 * m) for i in range(blocks)])]
  transfers between devices with their start and end apart: 6 -> 6, of which waited for: 3 -> 3; matrix products, arithmetic and copies ran while one was open for 2% -> 2% of each run, Pallas kernels for 29% -> 30%
where the time goes in v11:
time: 30.3 us; the launch traced here: 30.1 us
  Pallas kernels  15.4 us (51%)
  starting transfers between devices  7.6 us (25%)
  waiting for transfers between devices  4.06 us (13%)
  local copies, waits for them, and re-layouts  2.1 us (7%)
  other arithmetic  0.79 us (3%)
    pallas_call x3, Pallas kernels, accumulate(): pl.pallas_call(kernel, grid=(1,), cost_estimate=pl.CostEstimate(flops=flo...  15.4 us
    ppermute x3, starting transfers between devices, local(): lax.ppermute(greens, 'blk', [(i, i ^ 2 * m) for i in range(blocks)])  4.05 us
    ppermute x1, starting transfers between devices, passed_along(): lax.ppermute(value, axis, [(i, (i + by) % size) for i in range(size)])  3.02 us
    ppermute x3, waiting for transfers between devices, local(): lax.ppermute(greens, 'blk', [(i, i ^ 2 * m) for i in range(blocks)])  2.47 us
    unnamed x12, local copies, waits for them, and re-layouts  2.1 us
    ppermute x1, waiting for transfers between devices, passed_along(): lax.ppermute(value, axis, [(i, (i + by) % size) for i in range(size)])  1.58 us
    concatenate x1, other arithmetic, local(): jnp.concatenate([transfer_index, phase_index], axis=0)  0.71 us
  transfers between devices with their start and end apart: 6, of which 3 were waited for; matrix products, arithmetic and copies ran while one was open for 2% of the time, Pallas kernels for 30%

profile of v11, /device:TPU:0, one launch (start us, length us, event | category | flops | bytes accessed | tf_op | source)
XLA Modules:
  0.0 30.1 jit_solution(16644149215970535640)
XLA Ops:
  0.0 0.5 %collective-permute-start = (bf16[1,2,256,256]{3,2,1,0:T(8,128)(2,1)}, bf16[1,2,256,256]{3,2,1,0:T(8,128)(2,1)S(1)}, u32[]{:S(2)}, u32[]{:S(2)}) collective-permute-start(bf16[1,2,256,256]{3,2,1,0:T(8,128)(2,1)} %refs_0_.1), channel_id=1, source_target_pairs={{0,4},{4,0},{8,12},{12,8},{16,20},{20,16},{24,28},{28,24},{1,5},{5... | collective-permute-start | bytes 786440 | tf_op jit(solution)/shard_map/ppermute | solution.py:198
  0.5 2.5 %collective-permute-start.2 = (bf16[1,2,256,256]{3,2,1,0:T(8,128)(2,1)}, bf16[1,2,256,256]{3,2,1,0:T(8,128)(2,1)S(1)}, u32[]{:S(2)}, u32[]{:S(2)}) collective-permute-start(bf16[1,2,256,256]{3,2,1,0:T(8,128)(2,1)} %refs_0_.1), channel_id=1, source_target_pairs={{0,16},{4,20},{8,24},{12,28},{16,0},{20,4},{24,8},{28,12},{1,17},{... | collective-permute-start | bytes 786440 | tf_op jit(solution)/shard_map/ppermute | solution.py:199
  3.0 1.4 %collective-permute-start.4 = (bf16[1,2,256,256]{3,2,1,0:T(8,128)(2,1)}, bf16[1,2,256,256]{3,2,1,0:T(8,128)(2,1)S(1)}, u32[]{:S(2)}, u32[]{:S(2)}) collective-permute-start(bf16[1,2,256,256]{3,2,1,0:T(8,128)(2,1)} %refs_0_.1), channel_id=1, source_target_pairs={{0,24},{4,28},{8,16},{12,20},{16,8},{20,12},{24,0},{28,4},{1,25},{... | collective-permute-start | bytes 786440 | tf_op jit(solution)/shard_map/ppermute | solution.py:199
  4.4 0.1 collective-permute-start.3
  4.5 0.7 %pad_add_fusion = s32[4,256]{1,0:T(4,128)S(1)} fusion(s32[2,256]{1,0:T(2,128)} %refs_2_.3, s32[2,256]{1,0:T(2,128)} %refs_1_.1), kind=kLoop, calls=%fused_computation.1 | loop fusion | flops 1024 | bytes 8192 | tf_op jit(solution)/shard_map/concatenate | solution.py:200
  5.2 3.0 %collective-permute-start.1 = (s32[4,256]{1,0:T(4,128)S(1)}, s32[4,256]{1,0:T(4,128)S(1)}, u32[]{:S(2)}, u32[]{:S(2)}) collective-permute-start(s32[4,256]{1,0:T(4,128)S(1)} %pad_add_fusion), channel_id=1, source_target_pairs={{0,2},{1,3},{2,0},{3,1},{4,6},{5,7},{6,4},{7,5},{8,10},{9,11},{10,... | collective-permute-start | bytes 12296 | tf_op jit(solution)/shard_map/ppermute | solution.py:23
  8.2 1.6 %collective-permute-done.1.refs_4_.refs_5_.refs_3_ = s32[4,256]{1,0:T(4,128)S(1)} collective-permute-done((s32[4,256]{1,0:T(4,128)S(1)}, s32[4,256]{1,0:T(4,128)S(1)}, u32[]{:S(2)}, u32[]{:S(2)}) %collective-permute-start.1) | collective-permute-done | bytes 4128 | tf_op jit(solution)/shard_map/ppermute | solution.py:23
  9.8 0.0 copy-start.5
  9.8 0.0 collective-permute-done.refs_1_
  9.8 0.0 copy-start.4
  9.8 0.6 %copy-done.5 = s32[4,256]{1,0:T(4,128)} copy-done((s32[4,256]{1,0:T(4,128)}, s32[4,256]{1,0:T(4,128)S(1)}, u32[]{:S(2)}) %copy-start.5) | copy-done | bytes 4120
  10.4 0.1 copy-done.4
  10.5 4.1 %shard_map.55.refs_8_ = f32[4,2,256,256]{3,2,1,0:T(8,128)} custom-call(bf16[1,2,256,256]{3,2,1,0:T(8,128)(2,1)} %refs_0_.1, bf16[1,2,256,256]{3,2,1,0:T(8,128)(2,1)} %copy-done.4, s32[2,256]{1,0:T(2,128)} %refs_1_.1, s32[2,256]{1,0:T(2,128)} %refs_2_.3, s32[4,256]{1,0:T(4,128)} %copy-done.5, s32[2]{0:T(128)} %refs_4_.3, s32[1,256]{1,0:T(1,128)} %bitcast.1), custom_call_target="tpu_custom_call" | custom-call | flops 1073741824 | bytes 2621440 | tf_op jit(solution)/shard_map/pallas_call | solution.py:177
  14.6 1.2 %collective-permute-done.2.refs_0_ = bf16[1,2,256,256]{3,2,1,0:T(8,128)(2,1)S(1)} collective-permute-done((bf16[1,2,256,256]{3,2,1,0:T(8,128)(2,1)}, bf16[1,2,256,256]{3,2,1,0:T(8,128)(2,1)S(1)}, u32[]{:S(2)}, u32[]{:S(2)}) %collective-permute-start.2) | collective-permute-done | bytes 262176 | tf_op jit(solution)/shard_map/ppermute | solution.py:199
  15.8 0.0 copy-start
  15.8 0.0 collective-permute-done.4.refs_2_
  15.8 0.0 copy-start.1
  15.8 1.3 %collective-permute-done.3.refs_1_ = bf16[1,2,256,256]{3,2,1,0:T(8,128)(2,1)S(1)} collective-permute-done((bf16[1,2,256,256]{3,2,1,0:T(8,128)(2,1)}, bf16[1,2,256,256]{3,2,1,0:T(8,128)(2,1)S(1)}, u32[]{:S(2)}, u32[]{:S(2)}) %collective-permute-start.3) | collective-permute-done | bytes 262176 | tf_op jit(solution)/shard_map/ppermute | solution.py:199
  17.1 0.0 copy-start.2
  17.1 0.1 pad_maximum_fusion
  17.2 0.1 collective-permute-start.5
  17.2 0.0 copy-done
  17.2 0.0 copy-done.1
  17.3 0.5 %copy-done.2 = bf16[1,2,256,256]{3,2,1,0:T(8,128)(2,1)} copy-done((bf16[1,2,256,256]{3,2,1,0:T(8,128)(2,1)}, bf16[1,2,256,256]{3,2,1,0:T(8,128)(2,1)S(1)}, u32[]{:S(2)}) %copy-start.2) | copy-done | bytes 262168
  17.8 5.0 %shard_map.56.refs_6_ = f32[4,2,256,256]{3,2,1,0:T(8,128)} custom-call(bf16[1,2,256,256]{3,2,1,0:T(8,128)(2,1)} %copy-done, bf16[1,2,256,256]{3,2,1,0:T(8,128)(2,1)} %copy-done.2, bf16[1,2,256,256]{3,2,1,0:T(8,128)(2,1)} %copy-done.1, s32[2,256]{1,0:T(2,128)} %refs_1_.1, s32[2,256]{1,0:T(2,128)} %refs_2_.3, s32[4,256]{1,0:T(4,128)} %copy-done.5, s32[2]{0:T(128)} %refs_4_.3, ...), custom_call_target="tpu_custom_call" | custom-call | flops 1610612736 | bytes 4980736 | tf_op jit(solution)/shard_map/pallas_call | solution.py:177
  22.8 0.0 collective-permute-done.5.refs_0_
  22.8 0.0 copy-start.3
  22.8 0.9 %copy-done.3 = bf16[3,2,256,256]{3,2,1,0:T(8,128)(2,1)} copy-done((bf16[3,2,256,256]{3,2,1,0:T(8,128)(2,1)}, bf16[3,2,256,256]{3,2,1,0:T(8,128)(2,1)S(1)}, u32[]{:S(2)}) %copy-start.3) | copy-done | bytes 786456
  23.7 6.4 %shard_map.57 = f32[2,2,256,256]{3,2,1,0:T(8,128)} custom-call(bf16[3,2,256,256]{3,2,1,0:T(8,128)(2,1)} %copy-done.3, s32[2,256]{1,0:T(2,128)} %refs_1_.1, s32[2,256]{1,0:T(2,128)} %refs_2_.3, s32[4,256]{1,0:T(4,128)} %copy-done.5, s32[2]{0:T(128)} %refs_4_.3, s32[1,256]{1,0:T(1,128)} %bitcast.3, f32[4,2,256,256]{3,2,1,0:T(8,128)} %shard_map.56.refs_6_), custom_call_target="tpu_custom_call" | custom-call | flops 2147483648 | bytes 3932160 | tf_op jit(solution)/shard_map/pallas_call | solution.py:177
Async XLA Ops:
  0.0 9.8 %collective-permute-start = (bf16[1,2,256,256]{3,2,1,0:T(8,128)(2,1)}, bf16[1,2,256,256]{3,2,1,0:T(8,128)(2,1)S(1)}, u32[]{:S(2)}, u32[]{:S(2)}) collective-permute-start(bf16[1,2,256,256]{3,2,1,0:T(8,128)(2,1)} %refs_0_.1), channel_id=1, source_target_pairs={{0,4},{4,0},{8,12},{12,8},{16,20},{20,16},{24,28},{28,24},{1,5},{5... | collective-permute-start | bytes 786440 | tf_op jit(solution)/shard_map/ppermute | solution.py:198
  0.5 15.3 %collective-permute-start.2 = (bf16[1,2,256,256]{3,2,1,0:T(8,128)(2,1)}, bf16[1,2,256,256]{3,2,1,0:T(8,128)(2,1)S(1)}, u32[]{:S(2)}, u32[]{:S(2)}) collective-permute-start(bf16[1,2,256,256]{3,2,1,0:T(8,128)(2,1)} %refs_0_.1), channel_id=1, source_target_pairs={{0,16},{4,20},{8,24},{12,28},{16,0},{20,4},{24,8},{28,12},{1,17},{... | collective-permute-start | bytes 786440 | tf_op jit(solution)/shard_map/ppermute | solution.py:199
  3.0 12.8 %collective-permute-start.4 = (bf16[1,2,256,256]{3,2,1,0:T(8,128)(2,1)}, bf16[1,2,256,256]{3,2,1,0:T(8,128)(2,1)S(1)}, u32[]{:S(2)}, u32[]{:S(2)}) collective-permute-start(bf16[1,2,256,256]{3,2,1,0:T(8,128)(2,1)} %refs_0_.1), channel_id=1, source_target_pairs={{0,24},{4,28},{8,16},{12,20},{16,8},{20,12},{24,0},{28,4},{1,25},{... | collective-permute-start | bytes 786440 | tf_op jit(solution)/shard_map/ppermute | solution.py:199
  4.4 12.7 %collective-permute-start.3 = (bf16[1,2,256,256]{3,2,1,0:T(8,128)(2,1)}, bf16[1,2,256,256]{3,2,1,0:T(8,128)(2,1)S(1)}, u32[]{:S(2)}, u32[]{:S(2)}) collective-permute-start(bf16[1,2,256,256]{3,2,1,0:T(8,128)(2,1)} %refs_0_.1), channel_id=1, source_target_pairs={{0,8},{4,12},{8,0},{12,4},{16,24},{20,28},{24,16},{28,20},{1,9},{5... | collective-permute-start | bytes 786440 | tf_op jit(solution)/shard_map/ppermute | solution.py:199
  5.2 4.6 %collective-permute-start.1 = (s32[4,256]{1,0:T(4,128)S(1)}, s32[4,256]{1,0:T(4,128)S(1)}, u32[]{:S(2)}, u32[]{:S(2)}) collective-permute-start(s32[4,256]{1,0:T(4,128)S(1)} %pad_add_fusion), channel_id=1, source_target_pairs={{0,2},{1,3},{2,0},{3,1},{4,6},{5,7},{6,4},{7,5},{8,10},{9,11},{10,... | collective-permute-start | bytes 12296 | tf_op jit(solution)/shard_map/ppermute | solution.py:23
  9.8 0.6 %copy-start.5 = (s32[4,256]{1,0:T(4,128)}, s32[4,256]{1,0:T(4,128)S(1)}, u32[]{:S(2)}) copy-start(s32[4,256]{1,0:T(4,128)S(1)} %collective-permute-done.1.refs_4_.refs_5_.refs_3_) | copy-start | bytes 12292
  9.8 0.7 %copy-start.4 = (bf16[1,2,256,256]{3,2,1,0:T(8,128)(2,1)}, bf16[1,2,256,256]{3,2,1,0:T(8,128)(2,1)S(1)}, u32[]{:S(2)}) copy-start(bf16[1,2,256,256]{3,2,1,0:T(8,128)(2,1)S(1)} %collective-permute-done.refs_1_) | copy-start | bytes 786436
  15.8 1.5 %copy-start = (bf16[1,2,256,256]{3,2,1,0:T(8,128)(2,1)}, bf16[1,2,256,256]{3,2,1,0:T(8,128)(2,1)S(1)}, u32[]{:S(2)}) copy-start(bf16[1,2,256,256]{3,2,1,0:T(8,128)(2,1)S(1)} %collective-permute-done.2.refs_0_) | copy-start | bytes 786436
  15.8 1.5 %copy-start.1 = (bf16[1,2,256,256]{3,2,1,0:T(8,128)(2,1)}, bf16[1,2,256,256]{3,2,1,0:T(8,128)(2,1)S(1)}, u32[]{:S(2)}) copy-start(bf16[1,2,256,256]{3,2,1,0:T(8,128)(2,1)S(1)} %collective-permute-done.4.refs_2_) | copy-start | bytes 786436
  17.1 0.7 %copy-start.2 = (bf16[1,2,256,256]{3,2,1,0:T(8,128)(2,1)}, bf16[1,2,256,256]{3,2,1,0:T(8,128)(2,1)S(1)}, u32[]{:S(2)}) copy-start(bf16[1,2,256,256]{3,2,1,0:T(8,128)(2,1)S(1)} %collective-permute-done.3.refs_1_) | copy-start | bytes 786436
  17.2 5.6 %collective-permute-start.5 = (bf16[3,2,256,256]{3,2,1,0:T(8,128)(2,1)S(1)}, bf16[3,2,256,256]{3,2,1,0:T(8,128)(2,1)S(1)}, u32[]{:S(2)}, u32[]{:S(2)}) collective-permute-start(bf16[3,2,256,256]{3,2,1,0:T(8,128)(2,1)S(1)} %pad_maximum_fusion), channel_id=1, source_target_pairs={{0,4},{4,0},{8,12},{12,8},{16,20},{20,16},{24,28},{28,24},{1,5},{5... | collective-permute-start | bytes 2359304 | tf_op jit(solution)/shard_map/ppermute | solution.py:209
  22.8 0.9 %copy-start.3 = (bf16[3,2,256,256]{3,2,1,0:T(8,128)(2,1)}, bf16[3,2,256,256]{3,2,1,0:T(8,128)(2,1)S(1)}, u32[]{:S(2)}) copy-start(bf16[3,2,256,256]{3,2,1,0:T(8,128)(2,1)S(1)} %collective-permute-done.5.refs_0_) | copy-start | bytes 2359300

commit v12 on v11

--- a/solution.py
+++ b/solution.py
@@ -47,7 +47,8 @@
 def add_walkers(blocks, sel_ref, acc_ref, slots, width):
     sel = sel_ref[...]
     terms = []
-    for g_ref, k in blocks:
+    for g_ref, k, copy in blocks:
+        copy.wait()
         g_re = g_ref[k, 0]
         g_im = g_ref[k, 1]
         y = jnp.dot(sel, jnp.concatenate([g_re, g_im], axis=1), preferred_element_type=F32).astype(BF16)
@@ -71,11 +72,16 @@
     groups = len(counts)
     g_refs = refs[:groups]
     refs = refs[groups:]
+    refs, (g_buf, g_sem) = refs[:-2], refs[-2:]
     if has_prior:
         (ti_ref, ph_ref, far_ref, slot_ref, cj_ref, prior_hbm, out_ref,
          acc_ref, sel_ref, prior_ref, sem) = refs
     else:
         ti_ref, ph_ref, far_ref, slot_ref, cj_ref, out_ref, acc_ref, sel_ref = refs
+    places = [(g_ref, k) for g_ref, count in zip(g_refs, counts) for k in range(count)]
+    copies = [
+        pltpu.make_async_copy(g_ref.at[k], g_buf.at[n], g_sem.at[n]) for n, (g_ref, k) in enumerate(places)
+    ]
     w = pl.program_id(0)
     last = pl.num_programs(0) - 1
     nt = 2 * slots
@@ -94,6 +100,8 @@
 
     @pl.when(w == 0)
     def _():
+        for copy in copies:
+            copy.start()
         acc_ref[...] = jnp.zeros(acc_ref.shape, F32)
         if has_prior:
             pltpu.make_async_copy(prior_hbm, prior_ref, sem).start()
@@ -101,7 +109,7 @@
         for t in range(nt):
             sel_ref[t * width:(t + 1) * width] = (cols[:, t:t + 1] == lanes).astype(BF16)
 
-    pending = [(g_ref, k) for g_ref, count in zip(g_refs, counts) for k in range(count)]
+    pending = [(g_buf, n, copy) for n, copy in enumerate(copies)]
     for start in range(0, len(pending), CHUNK):
         add_walkers(pending[start:start + CHUNK], sel_ref, acc_ref, slots, width)
 
@@ -158,7 +166,7 @@
     acc_shape = (2 * slots, 2, width, width)
     out_shape = (slots, 2, width, width) if final else acc_shape
     ti, ph, far, slot, cj = info
-    in_specs = [full(g.shape) for g in walkers] + [
+    in_specs = [pl.BlockSpec(memory_space=pl.ANY) for g in walkers] + [
         full(ti.shape),
         full(ph.shape),
         full(far.shape),
@@ -167,6 +175,7 @@
     ]
     scratch = [pltpu.VMEM(acc_shape, F32), pltpu.VMEM((2 * slots * width, width), BF16)]
     operands = list(walkers) + [ti, ph, far, slot, cj]
+    tail = [pltpu.VMEM((sum(counts), 2, width, width), BF16), pltpu.SemaphoreType.DMA((sum(counts),))]
     if has_prior:
         in_specs.append(pl.BlockSpec(memory_space=pl.ANY))
         scratch += [pltpu.VMEM(acc_shape, F32), pltpu.SemaphoreType.DMA(())]
@@ -181,7 +190,7 @@
         in_specs=in_specs,
         out_specs=full(out_shape),
         out_shape=jax.ShapeDtypeStruct(out_shape, F32),
-        scratch_shapes=scratch,
+        scratch_shapes=scratch + tail,
         compiler_params=pltpu.CompilerParams(dimension_semantics=("arbitrary",)),
     )(*operands)
 

time: 30.3 us -> 31.2 us (1.030)
  Pallas kernels: 15.4 us -> 16.9 us
  waiting for transfers between devices: 4.06 us -> 3.46 us
    pallas_call x3, Pallas kernels: 15.4 us -> 16.9 us  [accumulate(): pl.pallas_call(kernel, grid=(1,), cost_estimate=pl.CostEstimate(flops=flo...]
    ppermute x3, waiting for transfers between devices: 2.47 us -> 1.88 us  [local(): lax.ppermute(greens, 'blk', [(i, i ^ 2 * m) for i in range(blocks)])]
  transfers between devices with their start and end apart: 6 -> 6, of which waited for: 3 -> 3; matrix products, arithmetic and copies ran while one was open for 2% -> 2% of each run, Pallas kernels for 30% -> 33%
where the time goes in v12:
time: 31.2 us; the launch traced here: 31 us
  Pallas kernels  16.9 us (54%)
  starting transfers between devices  7.6 us (24%)
  waiting for transfers between devices  3.46 us (11%)
  local copies, waits for them, and re-layouts  2.1 us (7%)
  other arithmetic  0.79 us (3%)
    pallas_call x3, Pallas kernels, accumulate(): pl.pallas_call(kernel, grid=(1,), cost_estimate=pl.CostEstimate(flops=flo...  16.9 us
    ppermute x3, starting transfers between devices, local(): lax.ppermute(greens, 'blk', [(i, i ^ 2 * m) for i in range(blocks)])  4.05 us
    ppermute x1, starting transfers between devices, passed_along(): lax.ppermute(value, axis, [(i, (i + by) % size) for i in range(size)])  3.02 us
    unnamed x12, local copies, waits for them, and re-layouts  2.1 us
    ppermute x3, waiting for transfers between devices, local(): lax.ppermute(greens, 'blk', [(i, i ^ 2 * m) for i in range(blocks)])  1.88 us
    ppermute x1, waiting for transfers between devices, passed_along(): lax.ppermute(value, axis, [(i, (i + by) % size) for i in range(size)])  1.58 us
    concatenate x1, other arithmetic, local(): jnp.concatenate([transfer_index, phase_index], axis=0)  0.71 us
  transfers between devices with their start and end apart: 6, of which 3 were waited for; matrix products, arithmetic and copies ran while one was open for 2% of the time, Pallas kernels for 33%

profile of v12, /device:TPU:0, one launch (start us, length us, event | category | flops | bytes accessed | tf_op | source)
XLA Modules:
  0.0 31.0 jit_solution(2875324541439287459)
XLA Ops:
  0.0 0.5 %collective-permute-start = (bf16[1,2,256,256]{3,2,1,0:T(8,128)(2,1)}, bf16[1,2,256,256]{3,2,1,0:T(8,128)(2,1)S(1)}, u32[]{:S(2)}, u32[]{:S(2)}) collective-permute-start(bf16[1,2,256,256]{3,2,1,0:T(8,128)(2,1)} %refs_0_.1), channel_id=1, source_target_pairs={{0,4},{4,0},{8,12},{12,8},{16,20},{20,16},{24,28},{28,24},{1,5},{5... | collective-permute-start | bytes 786440 | tf_op jit(solution)/shard_map/ppermute | solution.py:207
  0.5 2.5 %collective-permute-start.2 = (bf16[1,2,256,256]{3,2,1,0:T(8,128)(2,1)}, bf16[1,2,256,256]{3,2,1,0:T(8,128)(2,1)S(1)}, u32[]{:S(2)}, u32[]{:S(2)}) collective-permute-start(bf16[1,2,256,256]{3,2,1,0:T(8,128)(2,1)} %refs_0_.1), channel_id=1, source_target_pairs={{0,16},{4,20},{8,24},{12,28},{16,0},{20,4},{24,8},{28,12},{1,17},{... | collective-permute-start | bytes 786440 | tf_op jit(solution)/shard_map/ppermute | solution.py:208
  3.0 1.4 %collective-permute-start.4 = (bf16[1,2,256,256]{3,2,1,0:T(8,128)(2,1)}, bf16[1,2,256,256]{3,2,1,0:T(8,128)(2,1)S(1)}, u32[]{:S(2)}, u32[]{:S(2)}) collective-permute-start(bf16[1,2,256,256]{3,2,1,0:T(8,128)(2,1)} %refs_0_.1), channel_id=1, source_target_pairs={{0,24},{4,28},{8,16},{12,20},{16,8},{20,12},{24,0},{28,4},{1,25},{... | collective-permute-start | bytes 786440 | tf_op jit(solution)/shard_map/ppermute | solution.py:208
  4.4 0.1 collective-permute-start.3
  4.5 0.7 %pad_add_fusion = s32[4,256]{1,0:T(4,128)S(1)} fusion(s32[2,256]{1,0:T(2,128)} %refs_2_.3, s32[2,256]{1,0:T(2,128)} %refs_1_.1), kind=kLoop, calls=%fused_computation.1 | loop fusion | flops 1024 | bytes 8192 | tf_op jit(solution)/shard_map/concatenate | solution.py:209
  5.2 3.0 %collective-permute-start.1 = (s32[4,256]{1,0:T(4,128)S(1)}, s32[4,256]{1,0:T(4,128)S(1)}, u32[]{:S(2)}, u32[]{:S(2)}) collective-permute-start(s32[4,256]{1,0:T(4,128)S(1)} %pad_add_fusion), channel_id=1, source_target_pairs={{0,2},{1,3},{2,0},{3,1},{4,6},{5,7},{6,4},{7,5},{8,10},{9,11},{10,... | collective-permute-start | bytes 12296 | tf_op jit(solution)/shard_map/ppermute | solution.py:23
  8.2 1.6 %collective-permute-done.1.refs_4_.refs_5_.refs_3_ = s32[4,256]{1,0:T(4,128)S(1)} collective-permute-done((s32[4,256]{1,0:T(4,128)S(1)}, s32[4,256]{1,0:T(4,128)S(1)}, u32[]{:S(2)}, u32[]{:S(2)}) %collective-permute-start.1) | collective-permute-done | bytes 4128 | tf_op jit(solution)/shard_map/ppermute | solution.py:23
  9.8 0.0 copy-start.5
  9.8 0.0 collective-permute-done.refs_1_
  9.8 0.0 copy-start.4
  9.8 0.6 %copy-done.5 = s32[4,256]{1,0:T(4,128)} copy-done((s32[4,256]{1,0:T(4,128)}, s32[4,256]{1,0:T(4,128)S(1)}, u32[]{:S(2)}) %copy-start.5) | copy-done | bytes 4120
  10.4 0.1 copy-done.4
  10.5 4.6 %shard_map.55.refs_8_ = f32[4,2,256,256]{3,2,1,0:T(8,128)} custom-call(bf16[1,2,256,256]{3,2,1,0:T(8,128)(2,1)} %refs_0_.1, bf16[1,2,256,256]{3,2,1,0:T(8,128)(2,1)} %copy-done.4, s32[2,256]{1,0:T(2,128)} %refs_1_.1, s32[2,256]{1,0:T(2,128)} %refs_2_.3, s32[4,256]{1,0:T(4,128)} %copy-done.5, s32[2]{0:T(128)} %refs_4_.3, s32[1,256]{1,0:T(1,128)} %bitcast.1), custom_call_target="tpu_custom_call" | custom-call | flops 1073741824 | bytes 2621440 | tf_op jit(solution)/shard_map/pallas_call | solution.py:186
  15.2 0.6 %collective-permute-done.2.refs_0_ = bf16[1,2,256,256]{3,2,1,0:T(8,128)(2,1)S(1)} collective-permute-done((bf16[1,2,256,256]{3,2,1,0:T(8,128)(2,1)}, bf16[1,2,256,256]{3,2,1,0:T(8,128)(2,1)S(1)}, u32[]{:S(2)}, u32[]{:S(2)}) %collective-permute-start.2) | collective-permute-done | bytes 262176 | tf_op jit(solution)/shard_map/ppermute | solution.py:208
  15.8 0.0 copy-start
  15.8 0.0 collective-permute-done.4.refs_2_
  15.8 0.0 copy-start.1
  15.8 1.3 %collective-permute-done.3.refs_1_ = bf16[1,2,256,256]{3,2,1,0:T(8,128)(2,1)S(1)} collective-permute-done((bf16[1,2,256,256]{3,2,1,0:T(8,128)(2,1)}, bf16[1,2,256,256]{3,2,1,0:T(8,128)(2,1)S(1)}, u32[]{:S(2)}, u32[]{:S(2)}) %collective-permute-start.3) | collective-permute-done | bytes 262176 | tf_op jit(solution)/shard_map/ppermute | solution.py:208
  17.1 0.0 copy-start.2
  17.1 0.1 pad_maximum_fusion
  17.2 0.1 collective-permute-start.5
  17.2 0.0 copy-done
  17.2 0.0 copy-done.1
  17.3 0.5 %copy-done.2 = bf16[1,2,256,256]{3,2,1,0:T(8,128)(2,1)} copy-done((bf16[1,2,256,256]{3,2,1,0:T(8,128)(2,1)}, bf16[1,2,256,256]{3,2,1,0:T(8,128)(2,1)S(1)}, u32[]{:S(2)}) %copy-start.2) | copy-done | bytes 262168
  17.8 5.7 %shard_map.56.refs_6_ = f32[4,2,256,256]{3,2,1,0:T(8,128)} custom-call(bf16[1,2,256,256]{3,2,1,0:T(8,128)(2,1)} %copy-done, bf16[1,2,256,256]{3,2,1,0:T(8,128)(2,1)} %copy-done.2, bf16[1,2,256,256]{3,2,1,0:T(8,128)(2,1)} %copy-done.1, s32[2,256]{1,0:T(2,128)} %refs_1_.1, s32[2,256]{1,0:T(2,128)} %refs_2_.3, s32[4,256]{1,0:T(4,128)} %copy-done.5, s32[2]{0:T(128)} %refs_4_.3, ...), custom_call_target="tpu_custom_call" | custom-call | flops 1610612736 | bytes 4980736 | tf_op jit(solution)/shard_map/pallas_call | solution.py:186
  23.5 0.0 collective-permute-done.5.refs_0_
  23.5 0.0 copy-start.3
  23.5 0.9 %copy-done.3 = bf16[3,2,256,256]{3,2,1,0:T(8,128)(2,1)} copy-done((bf16[3,2,256,256]{3,2,1,0:T(8,128)(2,1)}, bf16[3,2,256,256]{3,2,1,0:T(8,128)(2,1)S(1)}, u32[]{:S(2)}) %copy-start.3) | copy-done | bytes 786456
  24.3 6.6 %shard_map.57 = f32[2,2,256,256]{3,2,1,0:T(8,128)} custom-call(bf16[3,2,256,256]{3,2,1,0:T(8,128)(2,1)} %copy-done.3, s32[2,256]{1,0:T(2,128)} %refs_1_.1, s32[2,256]{1,0:T(2,128)} %refs_2_.3, s32[4,256]{1,0:T(4,128)} %copy-done.5, s32[2]{0:T(128)} %refs_4_.3, s32[1,256]{1,0:T(1,128)} %bitcast.3, f32[4,2,256,256]{3,2,1,0:T(8,128)} %shard_map.56.refs_6_), custom_call_target="tpu_custom_call" | custom-call | flops 2147483648 | bytes 3932160 | tf_op jit(solution)/shard_map/pallas_call | solution.py:186
Async XLA Ops:
  0.0 9.8 %collective-permute-start = (bf16[1,2,256,256]{3,2,1,0:T(8,128)(2,1)}, bf16[1,2,256,256]{3,2,1,0:T(8,128)(2,1)S(1)}, u32[]{:S(2)}, u32[]{:S(2)}) collective-permute-start(bf16[1,2,256,256]{3,2,1,0:T(8,128)(2,1)} %refs_0_.1), channel_id=1, source_target_pairs={{0,4},{4,0},{8,12},{12,8},{16,20},{20,16},{24,28},{28,24},{1,5},{5... | collective-permute-start | bytes 786440 | tf_op jit(solution)/shard_map/ppermute | solution.py:207
  0.5 15.3 %collective-permute-start.2 = (bf16[1,2,256,256]{3,2,1,0:T(8,128)(2,1)}, bf16[1,2,256,256]{3,2,1,0:T(8,128)(2,1)S(1)}, u32[]{:S(2)}, u32[]{:S(2)}) collective-permute-start(bf16[1,2,256,256]{3,2,1,0:T(8,128)(2,1)} %refs_0_.1), channel_id=1, source_target_pairs={{0,16},{4,20},{8,24},{12,28},{16,0},{20,4},{24,8},{28,12},{1,17},{... | collective-permute-start | bytes 786440 | tf_op jit(solution)/shard_map/ppermute | solution.py:208
  3.0 12.8 %collective-permute-start.4 = (bf16[1,2,256,256]{3,2,1,0:T(8,128)(2,1)}, bf16[1,2,256,256]{3,2,1,0:T(8,128)(2,1)S(1)}, u32[]{:S(2)}, u32[]{:S(2)}) collective-permute-start(bf16[1,2,256,256]{3,2,1,0:T(8,128)(2,1)} %refs_0_.1), channel_id=1, source_target_pairs={{0,24},{4,28},{8,16},{12,20},{16,8},{20,12},{24,0},{28,4},{1,25},{... | collective-permute-start | bytes 786440 | tf_op jit(solution)/shard_map/ppermute | solution.py:208
  4.4 12.7 %collective-permute-start.3 = (bf16[1,2,256,256]{3,2,1,0:T(8,128)(2,1)}, bf16[1,2,256,256]{3,2,1,0:T(8,128)(2,1)S(1)}, u32[]{:S(2)}, u32[]{:S(2)}) collective-permute-start(bf16[1,2,256,256]{3,2,1,0:T(8,128)(2,1)} %refs_0_.1), channel_id=1, source_target_pairs={{0,8},{4,12},{8,0},{12,4},{16,24},{20,28},{24,16},{28,20},{1,9},{5... | collective-permute-start | bytes 786440 | tf_op jit(solution)/shard_map/ppermute | solution.py:208
  5.2 4.6 %collective-permute-start.1 = (s32[4,256]{1,0:T(4,128)S(1)}, s32[4,256]{1,0:T(4,128)S(1)}, u32[]{:S(2)}, u32[]{:S(2)}) collective-permute-start(s32[4,256]{1,0:T(4,128)S(1)} %pad_add_fusion), channel_id=1, source_target_pairs={{0,2},{1,3},{2,0},{3,1},{4,6},{5,7},{6,4},{7,5},{8,10},{9,11},{10,... | collective-permute-start | bytes 12296 | tf_op jit(solution)/shard_map/ppermute | solution.py:23
  9.8 0.6 %copy-start.5 = (s32[4,256]{1,0:T(4,128)}, s32[4,256]{1,0:T(4,128)S(1)}, u32[]{:S(2)}) copy-start(s32[4,256]{1,0:T(4,128)S(1)} %collective-permute-done.1.refs_4_.refs_5_.refs_3_) | copy-start | bytes 12292
  9.8 0.7 %copy-start.4 = (bf16[1,2,256,256]{3,2,1,0:T(8,128)(2,1)}, bf16[1,2,256,256]{3,2,1,0:T(8,128)(2,1)S(1)}, u32[]{:S(2)}) copy-start(bf16[1,2,256,256]{3,2,1,0:T(8,128)(2,1)S(1)} %collective-permute-done.refs_1_) | copy-start | bytes 786436
  15.8 1.5 %copy-start = (bf16[1,2,256,256]{3,2,1,0:T(8,128)(2,1)}, bf16[1,2,256,256]{3,2,1,0:T(8,128)(2,1)S(1)}, u32[]{:S(2)}) copy-start(bf16[1,2,256,256]{3,2,1,0:T(8,128)(2,1)S(1)} %collective-permute-done.2.refs_0_) | copy-start | bytes 786436
  15.8 1.5 %copy-start.1 = (bf16[1,2,256,256]{3,2,1,0:T(8,128)(2,1)}, bf16[1,2,256,256]{3,2,1,0:T(8,128)(2,1)S(1)}, u32[]{:S(2)}) copy-start(bf16[1,2,256,256]{3,2,1,0:T(8,128)(2,1)S(1)} %collective-permute-done.4.refs_2_) | copy-start | bytes 786436
  17.1 0.7 %copy-start.2 = (bf16[1,2,256,256]{3,2,1,0:T(8,128)(2,1)}, bf16[1,2,256,256]{3,2,1,0:T(8,128)(2,1)S(1)}, u32[]{:S(2)}) copy-start(bf16[1,2,256,256]{3,2,1,0:T(8,128)(2,1)S(1)} %collective-permute-done.3.refs_1_) | copy-start | bytes 786436
  17.2 6.3 %collective-permute-start.5 = (bf16[3,2,256,256]{3,2,1,0:T(8,128)(2,1)S(1)}, bf16[3,2,256,256]{3,2,1,0:T(8,128)(2,1)S(1)}, u32[]{:S(2)}, u32[]{:S(2)}) collective-permute-start(bf16[3,2,256,256]{3,2,1,0:T(8,128)(2,1)S(1)} %pad_maximum_fusion), channel_id=1, source_target_pairs={{0,4},{4,0},{8,12},{12,8},{16,20},{20,16},{24,28},{28,24},{1,5},{5... | collective-permute-start | bytes 2359304 | tf_op jit(solution)/shard_map/ppermute | solution.py:218
  23.5 0.9 %copy-start.3 = (bf16[3,2,256,256]{3,2,1,0:T(8,128)(2,1)}, bf16[3,2,256,256]{3,2,1,0:T(8,128)(2,1)S(1)}, u32[]{:S(2)}) copy-start(bf16[3,2,256,256]{3,2,1,0:T(8,128)(2,1)S(1)} %collective-permute-done.5.refs_0_) | copy-start | bytes 2359300

commit v13 on v11

--- a/solution.py
+++ b/solution.py
@@ -44,7 +44,7 @@
     return out
 
 
-def add_walkers(blocks, sel_ref, acc_ref, slots, width):
+def add_walkers(blocks, sel_ref, acc_ref, slots, width, finish=None):
     sel = sel_ref[...]
     terms = []
     for g_ref, k in blocks:
@@ -63,14 +63,19 @@
             m_im = m[:, width:]
             acc_re = acc_re + (gr * m_re - gi * m_im)
             acc_im = acc_im + (gr * m_im + gi * m_re)
-        acc_ref[t, 0] = acc_re
-        acc_ref[t, 1] = acc_im
+        if finish is None:
+            acc_ref[t, 0] = acc_re
+            acc_ref[t, 1] = acc_im
+        else:
+            finish(t, acc_re, acc_im)
 
 
 def accumulate_kernel(*refs, slots, width, scale, has_prior, final, counts):
     groups = len(counts)
     g_refs = refs[:groups]
     refs = refs[groups:]
+    if not final:
+        refs, out_sem = refs[:-1], refs[-1]
     if has_prior:
         (ti_ref, ph_ref, far_ref, slot_ref, cj_ref, prior_hbm, out_ref,
          acc_ref, sel_ref, prior_ref, sem) = refs
@@ -101,20 +106,34 @@
         for t in range(nt):
             sel_ref[t * width:(t + 1) * width] = (cols[:, t:t + 1] == lanes).astype(BF16)
 
+    out_copies = []
+
+    def finish(t, acc_re, acc_im):
+        if has_prior:
+            if t == 0:
+                pltpu.make_async_copy(prior_hbm, prior_ref, sem).wait()
+            acc_re = acc_re + prior_ref[t, 0]
+            acc_im = acc_im + prior_ref[t, 1]
+        acc_ref[t, 0] = acc_re
+        acc_ref[t, 1] = acc_im
+        copy = pltpu.make_async_copy(acc_ref.at[t], out_ref.at[t], out_sem.at[t])
+        copy.start()
+        out_copies.append(copy)
+
     pending = [(g_ref, k) for g_ref, count in zip(g_refs, counts) for k in range(count)]
-    for start in range(0, len(pending), CHUNK):
-        add_walkers(pending[start:start + CHUNK], sel_ref, acc_ref, slots, width)
+    starts = list(range(0, len(pending), CHUNK))
+    for start in starts:
+        hook = finish if (start == starts[-1] and not final) else None
+        add_walkers(pending[start:start + CHUNK], sel_ref, acc_ref, slots, width, hook)
+    for copy in out_copies:
+        copy.wait()
 
     @pl.when(w == last)
     def _():
+        if not final:
+            return
         if has_prior:
             pltpu.make_async_copy(prior_hbm, prior_ref, sem).wait()
-        if not final:
-            if has_prior:
-                out_ref[...] = acc_ref[...] + prior_ref[...]
-            else:
-                out_ref[...] = acc_ref[...]
-            return
         cols = columns()
         q = (cols[:, nt:nt + 1] == lanes).astype(BF16)
         far = far_ref[...]
@@ -179,9 +198,9 @@
         grid=(1,),
         cost_estimate=pl.CostEstimate(flops=flops, transcendentals=0, bytes_accessed=moved),
         in_specs=in_specs,
-        out_specs=full(out_shape),
+        out_specs=full(out_shape) if final else pl.BlockSpec(memory_space=pl.ANY),
         out_shape=jax.ShapeDtypeStruct(out_shape, F32),
-        scratch_shapes=scratch,
+        scratch_shapes=scratch + ([] if final else [pltpu.SemaphoreType.DMA((2 * slots,))]),
         compiler_params=pltpu.CompilerParams(dimension_semantics=("arbitrary",)),
     )(*operands)
 

time: 30.3 us -> 30.1 us (level)
  Pallas kernels: 15.4 us -> 15 us
    pallas_call x3, Pallas kernels: 15.4 us -> 15 us  [accumulate(): pl.pallas_call(kernel, grid=(1,), cost_estimate=pl.CostEstimate(flops=flo...]
  transfers between devices with their start and end apart: 6 -> 6, of which waited for: 3 -> 3; matrix products, arithmetic and copies ran while one was open for 2% -> 2% of each run, Pallas kernels for 30% -> 29%
where the time goes in v13:
time: 30.1 us; the launch traced here: 29.9 us
  Pallas kernels  15 us (50%)
  starting transfers between devices  7.6 us (25%)
  waiting for transfers between devices  4.36 us (14%)
  local copies, waits for them, and re-layouts  2.1 us (7%)
  other arithmetic  0.79 us (3%)
    pallas_call x3, Pallas kernels, accumulate(): pl.pallas_call(kernel, grid=(1,), cost_estimate=pl.CostEstimate(flops=flo...  15 us
    ppermute x3, starting transfers between devices, local(): lax.ppermute(greens, 'blk', [(i, i ^ 2 * m) for i in range(blocks)])  4.05 us
    ppermute x1, starting transfers between devices, passed_along(): lax.ppermute(value, axis, [(i, (i + by) % size) for i in range(size)])  3.02 us
    ppermute x3, waiting for transfers between devices, local(): lax.ppermute(greens, 'blk', [(i, i ^ 2 * m) for i in range(blocks)])  2.77 us
    unnamed x12, local copies, waits for them, and re-layouts  2.1 us
    ppermute x1, waiting for transfers between devices, passed_along(): lax.ppermute(value, axis, [(i, (i + by) % size) for i in range(size)])  1.58 us
    concatenate x1, other arithmetic, local(): jnp.concatenate([transfer_index, phase_index], axis=0)  0.71 us
  transfers between devices with their start and end apart: 6, of which 3 were waited for; matrix products, arithmetic and copies ran while one was open for 2% of the time, Pallas kernels for 29%

profile of v13, /device:TPU:0, one launch (start us, length us, event | category | flops | bytes accessed | tf_op | source)
XLA Modules:
  0.0 29.9 jit_solution(12016551940227349034)
XLA Ops:
  0.0 0.5 %collective-permute-start = (bf16[1,2,256,256]{3,2,1,0:T(8,128)(2,1)}, bf16[1,2,256,256]{3,2,1,0:T(8,128)(2,1)S(1)}, u32[]{:S(2)}, u32[]{:S(2)}) collective-permute-start(bf16[1,2,256,256]{3,2,1,0:T(8,128)(2,1)} %refs_0_.1), channel_id=1, source_target_pairs={{0,4},{4,0},{8,12},{12,8},{16,20},{20,16},{24,28},{28,24},{1,5},{5... | collective-permute-start | bytes 786440 | tf_op jit(solution)/shard_map/ppermute | solution.py:217
  0.5 2.5 %collective-permute-start.2 = (bf16[1,2,256,256]{3,2,1,0:T(8,128)(2,1)}, bf16[1,2,256,256]{3,2,1,0:T(8,128)(2,1)S(1)}, u32[]{:S(2)}, u32[]{:S(2)}) collective-permute-start(bf16[1,2,256,256]{3,2,1,0:T(8,128)(2,1)} %refs_0_.1), channel_id=1, source_target_pairs={{0,16},{4,20},{8,24},{12,28},{16,0},{20,4},{24,8},{28,12},{1,17},{... | collective-permute-start | bytes 786440 | tf_op jit(solution)/shard_map/ppermute | solution.py:218
  3.0 1.4 %collective-permute-start.4 = (bf16[1,2,256,256]{3,2,1,0:T(8,128)(2,1)}, bf16[1,2,256,256]{3,2,1,0:T(8,128)(2,1)S(1)}, u32[]{:S(2)}, u32[]{:S(2)}) collective-permute-start(bf16[1,2,256,256]{3,2,1,0:T(8,128)(2,1)} %refs_0_.1), channel_id=1, source_target_pairs={{0,24},{4,28},{8,16},{12,20},{16,8},{20,12},{24,0},{28,4},{1,25},{... | collective-permute-start | bytes 786440 | tf_op jit(solution)/shard_map/ppermute | solution.py:218
  4.4 0.1 collective-permute-start.3
  4.5 0.7 %pad_add_fusion = s32[4,256]{1,0:T(4,128)S(1)} fusion(s32[2,256]{1,0:T(2,128)} %refs_2_.3, s32[2,256]{1,0:T(2,128)} %refs_1_.1), kind=kLoop, calls=%fused_computation.1 | loop fusion | flops 1024 | bytes 8192 | tf_op jit(solution)/shard_map/concatenate | solution.py:219
  5.2 3.0 %collective-permute-start.1 = (s32[4,256]{1,0:T(4,128)S(1)}, s32[4,256]{1,0:T(4,128)S(1)}, u32[]{:S(2)}, u32[]{:S(2)}) collective-permute-start(s32[4,256]{1,0:T(4,128)S(1)} %pad_add_fusion), channel_id=1, source_target_pairs={{0,2},{1,3},{2,0},{3,1},{4,6},{5,7},{6,4},{7,5},{8,10},{9,11},{10,... | collective-permute-start | bytes 12296 | tf_op jit(solution)/shard_map/ppermute | solution.py:23
  8.2 1.6 %collective-permute-done.1.refs_4_.refs_5_.refs_3_ = s32[4,256]{1,0:T(4,128)S(1)} collective-permute-done((s32[4,256]{1,0:T(4,128)S(1)}, s32[4,256]{1,0:T(4,128)S(1)}, u32[]{:S(2)}, u32[]{:S(2)}) %collective-permute-start.1) | collective-permute-done | bytes 4128 | tf_op jit(solution)/shard_map/ppermute | solution.py:23
  9.8 0.0 copy-start.5
  9.8 0.0 collective-permute-done.refs_1_
  9.8 0.0 copy-start.4
  9.8 0.6 %copy-done.5 = s32[4,256]{1,0:T(4,128)} copy-done((s32[4,256]{1,0:T(4,128)}, s32[4,256]{1,0:T(4,128)S(1)}, u32[]{:S(2)}) %copy-start.5) | copy-done | bytes 4120
  10.4 0.1 copy-done.4
  10.5 3.7 %shard_map.55.refs_8_ = f32[4,2,256,256]{3,2,1,0:T(8,128)} custom-call(bf16[1,2,256,256]{3,2,1,0:T(8,128)(2,1)} %refs_0_.1, bf16[1,2,256,256]{3,2,1,0:T(8,128)(2,1)} %copy-done.4, s32[2,256]{1,0:T(2,128)} %refs_1_.1, s32[2,256]{1,0:T(2,128)} %refs_2_.3, s32[4,256]{1,0:T(4,128)} %copy-done.5, s32[2]{0:T(128)} %refs_4_.3, s32[1,256]{1,0:T(1,128)} %bitcast.1), custom_call_target="tpu_custom_call" | custom-call | flops 1073741824 | bytes 2621440 | tf_op jit(solution)/shard_map/pallas_call | solution.py:196
  14.3 1.5 %collective-permute-done.2.refs_0_ = bf16[1,2,256,256]{3,2,1,0:T(8,128)(2,1)S(1)} collective-permute-done((bf16[1,2,256,256]{3,2,1,0:T(8,128)(2,1)}, bf16[1,2,256,256]{3,2,1,0:T(8,128)(2,1)S(1)}, u32[]{:S(2)}, u32[]{:S(2)}) %collective-permute-start.2) | collective-permute-done | bytes 262176 | tf_op jit(solution)/shard_map/ppermute | solution.py:218
  15.8 0.0 copy-start
  15.8 0.0 collective-permute-done.4.refs_2_
  15.8 0.0 copy-start.1
  15.8 1.3 %collective-permute-done.3.refs_1_ = bf16[1,2,256,256]{3,2,1,0:T(8,128)(2,1)S(1)} collective-permute-done((bf16[1,2,256,256]{3,2,1,0:T(8,128)(2,1)}, bf16[1,2,256,256]{3,2,1,0:T(8,128)(2,1)S(1)}, u32[]{:S(2)}, u32[]{:S(2)}) %collective-permute-start.3) | collective-permute-done | bytes 262176 | tf_op jit(solution)/shard_map/ppermute | solution.py:218
  17.1 0.0 copy-start.2
  17.1 0.1 pad_maximum_fusion
  17.2 0.1 collective-permute-start.5
  17.2 0.0 copy-done
  17.2 0.0 copy-done.1
  17.3 0.5 %copy-done.2 = bf16[1,2,256,256]{3,2,1,0:T(8,128)(2,1)} copy-done((bf16[1,2,256,256]{3,2,1,0:T(8,128)(2,1)}, bf16[1,2,256,256]{3,2,1,0:T(8,128)(2,1)S(1)}, u32[]{:S(2)}) %copy-start.2) | copy-done | bytes 262168
  17.8 4.9 %shard_map.56.refs_6_ = f32[4,2,256,256]{3,2,1,0:T(8,128)} custom-call(bf16[1,2,256,256]{3,2,1,0:T(8,128)(2,1)} %copy-done, bf16[1,2,256,256]{3,2,1,0:T(8,128)(2,1)} %copy-done.2, bf16[1,2,256,256]{3,2,1,0:T(8,128)(2,1)} %copy-done.1, s32[2,256]{1,0:T(2,128)} %refs_1_.1, s32[2,256]{1,0:T(2,128)} %refs_2_.3, s32[4,256]{1,0:T(4,128)} %copy-done.5, s32[2]{0:T(128)} %refs_4_.3, ...), custom_call_target="tpu_custom_call" | custom-call | flops 1610612736 | bytes 4980736 | tf_op jit(solution)/shard_map/pallas_call | solution.py:196
  22.6 0.0 collective-permute-done.5.refs_0_
  22.6 0.0 copy-start.3
  22.6 0.9 %copy-done.3 = bf16[3,2,256,256]{3,2,1,0:T(8,128)(2,1)} copy-done((bf16[3,2,256,256]{3,2,1,0:T(8,128)(2,1)}, bf16[3,2,256,256]{3,2,1,0:T(8,128)(2,1)S(1)}, u32[]{:S(2)}) %copy-start.3) | copy-done | bytes 786456
  23.5 6.4 %shard_map.57 = f32[2,2,256,256]{3,2,1,0:T(8,128)} custom-call(bf16[3,2,256,256]{3,2,1,0:T(8,128)(2,1)} %copy-done.3, s32[2,256]{1,0:T(2,128)} %refs_1_.1, s32[2,256]{1,0:T(2,128)} %refs_2_.3, s32[4,256]{1,0:T(4,128)} %copy-done.5, s32[2]{0:T(128)} %refs_4_.3, s32[1,256]{1,0:T(1,128)} %bitcast.3, f32[4,2,256,256]{3,2,1,0:T(8,128)} %shard_map.56.refs_6_), custom_call_target="tpu_custom_call" | custom-call | flops 2147483648 | bytes 3932160 | tf_op jit(solution)/shard_map/pallas_call | solution.py:196
Async XLA Ops:
  0.0 9.8 %collective-permute-start = (bf16[1,2,256,256]{3,2,1,0:T(8,128)(2,1)}, bf16[1,2,256,256]{3,2,1,0:T(8,128)(2,1)S(1)}, u32[]{:S(2)}, u32[]{:S(2)}) collective-permute-start(bf16[1,2,256,256]{3,2,1,0:T(8,128)(2,1)} %refs_0_.1), channel_id=1, source_target_pairs={{0,4},{4,0},{8,12},{12,8},{16,20},{20,16},{24,28},{28,24},{1,5},{5... | collective-permute-start | bytes 786440 | tf_op jit(solution)/shard_map/ppermute | solution.py:217
  0.5 15.3 %collective-permute-start.2 = (bf16[1,2,256,256]{3,2,1,0:T(8,128)(2,1)}, bf16[1,2,256,256]{3,2,1,0:T(8,128)(2,1)S(1)}, u32[]{:S(2)}, u32[]{:S(2)}) collective-permute-start(bf16[1,2,256,256]{3,2,1,0:T(8,128)(2,1)} %refs_0_.1), channel_id=1, source_target_pairs={{0,16},{4,20},{8,24},{12,28},{16,0},{20,4},{24,8},{28,12},{1,17},{... | collective-permute-start | bytes 786440 | tf_op jit(solution)/shard_map/ppermute | solution.py:218
  3.0 12.8 %collective-permute-start.4 = (bf16[1,2,256,256]{3,2,1,0:T(8,128)(2,1)}, bf16[1,2,256,256]{3,2,1,0:T(8,128)(2,1)S(1)}, u32[]{:S(2)}, u32[]{:S(2)}) collective-permute-start(bf16[1,2,256,256]{3,2,1,0:T(8,128)(2,1)} %refs_0_.1), channel_id=1, source_target_pairs={{0,24},{4,28},{8,16},{12,20},{16,8},{20,12},{24,0},{28,4},{1,25},{... | collective-permute-start | bytes 786440 | tf_op jit(solution)/shard_map/ppermute | solution.py:218
  4.4 12.7 %collective-permute-start.3 = (bf16[1,2,256,256]{3,2,1,0:T(8,128)(2,1)}, bf16[1,2,256,256]{3,2,1,0:T(8,128)(2,1)S(1)}, u32[]{:S(2)}, u32[]{:S(2)}) collective-permute-start(bf16[1,2,256,256]{3,2,1,0:T(8,128)(2,1)} %refs_0_.1), channel_id=1, source_target_pairs={{0,8},{4,12},{8,0},{12,4},{16,24},{20,28},{24,16},{28,20},{1,9},{5... | collective-permute-start | bytes 786440 | tf_op jit(solution)/shard_map/ppermute | solution.py:218
  5.2 4.6 %collective-permute-start.1 = (s32[4,256]{1,0:T(4,128)S(1)}, s32[4,256]{1,0:T(4,128)S(1)}, u32[]{:S(2)}, u32[]{:S(2)}) collective-permute-start(s32[4,256]{1,0:T(4,128)S(1)} %pad_add_fusion), channel_id=1, source_target_pairs={{0,2},{1,3},{2,0},{3,1},{4,6},{5,7},{6,4},{7,5},{8,10},{9,11},{10,... | collective-permute-start | bytes 12296 | tf_op jit(solution)/shard_map/ppermute | solution.py:23
  9.8 0.6 %copy-start.5 = (s32[4,256]{1,0:T(4,128)}, s32[4,256]{1,0:T(4,128)S(1)}, u32[]{:S(2)}) copy-start(s32[4,256]{1,0:T(4,128)S(1)} %collective-permute-done.1.refs_4_.refs_5_.refs_3_) | copy-start | bytes 12292
  9.8 0.7 %copy-start.4 = (bf16[1,2,256,256]{3,2,1,0:T(8,128)(2,1)}, bf16[1,2,256,256]{3,2,1,0:T(8,128)(2,1)S(1)}, u32[]{:S(2)}) copy-start(bf16[1,2,256,256]{3,2,1,0:T(8,128)(2,1)S(1)} %collective-permute-done.refs_1_) | copy-start | bytes 786436
  15.8 1.5 %copy-start = (bf16[1,2,256,256]{3,2,1,0:T(8,128)(2,1)}, bf16[1,2,256,256]{3,2,1,0:T(8,128)(2,1)S(1)}, u32[]{:S(2)}) copy-start(bf16[1,2,256,256]{3,2,1,0:T(8,128)(2,1)S(1)} %collective-permute-done.2.refs_0_) | copy-start | bytes 786436
  15.8 1.5 %copy-start.1 = (bf16[1,2,256,256]{3,2,1,0:T(8,128)(2,1)}, bf16[1,2,256,256]{3,2,1,0:T(8,128)(2,1)S(1)}, u32[]{:S(2)}) copy-start(bf16[1,2,256,256]{3,2,1,0:T(8,128)(2,1)S(1)} %collective-permute-done.4.refs_2_) | copy-start | bytes 786436
  17.1 0.7 %copy-start.2 = (bf16[1,2,256,256]{3,2,1,0:T(8,128)(2,1)}, bf16[1,2,256,256]{3,2,1,0:T(8,128)(2,1)S(1)}, u32[]{:S(2)}) copy-start(bf16[1,2,256,256]{3,2,1,0:T(8,128)(2,1)S(1)} %collective-permute-done.3.refs_1_) | copy-start | bytes 786436
  17.2 5.5 %collective-permute-start.5 = (bf16[3,2,256,256]{3,2,1,0:T(8,128)(2,1)S(1)}, bf16[3,2,256,256]{3,2,1,0:T(8,128)(2,1)S(1)}, u32[]{:S(2)}, u32[]{:S(2)}) collective-permute-start(bf16[3,2,256,256]{3,2,1,0:T(8,128)(2,1)S(1)} %pad_maximum_fusion), channel_id=1, source_target_pairs={{0,4},{4,0},{8,12},{12,8},{16,20},{20,16},{24,28},{28,24},{1,5},{5... | collective-permute-start | bytes 2359304 | tf_op jit(solution)/shard_map/ppermute | solution.py:228
  22.6 0.9 %copy-start.3 = (bf16[3,2,256,256]{3,2,1,0:T(8,128)(2,1)}, bf16[3,2,256,256]{3,2,1,0:T(8,128)(2,1)S(1)}, u32[]{:S(2)}) copy-start(bf16[3,2,256,256]{3,2,1,0:T(8,128)(2,1)S(1)} %collective-permute-done.5.refs_0_) | copy-start | bytes 2359300

commit v14 on v13

--- a/solution.py
+++ b/solution.py
@@ -74,7 +74,9 @@
     groups = len(counts)
     g_refs = refs[:groups]
     refs = refs[groups:]
-    if not final:
+    if final:
+        refs, out_buf, out_sem = refs[:-2], refs[-2], refs[-1]
+    else:
         refs, out_sem = refs[:-1], refs[-1]
     if has_prior:
         (ti_ref, ph_ref, far_ref, slot_ref, cj_ref, prior_hbm, out_ref,
@@ -136,6 +138,7 @@
             pltpu.make_async_copy(prior_hbm, prior_ref, sem).wait()
         cols = columns()
         q = (cols[:, nt:nt + 1] == lanes).astype(BF16)
+        sent = []
         far = far_ref[...]
         partner = [jnp.where(slot_ref[s] == 0, far[2:3], far[3:4]) for s in range(slots)]
         partner = jnp.concatenate(partner + [jnp.zeros((8 - slots, width), jnp.int32)], axis=0)
@@ -151,16 +154,21 @@
                 if permute:
                     t_re = conj_permuted(q, t_re)
                     t_im = -conj_permuted(q, t_im)
-                ca = trig_cols[:, t:t + 1]
-                sa = trig_cols[:, nt + t:nt + t + 1]
+                ca = trig_cols[:, t:t + 1] * scale
+                sa = trig_cols[:, nt + t:nt + t + 1] * scale
                 cb = trig[t:t + 1]
                 sb = trig[nt + t:nt + t + 1]
                 rot_re = ca * cb + sa * sb
                 rot_im = sa * cb - ca * sb
                 parts.append((rot_re * t_re - rot_im * t_im, rot_re * t_im + rot_im * t_re))
             (own_re, own_im), (mir_re, mir_im) = parts
-            out_ref[s, 0] = (own_re + mir_re) * scale
-            out_ref[s, 1] = (own_im + mir_im) * scale
+            out_buf[s, 0] = own_re + mir_re
+            out_buf[s, 1] = own_im + mir_im
+            copy = pltpu.make_async_copy(out_buf.at[s], out_ref.at[s], out_sem.at[s])
+            copy.start()
+            sent.append(copy)
+        for copy in sent:
+            copy.wait()
 
 
 def walker_spec(width, offset, count):
@@ -198,9 +206,13 @@
         grid=(1,),
         cost_estimate=pl.CostEstimate(flops=flops, transcendentals=0, bytes_accessed=moved),
         in_specs=in_specs,
-        out_specs=full(out_shape) if final else pl.BlockSpec(memory_space=pl.ANY),
+        out_specs=pl.BlockSpec(memory_space=pl.ANY),
         out_shape=jax.ShapeDtypeStruct(out_shape, F32),
-        scratch_shapes=scratch + ([] if final else [pltpu.SemaphoreType.DMA((2 * slots,))]),
+        scratch_shapes=scratch + (
+            [pltpu.VMEM(out_shape, F32), pltpu.SemaphoreType.DMA((slots,))]
+            if final
+            else [pltpu.SemaphoreType.DMA((2 * slots,))]
+        ),
         compiler_params=pltpu.CompilerParams(dimension_semantics=("arbitrary",)),
     )(*operands)
 

time: 30.1 us -> 29.9 us (level)
  no operation moved by 1% of the time
where the time goes in v14:
time: 29.9 us; the launch traced here: 29.7 us
  Pallas kernels  14.8 us (49%)
  starting transfers between devices  7.6 us (25%)
  waiting for transfers between devices  4.36 us (15%)
  local copies, waits for them, and re-layouts  2.1 us (7%)
  other arithmetic  0.79 us (3%)
    pallas_call x3, Pallas kernels, accumulate(): pl.pallas_call(kernel, grid=(1,), cost_estimate=pl.CostEstimate(flops=flo...  14.8 us
    ppermute x3, starting transfers between devices, local(): lax.ppermute(greens, 'blk', [(i, i ^ 2 * m) for i in range(blocks)])  4.05 us
    ppermute x1, starting transfers between devices, passed_along(): lax.ppermute(value, axis, [(i, (i + by) % size) for i in range(size)])  3.02 us
    ppermute x3, waiting for transfers between devices, local(): lax.ppermute(greens, 'blk', [(i, i ^ 2 * m) for i in range(blocks)])  2.77 us
    unnamed x12, local copies, waits for them, and re-layouts  2.1 us
    ppermute x1, waiting for transfers between devices, passed_along(): lax.ppermute(value, axis, [(i, (i + by) % size) for i in range(size)])  1.58 us
    concatenate x1, other arithmetic, local(): jnp.concatenate([transfer_index, phase_index], axis=0)  0.71 us
  transfers between devices with their start and end apart: 6, of which 3 were waited for; matrix products, arithmetic and copies ran while one was open for 2% of the time, Pallas kernels for 29%

profile of v14, /device:TPU:0, one launch (start us, length us, event | category | flops | bytes accessed | tf_op | source)
XLA Modules:
  0.0 29.7 jit_solution(4380189220310623901)
XLA Ops:
  0.0 0.5 %collective-permute-start = (bf16[1,2,256,256]{3,2,1,0:T(8,128)(2,1)}, bf16[1,2,256,256]{3,2,1,0:T(8,128)(2,1)S(1)}, u32[]{:S(2)}, u32[]{:S(2)}) collective-permute-start(bf16[1,2,256,256]{3,2,1,0:T(8,128)(2,1)} %refs_0_.1), channel_id=1, source_target_pairs={{0,4},{4,0},{8,12},{12,8},{16,20},{20,16},{24,28},{28,24},{1,5},{5... | collective-permute-start | bytes 786440 | tf_op jit(solution)/shard_map/ppermute | solution.py:229
  0.5 2.5 %collective-permute-start.2 = (bf16[1,2,256,256]{3,2,1,0:T(8,128)(2,1)}, bf16[1,2,256,256]{3,2,1,0:T(8,128)(2,1)S(1)}, u32[]{:S(2)}, u32[]{:S(2)}) collective-permute-start(bf16[1,2,256,256]{3,2,1,0:T(8,128)(2,1)} %refs_0_.1), channel_id=1, source_target_pairs={{0,16},{4,20},{8,24},{12,28},{16,0},{20,4},{24,8},{28,12},{1,17},{... | collective-permute-start | bytes 786440 | tf_op jit(solution)/shard_map/ppermute | solution.py:230
  3.0 1.4 %collective-permute-start.4 = (bf16[1,2,256,256]{3,2,1,0:T(8,128)(2,1)}, bf16[1,2,256,256]{3,2,1,0:T(8,128)(2,1)S(1)}, u32[]{:S(2)}, u32[]{:S(2)}) collective-permute-start(bf16[1,2,256,256]{3,2,1,0:T(8,128)(2,1)} %refs_0_.1), channel_id=1, source_target_pairs={{0,24},{4,28},{8,16},{12,20},{16,8},{20,12},{24,0},{28,4},{1,25},{... | collective-permute-start | bytes 786440 | tf_op jit(solution)/shard_map/ppermute | solution.py:230
  4.4 0.1 collective-permute-start.3
  4.5 0.7 %pad_add_fusion = s32[4,256]{1,0:T(4,128)S(1)} fusion(s32[2,256]{1,0:T(2,128)} %refs_2_.3, s32[2,256]{1,0:T(2,128)} %refs_1_.1), kind=kLoop, calls=%fused_computation.1 | loop fusion | flops 1024 | bytes 8192 | tf_op jit(solution)/shard_map/concatenate | solution.py:231
  5.2 3.0 %collective-permute-start.1 = (s32[4,256]{1,0:T(4,128)S(1)}, s32[4,256]{1,0:T(4,128)S(1)}, u32[]{:S(2)}, u32[]{:S(2)}) collective-permute-start(s32[4,256]{1,0:T(4,128)S(1)} %pad_add_fusion), channel_id=1, source_target_pairs={{0,2},{1,3},{2,0},{3,1},{4,6},{5,7},{6,4},{7,5},{8,10},{9,11},{10,... | collective-permute-start | bytes 12296 | tf_op jit(solution)/shard_map/ppermute | solution.py:23
  8.2 1.6 %collective-permute-done.1.refs_4_.refs_5_.refs_3_ = s32[4,256]{1,0:T(4,128)S(1)} collective-permute-done((s32[4,256]{1,0:T(4,128)S(1)}, s32[4,256]{1,0:T(4,128)S(1)}, u32[]{:S(2)}, u32[]{:S(2)}) %collective-permute-start.1) | collective-permute-done | bytes 4128 | tf_op jit(solution)/shard_map/ppermute | solution.py:23
  9.8 0.0 copy-start.5
  9.8 0.0 collective-permute-done.refs_1_
  9.8 0.0 copy-start.4
  9.8 0.6 %copy-done.5 = s32[4,256]{1,0:T(4,128)} copy-done((s32[4,256]{1,0:T(4,128)}, s32[4,256]{1,0:T(4,128)S(1)}, u32[]{:S(2)}) %copy-start.5) | copy-done | bytes 4120
  10.4 0.1 copy-done.4
  10.5 3.7 %shard_map.55.refs_8_ = f32[4,2,256,256]{3,2,1,0:T(8,128)} custom-call(bf16[1,2,256,256]{3,2,1,0:T(8,128)(2,1)} %refs_0_.1, bf16[1,2,256,256]{3,2,1,0:T(8,128)(2,1)} %copy-done.4, s32[2,256]{1,0:T(2,128)} %refs_1_.1, s32[2,256]{1,0:T(2,128)} %refs_2_.3, s32[4,256]{1,0:T(4,128)} %copy-done.5, s32[2]{0:T(128)} %refs_4_.3, s32[1,256]{1,0:T(1,128)} %bitcast.1), custom_call_target="tpu_custom_call" | custom-call | flops 1073741824 | bytes 2621440 | tf_op jit(solution)/shard_map/pallas_call | solution.py:204
  14.3 1.5 %collective-permute-done.2.refs_0_ = bf16[1,2,256,256]{3,2,1,0:T(8,128)(2,1)S(1)} collective-permute-done((bf16[1,2,256,256]{3,2,1,0:T(8,128)(2,1)}, bf16[1,2,256,256]{3,2,1,0:T(8,128)(2,1)S(1)}, u32[]{:S(2)}, u32[]{:S(2)}) %collective-permute-start.2) | collective-permute-done | bytes 262176 | tf_op jit(solution)/shard_map/ppermute | solution.py:230
  15.8 0.0 copy-start
  15.8 0.0 collective-permute-done.4.refs_2_
  15.8 0.0 copy-start.1
  15.8 1.3 %collective-permute-done.3.refs_1_ = bf16[1,2,256,256]{3,2,1,0:T(8,128)(2,1)S(1)} collective-permute-done((bf16[1,2,256,256]{3,2,1,0:T(8,128)(2,1)}, bf16[1,2,256,256]{3,2,1,0:T(8,128)(2,1)S(1)}, u32[]{:S(2)}, u32[]{:S(2)}) %collective-permute-start.3) | collective-permute-done | bytes 262176 | tf_op jit(solution)/shard_map/ppermute | solution.py:230
  17.1 0.0 copy-start.2
  17.1 0.1 pad_maximum_fusion
  17.2 0.1 collective-permute-start.5
  17.2 0.0 copy-done
  17.2 0.0 copy-done.1
  17.3 0.5 %copy-done.2 = bf16[1,2,256,256]{3,2,1,0:T(8,128)(2,1)} copy-done((bf16[1,2,256,256]{3,2,1,0:T(8,128)(2,1)}, bf16[1,2,256,256]{3,2,1,0:T(8,128)(2,1)S(1)}, u32[]{:S(2)}) %copy-start.2) | copy-done | bytes 262168
  17.8 4.9 %shard_map.56.refs_6_ = f32[4,2,256,256]{3,2,1,0:T(8,128)} custom-call(bf16[1,2,256,256]{3,2,1,0:T(8,128)(2,1)} %copy-done, bf16[1,2,256,256]{3,2,1,0:T(8,128)(2,1)} %copy-done.2, bf16[1,2,256,256]{3,2,1,0:T(8,128)(2,1)} %copy-done.1, s32[2,256]{1,0:T(2,128)} %refs_1_.1, s32[2,256]{1,0:T(2,128)} %refs_2_.3, s32[4,256]{1,0:T(4,128)} %copy-done.5, s32[2]{0:T(128)} %refs_4_.3, ...), custom_call_target="tpu_custom_call" | custom-call | flops 1610612736 | bytes 4980736 | tf_op jit(solution)/shard_map/pallas_call | solution.py:204
  22.6 0.0 collective-permute-done.5.refs_0_
  22.6 0.0 copy-start.3
  22.6 0.9 %copy-done.3 = bf16[3,2,256,256]{3,2,1,0:T(8,128)(2,1)} copy-done((bf16[3,2,256,256]{3,2,1,0:T(8,128)(2,1)}, bf16[3,2,256,256]{3,2,1,0:T(8,128)(2,1)S(1)}, u32[]{:S(2)}) %copy-start.3) | copy-done | bytes 786456
  23.5 6.2 %shard_map.57 = f32[2,2,256,256]{3,2,1,0:T(8,128)} custom-call(bf16[3,2,256,256]{3,2,1,0:T(8,128)(2,1)} %copy-done.3, s32[2,256]{1,0:T(2,128)} %refs_1_.1, s32[2,256]{1,0:T(2,128)} %refs_2_.3, s32[4,256]{1,0:T(4,128)} %copy-done.5, s32[2]{0:T(128)} %refs_4_.3, s32[1,256]{1,0:T(1,128)} %bitcast.3, f32[4,2,256,256]{3,2,1,0:T(8,128)} %shard_map.56.refs_6_), custom_call_target="tpu_custom_call" | custom-call | flops 2147483648 | bytes 3932160 | tf_op jit(solution)/shard_map/pallas_call | solution.py:204
Async XLA Ops:
  0.0 9.8 %collective-permute-start = (bf16[1,2,256,256]{3,2,1,0:T(8,128)(2,1)}, bf16[1,2,256,256]{3,2,1,0:T(8,128)(2,1)S(1)}, u32[]{:S(2)}, u32[]{:S(2)}) collective-permute-start(bf16[1,2,256,256]{3,2,1,0:T(8,128)(2,1)} %refs_0_.1), channel_id=1, source_target_pairs={{0,4},{4,0},{8,12},{12,8},{16,20},{20,16},{24,28},{28,24},{1,5},{5... | collective-permute-start | bytes 786440 | tf_op jit(solution)/shard_map/ppermute | solution.py:229
  0.5 15.3 %collective-permute-start.2 = (bf16[1,2,256,256]{3,2,1,0:T(8,128)(2,1)}, bf16[1,2,256,256]{3,2,1,0:T(8,128)(2,1)S(1)}, u32[]{:S(2)}, u32[]{:S(2)}) collective-permute-start(bf16[1,2,256,256]{3,2,1,0:T(8,128)(2,1)} %refs_0_.1), channel_id=1, source_target_pairs={{0,16},{4,20},{8,24},{12,28},{16,0},{20,4},{24,8},{28,12},{1,17},{... | collective-permute-start | bytes 786440 | tf_op jit(solution)/shard_map/ppermute | solution.py:230
  3.0 12.8 %collective-permute-start.4 = (bf16[1,2,256,256]{3,2,1,0:T(8,128)(2,1)}, bf16[1,2,256,256]{3,2,1,0:T(8,128)(2,1)S(1)}, u32[]{:S(2)}, u32[]{:S(2)}) collective-permute-start(bf16[1,2,256,256]{3,2,1,0:T(8,128)(2,1)} %refs_0_.1), channel_id=1, source_target_pairs={{0,24},{4,28},{8,16},{12,20},{16,8},{20,12},{24,0},{28,4},{1,25},{... | collective-permute-start | bytes 786440 | tf_op jit(solution)/shard_map/ppermute | solution.py:230
  4.4 12.7 %collective-permute-start.3 = (bf16[1,2,256,256]{3,2,1,0:T(8,128)(2,1)}, bf16[1,2,256,256]{3,2,1,0:T(8,128)(2,1)S(1)}, u32[]{:S(2)}, u32[]{:S(2)}) collective-permute-start(bf16[1,2,256,256]{3,2,1,0:T(8,128)(2,1)} %refs_0_.1), channel_id=1, source_target_pairs={{0,8},{4,12},{8,0},{12,4},{16,24},{20,28},{24,16},{28,20},{1,9},{5... | collective-permute-start | bytes 786440 | tf_op jit(solution)/shard_map/ppermute | solution.py:230
  5.2 4.6 %collective-permute-start.1 = (s32[4,256]{1,0:T(4,128)S(1)}, s32[4,256]{1,0:T(4,128)S(1)}, u32[]{:S(2)}, u32[]{:S(2)}) collective-permute-start(s32[4,256]{1,0:T(4,128)S(1)} %pad_add_fusion), channel_id=1, source_target_pairs={{0,2},{1,3},{2,0},{3,1},{4,6},{5,7},{6,4},{7,5},{8,10},{9,11},{10,... | collective-permute-start | bytes 12296 | tf_op jit(solution)/shard_map/ppermute | solution.py:23
  9.8 0.6 %copy-start.5 = (s32[4,256]{1,0:T(4,128)}, s32[4,256]{1,0:T(4,128)S(1)}, u32[]{:S(2)}) copy-start(s32[4,256]{1,0:T(4,128)S(1)} %collective-permute-done.1.refs_4_.refs_5_.refs_3_) | copy-start | bytes 12292
  9.8 0.7 %copy-start.4 = (bf16[1,2,256,256]{3,2,1,0:T(8,128)(2,1)}, bf16[1,2,256,256]{3,2,1,0:T(8,128)(2,1)S(1)}, u32[]{:S(2)}) copy-start(bf16[1,2,256,256]{3,2,1,0:T(8,128)(2,1)S(1)} %collective-permute-done.refs_1_) | copy-start | bytes 786436
  15.8 1.5 %copy-start = (bf16[1,2,256,256]{3,2,1,0:T(8,128)(2,1)}, bf16[1,2,256,256]{3,2,1,0:T(8,128)(2,1)S(1)}, u32[]{:S(2)}) copy-start(bf16[1,2,256,256]{3,2,1,0:T(8,128)(2,1)S(1)} %collective-permute-done.2.refs_0_) | copy-start | bytes 786436
  15.8 1.5 %copy-start.1 = (bf16[1,2,256,256]{3,2,1,0:T(8,128)(2,1)}, bf16[1,2,256,256]{3,2,1,0:T(8,128)(2,1)S(1)}, u32[]{:S(2)}) copy-start(bf16[1,2,256,256]{3,2,1,0:T(8,128)(2,1)S(1)} %collective-permute-done.4.refs_2_) | copy-start | bytes 786436
  17.1 0.7 %copy-start.2 = (bf16[1,2,256,256]{3,2,1,0:T(8,128)(2,1)}, bf16[1,2,256,256]{3,2,1,0:T(8,128)(2,1)S(1)}, u32[]{:S(2)}) copy-start(bf16[1,2,256,256]{3,2,1,0:T(8,128)(2,1)S(1)} %collective-permute-done.3.refs_1_) | copy-start | bytes 786436
  17.2 5.5 %collective-permute-start.5 = (bf16[3,2,256,256]{3,2,1,0:T(8,128)(2,1)S(1)}, bf16[3,2,256,256]{3,2,1,0:T(8,128)(2,1)S(1)}, u32[]{:S(2)}, u32[]{:S(2)}) collective-permute-start(bf16[3,2,256,256]{3,2,1,0:T(8,128)(2,1)S(1)} %pad_maximum_fusion), channel_id=1, source_target_pairs={{0,4},{4,0},{8,12},{12,8},{16,20},{20,16},{24,28},{28,24},{1,5},{5... | collective-permute-start | bytes 2359304 | tf_op jit(solution)/shard_map/ppermute | solution.py:240
  22.6 0.9 %copy-start.3 = (bf16[3,2,256,256]{3,2,1,0:T(8,128)(2,1)}, bf16[3,2,256,256]{3,2,1,0:T(8,128)(2,1)S(1)}, u32[]{:S(2)}) copy-start(bf16[3,2,256,256]{3,2,1,0:T(8,128)(2,1)S(1)} %collective-permute-done.5.refs_0_) | copy-start | bytes 2359300

commit v15 on v14

--- a/solution.py
+++ b/solution.py
@@ -12,7 +12,7 @@
 F32 = jnp.float32
 BF16 = jnp.bfloat16
 NT = (((1,), (1,)), ((), ()))
-CHUNK = 3
+CHUNK = 2
 ROOT_HALF = math.sqrt(0.5)
 COSINES = (1.0, ROOT_HALF, 0.0, -ROOT_HALF, -1.0, -ROOT_HALF, 0.0, ROOT_HALF)
 SINES = (0.0, ROOT_HALF, 1.0, ROOT_HALF, 0.0, -ROOT_HALF, -1.0, -ROOT_HALF)

time: 29.9 us -> 29.7 us (level)
  no operation moved by 1% of the time
where the time goes in v15:
time: 29.7 us; the launch traced here: 29.5 us
  Pallas kernels  14.6 us (49%)
  starting transfers between devices  7.6 us (26%)
  waiting for transfers between devices  4.36 us (15%)
  local copies, waits for them, and re-layouts  2.1 us (7%)
  other arithmetic  0.79 us (3%)
    pallas_call x3, Pallas kernels, accumulate(): pl.pallas_call(kernel, grid=(1,), cost_estimate=pl.CostEstimate(flops=flo...  14.6 us
    ppermute x3, starting transfers between devices, local(): lax.ppermute(greens, 'blk', [(i, i ^ 2 * m) for i in range(blocks)])  4.05 us
    ppermute x1, starting transfers between devices, passed_along(): lax.ppermute(value, axis, [(i, (i + by) % size) for i in range(size)])  3.02 us
    ppermute x3, waiting for transfers between devices, local(): lax.ppermute(greens, 'blk', [(i, i ^ 2 * m) for i in range(blocks)])  2.77 us
    unnamed x12, local copies, waits for them, and re-layouts  2.1 us
    ppermute x1, waiting for transfers between devices, passed_along(): lax.ppermute(value, axis, [(i, (i + by) % size) for i in range(size)])  1.58 us
    concatenate x1, other arithmetic, local(): jnp.concatenate([transfer_index, phase_index], axis=0)  0.71 us
  transfers between devices with their start and end apart: 6, of which 3 were waited for; matrix products, arithmetic and copies ran while one was open for 2% of the time, Pallas kernels for 29%

profile of v15, /device:TPU:0, one launch (start us, length us, event | category | flops | bytes accessed | tf_op | source)
XLA Modules:
  0.0 29.5 jit_solution(1747791900134246078)
XLA Ops:
  0.0 0.5 %collective-permute-start = (bf16[1,2,256,256]{3,2,1,0:T(8,128)(2,1)}, bf16[1,2,256,256]{3,2,1,0:T(8,128)(2,1)S(1)}, u32[]{:S(2)}, u32[]{:S(2)}) collective-permute-start(bf16[1,2,256,256]{3,2,1,0:T(8,128)(2,1)} %refs_0_.1), channel_id=1, source_target_pairs={{0,4},{4,0},{8,12},{12,8},{16,20},{20,16},{24,28},{28,24},{1,5},{5... | collective-permute-start | bytes 786440 | tf_op jit(solution)/shard_map/ppermute | solution.py:229
  0.5 2.5 %collective-permute-start.2 = (bf16[1,2,256,256]{3,2,1,0:T(8,128)(2,1)}, bf16[1,2,256,256]{3,2,1,0:T(8,128)(2,1)S(1)}, u32[]{:S(2)}, u32[]{:S(2)}) collective-permute-start(bf16[1,2,256,256]{3,2,1,0:T(8,128)(2,1)} %refs_0_.1), channel_id=1, source_target_pairs={{0,16},{4,20},{8,24},{12,28},{16,0},{20,4},{24,8},{28,12},{1,17},{... | collective-permute-start | bytes 786440 | tf_op jit(solution)/shard_map/ppermute | solution.py:230
  3.0 1.4 %collective-permute-start.4 = (bf16[1,2,256,256]{3,2,1,0:T(8,128)(2,1)}, bf16[1,2,256,256]{3,2,1,0:T(8,128)(2,1)S(1)}, u32[]{:S(2)}, u32[]{:S(2)}) collective-permute-start(bf16[1,2,256,256]{3,2,1,0:T(8,128)(2,1)} %refs_0_.1), channel_id=1, source_target_pairs={{0,24},{4,28},{8,16},{12,20},{16,8},{20,12},{24,0},{28,4},{1,25},{... | collective-permute-start | bytes 786440 | tf_op jit(solution)/shard_map/ppermute | solution.py:230
  4.4 0.1 collective-permute-start.3
  4.5 0.7 %pad_add_fusion = s32[4,256]{1,0:T(4,128)S(1)} fusion(s32[2,256]{1,0:T(2,128)} %refs_2_.3, s32[2,256]{1,0:T(2,128)} %refs_1_.1), kind=kLoop, calls=%fused_computation.1 | loop fusion | flops 1024 | bytes 8192 | tf_op jit(solution)/shard_map/concatenate | solution.py:231
  5.2 3.0 %collective-permute-start.1 = (s32[4,256]{1,0:T(4,128)S(1)}, s32[4,256]{1,0:T(4,128)S(1)}, u32[]{:S(2)}, u32[]{:S(2)}) collective-permute-start(s32[4,256]{1,0:T(4,128)S(1)} %pad_add_fusion), channel_id=1, source_target_pairs={{0,2},{1,3},{2,0},{3,1},{4,6},{5,7},{6,4},{7,5},{8,10},{9,11},{10,... | collective-permute-start | bytes 12296 | tf_op jit(solution)/shard_map/ppermute | solution.py:23
  8.2 1.6 %collective-permute-done.1.refs_4_.refs_5_.refs_3_ = s32[4,256]{1,0:T(4,128)S(1)} collective-permute-done((s32[4,256]{1,0:T(4,128)S(1)}, s32[4,256]{1,0:T(4,128)S(1)}, u32[]{:S(2)}, u32[]{:S(2)}) %collective-permute-start.1) | collective-permute-done | bytes 4128 | tf_op jit(solution)/shard_map/ppermute | solution.py:23
  9.8 0.0 copy-start.5
  9.8 0.0 collective-permute-done.refs_1_
  9.8 0.0 copy-start.4
  9.8 0.6 %copy-done.5 = s32[4,256]{1,0:T(4,128)} copy-done((s32[4,256]{1,0:T(4,128)}, s32[4,256]{1,0:T(4,128)S(1)}, u32[]{:S(2)}) %copy-start.5) | copy-done | bytes 4120
  10.4 0.1 copy-done.4
  10.5 3.7 %shard_map.55.refs_8_ = f32[4,2,256,256]{3,2,1,0:T(8,128)} custom-call(bf16[1,2,256,256]{3,2,1,0:T(8,128)(2,1)} %refs_0_.1, bf16[1,2,256,256]{3,2,1,0:T(8,128)(2,1)} %copy-done.4, s32[2,256]{1,0:T(2,128)} %refs_1_.1, s32[2,256]{1,0:T(2,128)} %refs_2_.3, s32[4,256]{1,0:T(4,128)} %copy-done.5, s32[2]{0:T(128)} %refs_4_.3, s32[1,256]{1,0:T(1,128)} %bitcast.1), custom_call_target="tpu_custom_call" | custom-call | flops 1073741824 | bytes 2621440 | tf_op jit(solution)/shard_map/pallas_call | solution.py:204
  14.3 1.5 %collective-permute-done.2.refs_0_ = bf16[1,2,256,256]{3,2,1,0:T(8,128)(2,1)S(1)} collective-permute-done((bf16[1,2,256,256]{3,2,1,0:T(8,128)(2,1)}, bf16[1,2,256,256]{3,2,1,0:T(8,128)(2,1)S(1)}, u32[]{:S(2)}, u32[]{:S(2)}) %collective-permute-start.2) | collective-permute-done | bytes 262176 | tf_op jit(solution)/shard_map/ppermute | solution.py:230
  15.8 0.0 copy-start
  15.8 0.0 collective-permute-done.4.refs_2_
  15.8 0.0 copy-start.1
  15.8 1.3 %collective-permute-done.3.refs_1_ = bf16[1,2,256,256]{3,2,1,0:T(8,128)(2,1)S(1)} collective-permute-done((bf16[1,2,256,256]{3,2,1,0:T(8,128)(2,1)}, bf16[1,2,256,256]{3,2,1,0:T(8,128)(2,1)S(1)}, u32[]{:S(2)}, u32[]{:S(2)}) %collective-permute-start.3) | collective-permute-done | bytes 262176 | tf_op jit(solution)/shard_map/ppermute | solution.py:230
  17.1 0.0 copy-start.2
  17.1 0.1 pad_maximum_fusion
  17.2 0.1 collective-permute-start.5
  17.2 0.0 copy-done
  17.2 0.0 copy-done.1
  17.3 0.5 %copy-done.2 = bf16[1,2,256,256]{3,2,1,0:T(8,128)(2,1)} copy-done((bf16[1,2,256,256]{3,2,1,0:T(8,128)(2,1)}, bf16[1,2,256,256]{3,2,1,0:T(8,128)(2,1)S(1)}, u32[]{:S(2)}) %copy-start.2) | copy-done | bytes 262168
  17.8 4.8 %shard_map.56.refs_6_ = f32[4,2,256,256]{3,2,1,0:T(8,128)} custom-call(bf16[1,2,256,256]{3,2,1,0:T(8,128)(2,1)} %copy-done, bf16[1,2,256,256]{3,2,1,0:T(8,128)(2,1)} %copy-done.2, bf16[1,2,256,256]{3,2,1,0:T(8,128)(2,1)} %copy-done.1, s32[2,256]{1,0:T(2,128)} %refs_1_.1, s32[2,256]{1,0:T(2,128)} %refs_2_.3, s32[4,256]{1,0:T(4,128)} %copy-done.5, s32[2]{0:T(128)} %refs_4_.3, ...), custom_call_target="tpu_custom_call" | custom-call | flops 1610612736 | bytes 4980736 | tf_op jit(solution)/shard_map/pallas_call | solution.py:204
  22.6 0.0 collective-permute-done.5.refs_0_
  22.6 0.0 copy-start.3
  22.6 0.9 %copy-done.3 = bf16[3,2,256,256]{3,2,1,0:T(8,128)(2,1)} copy-done((bf16[3,2,256,256]{3,2,1,0:T(8,128)(2,1)}, bf16[3,2,256,256]{3,2,1,0:T(8,128)(2,1)S(1)}, u32[]{:S(2)}) %copy-start.3) | copy-done | bytes 786456
  23.5 6.0 %shard_map.57 = f32[2,2,256,256]{3,2,1,0:T(8,128)} custom-call(bf16[3,2,256,256]{3,2,1,0:T(8,128)(2,1)} %copy-done.3, s32[2,256]{1,0:T(2,128)} %refs_1_.1, s32[2,256]{1,0:T(2,128)} %refs_2_.3, s32[4,256]{1,0:T(4,128)} %copy-done.5, s32[2]{0:T(128)} %refs_4_.3, s32[1,256]{1,0:T(1,128)} %bitcast.3, f32[4,2,256,256]{3,2,1,0:T(8,128)} %shard_map.56.refs_6_), custom_call_target="tpu_custom_call" | custom-call | flops 2147483648 | bytes 3932160 | tf_op jit(solution)/shard_map/pallas_call | solution.py:204
Async XLA Ops:
  0.0 9.8 %collective-permute-start = (bf16[1,2,256,256]{3,2,1,0:T(8,128)(2,1)}, bf16[1,2,256,256]{3,2,1,0:T(8,128)(2,1)S(1)}, u32[]{:S(2)}, u32[]{:S(2)}) collective-permute-start(bf16[1,2,256,256]{3,2,1,0:T(8,128)(2,1)} %refs_0_.1), channel_id=1, source_target_pairs={{0,4},{4,0},{8,12},{12,8},{16,20},{20,16},{24,28},{28,24},{1,5},{5... | collective-permute-start | bytes 786440 | tf_op jit(solution)/shard_map/ppermute | solution.py:229
  0.5 15.3 %collective-permute-start.2 = (bf16[1,2,256,256]{3,2,1,0:T(8,128)(2,1)}, bf16[1,2,256,256]{3,2,1,0:T(8,128)(2,1)S(1)}, u32[]{:S(2)}, u32[]{:S(2)}) collective-permute-start(bf16[1,2,256,256]{3,2,1,0:T(8,128)(2,1)} %refs_0_.1), channel_id=1, source_target_pairs={{0,16},{4,20},{8,24},{12,28},{16,0},{20,4},{24,8},{28,12},{1,17},{... | collective-permute-start | bytes 786440 | tf_op jit(solution)/shard_map/ppermute | solution.py:230
  3.0 12.8 %collective-permute-start.4 = (bf16[1,2,256,256]{3,2,1,0:T(8,128)(2,1)}, bf16[1,2,256,256]{3,2,1,0:T(8,128)(2,1)S(1)}, u32[]{:S(2)}, u32[]{:S(2)}) collective-permute-start(bf16[1,2,256,256]{3,2,1,0:T(8,128)(2,1)} %refs_0_.1), channel_id=1, source_target_pairs={{0,24},{4,28},{8,16},{12,20},{16,8},{20,12},{24,0},{28,4},{1,25},{... | collective-permute-start | bytes 786440 | tf_op jit(solution)/shard_map/ppermute | solution.py:230
  4.4 12.7 %collective-permute-start.3 = (bf16[1,2,256,256]{3,2,1,0:T(8,128)(2,1)}, bf16[1,2,256,256]{3,2,1,0:T(8,128)(2,1)S(1)}, u32[]{:S(2)}, u32[]{:S(2)}) collective-permute-start(bf16[1,2,256,256]{3,2,1,0:T(8,128)(2,1)} %refs_0_.1), channel_id=1, source_target_pairs={{0,8},{4,12},{8,0},{12,4},{16,24},{20,28},{24,16},{28,20},{1,9},{5... | collective-permute-start | bytes 786440 | tf_op jit(solution)/shard_map/ppermute | solution.py:230
  5.2 4.6 %collective-permute-start.1 = (s32[4,256]{1,0:T(4,128)S(1)}, s32[4,256]{1,0:T(4,128)S(1)}, u32[]{:S(2)}, u32[]{:S(2)}) collective-permute-start(s32[4,256]{1,0:T(4,128)S(1)} %pad_add_fusion), channel_id=1, source_target_pairs={{0,2},{1,3},{2,0},{3,1},{4,6},{5,7},{6,4},{7,5},{8,10},{9,11},{10,... | collective-permute-start | bytes 12296 | tf_op jit(solution)/shard_map/ppermute | solution.py:23
  9.8 0.6 %copy-start.5 = (s32[4,256]{1,0:T(4,128)}, s32[4,256]{1,0:T(4,128)S(1)}, u32[]{:S(2)}) copy-start(s32[4,256]{1,0:T(4,128)S(1)} %collective-permute-done.1.refs_4_.refs_5_.refs_3_) | copy-start | bytes 12292
  9.8 0.7 %copy-start.4 = (bf16[1,2,256,256]{3,2,1,0:T(8,128)(2,1)}, bf16[1,2,256,256]{3,2,1,0:T(8,128)(2,1)S(1)}, u32[]{:S(2)}) copy-start(bf16[1,2,256,256]{3,2,1,0:T(8,128)(2,1)S(1)} %collective-permute-done.refs_1_) | copy-start | bytes 786436
  15.8 1.5 %copy-start = (bf16[1,2,256,256]{3,2,1,0:T(8,128)(2,1)}, bf16[1,2,256,256]{3,2,1,0:T(8,128)(2,1)S(1)}, u32[]{:S(2)}) copy-start(bf16[1,2,256,256]{3,2,1,0:T(8,128)(2,1)S(1)} %collective-permute-done.2.refs_0_) | copy-start | bytes 786436
  15.8 1.5 %copy-start.1 = (bf16[1,2,256,256]{3,2,1,0:T(8,128)(2,1)}, bf16[1,2,256,256]{3,2,1,0:T(8,128)(2,1)S(1)}, u32[]{:S(2)}) copy-start(bf16[1,2,256,256]{3,2,1,0:T(8,128)(2,1)S(1)} %collective-permute-done.4.refs_2_) | copy-start | bytes 786436
  17.1 0.7 %copy-start.2 = (bf16[1,2,256,256]{3,2,1,0:T(8,128)(2,1)}, bf16[1,2,256,256]{3,2,1,0:T(8,128)(2,1)S(1)}, u32[]{:S(2)}) copy-start(bf16[1,2,256,256]{3,2,1,0:T(8,128)(2,1)S(1)} %collective-permute-done.3.refs_1_) | copy-start | bytes 786436
  17.2 5.4 %collective-permute-start.5 = (bf16[3,2,256,256]{3,2,1,0:T(8,128)(2,1)S(1)}, bf16[3,2,256,256]{3,2,1,0:T(8,128)(2,1)S(1)}, u32[]{:S(2)}, u32[]{:S(2)}) collective-permute-start(bf16[3,2,256,256]{3,2,1,0:T(8,128)(2,1)S(1)} %pad_maximum_fusion), channel_id=1, source_target_pairs={{0,4},{4,0},{8,12},{12,8},{16,20},{20,16},{24,28},{28,24},{1,5},{5... | collective-permute-start | bytes 2359304 | tf_op jit(solution)/shard_map/ppermute | solution.py:240
  22.6 0.9 %copy-start.3 = (bf16[3,2,256,256]{3,2,1,0:T(8,128)(2,1)}, bf16[3,2,256,256]{3,2,1,0:T(8,128)(2,1)S(1)}, u32[]{:S(2)}) copy-start(bf16[3,2,256,256]{3,2,1,0:T(8,128)(2,1)S(1)} %collective-permute-done.5.refs_0_) | copy-start | bytes 2359300

commit v16 on v15

--- a/solution.py
+++ b/solution.py
@@ -12,7 +12,7 @@
 F32 = jnp.float32
 BF16 = jnp.bfloat16
 NT = (((1,), (1,)), ((), ()))
-CHUNK = 2
+CHUNK = 1
 ROOT_HALF = math.sqrt(0.5)
 COSINES = (1.0, ROOT_HALF, 0.0, -ROOT_HALF, -1.0, -ROOT_HALF, 0.0, ROOT_HALF)
 SINES = (0.0, ROOT_HALF, 1.0, ROOT_HALF, 0.0, -ROOT_HALF, -1.0, -ROOT_HALF)

time: 29.7 us -> 29.4 us (0.990)
  Pallas kernels: 14.6 us -> 14.3 us
where the time goes in v16:
time: 29.4 us; the launch traced here: 29.2 us
  Pallas kernels  14.3 us (49%)
  starting transfers between devices  7.6 us (26%)
  waiting for transfers between devices  4.28 us (15%)
  local copies, waits for them, and re-layouts  2.1 us (7%)
  other arithmetic  0.79 us (3%)
    pallas_call x3, Pallas kernels, accumulate(): pl.pallas_call(kernel, grid=(1,), cost_estimate=pl.CostEstimate(flops=flo...  14.3 us
    ppermute x3, starting transfers between devices, local(): lax.ppermute(greens, 'blk', [(i, i ^ 2 * m) for i in range(blocks)])  4.05 us
    ppermute x1, starting transfers between devices, passed_along(): lax.ppermute(value, axis, [(i, (i + by) % size) for i in range(size)])  3.02 us
    ppermute x3, waiting for transfers between devices, local(): lax.ppermute(greens, 'blk', [(i, i ^ 2 * m) for i in range(blocks)])  2.69 us
    unnamed x12, local copies, waits for them, and re-layouts  2.1 us
    ppermute x1, waiting for transfers between devices, passed_along(): lax.ppermute(value, axis, [(i, (i + by) % size) for i in range(size)])  1.58 us
    concatenate x1, other arithmetic, local(): jnp.concatenate([transfer_index, phase_index], axis=0)  0.71 us
  transfers between devices with their start and end apart: 6, of which 3 were waited for; matrix products, arithmetic and copies ran while one was open for 2% of the time, Pallas kernels for 29%

profile of v16, /device:TPU:0, one launch (start us, length us, event | category | flops | bytes accessed | tf_op | source)
XLA Modules:
  0.0 29.2 jit_solution(14871414891377946608)
XLA Ops:
  0.0 0.5 %collective-permute-start = (bf16[1,2,256,256]{3,2,1,0:T(8,128)(2,1)}, bf16[1,2,256,256]{3,2,1,0:T(8,128)(2,1)S(1)}, u32[]{:S(2)}, u32[]{:S(2)}) collective-permute-start(bf16[1,2,256,256]{3,2,1,0:T(8,128)(2,1)} %refs_0_.1), channel_id=1, source_target_pairs={{0,4},{4,0},{8,12},{12,8},{16,20},{20,16},{24,28},{28,24},{1,5},{5... | collective-permute-start | bytes 786440 | tf_op jit(solution)/shard_map/ppermute | solution.py:229
  0.5 2.5 %collective-permute-start.2 = (bf16[1,2,256,256]{3,2,1,0:T(8,128)(2,1)}, bf16[1,2,256,256]{3,2,1,0:T(8,128)(2,1)S(1)}, u32[]{:S(2)}, u32[]{:S(2)}) collective-permute-start(bf16[1,2,256,256]{3,2,1,0:T(8,128)(2,1)} %refs_0_.1), channel_id=1, source_target_pairs={{0,16},{4,20},{8,24},{12,28},{16,0},{20,4},{24,8},{28,12},{1,17},{... | collective-permute-start | bytes 786440 | tf_op jit(solution)/shard_map/ppermute | solution.py:230
  3.0 1.4 %collective-permute-start.4 = (bf16[1,2,256,256]{3,2,1,0:T(8,128)(2,1)}, bf16[1,2,256,256]{3,2,1,0:T(8,128)(2,1)S(1)}, u32[]{:S(2)}, u32[]{:S(2)}) collective-permute-start(bf16[1,2,256,256]{3,2,1,0:T(8,128)(2,1)} %refs_0_.1), channel_id=1, source_target_pairs={{0,24},{4,28},{8,16},{12,20},{16,8},{20,12},{24,0},{28,4},{1,25},{... | collective-permute-start | bytes 786440 | tf_op jit(solution)/shard_map/ppermute | solution.py:230
  4.4 0.1 collective-permute-start.3
  4.5 0.7 %pad_add_fusion = s32[4,256]{1,0:T(4,128)S(1)} fusion(s32[2,256]{1,0:T(2,128)} %refs_2_.3, s32[2,256]{1,0:T(2,128)} %refs_1_.1), kind=kLoop, calls=%fused_computation.1 | loop fusion | flops 1024 | bytes 8192 | tf_op jit(solution)/shard_map/concatenate | solution.py:231
  5.2 3.0 %collective-permute-start.1 = (s32[4,256]{1,0:T(4,128)S(1)}, s32[4,256]{1,0:T(4,128)S(1)}, u32[]{:S(2)}, u32[]{:S(2)}) collective-permute-start(s32[4,256]{1,0:T(4,128)S(1)} %pad_add_fusion), channel_id=1, source_target_pairs={{0,2},{1,3},{2,0},{3,1},{4,6},{5,7},{6,4},{7,5},{8,10},{9,11},{10,... | collective-permute-start | bytes 12296 | tf_op jit(solution)/shard_map/ppermute | solution.py:23
  8.2 1.6 %collective-permute-done.1.refs_4_.refs_5_.refs_3_ = s32[4,256]{1,0:T(4,128)S(1)} collective-permute-done((s32[4,256]{1,0:T(4,128)S(1)}, s32[4,256]{1,0:T(4,128)S(1)}, u32[]{:S(2)}, u32[]{:S(2)}) %collective-permute-start.1) | collective-permute-done | bytes 4128 | tf_op jit(solution)/shard_map/ppermute | solution.py:23
  9.8 0.0 copy-start.5
  9.8 0.0 collective-permute-done.refs_1_
  9.8 0.0 copy-start.4
  9.8 0.6 %copy-done.5 = s32[4,256]{1,0:T(4,128)} copy-done((s32[4,256]{1,0:T(4,128)}, s32[4,256]{1,0:T(4,128)S(1)}, u32[]{:S(2)}) %copy-start.5) | copy-done | bytes 4120
  10.4 0.1 copy-done.4
  10.5 3.8 %shard_map.55.refs_8_ = f32[4,2,256,256]{3,2,1,0:T(8,128)} custom-call(bf16[1,2,256,256]{3,2,1,0:T(8,128)(2,1)} %refs_0_.1, bf16[1,2,256,256]{3,2,1,0:T(8,128)(2,1)} %copy-done.4, s32[2,256]{1,0:T(2,128)} %refs_1_.1, s32[2,256]{1,0:T(2,128)} %refs_2_.3, s32[4,256]{1,0:T(4,128)} %copy-done.5, s32[2]{0:T(128)} %refs_4_.3, s32[1,256]{1,0:T(1,128)} %bitcast.1), custom_call_target="tpu_custom_call" | custom-call | flops 1073741824 | bytes 2621440 | tf_op jit(solution)/shard_map/pallas_call | solution.py:204
  14.4 1.4 %collective-permute-done.2.refs_0_ = bf16[1,2,256,256]{3,2,1,0:T(8,128)(2,1)S(1)} collective-permute-done((bf16[1,2,256,256]{3,2,1,0:T(8,128)(2,1)}, bf16[1,2,256,256]{3,2,1,0:T(8,128)(2,1)S(1)}, u32[]{:S(2)}, u32[]{:S(2)}) %collective-permute-start.2) | collective-permute-done | bytes 262176 | tf_op jit(solution)/shard_map/ppermute | solution.py:230
  15.8 0.0 copy-start
  15.8 0.0 collective-permute-done.4.refs_2_
  15.8 0.0 copy-start.1
  15.8 1.3 %collective-permute-done.3.refs_1_ = bf16[1,2,256,256]{3,2,1,0:T(8,128)(2,1)S(1)} collective-permute-done((bf16[1,2,256,256]{3,2,1,0:T(8,128)(2,1)}, bf16[1,2,256,256]{3,2,1,0:T(8,128)(2,1)S(1)}, u32[]{:S(2)}, u32[]{:S(2)}) %collective-permute-start.3) | collective-permute-done | bytes 262176 | tf_op jit(solution)/shard_map/ppermute | solution.py:230
  17.1 0.0 copy-start.2
  17.1 0.1 pad_maximum_fusion
  17.2 0.1 collective-permute-start.5
  17.2 0.0 copy-done
  17.2 0.0 copy-done.1
  17.3 0.5 %copy-done.2 = bf16[1,2,256,256]{3,2,1,0:T(8,128)(2,1)} copy-done((bf16[1,2,256,256]{3,2,1,0:T(8,128)(2,1)}, bf16[1,2,256,256]{3,2,1,0:T(8,128)(2,1)S(1)}, u32[]{:S(2)}) %copy-start.2) | copy-done | bytes 262168
  17.8 4.8 %shard_map.56.refs_6_ = f32[4,2,256,256]{3,2,1,0:T(8,128)} custom-call(bf16[1,2,256,256]{3,2,1,0:T(8,128)(2,1)} %copy-done, bf16[1,2,256,256]{3,2,1,0:T(8,128)(2,1)} %copy-done.2, bf16[1,2,256,256]{3,2,1,0:T(8,128)(2,1)} %copy-done.1, s32[2,256]{1,0:T(2,128)} %refs_1_.1, s32[2,256]{1,0:T(2,128)} %refs_2_.3, s32[4,256]{1,0:T(4,128)} %copy-done.5, s32[2]{0:T(128)} %refs_4_.3, ...), custom_call_target="tpu_custom_call" | custom-call | flops 1610612736 | bytes 4980736 | tf_op jit(solution)/shard_map/pallas_call | solution.py:204
  22.5 0.0 collective-permute-done.5.refs_0_
  22.5 0.0 copy-start.3
  22.6 0.9 %copy-done.3 = bf16[3,2,256,256]{3,2,1,0:T(8,128)(2,1)} copy-done((bf16[3,2,256,256]{3,2,1,0:T(8,128)(2,1)}, bf16[3,2,256,256]{3,2,1,0:T(8,128)(2,1)S(1)}, u32[]{:S(2)}) %copy-start.3) | copy-done | bytes 786456
  23.4 5.7 %shard_map.57 = f32[2,2,256,256]{3,2,1,0:T(8,128)} custom-call(bf16[3,2,256,256]{3,2,1,0:T(8,128)(2,1)} %copy-done.3, s32[2,256]{1,0:T(2,128)} %refs_1_.1, s32[2,256]{1,0:T(2,128)} %refs_2_.3, s32[4,256]{1,0:T(4,128)} %copy-done.5, s32[2]{0:T(128)} %refs_4_.3, s32[1,256]{1,0:T(1,128)} %bitcast.3, f32[4,2,256,256]{3,2,1,0:T(8,128)} %shard_map.56.refs_6_), custom_call_target="tpu_custom_call" | custom-call | flops 2147483648 | bytes 3932160 | tf_op jit(solution)/shard_map/pallas_call | solution.py:204
Async XLA Ops:
  0.0 9.8 %collective-permute-start = (bf16[1,2,256,256]{3,2,1,0:T(8,128)(2,1)}, bf16[1,2,256,256]{3,2,1,0:T(8,128)(2,1)S(1)}, u32[]{:S(2)}, u32[]{:S(2)}) collective-permute-start(bf16[1,2,256,256]{3,2,1,0:T(8,128)(2,1)} %refs_0_.1), channel_id=1, source_target_pairs={{0,4},{4,0},{8,12},{12,8},{16,20},{20,16},{24,28},{28,24},{1,5},{5... | collective-permute-start | bytes 786440 | tf_op jit(solution)/shard_map/ppermute | solution.py:229
  0.5 15.3 %collective-permute-start.2 = (bf16[1,2,256,256]{3,2,1,0:T(8,128)(2,1)}, bf16[1,2,256,256]{3,2,1,0:T(8,128)(2,1)S(1)}, u32[]{:S(2)}, u32[]{:S(2)}) collective-permute-start(bf16[1,2,256,256]{3,2,1,0:T(8,128)(2,1)} %refs_0_.1), channel_id=1, source_target_pairs={{0,16},{4,20},{8,24},{12,28},{16,0},{20,4},{24,8},{28,12},{1,17},{... | collective-permute-start | bytes 786440 | tf_op jit(solution)/shard_map/ppermute | solution.py:230
  3.0 12.8 %collective-permute-start.4 = (bf16[1,2,256,256]{3,2,1,0:T(8,128)(2,1)}, bf16[1,2,256,256]{3,2,1,0:T(8,128)(2,1)S(1)}, u32[]{:S(2)}, u32[]{:S(2)}) collective-permute-start(bf16[1,2,256,256]{3,2,1,0:T(8,128)(2,1)} %refs_0_.1), channel_id=1, source_target_pairs={{0,24},{4,28},{8,16},{12,20},{16,8},{20,12},{24,0},{28,4},{1,25},{... | collective-permute-start | bytes 786440 | tf_op jit(solution)/shard_map/ppermute | solution.py:230
  4.4 12.7 %collective-permute-start.3 = (bf16[1,2,256,256]{3,2,1,0:T(8,128)(2,1)}, bf16[1,2,256,256]{3,2,1,0:T(8,128)(2,1)S(1)}, u32[]{:S(2)}, u32[]{:S(2)}) collective-permute-start(bf16[1,2,256,256]{3,2,1,0:T(8,128)(2,1)} %refs_0_.1), channel_id=1, source_target_pairs={{0,8},{4,12},{8,0},{12,4},{16,24},{20,28},{24,16},{28,20},{1,9},{5... | collective-permute-start | bytes 786440 | tf_op jit(solution)/shard_map/ppermute | solution.py:230
  5.2 4.6 %collective-permute-start.1 = (s32[4,256]{1,0:T(4,128)S(1)}, s32[4,256]{1,0:T(4,128)S(1)}, u32[]{:S(2)}, u32[]{:S(2)}) collective-permute-start(s32[4,256]{1,0:T(4,128)S(1)} %pad_add_fusion), channel_id=1, source_target_pairs={{0,2},{1,3},{2,0},{3,1},{4,6},{5,7},{6,4},{7,5},{8,10},{9,11},{10,... | collective-permute-start | bytes 12296 | tf_op jit(solution)/shard_map/ppermute | solution.py:23
  9.8 0.6 %copy-start.5 = (s32[4,256]{1,0:T(4,128)}, s32[4,256]{1,0:T(4,128)S(1)}, u32[]{:S(2)}) copy-start(s32[4,256]{1,0:T(4,128)S(1)} %collective-permute-done.1.refs_4_.refs_5_.refs_3_) | copy-start | bytes 12292
  9.8 0.7 %copy-start.4 = (bf16[1,2,256,256]{3,2,1,0:T(8,128)(2,1)}, bf16[1,2,256,256]{3,2,1,0:T(8,128)(2,1)S(1)}, u32[]{:S(2)}) copy-start(bf16[1,2,256,256]{3,2,1,0:T(8,128)(2,1)S(1)} %collective-permute-done.refs_1_) | copy-start | bytes 786436
  15.8 1.5 %copy-start = (bf16[1,2,256,256]{3,2,1,0:T(8,128)(2,1)}, bf16[1,2,256,256]{3,2,1,0:T(8,128)(2,1)S(1)}, u32[]{:S(2)}) copy-start(bf16[1,2,256,256]{3,2,1,0:T(8,128)(2,1)S(1)} %collective-permute-done.2.refs_0_) | copy-start | bytes 786436
  15.8 1.5 %copy-start.1 = (bf16[1,2,256,256]{3,2,1,0:T(8,128)(2,1)}, bf16[1,2,256,256]{3,2,1,0:T(8,128)(2,1)S(1)}, u32[]{:S(2)}) copy-start(bf16[1,2,256,256]{3,2,1,0:T(8,128)(2,1)S(1)} %collective-permute-done.4.refs_2_) | copy-start | bytes 786436
  17.1 0.7 %copy-start.2 = (bf16[1,2,256,256]{3,2,1,0:T(8,128)(2,1)}, bf16[1,2,256,256]{3,2,1,0:T(8,128)(2,1)S(1)}, u32[]{:S(2)}) copy-start(bf16[1,2,256,256]{3,2,1,0:T(8,128)(2,1)S(1)} %collective-permute-done.3.refs_1_) | copy-start | bytes 786436
  17.2 5.4 %collective-permute-start.5 = (bf16[3,2,256,256]{3,2,1,0:T(8,128)(2,1)S(1)}, bf16[3,2,256,256]{3,2,1,0:T(8,128)(2,1)S(1)}, u32[]{:S(2)}, u32[]{:S(2)}) collective-permute-start(bf16[3,2,256,256]{3,2,1,0:T(8,128)(2,1)S(1)} %pad_maximum_fusion), channel_id=1, source_target_pairs={{0,4},{4,0},{8,12},{12,8},{16,20},{20,16},{24,28},{28,24},{1,5},{5... | collective-permute-start | bytes 2359304 | tf_op jit(solution)/shard_map/ppermute | solution.py:240
  22.5 0.9 %copy-start.3 = (bf16[3,2,256,256]{3,2,1,0:T(8,128)(2,1)}, bf16[3,2,256,256]{3,2,1,0:T(8,128)(2,1)S(1)}, u32[]{:S(2)}) copy-start(bf16[3,2,256,256]{3,2,1,0:T(8,128)(2,1)S(1)} %collective-permute-done.5.refs_0_) | copy-start | bytes 2359300

commit v17 on v16

--- a/solution.py
+++ b/solution.py
@@ -235,7 +235,7 @@
     if not fetched:
         return run([greens, sibling], prior=None, final=True)
     partial_sums = run([greens, sibling], prior=None, final=False)
-    partial_sums, fetched = lax.optimization_barrier((partial_sums, [fetched[1], fetched[0]] + fetched[2:]))
+    partial_sums, fetched = lax.optimization_barrier((partial_sums, [fetched[1]] + fetched[2:] + [fetched[0]]))
     near = jnp.concatenate(fetched, axis=0)
     forwarded = lax.ppermute(near, "blk", swap)
     partial_sums = run(fetched, prior=partial_sums, final=False)

time: 29.4 us -> 29.3 us (level)
  transfers between devices with their start and end apart: 6 -> 6, of which waited for: 3 -> 2; matrix products, arithmetic and copies ran while one was open for 2% -> 2% of each run, Pallas kernels for 29% -> 30%
where the time goes in v17:
time: 29.3 us; the launch traced here: 29.1 us
  Pallas kernels  14.3 us (49%)
  starting transfers between devices  7.6 us (26%)
  waiting for transfers between devices  4.15 us (14%)
  local copies, waits for them, and re-layouts  2.11 us (7%)
  other arithmetic  0.79 us (3%)
    pallas_call x3, Pallas kernels, accumulate(): pl.pallas_call(kernel, grid=(1,), cost_estimate=pl.CostEstimate(flops=flo...  14.3 us
    ppermute x3, starting transfers between devices, local(): lax.ppermute(greens, 'blk', [(i, i ^ 2 * m) for i in range(blocks)])  4.05 us
    ppermute x1, starting transfers between devices, passed_along(): lax.ppermute(value, axis, [(i, (i + by) % size) for i in range(size)])  3.02 us
    ppermute x3, waiting for transfers between devices, local(): lax.ppermute(greens, 'blk', [(i, i ^ 2 * m) for i in range(blocks)])  2.56 us
    unnamed x12, local copies, waits for them, and re-layouts  2.11 us
    ppermute x1, waiting for transfers between devices, passed_along(): lax.ppermute(value, axis, [(i, (i + by) % size) for i in range(size)])  1.58 us
    concatenate x1, other arithmetic, local(): jnp.concatenate([transfer_index, phase_index], axis=0)  0.71 us
  transfers between devices with their start and end apart: 6, of which 2 were waited for; matrix products, arithmetic and copies ran while one was open for 2% of the time, Pallas kernels for 30%

profile of v17, /device:TPU:0, one launch (start us, length us, event | category | flops | bytes accessed | tf_op | source)
XLA Modules:
  0.0 29.1 jit_solution(7363986491839339171)
XLA Ops:
  0.0 0.5 %collective-permute-start = (bf16[1,2,256,256]{3,2,1,0:T(8,128)(2,1)}, bf16[1,2,256,256]{3,2,1,0:T(8,128)(2,1)S(1)}, u32[]{:S(2)}, u32[]{:S(2)}) collective-permute-start(bf16[1,2,256,256]{3,2,1,0:T(8,128)(2,1)} %refs_0_.1), channel_id=1, source_target_pairs={{0,4},{4,0},{8,12},{12,8},{16,20},{20,16},{24,28},{28,24},{1,5},{5... | collective-permute-start | bytes 786440 | tf_op jit(solution)/shard_map/ppermute | solution.py:229
  0.5 2.5 %collective-permute-start.2 = (bf16[1,2,256,256]{3,2,1,0:T(8,128)(2,1)}, bf16[1,2,256,256]{3,2,1,0:T(8,128)(2,1)S(1)}, u32[]{:S(2)}, u32[]{:S(2)}) collective-permute-start(bf16[1,2,256,256]{3,2,1,0:T(8,128)(2,1)} %refs_0_.1), channel_id=1, source_target_pairs={{0,16},{4,20},{8,24},{12,28},{16,0},{20,4},{24,8},{28,12},{1,17},{... | collective-permute-start | bytes 786440 | tf_op jit(solution)/shard_map/ppermute | solution.py:230
  3.0 1.5 %collective-permute-start.4 = (bf16[1,2,256,256]{3,2,1,0:T(8,128)(2,1)}, bf16[1,2,256,256]{3,2,1,0:T(8,128)(2,1)S(1)}, u32[]{:S(2)}, u32[]{:S(2)}) collective-permute-start(bf16[1,2,256,256]{3,2,1,0:T(8,128)(2,1)} %refs_0_.1), channel_id=1, source_target_pairs={{0,8},{4,12},{8,0},{12,4},{16,24},{20,28},{24,16},{28,20},{1,9},{5... | collective-permute-start | bytes 786440 | tf_op jit(solution)/shard_map/ppermute | solution.py:230
  4.5 0.0 collective-permute-start.3
  4.5 0.7 %pad_add_fusion = s32[4,256]{1,0:T(4,128)S(1)} fusion(s32[2,256]{1,0:T(2,128)} %refs_2_.3, s32[2,256]{1,0:T(2,128)} %refs_1_.1), kind=kLoop, calls=%fused_computation.1 | loop fusion | flops 1024 | bytes 8192 | tf_op jit(solution)/shard_map/concatenate | solution.py:231
  5.2 3.0 %collective-permute-start.1 = (s32[4,256]{1,0:T(4,128)S(1)}, s32[4,256]{1,0:T(4,128)S(1)}, u32[]{:S(2)}, u32[]{:S(2)}) collective-permute-start(s32[4,256]{1,0:T(4,128)S(1)} %pad_add_fusion), channel_id=1, source_target_pairs={{0,2},{1,3},{2,0},{3,1},{4,6},{5,7},{6,4},{7,5},{8,10},{9,11},{10,... | collective-permute-start | bytes 12296 | tf_op jit(solution)/shard_map/ppermute | solution.py:23
  8.2 1.6 %collective-permute-done.1.refs_4_.refs_5_.refs_3_ = s32[4,256]{1,0:T(4,128)S(1)} collective-permute-done((s32[4,256]{1,0:T(4,128)S(1)}, s32[4,256]{1,0:T(4,128)S(1)}, u32[]{:S(2)}, u32[]{:S(2)}) %collective-permute-start.1) | collective-permute-done | bytes 4128 | tf_op jit(solution)/shard_map/ppermute | solution.py:23
  9.8 0.0 copy-start.5
  9.8 0.0 collective-permute-done.refs_1_
  9.8 0.0 copy-start.4
  9.8 0.6 %copy-done.5 = s32[4,256]{1,0:T(4,128)} copy-done((s32[4,256]{1,0:T(4,128)}, s32[4,256]{1,0:T(4,128)S(1)}, u32[]{:S(2)}) %copy-start.5) | copy-done | bytes 4120
  10.4 0.1 copy-done.4
  10.5 3.8 %shard_map.55.refs_8_ = f32[4,2,256,256]{3,2,1,0:T(8,128)} custom-call(bf16[1,2,256,256]{3,2,1,0:T(8,128)(2,1)} %refs_0_.1, bf16[1,2,256,256]{3,2,1,0:T(8,128)(2,1)} %copy-done.4, s32[2,256]{1,0:T(2,128)} %refs_1_.1, s32[2,256]{1,0:T(2,128)} %refs_2_.3, s32[4,256]{1,0:T(4,128)} %copy-done.5, s32[2]{0:T(128)} %refs_4_.3, s32[1,256]{1,0:T(1,128)} %bitcast.1), custom_call_target="tpu_custom_call" | custom-call | flops 1073741824 | bytes 2621440 | tf_op jit(solution)/shard_map/pallas_call | solution.py:204
  14.4 0.0 collective-permute-done.2.refs_0_
  14.4 0.0 copy-start
  14.4 0.0 collective-permute-done.4.refs_2_
  14.4 0.0 copy-start.1
  14.4 2.6 %collective-permute-done.3.refs_1_ = bf16[1,2,256,256]{3,2,1,0:T(8,128)(2,1)S(1)} collective-permute-done((bf16[1,2,256,256]{3,2,1,0:T(8,128)(2,1)}, bf16[1,2,256,256]{3,2,1,0:T(8,128)(2,1)S(1)}, u32[]{:S(2)}, u32[]{:S(2)}) %collective-permute-start.3) | collective-permute-done | bytes 262176 | tf_op jit(solution)/shard_map/ppermute | solution.py:230
  17.0 0.0 copy-start.2
  17.0 0.1 pad_maximum_fusion
  17.1 0.1 collective-permute-start.5
  17.1 0.0 copy-done
  17.1 0.0 copy-done.1
  17.2 0.5 %copy-done.2 = bf16[1,2,256,256]{3,2,1,0:T(8,128)(2,1)} copy-done((bf16[1,2,256,256]{3,2,1,0:T(8,128)(2,1)}, bf16[1,2,256,256]{3,2,1,0:T(8,128)(2,1)S(1)}, u32[]{:S(2)}) %copy-start.2) | copy-done | bytes 262168
  17.7 4.8 %shard_map.56.refs_6_ = f32[4,2,256,256]{3,2,1,0:T(8,128)} custom-call(bf16[1,2,256,256]{3,2,1,0:T(8,128)(2,1)} %copy-done, bf16[1,2,256,256]{3,2,1,0:T(8,128)(2,1)} %copy-done.2, bf16[1,2,256,256]{3,2,1,0:T(8,128)(2,1)} %copy-done.1, s32[2,256]{1,0:T(2,128)} %refs_1_.1, s32[2,256]{1,0:T(2,128)} %refs_2_.3, s32[4,256]{1,0:T(4,128)} %copy-done.5, s32[2]{0:T(128)} %refs_4_.3, ...), custom_call_target="tpu_custom_call" | custom-call | flops 1610612736 | bytes 4980736 | tf_op jit(solution)/shard_map/pallas_call | solution.py:204
  22.4 0.0 collective-permute-done.5.refs_0_
  22.4 0.0 copy-start.3
  22.5 0.9 %copy-done.3 = bf16[3,2,256,256]{3,2,1,0:T(8,128)(2,1)} copy-done((bf16[3,2,256,256]{3,2,1,0:T(8,128)(2,1)}, bf16[3,2,256,256]{3,2,1,0:T(8,128)(2,1)S(1)}, u32[]{:S(2)}) %copy-start.3) | copy-done | bytes 786456
  23.3 5.7 %shard_map.57 = f32[2,2,256,256]{3,2,1,0:T(8,128)} custom-call(bf16[3,2,256,256]{3,2,1,0:T(8,128)(2,1)} %copy-done.3, s32[2,256]{1,0:T(2,128)} %refs_1_.1, s32[2,256]{1,0:T(2,128)} %refs_2_.3, s32[4,256]{1,0:T(4,128)} %copy-done.5, s32[2]{0:T(128)} %refs_4_.3, s32[1,256]{1,0:T(1,128)} %bitcast.3, f32[4,2,256,256]{3,2,1,0:T(8,128)} %shard_map.56.refs_6_), custom_call_target="tpu_custom_call" | custom-call | flops 2147483648 | bytes 3932160 | tf_op jit(solution)/shard_map/pallas_call | solution.py:204
Async XLA Ops:
  0.0 9.8 %collective-permute-start = (bf16[1,2,256,256]{3,2,1,0:T(8,128)(2,1)}, bf16[1,2,256,256]{3,2,1,0:T(8,128)(2,1)S(1)}, u32[]{:S(2)}, u32[]{:S(2)}) collective-permute-start(bf16[1,2,256,256]{3,2,1,0:T(8,128)(2,1)} %refs_0_.1), channel_id=1, source_target_pairs={{0,4},{4,0},{8,12},{12,8},{16,20},{20,16},{24,28},{28,24},{1,5},{5... | collective-permute-start | bytes 786440 | tf_op jit(solution)/shard_map/ppermute | solution.py:229
  0.5 13.9 %collective-permute-start.2 = (bf16[1,2,256,256]{3,2,1,0:T(8,128)(2,1)}, bf16[1,2,256,256]{3,2,1,0:T(8,128)(2,1)S(1)}, u32[]{:S(2)}, u32[]{:S(2)}) collective-permute-start(bf16[1,2,256,256]{3,2,1,0:T(8,128)(2,1)} %refs_0_.1), channel_id=1, source_target_pairs={{0,16},{4,20},{8,24},{12,28},{16,0},{20,4},{24,8},{28,12},{1,17},{... | collective-permute-start | bytes 786440 | tf_op jit(solution)/shard_map/ppermute | solution.py:230
  3.0 11.4 %collective-permute-start.4 = (bf16[1,2,256,256]{3,2,1,0:T(8,128)(2,1)}, bf16[1,2,256,256]{3,2,1,0:T(8,128)(2,1)S(1)}, u32[]{:S(2)}, u32[]{:S(2)}) collective-permute-start(bf16[1,2,256,256]{3,2,1,0:T(8,128)(2,1)} %refs_0_.1), channel_id=1, source_target_pairs={{0,8},{4,12},{8,0},{12,4},{16,24},{20,28},{24,16},{28,20},{1,9},{5... | collective-permute-start | bytes 786440 | tf_op jit(solution)/shard_map/ppermute | solution.py:230
  4.5 12.5 %collective-permute-start.3 = (bf16[1,2,256,256]{3,2,1,0:T(8,128)(2,1)}, bf16[1,2,256,256]{3,2,1,0:T(8,128)(2,1)S(1)}, u32[]{:S(2)}, u32[]{:S(2)}) collective-permute-start(bf16[1,2,256,256]{3,2,1,0:T(8,128)(2,1)} %refs_0_.1), channel_id=1, source_target_pairs={{0,24},{4,28},{8,16},{12,20},{16,8},{20,12},{24,0},{28,4},{1,25},{... | collective-permute-start | bytes 786440 | tf_op jit(solution)/shard_map/ppermute | solution.py:230
  5.2 4.6 %collective-permute-start.1 = (s32[4,256]{1,0:T(4,128)S(1)}, s32[4,256]{1,0:T(4,128)S(1)}, u32[]{:S(2)}, u32[]{:S(2)}) collective-permute-start(s32[4,256]{1,0:T(4,128)S(1)} %pad_add_fusion), channel_id=1, source_target_pairs={{0,2},{1,3},{2,0},{3,1},{4,6},{5,7},{6,4},{7,5},{8,10},{9,11},{10,... | collective-permute-start | bytes 12296 | tf_op jit(solution)/shard_map/ppermute | solution.py:23
  9.8 0.6 %copy-start.5 = (s32[4,256]{1,0:T(4,128)}, s32[4,256]{1,0:T(4,128)S(1)}, u32[]{:S(2)}) copy-start(s32[4,256]{1,0:T(4,128)S(1)} %collective-permute-done.1.refs_4_.refs_5_.refs_3_) | copy-start | bytes 12292
  9.8 0.7 %copy-start.4 = (bf16[1,2,256,256]{3,2,1,0:T(8,128)(2,1)}, bf16[1,2,256,256]{3,2,1,0:T(8,128)(2,1)S(1)}, u32[]{:S(2)}) copy-start(bf16[1,2,256,256]{3,2,1,0:T(8,128)(2,1)S(1)} %collective-permute-done.refs_1_) | copy-start | bytes 786436
  14.4 2.8 %copy-start = (bf16[1,2,256,256]{3,2,1,0:T(8,128)(2,1)}, bf16[1,2,256,256]{3,2,1,0:T(8,128)(2,1)S(1)}, u32[]{:S(2)}) copy-start(bf16[1,2,256,256]{3,2,1,0:T(8,128)(2,1)S(1)} %collective-permute-done.2.refs_0_) | copy-start | bytes 786436
  14.4 2.7 %copy-start.1 = (bf16[1,2,256,256]{3,2,1,0:T(8,128)(2,1)}, bf16[1,2,256,256]{3,2,1,0:T(8,128)(2,1)S(1)}, u32[]{:S(2)}) copy-start(bf16[1,2,256,256]{3,2,1,0:T(8,128)(2,1)S(1)} %collective-permute-done.4.refs_2_) | copy-start | bytes 786436
  17.0 0.7 %copy-start.2 = (bf16[1,2,256,256]{3,2,1,0:T(8,128)(2,1)}, bf16[1,2,256,256]{3,2,1,0:T(8,128)(2,1)S(1)}, u32[]{:S(2)}) copy-start(bf16[1,2,256,256]{3,2,1,0:T(8,128)(2,1)S(1)} %collective-permute-done.3.refs_1_) | copy-start | bytes 786436
  17.1 5.4 %collective-permute-start.5 = (bf16[3,2,256,256]{3,2,1,0:T(8,128)(2,1)S(1)}, bf16[3,2,256,256]{3,2,1,0:T(8,128)(2,1)S(1)}, u32[]{:S(2)}, u32[]{:S(2)}) collective-permute-start(bf16[3,2,256,256]{3,2,1,0:T(8,128)(2,1)S(1)} %pad_maximum_fusion), channel_id=1, source_target_pairs={{0,4},{4,0},{8,12},{12,8},{16,20},{20,16},{24,28},{28,24},{1,5},{5... | collective-permute-start | bytes 2359304 | tf_op jit(solution)/shard_map/ppermute | solution.py:240
  22.4 0.9 %copy-start.3 = (bf16[3,2,256,256]{3,2,1,0:T(8,128)(2,1)}, bf16[3,2,256,256]{3,2,1,0:T(8,128)(2,1)S(1)}, u32[]{:S(2)}) copy-start(bf16[3,2,256,256]{3,2,1,0:T(8,128)(2,1)S(1)} %collective-permute-done.5.refs_0_) | copy-start | bytes 2359300

commit v18 on v16

--- a/solution.py
+++ b/solution.py
@@ -51,12 +51,14 @@
         g_re = g_ref[k, 0]
         g_im = g_ref[k, 1]
         y = jnp.dot(sel, jnp.concatenate([g_re, g_im], axis=1), preferred_element_type=F32).astype(BF16)
-        terms.append((g_re.astype(F32), g_im.astype(F32), y))
+        terms.append((g_ref, k, y))
     for t in range(2 * slots):
         lo, hi = t * width, (t + 1) * width
         acc_re = acc_ref[t, 0]
         acc_im = acc_ref[t, 1]
-        for gr, gi, y in terms:
+        for g_ref, k, y in terms:
+            gr = g_ref[k, 0].astype(F32)
+            gi = g_ref[k, 1].astype(F32)
             stacked = jnp.concatenate([y[lo:hi, :width], y[lo:hi, width:]], axis=0)
             m = lax.dot_general(sel[lo:hi], stacked, NT, preferred_element_type=F32)
             m_re = m[:, :width]

time: 29.4 us -> 29.6 us (level)
  no operation moved by 1% of the time
where the time goes in v18:
time: 29.6 us; the launch traced here: 29.4 us
  Pallas kernels  14.5 us (49%)
  starting transfers between devices  7.6 us (26%)
  waiting for transfers between devices  4.27 us (14%)
  local copies, waits for them, and re-layouts  2.1 us (7%)
  other arithmetic  0.79 us (3%)
    pallas_call x3, Pallas kernels, accumulate(): pl.pallas_call(kernel, grid=(1,), cost_estimate=pl.CostEstimate(flops=flo...  14.5 us
    ppermute x3, starting transfers between devices, local(): lax.ppermute(greens, 'blk', [(i, i ^ 2 * m) for i in range(blocks)])  4.05 us
    ppermute x1, starting transfers between devices, passed_along(): lax.ppermute(value, axis, [(i, (i + by) % size) for i in range(size)])  3.02 us
    ppermute x3, waiting for transfers between devices, local(): lax.ppermute(greens, 'blk', [(i, i ^ 2 * m) for i in range(blocks)])  2.68 us
    unnamed x12, local copies, waits for them, and re-layouts  2.1 us
    ppermute x1, waiting for transfers between devices, passed_along(): lax.ppermute(value, axis, [(i, (i + by) % size) for i in range(size)])  1.58 us
    concatenate x1, other arithmetic, local(): jnp.concatenate([transfer_index, phase_index], axis=0)  0.71 us
  transfers between devices with their start and end apart: 6, of which 3 were waited for; matrix products, arithmetic and copies ran while one was open for 2% of the time, Pallas kernels for 29%

profile of v18, /device:TPU:0, one launch (start us, length us, event | category | flops | bytes accessed | tf_op | source)
XLA Modules:
  0.0 29.4 jit_solution(14624073853280098960)
XLA Ops:
  0.0 0.5 %collective-permute-start = (bf16[1,2,256,256]{3,2,1,0:T(8,128)(2,1)}, bf16[1,2,256,256]{3,2,1,0:T(8,128)(2,1)S(1)}, u32[]{:S(2)}, u32[]{:S(2)}) collective-permute-start(bf16[1,2,256,256]{3,2,1,0:T(8,128)(2,1)} %refs_0_.1), channel_id=1, source_target_pairs={{0,4},{4,0},{8,12},{12,8},{16,20},{20,16},{24,28},{28,24},{1,5},{5... | collective-permute-start | bytes 786440 | tf_op jit(solution)/shard_map/ppermute | solution.py:231
  0.5 2.5 %collective-permute-start.2 = (bf16[1,2,256,256]{3,2,1,0:T(8,128)(2,1)}, bf16[1,2,256,256]{3,2,1,0:T(8,128)(2,1)S(1)}, u32[]{:S(2)}, u32[]{:S(2)}) collective-permute-start(bf16[1,2,256,256]{3,2,1,0:T(8,128)(2,1)} %refs_0_.1), channel_id=1, source_target_pairs={{0,16},{4,20},{8,24},{12,28},{16,0},{20,4},{24,8},{28,12},{1,17},{... | collective-permute-start | bytes 786440 | tf_op jit(solution)/shard_map/ppermute | solution.py:232
  3.0 1.4 %collective-permute-start.4 = (bf16[1,2,256,256]{3,2,1,0:T(8,128)(2,1)}, bf16[1,2,256,256]{3,2,1,0:T(8,128)(2,1)S(1)}, u32[]{:S(2)}, u32[]{:S(2)}) collective-permute-start(bf16[1,2,256,256]{3,2,1,0:T(8,128)(2,1)} %refs_0_.1), channel_id=1, source_target_pairs={{0,24},{4,28},{8,16},{12,20},{16,8},{20,12},{24,0},{28,4},{1,25},{... | collective-permute-start | bytes 786440 | tf_op jit(solution)/shard_map/ppermute | solution.py:232
  4.4 0.1 collective-permute-start.3
  4.5 0.7 %pad_add_fusion = s32[4,256]{1,0:T(4,128)S(1)} fusion(s32[2,256]{1,0:T(2,128)} %refs_2_.3, s32[2,256]{1,0:T(2,128)} %refs_1_.1), kind=kLoop, calls=%fused_computation.1 | loop fusion | flops 1024 | bytes 8192 | tf_op jit(solution)/shard_map/concatenate | solution.py:233
  5.2 3.0 %collective-permute-start.1 = (s32[4,256]{1,0:T(4,128)S(1)}, s32[4,256]{1,0:T(4,128)S(1)}, u32[]{:S(2)}, u32[]{:S(2)}) collective-permute-start(s32[4,256]{1,0:T(4,128)S(1)} %pad_add_fusion), channel_id=1, source_target_pairs={{0,2},{1,3},{2,0},{3,1},{4,6},{5,7},{6,4},{7,5},{8,10},{9,11},{10,... | collective-permute-start | bytes 12296 | tf_op jit(solution)/shard_map/ppermute | solution.py:23
  8.2 1.6 %collective-permute-done.1.refs_4_.refs_5_.refs_3_ = s32[4,256]{1,0:T(4,128)S(1)} collective-permute-done((s32[4,256]{1,0:T(4,128)S(1)}, s32[4,256]{1,0:T(4,128)S(1)}, u32[]{:S(2)}, u32[]{:S(2)}) %collective-permute-start.1) | collective-permute-done | bytes 4128 | tf_op jit(solution)/shard_map/ppermute | solution.py:23
  9.8 0.0 copy-start.5
  9.8 0.0 collective-permute-done.refs_1_
  9.8 0.0 copy-start.4
  9.8 0.6 %copy-done.5 = s32[4,256]{1,0:T(4,128)} copy-done((s32[4,256]{1,0:T(4,128)}, s32[4,256]{1,0:T(4,128)S(1)}, u32[]{:S(2)}) %copy-start.5) | copy-done | bytes 4120
  10.4 0.1 copy-done.4
  10.5 3.8 %shard_map.55.refs_8_ = f32[4,2,256,256]{3,2,1,0:T(8,128)} custom-call(bf16[1,2,256,256]{3,2,1,0:T(8,128)(2,1)} %refs_0_.1, bf16[1,2,256,256]{3,2,1,0:T(8,128)(2,1)} %copy-done.4, s32[2,256]{1,0:T(2,128)} %refs_1_.1, s32[2,256]{1,0:T(2,128)} %refs_2_.3, s32[4,256]{1,0:T(4,128)} %copy-done.5, s32[2]{0:T(128)} %refs_4_.3, s32[1,256]{1,0:T(1,128)} %bitcast.1), custom_call_target="tpu_custom_call" | custom-call | flops 1073741824 | bytes 2621440 | tf_op jit(solution)/shard_map/pallas_call | solution.py:206
  14.4 1.4 %collective-permute-done.2.refs_0_ = bf16[1,2,256,256]{3,2,1,0:T(8,128)(2,1)S(1)} collective-permute-done((bf16[1,2,256,256]{3,2,1,0:T(8,128)(2,1)}, bf16[1,2,256,256]{3,2,1,0:T(8,128)(2,1)S(1)}, u32[]{:S(2)}, u32[]{:S(2)}) %collective-permute-start.2) | collective-permute-done | bytes 262176 | tf_op jit(solution)/shard_map/ppermute | solution.py:232
  15.8 0.0 copy-start
  15.8 0.0 collective-permute-done.4.refs_2_
  15.8 0.0 copy-start.1
  15.8 1.3 %collective-permute-done.3.refs_1_ = bf16[1,2,256,256]{3,2,1,0:T(8,128)(2,1)S(1)} collective-permute-done((bf16[1,2,256,256]{3,2,1,0:T(8,128)(2,1)}, bf16[1,2,256,256]{3,2,1,0:T(8,128)(2,1)S(1)}, u32[]{:S(2)}, u32[]{:S(2)}) %collective-permute-start.3) | collective-permute-done | bytes 262176 | tf_op jit(solution)/shard_map/ppermute | solution.py:232
  17.1 0.0 copy-start.2
  17.1 0.1 pad_maximum_fusion
  17.2 0.1 collective-permute-start.5
  17.2 0.0 copy-done
  17.2 0.0 copy-done.1
  17.3 0.5 %copy-done.2 = bf16[1,2,256,256]{3,2,1,0:T(8,128)(2,1)} copy-done((bf16[1,2,256,256]{3,2,1,0:T(8,128)(2,1)}, bf16[1,2,256,256]{3,2,1,0:T(8,128)(2,1)S(1)}, u32[]{:S(2)}) %copy-start.2) | copy-done | bytes 262168
  17.8 4.8 %shard_map.56.refs_6_ = f32[4,2,256,256]{3,2,1,0:T(8,128)} custom-call(bf16[1,2,256,256]{3,2,1,0:T(8,128)(2,1)} %copy-done, bf16[1,2,256,256]{3,2,1,0:T(8,128)(2,1)} %copy-done.2, bf16[1,2,256,256]{3,2,1,0:T(8,128)(2,1)} %copy-done.1, s32[2,256]{1,0:T(2,128)} %refs_1_.1, s32[2,256]{1,0:T(2,128)} %refs_2_.3, s32[4,256]{1,0:T(4,128)} %copy-done.5, s32[2]{0:T(128)} %refs_4_.3, ...), custom_call_target="tpu_custom_call" | custom-call | flops 1610612736 | bytes 4980736 | tf_op jit(solution)/shard_map/pallas_call | solution.py:206
  22.6 0.0 collective-permute-done.5.refs_0_
  22.6 0.0 copy-start.3
  22.6 0.9 %copy-done.3 = bf16[3,2,256,256]{3,2,1,0:T(8,128)(2,1)} copy-done((bf16[3,2,256,256]{3,2,1,0:T(8,128)(2,1)}, bf16[3,2,256,256]{3,2,1,0:T(8,128)(2,1)S(1)}, u32[]{:S(2)}) %copy-start.3) | copy-done | bytes 786456
  23.5 5.9 %shard_map.57 = f32[2,2,256,256]{3,2,1,0:T(8,128)} custom-call(bf16[3,2,256,256]{3,2,1,0:T(8,128)(2,1)} %copy-done.3, s32[2,256]{1,0:T(2,128)} %refs_1_.1, s32[2,256]{1,0:T(2,128)} %refs_2_.3, s32[4,256]{1,0:T(4,128)} %copy-done.5, s32[2]{0:T(128)} %refs_4_.3, s32[1,256]{1,0:T(1,128)} %bitcast.3, f32[4,2,256,256]{3,2,1,0:T(8,128)} %shard_map.56.refs_6_), custom_call_target="tpu_custom_call" | custom-call | flops 2147483648 | bytes 3932160 | tf_op jit(solution)/shard_map/pallas_call | solution.py:206
Async XLA Ops:
  0.0 9.8 %collective-permute-start = (bf16[1,2,256,256]{3,2,1,0:T(8,128)(2,1)}, bf16[1,2,256,256]{3,2,1,0:T(8,128)(2,1)S(1)}, u32[]{:S(2)}, u32[]{:S(2)}) collective-permute-start(bf16[1,2,256,256]{3,2,1,0:T(8,128)(2,1)} %refs_0_.1), channel_id=1, source_target_pairs={{0,4},{4,0},{8,12},{12,8},{16,20},{20,16},{24,28},{28,24},{1,5},{5... | collective-permute-start | bytes 786440 | tf_op jit(solution)/shard_map/ppermute | solution.py:231
  0.5 15.3 %collective-permute-start.2 = (bf16[1,2,256,256]{3,2,1,0:T(8,128)(2,1)}, bf16[1,2,256,256]{3,2,1,0:T(8,128)(2,1)S(1)}, u32[]{:S(2)}, u32[]{:S(2)}) collective-permute-start(bf16[1,2,256,256]{3,2,1,0:T(8,128)(2,1)} %refs_0_.1), channel_id=1, source_target_pairs={{0,16},{4,20},{8,24},{12,28},{16,0},{20,4},{24,8},{28,12},{1,17},{... | collective-permute-start | bytes 786440 | tf_op jit(solution)/shard_map/ppermute | solution.py:232
  3.0 12.8 %collective-permute-start.4 = (bf16[1,2,256,256]{3,2,1,0:T(8,128)(2,1)}, bf16[1,2,256,256]{3,2,1,0:T(8,128)(2,1)S(1)}, u32[]{:S(2)}, u32[]{:S(2)}) collective-permute-start(bf16[1,2,256,256]{3,2,1,0:T(8,128)(2,1)} %refs_0_.1), channel_id=1, source_target_pairs={{0,24},{4,28},{8,16},{12,20},{16,8},{20,12},{24,0},{28,4},{1,25},{... | collective-permute-start | bytes 786440 | tf_op jit(solution)/shard_map/ppermute | solution.py:232
  4.4 12.7 %collective-permute-start.3 = (bf16[1,2,256,256]{3,2,1,0:T(8,128)(2,1)}, bf16[1,2,256,256]{3,2,1,0:T(8,128)(2,1)S(1)}, u32[]{:S(2)}, u32[]{:S(2)}) collective-permute-start(bf16[1,2,256,256]{3,2,1,0:T(8,128)(2,1)} %refs_0_.1), channel_id=1, source_target_pairs={{0,8},{4,12},{8,0},{12,4},{16,24},{20,28},{24,16},{28,20},{1,9},{5... | collective-permute-start | bytes 786440 | tf_op jit(solution)/shard_map/ppermute | solution.py:232
  5.2 4.6 %collective-permute-start.1 = (s32[4,256]{1,0:T(4,128)S(1)}, s32[4,256]{1,0:T(4,128)S(1)}, u32[]{:S(2)}, u32[]{:S(2)}) collective-permute-start(s32[4,256]{1,0:T(4,128)S(1)} %pad_add_fusion), channel_id=1, source_target_pairs={{0,2},{1,3},{2,0},{3,1},{4,6},{5,7},{6,4},{7,5},{8,10},{9,11},{10,... | collective-permute-start | bytes 12296 | tf_op jit(solution)/shard_map/ppermute | solution.py:23
  9.8 0.6 %copy-start.5 = (s32[4,256]{1,0:T(4,128)}, s32[4,256]{1,0:T(4,128)S(1)}, u32[]{:S(2)}) copy-start(s32[4,256]{1,0:T(4,128)S(1)} %collective-permute-done.1.refs_4_.refs_5_.refs_3_) | copy-start | bytes 12292
  9.8 0.7 %copy-start.4 = (bf16[1,2,256,256]{3,2,1,0:T(8,128)(2,1)}, bf16[1,2,256,256]{3,2,1,0:T(8,128)(2,1)S(1)}, u32[]{:S(2)}) copy-start(bf16[1,2,256,256]{3,2,1,0:T(8,128)(2,1)S(1)} %collective-permute-done.refs_1_) | copy-start | bytes 786436
  15.8 1.5 %copy-start = (bf16[1,2,256,256]{3,2,1,0:T(8,128)(2,1)}, bf16[1,2,256,256]{3,2,1,0:T(8,128)(2,1)S(1)}, u32[]{:S(2)}) copy-start(bf16[1,2,256,256]{3,2,1,0:T(8,128)(2,1)S(1)} %collective-permute-done.2.refs_0_) | copy-start | bytes 786436
  15.8 1.5 %copy-start.1 = (bf16[1,2,256,256]{3,2,1,0:T(8,128)(2,1)}, bf16[1,2,256,256]{3,2,1,0:T(8,128)(2,1)S(1)}, u32[]{:S(2)}) copy-start(bf16[1,2,256,256]{3,2,1,0:T(8,128)(2,1)S(1)} %collective-permute-done.4.refs_2_) | copy-start | bytes 786436
  17.1 0.7 %copy-start.2 = (bf16[1,2,256,256]{3,2,1,0:T(8,128)(2,1)}, bf16[1,2,256,256]{3,2,1,0:T(8,128)(2,1)S(1)}, u32[]{:S(2)}) copy-start(bf16[1,2,256,256]{3,2,1,0:T(8,128)(2,1)S(1)} %collective-permute-done.3.refs_1_) | copy-start | bytes 786436
  17.2 5.4 %collective-permute-start.5 = (bf16[3,2,256,256]{3,2,1,0:T(8,128)(2,1)S(1)}, bf16[3,2,256,256]{3,2,1,0:T(8,128)(2,1)S(1)}, u32[]{:S(2)}, u32[]{:S(2)}) collective-permute-start(bf16[3,2,256,256]{3,2,1,0:T(8,128)(2,1)S(1)} %pad_maximum_fusion), channel_id=1, source_target_pairs={{0,4},{4,0},{8,12},{12,8},{16,20},{20,16},{24,28},{28,24},{1,5},{5... | collective-permute-start | bytes 2359304 | tf_op jit(solution)/shard_map/ppermute | solution.py:242
  22.6 0.9 %copy-start.3 = (bf16[3,2,256,256]{3,2,1,0:T(8,128)(2,1)}, bf16[3,2,256,256]{3,2,1,0:T(8,128)(2,1)S(1)}, u32[]{:S(2)}) copy-start(bf16[3,2,256,256]{3,2,1,0:T(8,128)(2,1)S(1)} %collective-permute-done.5.refs_0_) | copy-start | bytes 2359300

commit v19 on v16

--- a/solution.py
+++ b/solution.py
@@ -45,7 +45,7 @@
 
 
 def add_walkers(blocks, sel_ref, acc_ref, slots, width, finish=None):
-    sel = sel_ref[...]
+    sel = sel_ref[0:2 * slots * width]
     terms = []
     for g_ref, k in blocks:
         g_re = g_ref[k, 0]
@@ -107,6 +107,8 @@
         cols = columns()
         for t in range(nt):
             sel_ref[t * width:(t + 1) * width] = (cols[:, t:t + 1] == lanes).astype(BF16)
+        if final:
+            sel_ref[nt * width:(nt + 1) * width] = (cols[:, nt:nt + 1] == lanes).astype(BF16)
 
     out_copies = []
 
@@ -136,8 +138,7 @@
             return
         if has_prior:
             pltpu.make_async_copy(prior_hbm, prior_ref, sem).wait()
-        cols = columns()
-        q = (cols[:, nt:nt + 1] == lanes).astype(BF16)
+        q = sel_ref[nt * width:(nt + 1) * width]
         sent = []
         far = far_ref[...]
         partner = [jnp.where(slot_ref[s] == 0, far[2:3], far[3:4]) for s in range(slots)]
@@ -192,7 +193,7 @@
         pl.BlockSpec(memory_space=pltpu.SMEM),
         full(cj.shape),
     ]
-    scratch = [pltpu.VMEM(acc_shape, F32), pltpu.VMEM((2 * slots * width, width), BF16)]
+    scratch = [pltpu.VMEM(acc_shape, F32), pltpu.VMEM(((2 * slots + 1) * width, width), BF16)]
     operands = list(walkers) + [ti, ph, far, slot, cj]
     if has_prior:
         in_specs.append(pl.BlockSpec(memory_space=pl.ANY))

time: 29.4 us -> 29.2 us (level)
  transfers between devices with their start and end apart: 6 -> 6, of which waited for: 3 -> 3; matrix products, arithmetic and copies ran while one was open for 2% -> 2% of each run, Pallas kernels for 29% -> 30%
where the time goes in v19:
time: 29.2 us; the launch traced here: 29 us
  Pallas kernels  14.1 us (48%)
  starting transfers between devices  7.6 us (26%)
  waiting for transfers between devices  4.28 us (15%)
  local copies, waits for them, and re-layouts  2.1 us (7%)
  other arithmetic  0.79 us (3%)
    pallas_call x3, Pallas kernels, accumulate(): pl.pallas_call(kernel, grid=(1,), cost_estimate=pl.CostEstimate(flops=flo...  14.1 us
    ppermute x3, starting transfers between devices, local(): lax.ppermute(greens, 'blk', [(i, i ^ 2 * m) for i in range(blocks)])  4.05 us
    ppermute x1, starting transfers between devices, passed_along(): lax.ppermute(value, axis, [(i, (i + by) % size) for i in range(size)])  3.02 us
    ppermute x3, waiting for transfers between devices, local(): lax.ppermute(greens, 'blk', [(i, i ^ 2 * m) for i in range(blocks)])  2.69 us
    unnamed x12, local copies, waits for them, and re-layouts  2.1 us
    ppermute x1, waiting for transfers between devices, passed_along(): lax.ppermute(value, axis, [(i, (i + by) % size) for i in range(size)])  1.58 us
    concatenate x1, other arithmetic, local(): jnp.concatenate([transfer_index, phase_index], axis=0)  0.71 us
  transfers between devices with their start and end apart: 6, of which 3 were waited for; matrix products, arithmetic and copies ran while one was open for 2% of the time, Pallas kernels for 30%

profile of v19, /device:TPU:0, one launch (start us, length us, event | category | flops | bytes accessed | tf_op | source)
XLA Modules:
  0.0 29.0 jit_solution(11618772710197597968)
XLA Ops:
  0.0 0.5 %collective-permute-start = (bf16[1,2,256,256]{3,2,1,0:T(8,128)(2,1)}, bf16[1,2,256,256]{3,2,1,0:T(8,128)(2,1)S(1)}, u32[]{:S(2)}, u32[]{:S(2)}) collective-permute-start(bf16[1,2,256,256]{3,2,1,0:T(8,128)(2,1)} %refs_0_.1), channel_id=1, source_target_pairs={{0,4},{4,0},{8,12},{12,8},{16,20},{20,16},{24,28},{28,24},{1,5},{5... | collective-permute-start | bytes 786440 | tf_op jit(solution)/shard_map/ppermute | solution.py:230
  0.5 2.5 %collective-permute-start.2 = (bf16[1,2,256,256]{3,2,1,0:T(8,128)(2,1)}, bf16[1,2,256,256]{3,2,1,0:T(8,128)(2,1)S(1)}, u32[]{:S(2)}, u32[]{:S(2)}) collective-permute-start(bf16[1,2,256,256]{3,2,1,0:T(8,128)(2,1)} %refs_0_.1), channel_id=1, source_target_pairs={{0,16},{4,20},{8,24},{12,28},{16,0},{20,4},{24,8},{28,12},{1,17},{... | collective-permute-start | bytes 786440 | tf_op jit(solution)/shard_map/ppermute | solution.py:231
  3.0 1.4 %collective-permute-start.4 = (bf16[1,2,256,256]{3,2,1,0:T(8,128)(2,1)}, bf16[1,2,256,256]{3,2,1,0:T(8,128)(2,1)S(1)}, u32[]{:S(2)}, u32[]{:S(2)}) collective-permute-start(bf16[1,2,256,256]{3,2,1,0:T(8,128)(2,1)} %refs_0_.1), channel_id=1, source_target_pairs={{0,24},{4,28},{8,16},{12,20},{16,8},{20,12},{24,0},{28,4},{1,25},{... | collective-permute-start | bytes 786440 | tf_op jit(solution)/shard_map/ppermute | solution.py:231
  4.4 0.1 collective-permute-start.3
  4.5 0.7 %pad_add_fusion = s32[4,256]{1,0:T(4,128)S(1)} fusion(s32[2,256]{1,0:T(2,128)} %refs_2_.3, s32[2,256]{1,0:T(2,128)} %refs_1_.1), kind=kLoop, calls=%fused_computation.1 | loop fusion | flops 1024 | bytes 8192 | tf_op jit(solution)/shard_map/concatenate | solution.py:232
  5.2 3.0 %collective-permute-start.1 = (s32[4,256]{1,0:T(4,128)S(1)}, s32[4,256]{1,0:T(4,128)S(1)}, u32[]{:S(2)}, u32[]{:S(2)}) collective-permute-start(s32[4,256]{1,0:T(4,128)S(1)} %pad_add_fusion), channel_id=1, source_target_pairs={{0,2},{1,3},{2,0},{3,1},{4,6},{5,7},{6,4},{7,5},{8,10},{9,11},{10,... | collective-permute-start | bytes 12296 | tf_op jit(solution)/shard_map/ppermute | solution.py:23
  8.2 1.6 %collective-permute-done.1.refs_4_.refs_5_.refs_3_ = s32[4,256]{1,0:T(4,128)S(1)} collective-permute-done((s32[4,256]{1,0:T(4,128)S(1)}, s32[4,256]{1,0:T(4,128)S(1)}, u32[]{:S(2)}, u32[]{:S(2)}) %collective-permute-start.1) | collective-permute-done | bytes 4128 | tf_op jit(solution)/shard_map/ppermute | solution.py:23
  9.8 0.0 copy-start.5
  9.8 0.0 collective-permute-done.refs_1_
  9.8 0.0 copy-start.4
  9.8 0.6 %copy-done.5 = s32[4,256]{1,0:T(4,128)} copy-done((s32[4,256]{1,0:T(4,128)}, s32[4,256]{1,0:T(4,128)S(1)}, u32[]{:S(2)}) %copy-start.5) | copy-done | bytes 4120
  10.4 0.1 copy-done.4
  10.5 3.8 %shard_map.55.refs_8_ = f32[4,2,256,256]{3,2,1,0:T(8,128)} custom-call(bf16[1,2,256,256]{3,2,1,0:T(8,128)(2,1)} %refs_0_.1, bf16[1,2,256,256]{3,2,1,0:T(8,128)(2,1)} %copy-done.4, s32[2,256]{1,0:T(2,128)} %refs_1_.1, s32[2,256]{1,0:T(2,128)} %refs_2_.3, s32[4,256]{1,0:T(4,128)} %copy-done.5, s32[2]{0:T(128)} %refs_4_.3, s32[1,256]{1,0:T(1,128)} %bitcast.1), custom_call_target="tpu_custom_call" | custom-call | flops 1073741824 | bytes 2621440 | tf_op jit(solution)/shard_map/pallas_call | solution.py:205
  14.4 1.4 %collective-permute-done.2.refs_0_ = bf16[1,2,256,256]{3,2,1,0:T(8,128)(2,1)S(1)} collective-permute-done((bf16[1,2,256,256]{3,2,1,0:T(8,128)(2,1)}, bf16[1,2,256,256]{3,2,1,0:T(8,128)(2,1)S(1)}, u32[]{:S(2)}, u32[]{:S(2)}) %collective-permute-start.2) | collective-permute-done | bytes 262176 | tf_op jit(solution)/shard_map/ppermute | solution.py:231
  15.8 0.0 copy-start
  15.8 0.0 collective-permute-done.4.refs_2_
  15.8 0.0 copy-start.1
  15.8 1.3 %collective-permute-done.3.refs_1_ = bf16[1,2,256,256]{3,2,1,0:T(8,128)(2,1)S(1)} collective-permute-done((bf16[1,2,256,256]{3,2,1,0:T(8,128)(2,1)}, bf16[1,2,256,256]{3,2,1,0:T(8,128)(2,1)S(1)}, u32[]{:S(2)}, u32[]{:S(2)}) %collective-permute-start.3) | collective-permute-done | bytes 262176 | tf_op jit(solution)/shard_map/ppermute | solution.py:231
  17.1 0.0 copy-start.2
  17.1 0.1 pad_maximum_fusion
  17.2 0.1 collective-permute-start.5
  17.2 0.0 copy-done
  17.2 0.0 copy-done.1
  17.3 0.5 %copy-done.2 = bf16[1,2,256,256]{3,2,1,0:T(8,128)(2,1)} copy-done((bf16[1,2,256,256]{3,2,1,0:T(8,128)(2,1)}, bf16[1,2,256,256]{3,2,1,0:T(8,128)(2,1)S(1)}, u32[]{:S(2)}) %copy-start.2) | copy-done | bytes 262168
  17.8 4.8 %shard_map.56.refs_6_ = f32[4,2,256,256]{3,2,1,0:T(8,128)} custom-call(bf16[1,2,256,256]{3,2,1,0:T(8,128)(2,1)} %copy-done, bf16[1,2,256,256]{3,2,1,0:T(8,128)(2,1)} %copy-done.2, bf16[1,2,256,256]{3,2,1,0:T(8,128)(2,1)} %copy-done.1, s32[2,256]{1,0:T(2,128)} %refs_1_.1, s32[2,256]{1,0:T(2,128)} %refs_2_.3, s32[4,256]{1,0:T(4,128)} %copy-done.5, s32[2]{0:T(128)} %refs_4_.3, ...), custom_call_target="tpu_custom_call" | custom-call | flops 1610612736 | bytes 4980736 | tf_op jit(solution)/shard_map/pallas_call | solution.py:205
  22.5 0.0 collective-permute-done.5.refs_0_
  22.5 0.0 copy-start.3
  22.6 0.9 %copy-done.3 = bf16[3,2,256,256]{3,2,1,0:T(8,128)(2,1)} copy-done((bf16[3,2,256,256]{3,2,1,0:T(8,128)(2,1)}, bf16[3,2,256,256]{3,2,1,0:T(8,128)(2,1)S(1)}, u32[]{:S(2)}) %copy-start.3) | copy-done | bytes 786456
  23.4 5.6 %shard_map.57 = f32[2,2,256,256]{3,2,1,0:T(8,128)} custom-call(bf16[3,2,256,256]{3,2,1,0:T(8,128)(2,1)} %copy-done.3, s32[2,256]{1,0:T(2,128)} %refs_1_.1, s32[2,256]{1,0:T(2,128)} %refs_2_.3, s32[4,256]{1,0:T(4,128)} %copy-done.5, s32[2]{0:T(128)} %refs_4_.3, s32[1,256]{1,0:T(1,128)} %bitcast.3, f32[4,2,256,256]{3,2,1,0:T(8,128)} %shard_map.56.refs_6_), custom_call_target="tpu_custom_call" | custom-call | flops 2147483648 | bytes 3932160 | tf_op jit(solution)/shard_map/pallas_call | solution.py:205
Async XLA Ops:
  0.0 9.8 %collective-permute-start = (bf16[1,2,256,256]{3,2,1,0:T(8,128)(2,1)}, bf16[1,2,256,256]{3,2,1,0:T(8,128)(2,1)S(1)}, u32[]{:S(2)}, u32[]{:S(2)}) collective-permute-start(bf16[1,2,256,256]{3,2,1,0:T(8,128)(2,1)} %refs_0_.1), channel_id=1, source_target_pairs={{0,4},{4,0},{8,12},{12,8},{16,20},{20,16},{24,28},{28,24},{1,5},{5... | collective-permute-start | bytes 786440 | tf_op jit(solution)/shard_map/ppermute | solution.py:230
  0.5 15.3 %collective-permute-start.2 = (bf16[1,2,256,256]{3,2,1,0:T(8,128)(2,1)}, bf16[1,2,256,256]{3,2,1,0:T(8,128)(2,1)S(1)}, u32[]{:S(2)}, u32[]{:S(2)}) collective-permute-start(bf16[1,2,256,256]{3,2,1,0:T(8,128)(2,1)} %refs_0_.1), channel_id=1, source_target_pairs={{0,16},{4,20},{8,24},{12,28},{16,0},{20,4},{24,8},{28,12},{1,17},{... | collective-permute-start | bytes 786440 | tf_op jit(solution)/shard_map/ppermute | solution.py:231
  3.0 12.8 %collective-permute-start.4 = (bf16[1,2,256,256]{3,2,1,0:T(8,128)(2,1)}, bf16[1,2,256,256]{3,2,1,0:T(8,128)(2,1)S(1)}, u32[]{:S(2)}, u32[]{:S(2)}) collective-permute-start(bf16[1,2,256,256]{3,2,1,0:T(8,128)(2,1)} %refs_0_.1), channel_id=1, source_target_pairs={{0,24},{4,28},{8,16},{12,20},{16,8},{20,12},{24,0},{28,4},{1,25},{... | collective-permute-start | bytes 786440 | tf_op jit(solution)/shard_map/ppermute | solution.py:231
  4.4 12.7 %collective-permute-start.3 = (bf16[1,2,256,256]{3,2,1,0:T(8,128)(2,1)}, bf16[1,2,256,256]{3,2,1,0:T(8,128)(2,1)S(1)}, u32[]{:S(2)}, u32[]{:S(2)}) collective-permute-start(bf16[1,2,256,256]{3,2,1,0:T(8,128)(2,1)} %refs_0_.1), channel_id=1, source_target_pairs={{0,8},{4,12},{8,0},{12,4},{16,24},{20,28},{24,16},{28,20},{1,9},{5... | collective-permute-start | bytes 786440 | tf_op jit(solution)/shard_map/ppermute | solution.py:231
  5.2 4.6 %collective-permute-start.1 = (s32[4,256]{1,0:T(4,128)S(1)}, s32[4,256]{1,0:T(4,128)S(1)}, u32[]{:S(2)}, u32[]{:S(2)}) collective-permute-start(s32[4,256]{1,0:T(4,128)S(1)} %pad_add_fusion), channel_id=1, source_target_pairs={{0,2},{1,3},{2,0},{3,1},{4,6},{5,7},{6,4},{7,5},{8,10},{9,11},{10,... | collective-permute-start | bytes 12296 | tf_op jit(solution)/shard_map/ppermute | solution.py:23
  9.8 0.6 %copy-start.5 = (s32[4,256]{1,0:T(4,128)}, s32[4,256]{1,0:T(4,128)S(1)}, u32[]{:S(2)}) copy-start(s32[4,256]{1,0:T(4,128)S(1)} %collective-permute-done.1.refs_4_.refs_5_.refs_3_) | copy-start | bytes 12292
  9.8 0.7 %copy-start.4 = (bf16[1,2,256,256]{3,2,1,0:T(8,128)(2,1)}, bf16[1,2,256,256]{3,2,1,0:T(8,128)(2,1)S(1)}, u32[]{:S(2)}) copy-start(bf16[1,2,256,256]{3,2,1,0:T(8,128)(2,1)S(1)} %collective-permute-done.refs_1_) | copy-start | bytes 786436
  15.8 1.5 %copy-start = (bf16[1,2,256,256]{3,2,1,0:T(8,128)(2,1)}, bf16[1,2,256,256]{3,2,1,0:T(8,128)(2,1)S(1)}, u32[]{:S(2)}) copy-start(bf16[1,2,256,256]{3,2,1,0:T(8,128)(2,1)S(1)} %collective-permute-done.2.refs_0_) | copy-start | bytes 786436
  15.8 1.5 %copy-start.1 = (bf16[1,2,256,256]{3,2,1,0:T(8,128)(2,1)}, bf16[1,2,256,256]{3,2,1,0:T(8,128)(2,1)S(1)}, u32[]{:S(2)}) copy-start(bf16[1,2,256,256]{3,2,1,0:T(8,128)(2,1)S(1)} %collective-permute-done.4.refs_2_) | copy-start | bytes 786436
  17.1 0.7 %copy-start.2 = (bf16[1,2,256,256]{3,2,1,0:T(8,128)(2,1)}, bf16[1,2,256,256]{3,2,1,0:T(8,128)(2,1)S(1)}, u32[]{:S(2)}) copy-start(bf16[1,2,256,256]{3,2,1,0:T(8,128)(2,1)S(1)} %collective-permute-done.3.refs_1_) | copy-start | bytes 786436
  17.2 5.4 %collective-permute-start.5 = (bf16[3,2,256,256]{3,2,1,0:T(8,128)(2,1)S(1)}, bf16[3,2,256,256]{3,2,1,0:T(8,128)(2,1)S(1)}, u32[]{:S(2)}, u32[]{:S(2)}) collective-permute-start(bf16[3,2,256,256]{3,2,1,0:T(8,128)(2,1)S(1)} %pad_maximum_fusion), channel_id=1, source_target_pairs={{0,4},{4,0},{8,12},{12,8},{16,20},{20,16},{24,28},{28,24},{1,5},{5... | collective-permute-start | bytes 2359304 | tf_op jit(solution)/shard_map/ppermute | solution.py:241
  22.5 0.9 %copy-start.3 = (bf16[3,2,256,256]{3,2,1,0:T(8,128)(2,1)}, bf16[3,2,256,256]{3,2,1,0:T(8,128)(2,1)S(1)}, u32[]{:S(2)}) copy-start(bf16[3,2,256,256]{3,2,1,0:T(8,128)(2,1)S(1)} %collective-permute-done.5.refs_0_) | copy-start | bytes 2359300
